TPU v7x, 32 devices: a whole 2x2x4 slice. The times are simulated.
32 devices in a mesh: grp: 2 (over y), seq: 4 (over z), mdl: 4 (over x, core).
Axes of the slice: x: 2, y: 2, z: 4, core: 2. Of those that a mesh axis runs over, the one named last changes fastest.
Arguments:
- query_proj: bfloat16 [2048, 4096], P(('grp', 'seq'), 'mdl'), parts along dimension 0, may hold values from -12 to 12, as said below
- key_proj: bfloat16 [2048, 4096], P(('grp', 'seq'), 'mdl'), parts along dimension 0, may hold values from -6 to 6
- value_proj: bfloat16 [2048, 4096], P(('grp', 'seq'), 'mdl'), parts along dimension 0, may hold values from -12 to 12, as said below
- gate_proj: bfloat16 [2048, 4096], P(('grp', 'seq'), 'mdl'), parts along dimension 0, may hold values from -6 to 6
- log_decay: float32 [32, 2048], P('mdl', ('grp', 'seq')), parts along dimension 1, may hold values from -2 to 0, as said below
- act_exponent: int32 [3, 4096], P(None, 'mdl'), may hold values from -5 to -2
- norm_gain: float32 [4096], P('mdl'), may hold values from 0.1 to 1.9
- out_weight: bfloat16 [4096, 6144], P('seq', 'mdl'), may hold values from -0.09375 to 0.09375
- weight_exponent: int32 [6144], P('mdl'), may hold values from -12 to -9
Outputs:
- layer_out: bfloat16 [2048, 6144], P(('grp', 'seq'), 'mdl'), parts along dimension 0
There are 2 independent parts, one for each index of `grp`. A program takes and returns all parts, laid end to end along the dimension named above; an argument that names none is the same for every part. Nothing has to cross between parts.
Inputs may be any that keep to these rules, and one draw needn't show every extreme that they name: Rows of query_proj differ in scale. Columns of value_proj differ in scale. `log_decay`: negative everywhere.
All inputs are finite; a program needn't handle non-finite values.
Results may differ from a plain program's by a relative error of at most 0.0062.
Values may be sent and summed in bfloat16 or wider, within the bound.
No kernel may reach another device: no remote copies, remote signals or barrier semaphores. Data moves between devices by JAX's collectives and lax.ppermute only.
A program may use at most 64 MiB of HBM per device.

v0:
```python
import jax
import jax.numpy as jnp
from jax import lax
from jax.sharding import PartitionSpec as P

HDIM = 128
BLK = 256


def power_two(exponent):
    result = jnp.zeros(exponent.shape, jnp.float32)
    for exponent_value in range(-16, 0):
        result = result + jnp.where(exponent == exponent_value, 2.0**exponent_value, 0.0)
    return result


def fake_quant(matrix, exponent):
    scale = power_two(exponent)
    levels = jnp.clip(jnp.floor(matrix.astype(jnp.float32) / scale + 0.5), -127.0, 127.0)
    return (levels * scale).astype(jnp.bfloat16)


def per_device(
    query_proj,
    key_proj,
    value_proj,
    gate_proj,
    log_decay,
    act_exponent,
    norm_gain,
    out_weight,
    weight_exponent,
):
    weights = fake_quant(out_weight, weight_exponent[None, :])
    panels = lax.all_gather(weights, "seq", axis=0, tiled=True)
    tok_rows = query_proj.shape[0]
    heads_here = log_decay.shape[0]
    nblocks = tok_rows // BLK
    queries = fake_quant(query_proj, act_exponent[0][None, :])
    keys_quant = fake_quant(key_proj, act_exponent[1][None, :])
    values = fake_quant(value_proj, act_exponent[2][None, :]).reshape(
        nblocks, BLK, heads_here, HDIM
    )
    query_feat = (
        jax.nn.silu(queries.astype(jnp.float32))
        .astype(jnp.bfloat16)
        .reshape(nblocks, BLK, heads_here, HDIM)
    )
    key_feat = (
        jax.nn.silu(keys_quant.astype(jnp.float32))
        .astype(jnp.bfloat16)
        .reshape(nblocks, BLK, heads_here, HDIM)
    )
    decay_cum = jnp.cumsum(log_decay.reshape(heads_here, nblocks, BLK), axis=2)
    block_total = decay_cum[:, :, -1]
    scores = jnp.einsum("bihd,bjhd->hbij", query_feat, key_feat, preferred_element_type=jnp.float32)
    decay_gap = decay_cum[:, :, :, None] - decay_cum[:, :, None, :]
    causal_mask = jnp.arange(BLK)[:, None] >= jnp.arange(BLK)[None, :]
    decay_mask = jnp.where(causal_mask, jnp.exp(jnp.minimum(decay_gap, 0.0)), 0.0)
    block_probs = (scores * decay_mask).astype(jnp.bfloat16)
    within_block = jnp.einsum(
        "hbij,bjhd->bihd", block_probs, values, preferred_element_type=jnp.float32
    )
    tail_decay = jnp.transpose(jnp.exp(block_total[:, :, None] - decay_cum), (1, 2, 0))
    weighted = (key_feat.astype(jnp.float32) * tail_decay[..., None]).astype(jnp.bfloat16)
    block_states = jnp.einsum(
        "bjhd,bjhe->bhde", weighted, values, preferred_element_type=jnp.float32
    )
    block_gain = jnp.exp(block_total).T

    def advance(carried, inputs):
        gain_here, state_here = inputs
        return (gain_here[:, None, None] * carried + state_here, carried)

    local_end, entry_local = lax.scan(
        advance, jnp.zeros((heads_here, HDIM, HDIM), jnp.float32), (block_gain, block_states)
    )
    device_log = jnp.sum(block_total, axis=1)
    gathered_logs, gathered_states = (
        lax.all_gather(device_log[None], "seq", axis=0, tiled=True),
        lax.all_gather(local_end[None], "seq", axis=0, tiled=True),
    )
    position = lax.axis_index("seq")
    end_offsets = jnp.cumsum(gathered_logs, axis=0)
    start_offsets = end_offsets - gathered_logs
    own_start = lax.dynamic_index_in_dim(start_offsets, position, 0, keepdims=False)
    earlier = jnp.arange(gathered_logs.shape[0])[:, None] < position
    state_weight = jnp.where(
        earlier, jnp.exp(jnp.minimum(own_start[None, :] - end_offsets, 0.0)), 0.0
    )
    incoming = jnp.einsum(
        "nh,nhde->hde", state_weight, gathered_states, precision=lax.Precision.HIGHEST
    )
    before = jnp.cumsum(block_total, axis=1) - block_total
    entry_state = entry_local + jnp.exp(before).T[:, :, None, None] * incoming[None]
    from_state = jnp.einsum(
        "bihd,bhde->bihe",
        query_feat.astype(jnp.float32),
        entry_state,
        precision=lax.Precision.HIGHEST,
    )
    position_decay = jnp.transpose(jnp.exp(decay_cum), (1, 2, 0))[..., None]
    attended = within_block + position_decay * from_state
    mean_square = jnp.mean(attended * attended, axis=-1, keepdims=True)
    normed = (attended * lax.rsqrt(mean_square + 1e-05)).reshape(tok_rows, heads_here * HDIM)
    attn = (normed * norm_gain[None, :] * jax.nn.sigmoid(gate_proj.astype(jnp.float32))).astype(
        jnp.bfloat16
    )
    result = jnp.dot(
        lax.all_gather(attn, "mdl", axis=1, tiled=True), panels, preferred_element_type=jnp.float32
    )
    return result.astype(jnp.bfloat16)


def solution(mesh):
    in_specs = (
        P(("grp", "seq"), "mdl"),
        P(("grp", "seq"), "mdl"),
        P(("grp", "seq"), "mdl"),
        P(("grp", "seq"), "mdl"),
        P("mdl", ("grp", "seq")),
        P(None, "mdl"),
        P("mdl"),
        P("seq", "mdl"),
        P("mdl"),
    )
    out_specs = P(("grp", "seq"), "mdl")
    return jax.shard_map(
        per_device, mesh=mesh, in_specs=in_specs, out_specs=out_specs, check_vma=False
    )
```

profile of v0, /device:TPU:0, one launch (start us, length us, event | category | flops | bytes accessed | tf_op | source)
XLA Modules:
  0.0 324.8 jit_solution(14562951297802620466)
XLA Ops:
  6.5 1.2 reduce-window.6
  7.8 0.2 slice_reduce_fusion
  8.0 0.1 exponential_bitcast_fusion.1
  8.1 0.2 multiply_reduce_fusion.2
  8.3 0.1 exponential_bitcast_fusion
  8.3 1.0 fusion.45
  9.3 1.4 fusion.11
  10.8 0.2 copy.49
  11.0 2.4 convolution_add_fusion
  13.4 0.0 all-gather.10.cloned.1.call-update
  13.4 0.0 all-gather.6.cloned.1.call-start
  13.5 0.6 dynamic-slice.1
  14.7 0.2 dynamic-update-slice
  15.0 13.6 %all-reduce = f32[32]{0:T(128)S(1)} all-reduce(f32[32]{0:T(128)S(1)} %dynamic-update-slice), channel_id=2, replica_groups=mesh['grp'=2,'seq'=4,'mdl'=4] {'seq'}, use_global_device_ids=true, to_apply=%add | all-reduce | flops 32 | bytes 256
  28.6 0.1 reshape.291
  28.8 0.1 select_bitcast_fusion
  28.9 0.1 bitcast_add_fusion.1
  28.9 1.4 fusion.1
  30.3 32.0 %all-gather.10.cloned.1.call-done = f32[32,128,128]{2,1,0:T(8,128)} async-done(((f32[8,128,128]{2,1,0:T(8,128)}), f32[32,128,128]{2,1,0:T(8,128)}) %all-gather.10.cloned.1.call-update) | async-done | bytes 2097168 | tf_op jit(solution)/shard_map/all_gather | solution.py:81
  62.3 1.9 multiply_reduce_fusion
  64.2 0.2 copy.47
  64.4 1.0 multiply_reduce_fusion.1
  65.5 0.1 broadcast_multiply_fusion
  65.6 0.3 copy.40
  65.9 0.6 copy-done
  66.5 1.1 multiply_convert_fusion.2
  67.6 0.0 all-gather.6.cloned.1.call-update
  67.6 0.0 all-gather.8.cloned.1.call-start
  67.7 4.1 %multiply_convert_fusion = bf16[1024,1536]{1,0:T(8,128)(2,1)} fusion(bf16[1024,1536]{1,0:T(8,128)(2,1)} %param.16, f32[1536]{0:T(1024)S(1)} %select_add_fusion), kind=kLoop, calls=%fused_computation | loop fusion | flops 11010048 | bytes 6297600 | tf_op jit(solution)/shard_map/convert_element_type | solution.py:20
  71.8 17.2 %all-gather.6.cloned.1.call-done = bf16[256,4096]{1,0:T(8,128)(2,1)} async-done(((bf16[256,1024]{1,0:T(8,128)(2,1)}), bf16[256,4096]{1,0:T(8,128)(2,1)}) %all-gather.6.cloned.1.call-update) | async-done | bytes 2097168 | tf_op jit(solution)/shard_map/all_gather | solution.py:110
  89.0 219.8 %all-gather.8.cloned.1.call-done = bf16[4096,1536]{1,0:T(8,128)(2,1)} async-done(((bf16[1024,1536]{1,0:T(8,128)(2,1)}), bf16[4096,1536]{1,0:T(8,128)(2,1)}) %all-gather.8.cloned.1.call-update) | async-done | bytes 12582928 | tf_op jit(solution)/shard_map/all_gather | solution.py:35
  308.8 9.5 %convolution_convert_fusion = bf16[256,1536]{1,0:T(8,128)(2,1)} fusion(bf16[256,4096]{1,0:T(8,128)(2,1)} %all-gather.6.cloned.1.call-done, bf16[4096,1536]{1,0:T(8,128)(2,1)} %all-gather.8.cloned.1.call-done), kind=kOutput, calls=%fused_computation.1 | convolution fusion | flops 3221618688 | bytes 15466496 | tf_op jit(solution)/shard_map/dot_general | solution.py:109
  (24 shorter events, 0.2 us)
Async XLA Ops:
  6.5 55.8 %all-gather.10.cloned.1.call-start = ((), (), s32[]{:S(2)}) async-start(), calls=%async_computation.2 | async-start | bytes 2621440 | tf_op jit(solution)/shard_map/all_gather | solution.py:81
  11.0 2.5 copy-start.5
  11.0 17.9 %copy-start.3 = (bf16[256,1024]{1,0:T(8,128)(2,1)S(1)}, bf16[256,1024]{1,0:T(8,128)(2,1)}, u32[]{:S(2)}) copy-start(bf16[256,1024]{1,0:T(8,128)(2,1)} %param.11) | copy-start | bytes 1572868
  11.0 17.9 %copy-start.4 = (bf16[256,1024]{1,0:T(8,128)(2,1)S(1)}, bf16[256,1024]{1,0:T(8,128)(2,1)}, u32[]{:S(2)}) copy-start(bf16[256,1024]{1,0:T(8,128)(2,1)} %param.9) | copy-start | bytes 1572868
  13.4 75.6 %all-gather.6.cloned.1.call-start = ((), (), s32[]{:S(2)}) async-start(), calls=%async_computation | async-start | bytes 2621440 | tf_op jit(solution)/shard_map/all_gather | solution.py:110
  65.4 1.0 copy-start
  65.4 1.0 copy-start.2
  65.5 2.2 copy-start.1
  67.6 241.2 %all-gather.8.cloned.1.call-start = ((), (), s32[]{:S(2)}) async-start(), calls=%async_computation.1 | async-start | bytes 15728640 | tf_op jit(solution)/shard_map/all_gather | solution.py:35
Sparse Core Ops, SparseCore 0:
  13.6 48.6 all-gather.9
  67.7 21.2 all-gather.5
  90.6 218.2 all-gather.7
where the time goes:
time: 325 us
  waiting for transfers between devices  269 us (83%)
  matrix products  14.3 us (4%)
  between operations  13.9 us (4%)
  blocking collectives  13.6 us (4%)
  other arithmetic  11.5 us (4%)
    all_gather x1, waiting for transfers between devices, per_device(): panels = lax.all_gather(weights, 'seq', axis=0, tiled=True)  220 us
    all_gather x1, waiting for transfers between devices, per_device(): lax.all_gather(local_end[None], 'seq', axis=0, tiled=True)  32 us
    all_gather x1, waiting for transfers between devices, per_device(): lax.all_gather(attn, 'mdl', axis=1, tiled=True)  17.2 us
    unnamed x1, blocking collectives  13.6 us
    dot_general x1, matrix products, per_device(): jnp.dot(lax.all_gather(attn, 'mdl', axis=1, tiled=True), panels, preferre...  9.5 us
  transfers between devices with their start and end apart: 3, of which 3 were waited for; matrix products, arithmetic and copies ran while one was open for 2% of the time, Pallas kernels for 0%

commit v1 on v0

--- a/solution.py
+++ b/solution.py
@@ -21,6 +21,8 @@
 
 
 def per_device(
+    n_seq,
+    n_mdl,
     query_proj,
     key_proj,
     value_proj,
@@ -32,8 +34,8 @@
     weight_exponent,
 ):
     weights = fake_quant(out_weight, weight_exponent[None, :])
-    panels = lax.all_gather(weights, "seq", axis=0, tiled=True)
     tok_rows = query_proj.shape[0]
+    feat_here = query_proj.shape[1]
     heads_here = log_decay.shape[0]
     nblocks = tok_rows // BLK
     queries = fake_quant(query_proj, act_exponent[0][None, :])
@@ -76,10 +78,16 @@
         advance, jnp.zeros((heads_here, HDIM, HDIM), jnp.float32), (block_gain, block_states)
     )
     device_log = jnp.sum(block_total, axis=1)
-    gathered_logs, gathered_states = (
-        lax.all_gather(device_log[None], "seq", axis=0, tiled=True),
-        lax.all_gather(local_end[None], "seq", axis=0, tiled=True),
+    packed = jnp.concatenate(
+        [
+            local_end.reshape(heads_here, HDIM * HDIM),
+            jnp.broadcast_to(device_log[:, None], (heads_here, HDIM)),
+        ],
+        axis=1,
     )
+    gathered = lax.all_gather(packed, "seq", axis=0, tiled=False)
+    gathered_states = gathered[:, :, : HDIM * HDIM].reshape(n_seq, heads_here, HDIM, HDIM)
+    gathered_logs = gathered[:, :, HDIM * HDIM]
     position = lax.axis_index("seq")
     end_offsets = jnp.cumsum(gathered_logs, axis=0)
     start_offsets = end_offsets - gathered_logs
@@ -106,10 +114,24 @@
     attn = (normed * norm_gain[None, :] * jax.nn.sigmoid(gate_proj.astype(jnp.float32))).astype(
         jnp.bfloat16
     )
-    result = jnp.dot(
-        lax.all_gather(attn, "mdl", axis=1, tiled=True), panels, preferred_element_type=jnp.float32
-    )
-    return result.astype(jnp.bfloat16)
+
+    rows_w = out_weight.shape[0]
+    blocks_here = feat_here // rows_w
+    piece = rows_w // n_mdl
+    x = attn.reshape(tok_rows, blocks_here, n_mdl, piece)
+    x = jnp.transpose(x, (2, 0, 1, 3))
+    x = lax.all_to_all(x, "mdl", 0, 0)
+    x = jnp.transpose(x, (0, 2, 1, 3)).reshape(n_seq, tok_rows, piece)
+    x = lax.all_to_all(x, "seq", 0, 0)
+    x = lax.all_gather(x, "mdl", axis=0, tiled=False)
+    partial = jnp.einsum(
+        "usti,uic->stc",
+        x,
+        weights.reshape(n_mdl, piece, weights.shape[1]),
+        preferred_element_type=jnp.float32,
+    ).astype(jnp.bfloat16)
+    partial = partial.reshape(n_seq * tok_rows, weights.shape[1])
+    return lax.psum_scatter(partial, "seq", scatter_dimension=0, tiled=True)
 
 
 def solution(mesh):
@@ -125,6 +147,12 @@
         P("mdl"),
     )
     out_specs = P(("grp", "seq"), "mdl")
+    n_seq = mesh.shape["seq"]
+    n_mdl = mesh.shape["mdl"]
+
+    def body(*args):
+        return per_device(n_seq, n_mdl, *args)
+
     return jax.shard_map(
-        per_device, mesh=mesh, in_specs=in_specs, out_specs=out_specs, check_vma=False
+        body, mesh=mesh, in_specs=in_specs, out_specs=out_specs, check_vma=False
     )

time: 325 us -> 195 us (0.60)
  waiting for transfers between devices: 269 us -> 125 us
  blocking collectives: 13.6 us -> 29 us
  local copies, waits for them, and re-layouts: 2.43 us -> 7.23 us
  matrix products: 14.3 us -> 9.59 us
    all_gather x3 -> x2, waiting for transfers between devices: 269 us -> 64.6 us  [the longest x1 46.2 us: per_device(): gathered = lax.all_gather(packed, 'seq', axis=0, tiled=False)]
    reduce_scatter x0 -> x1, waiting for transfers between devices: none -> 60.4 us  [per_device(): return lax.psum_scatter(partial, 'seq', scatter_dimension=0, tiled=True)]
    all_to_all x0 -> x2, blocking collectives: none -> 29 us  [the longest x1 17.5 us: per_device(): x = lax.all_to_all(x, 'seq', 0, 0)]
    unnamed x1 -> x0, blocking collectives: 13.6 us -> none
  transfers between devices with their start and end apart: 3 -> 3, of which waited for: 3 -> 3; matrix products, arithmetic and copies ran while one was open for 2% -> 3% of each run, Pallas kernels for 0% -> 0%
where the time goes in v1:
time: 195 us
  waiting for transfers between devices  125 us (64%)
  blocking collectives  29 us (15%)
  between operations  13.3 us (7%)
  other arithmetic  10.3 us (5%)
  matrix products  9.59 us (5%)
  local copies, waits for them, and re-layouts  7.23 us (4%)
    reduce_scatter x1, waiting for transfers between devices, per_device(): return lax.psum_scatter(partial, 'seq', scatter_dimension=0, tiled=True)  60.4 us
    all_gather x1, waiting for transfers between devices, per_device(): gathered = lax.all_gather(packed, 'seq', axis=0, tiled=False)  46.2 us
    all_gather x1, waiting for transfers between devices, per_device(): x = lax.all_gather(x, 'mdl', axis=0, tiled=False)  18.4 us
    all_to_all x1, blocking collectives, per_device(): x = lax.all_to_all(x, 'seq', 0, 0)  17.5 us
    all_to_all x1, blocking collectives, per_device(): x = lax.all_to_all(x, 'mdl', 0, 0)  11.5 us
    dot_general x1, matrix products, per_device(): jnp.einsum('usti,uic->stc', x, weights.reshape(n_mdl, piece, weights.shap...  7.63 us
    unnamed x16, local copies, waits for them, and re-layouts  3.92 us
  transfers between devices with their start and end apart: 3, of which 3 were waited for; matrix products, arithmetic and copies ran while one was open for 3% of the time, Pallas kernels for 0%

profile of v1, /device:TPU:0, one launch (start us, length us, event | category | flops | bytes accessed | tf_op | source)
XLA Modules:
  0.0 194.6 jit_solution(16025454318778253392)
XLA Ops:
  6.5 1.2 reduce-window.6
  7.8 0.2 slice_reduce_fusion.1
  8.0 0.1 exponential_bitcast_fusion.1
  8.1 0.2 multiply_reduce_fusion.1
  8.3 0.1 exponential_bitcast_fusion
  8.3 1.0 fusion.67
  9.3 1.2 copy.39
  10.6 1.2 copy.37
  11.8 0.5 fusion.13
  12.4 0.3 multiply_convert_fusion.5
  12.7 0.3 convolution_bitcast_fusion.1
  13.0 0.3 bitcast_add_fusion
  13.4 0.8 pad_maximum_fusion
  14.3 0.2 copy.38
  14.6 1.0 copy.45
  15.7 0.5 fusion.9
  16.2 0.9 fusion.3
  17.2 46.2 %all-gather.5.cloned.1.call-done = f32[32,16512]{1,0:T(8,128)} async-done(((f32[8,16512]{1,0:T(8,128)}), f32[32,16512]{1,0:T(8,128)}) %all-gather.5.cloned.1.call-update) | async-done | bytes 2113552 | tf_op jit(solution)/shard_map/all_gather | solution.py:88
  63.4 0.8 slice_reduce_fusion
  64.3 1.9 fusion.1
  66.2 0.2 copy.57
  66.4 0.7 multiply_reduce_fusion
  67.2 0.1 broadcast_multiply_fusion
  67.3 0.2 copy-done.1
  67.5 0.3 fusion.15
  67.8 11.5 %all_to_all.10 = bf16[4,256,1,256]{1,3,2,0:T(8,128)(2,1)S(1)} all-to-all(bf16[4,256,1,256]{1,3,2,0:T(8,128)(2,1)S(1)} %bitcast.98), channel_id=1, replica_groups=mesh['grp'=2,'seq'=4,'mdl'=4] {'mdl'}, dimensions={0} | all-to-all | bytes 1048576 | tf_op jit(solution)/shard_map/all_to_all | solution.py:123
  79.3 17.5 %all_to_all.11 = bf16[4,256,256]{1,2,0:T(8,128)(2,1)} all-to-all(bf16[4,256,256]{1,2,0:T(8,128)(2,1)S(1)} %bitcast.95), channel_id=1, replica_groups=mesh['grp'=2,'seq'=4,'mdl'=4] {'seq'}, dimensions={0} | all-to-all | bytes 1048576 | tf_op jit(solution)/shard_map/all_to_all | solution.py:125
  96.8 2.0 %copy.47 = bf16[4,256,256]{2,1,0:T(8,128)(2,1)} copy(bf16[4,256,256]{1,2,0:T(8,128)(2,1)} %all_to_all.11) | data formatting | bytes 1048576 | tf_op jit(solution)/shard_map/all_to_all | solution.py:125
  98.9 2.6 %multiply_convert_fusion = bf16[1024,1536]{1,0:T(8,128)(2,1)} fusion(bf16[1024,1536]{1,0:T(8,128)(2,1)S(1)} %copy-done, f32[1536]{0:T(1024)S(1)} %select_add_fusion), kind=kLoop, calls=%fused_computation.1 | loop fusion | flops 11010048 | bytes 6297600 | tf_op jit(solution)/shard_map/convert_element_type | solution.py:20
  101.6 18.4 %all-gather.7.cloned.1.call-done = bf16[16,256,256]{2,1,0:T(8,128)(2,1)} async-done(((bf16[4,256,256]{2,1,0:T(8,128)(2,1)}), bf16[16,256,256]{2,1,0:T(8,128)(2,1)}) %all-gather.7.cloned.1.call-update) | async-done | bytes 2097168 | tf_op jit(solution)/shard_map/all_gather | solution.py:126
  120.0 7.6 %bitcast_convert_fusion = bf16[4,256,1536]{2,1,0:T(8,128)(2,1)} fusion(bf16[4,4,256,256]{3,2,1,0:T(8,128)(2,1)} %bitcast.104, bf16[4,256,1536,1]{2,1,3,0:T(8,128)(2,1)} %bitcast.88), kind=kOutput, calls=%fused_computation | convolution fusion | flops 3222798336 | bytes 8388608 | tf_op jit(solution)/shard_map/usti,uic->stc/dot_general | solution.py:127
  127.6 60.4 %reduce-scatter.2.cloned.1.call-done = bf16[256,1536]{1,0:T(8,128)(2,1)} async-done(((bf16[1024,1536]{1,0:T(8,128)(2,1)}), bf16[256,1536]{1,0:T(8,128)(2,1)}) %reduce-scatter.2.cloned.1.call-update) | async-done | bytes 786448 | tf_op jit(solution)/shard_map/reduce_scatter | solution.py:134
  (30 shorter events, 0.5 us)
Async XLA Ops:
  6.5 56.9 %all-gather.5.cloned.1.call-start = ((), (), s32[]{:S(2)}) async-start(), calls=%async_computation.4 | async-start | bytes 2641920 | tf_op jit(solution)/shard_map/all_gather | solution.py:88
  11.8 2.5 %copy-start.2 = (bf16[256,1024]{1,0:T(8,128)(2,1)S(1)}, bf16[256,1024]{1,0:T(8,128)(2,1)}, u32[]{:S(2)}) copy-start(bf16[256,1024]{1,0:T(8,128)(2,1)} %param.9) | copy-start | bytes 1572868
  12.4 2.2 %copy-start.3 = (bf16[256,1024]{1,0:T(8,128)(2,1)S(1)}, bf16[256,1024]{1,0:T(8,128)(2,1)}, u32[]{:S(2)}) copy-start(bf16[256,1024]{1,0:T(8,128)(2,1)} %param.12) | copy-start | bytes 1572868
  14.3 105.7 %all-gather.7.cloned.1.call-start = ((), (), s32[]{:S(2)}) async-start(), calls=%async_computation.5 | async-start | bytes 2621440 | tf_op jit(solution)/shard_map/all_gather | solution.py:126
  66.2 1.1 copy-start.5
  66.4 1.0 copy-start.1
  67.5 31.4 %copy-start.4 = (s32[1536]{0:T(1024)S(1)}, s32[1536]{0:T(1024)}, u32[]{:S(2)}) copy-start(s32[1536]{0:T(1024)} %param.17) | copy-start | bytes 18436
  67.5 31.4 %copy-start = (bf16[1024,1536]{1,0:T(8,128)(2,1)S(1)}, bf16[1024,1536]{1,0:T(8,128)(2,1)}, u32[]{:S(2)}) copy-start(bf16[1024,1536]{1,0:T(8,128)(2,1)} %param.16) | copy-start | bytes 9437188
  98.8 89.2 %reduce-scatter.2.cloned.1.call-start = ((), (), s32[]{:S(2)}) async-start(), calls=%async_computation.3 | async-start | bytes 3932160 | tf_op jit(solution)/shard_map/reduce_scatter | solution.py:134
Sparse Core Ops, SparseCore 0:
  14.4 48.9 all-gather.4
  99.0 20.9 all-gather.6
  127.7 60.2 reduce-scatter.1

commit v2 on v1

--- a/solution.py
+++ b/solution.py
@@ -78,16 +78,23 @@
         advance, jnp.zeros((heads_here, HDIM, HDIM), jnp.float32), (block_gain, block_states)
     )
     device_log = jnp.sum(block_total, axis=1)
+    log_hi = device_log.astype(jnp.bfloat16)
+    log_lo = (device_log - log_hi.astype(jnp.float32)).astype(jnp.bfloat16)
     packed = jnp.concatenate(
         [
-            local_end.reshape(heads_here, HDIM * HDIM),
-            jnp.broadcast_to(device_log[:, None], (heads_here, HDIM)),
+            local_end.astype(jnp.bfloat16).reshape(heads_here, HDIM * HDIM),
+            jnp.broadcast_to(log_hi[:, None], (heads_here, HDIM)),
+            jnp.broadcast_to(log_lo[:, None], (heads_here, HDIM)),
         ],
         axis=1,
     )
     gathered = lax.all_gather(packed, "seq", axis=0, tiled=False)
-    gathered_states = gathered[:, :, : HDIM * HDIM].reshape(n_seq, heads_here, HDIM, HDIM)
-    gathered_logs = gathered[:, :, HDIM * HDIM]
+    gathered_states = (
+        gathered[:, :, : HDIM * HDIM].astype(jnp.float32).reshape(n_seq, heads_here, HDIM, HDIM)
+    )
+    gathered_logs = gathered[:, :, HDIM * HDIM].astype(jnp.float32) + gathered[
+        :, :, HDIM * HDIM + HDIM
+    ].astype(jnp.float32)
     position = lax.axis_index("seq")
     end_offsets = jnp.cumsum(gathered_logs, axis=0)
     start_offsets = end_offsets - gathered_logs
@@ -118,11 +125,22 @@
     rows_w = out_weight.shape[0]
     blocks_here = feat_here // rows_w
     piece = rows_w // n_mdl
-    x = attn.reshape(tok_rows, blocks_here, n_mdl, piece)
-    x = jnp.transpose(x, (2, 0, 1, 3))
-    x = lax.all_to_all(x, "mdl", 0, 0)
-    x = jnp.transpose(x, (0, 2, 1, 3)).reshape(n_seq, tok_rows, piece)
-    x = lax.all_to_all(x, "seq", 0, 0)
+    s_me = lax.axis_index("seq")
+    m_me = lax.axis_index("mdl")
+    pieces = jnp.transpose(attn.reshape(tok_rows, n_seq, piece), (1, 0, 2))
+    pieces = jnp.roll(pieces, -s_me, axis=0)
+    received = []
+    for k in range(n_seq):
+        perm = []
+        for s in range(n_seq):
+            for m in range(n_mdl):
+                j = (s + k) % n_seq
+                f = m * blocks_here + j // n_mdl
+                perm.append((s * n_mdl + m, f * n_mdl + j % n_mdl))
+        received.append(lax.ppermute(pieces[k], ("seq", "mdl"), perm))
+    received = jnp.stack(received)
+    j_me = (s_me % blocks_here) * n_mdl + m_me
+    x = jnp.roll(jnp.flip(received, 0), j_me + 1, axis=0)
     x = lax.all_gather(x, "mdl", axis=0, tiled=False)
     partial = jnp.einsum(
         "usti,uic->stc",

time: 195 us -> 185 us (0.949)
  blocking collectives: 29 us -> 0 us
  starting transfers between devices: 0.09 us -> 7.07 us
  other arithmetic: 10.3 us -> 14.9 us
  waiting for transfers between devices: 125 us -> 129 us
  matrix products: 9.59 us -> 11.9 us
    all_to_all x2 -> x0, blocking collectives: 29 us -> none  [the longest x1 17.5 us: per_device(): x = lax.all_to_all(x, 'seq', 0, 0)]
    all_gather x1, waiting for transfers between devices: 46.2 us -> 27.9 us  [per_device(): gathered = lax.all_gather(packed, 'seq', axis=0, tiled=False)]
    ppermute x0 -> x4, waiting for transfers between devices: none -> 17.2 us  [per_device(): received.append(lax.ppermute(pieces[k], ('seq', 'mdl'), perm))]
    ppermute x0 -> x4, starting transfers between devices: none -> 6.99 us  [per_device(): received.append(lax.ppermute(pieces[k], ('seq', 'mdl'), perm))]
    all_gather x1, waiting for transfers between devices: 18.4 us -> 23.2 us  [per_device(): x = lax.all_gather(x, 'mdl', axis=0, tiled=False)]
    concatenate x1 -> x3, other arithmetic: 0.83 us -> 2.98 us  [the longest x1 2.05 us: per_device(): x = jnp.roll(jnp.flip(received, 0), j_me + 1, axis=0)]
    all_to_all x1 -> x0, local copies, waits for them, and re-layouts: 2.04 us -> none  [per_device(): x = lax.all_to_all(x, 'seq', 0, 0)]
    dynamic_slice x0 -> x1, local copies, waits for them, and re-layouts: none -> 2.04 us  [per_device(): x = jnp.roll(jnp.flip(received, 0), j_me + 1, axis=0)]
  transfers between devices with their start and end apart: 3 -> 7, of which waited for: 3 -> 4; matrix products, arithmetic and copies ran while one was open for 3% -> 3% of each run, Pallas kernels for 0% -> 0%
where the time goes in v2:
time: 185 us; the launch traced here: 184 us
  waiting for transfers between devices  129 us (70%)
  other arithmetic  14.9 us (8%)
  between operations  13.3 us (7%)
  matrix products  11.9 us (6%)
  local copies, waits for them, and re-layouts  8.14 us (4%)
  starting transfers between devices  7.07 us (4%)
    reduce_scatter x1, waiting for transfers between devices, per_device(): return lax.psum_scatter(partial, 'seq', scatter_dimension=0, tiled=True)  60.4 us
    all_gather x1, waiting for transfers between devices, per_device(): gathered = lax.all_gather(packed, 'seq', axis=0, tiled=False)  27.9 us
    all_gather x1, waiting for transfers between devices, per_device(): x = lax.all_gather(x, 'mdl', axis=0, tiled=False)  23.2 us
    ppermute x4, waiting for transfers between devices, per_device(): received.append(lax.ppermute(pieces[k], ('seq', 'mdl'), perm))  17.2 us
    dot_general x1, matrix products, per_device(): jnp.einsum('usti,uic->stc', x, weights.reshape(n_mdl, piece, weights.shap...  7.63 us
    ppermute x4, starting transfers between devices, per_device(): received.append(lax.ppermute(pieces[k], ('seq', 'mdl'), perm))  6.99 us
  transfers between devices with their start and end apart: 7, of which 4 were waited for; matrix products, arithmetic and copies ran while one was open for 3% of the time, Pallas kernels for 0%

profile of v2, /device:TPU:0, one launch (start us, length us, event | category | flops | bytes accessed | tf_op | source)
XLA Modules:
  0.0 184.1 jit_solution(2078039988189997640)
XLA Ops:
  6.5 1.2 reduce-window.6
  8.3 1.0 fusion.68
  9.3 1.2 copy.44
  10.6 1.3 copy.42
  11.9 0.5 fusion.11
  12.5 0.3 multiply_convert_fusion.5
  12.8 0.3 convolution_bitcast_fusion.1
  13.1 0.3 fusion.20
  13.6 0.7 pad_maximum_fusion.1
  14.4 0.2 copy.43
  14.9 0.5 fusion.7
  15.5 2.0 %fusion.1 = f32[1,256,8,128]{1,3,2,0:T(8,128)} fusion(bf16[256,8,128]{0,2,1:T(8,128)(2,1)S(1)} %bitcast.101, bf16[256,8,128]{0,2,1:T(8,128)(2,1)S(1)} %bitcast.102, bf16[256,8,128]{0,2,1:T(8,128)(2,1)S(1)} %bitcast.99, f32[8,256]{1,0:T(8,128)S(1)} %bitcast_add_fusion.2, pred[256,256]{1,0:T(8,128)(4,1)S(1)} %iota_compare_fusion), kind=kOutput, calls=%fused_computation.5 | convolution fusion | flops 271056896 | bytes 2695168 | tf_op jit(solution)/shard_map/hbij,bjhd->bihd/dot_general | solution.py:63
  17.4 27.9 %all-gather.5.cloned.1.call-done = bf16[32,16640]{1,0:T(8,128)(2,1)} async-done(((bf16[8,16640]{1,0:T(8,128)(2,1)}), bf16[32,16640]{1,0:T(8,128)(2,1)}) %all-gather.5.cloned.1.call-update) | async-done | bytes 1064976 | tf_op jit(solution)/shard_map/all_gather | solution.py:91
  45.4 0.8 add_reduce_fusion
  46.3 1.6 multiply_reduce_fusion
  47.9 0.2 copy.63
  48.1 2.0 %multiply_reduce_fusion.1 = (f32[256,8]{0,1:T(8,128)S(1)}, f32[1,256,8,128]{1,3,2,0:T(8,128)S(1)}) fusion(f32[1,256,8,128]{1,3,2,0:T(8,128)} %fusion.1, bf16[256,8,128]{0,2,1:T(8,128)(2,1)S(1)} %bitcast.103, f32[8,128,128]{1,2,0:T(8,128)S(1)} %copy.63, f32[8]{0:T(128)S(1)} %get-tuple-element.32, f32[256,8]{0,1:T(8,128)S(1)} %get-tuple-element.22), kind=kOutput, calls=%fused_computation.30 | convolution fusion | flops 403830784 | bytes 3162144 | tf_op jit(solution)/shard_map/bihd,bhde->bihe/dot_general | solution.py:111
  50.2 0.3 fusion.13
  50.5 0.2 fusion.19
  50.7 0.7 slice_bitcast_fusion.4
  51.5 1.7 collective-permute-start
  53.1 3.8 %collective-permute-start.2 = (bf16[256,256]{0,1:T(8,128)(2,1)}, bf16[256,256]{0,1:T(8,128)(2,1)}, u32[]{:S(2)}, u32[]{:S(2)}) collective-permute-start(bf16[256,256]{0,1:T(8,128)(2,1)} %get-tuple-element.26), channel_id=1, source_target_pairs={{0,2},{1,6},{2,10},{3,14},{4,3},{5,7},{6,11},{7,15},{8,0},{9,4},{1... | collective-permute-start | bytes 393224 | tf_op jit(solution)/shard_map/ppermute | solution.py:140
  56.9 1.5 collective-permute-start.3
  58.4 17.2 %collective-permute-done.2 = bf16[256,256]{0,1:T(8,128)(2,1)} collective-permute-done((bf16[256,256]{0,1:T(8,128)(2,1)}, bf16[256,256]{0,1:T(8,128)(2,1)}, u32[]{:S(2)}, u32[]{:S(2)}) %collective-permute-start.2) | collective-permute-done | bytes 131104 | tf_op jit(solution)/shard_map/ppermute | solution.py:140
  75.6 1.9 %pad_maximum_fusion = bf16[4,256,256]{1,2,0:T(8,128)(2,1)} fusion(bf16[1,256,256]{1,2,0:T(8,128)(2,1)} %bitcast.37, bf16[1,256,256]{1,2,0:T(8,128)(2,1)} %bitcast.35, bf16[1,256,256]{1,2,0:T(8,128)(2,1)} %bitcast.33, bf16[1,256,256]{1,2,0:T(8,128)(2,1)S(1)} %bitcast.107), kind=kLoop, calls=%fused_computation.43 | loop fusion | flops 786432 | bytes 1048576 | tf_op jit(solution)/shard_map/stack | solution.py:141
  77.5 1.9 %rev.4 = bf16[4,256,256]{1,2,0:T(8,128)(2,1)} reverse(bf16[4,256,256]{1,2,0:T(8,128)(2,1)} %pad_maximum_fusion), dimensions={0} | reverse | bytes 1048576 | tf_op jit(solution)/shard_map/jit(_flip)/rev | solution.py:143
  79.4 2.1 %fusion.18 = bf16[4,256,256]{1,2,0:T(8,128)(2,1)} fusion(s32[]{:T(128)S(6)} %select_n.309, bf16[4,256,256]{1,2,0:T(8,128)(2,1)} %rev.4), kind=kLoop, calls=%fused_computation.39 | loop fusion | flops 262144 | bytes 1048580 | tf_op jit(solution)/shard_map/jit(_roll_dynamic)/concatenate | solution.py:143
  81.4 2.0 %copy.53 = bf16[4,256,256]{2,1,0:T(8,128)(2,1)} copy(bf16[4,256,256]{1,2,0:T(8,128)(2,1)} %fusion.18) | data formatting | bytes 1048576 | tf_op jit(solution)/shard_map/jit(_roll_dynamic)/dynamic_slice | solution.py:143
  83.6 2.6 %multiply_convert_fusion = bf16[1024,1536]{1,0:T(8,128)(2,1)} fusion(bf16[1024,1536]{1,0:T(8,128)(2,1)S(1)} %copy-done, f32[1536]{0:T(1024)S(1)} %select_add_fusion), kind=kLoop, calls=%fused_computation.1 | loop fusion | flops 11010048 | bytes 6297600 | tf_op jit(solution)/shard_map/convert_element_type | solution.py:20
  86.2 23.2 %all-gather.7.cloned.1.call-done = bf16[16,256,256]{2,1,0:T(8,128)(2,1)} async-done(((bf16[4,256,256]{2,1,0:T(8,128)(2,1)}), bf16[16,256,256]{2,1,0:T(8,128)(2,1)}) %all-gather.7.cloned.1.call-update) | async-done | bytes 2097168 | tf_op jit(solution)/shard_map/all_gather | solution.py:144
  109.5 7.6 %bitcast_convert_fusion = bf16[4,256,1536]{2,1,0:T(8,128)(2,1)} fusion(bf16[4,4,256,256]{3,2,1,0:T(8,128)(2,1)} %bitcast.113, bf16[4,256,1536,1]{2,1,3,0:T(8,128)(2,1)} %bitcast.97), kind=kOutput, calls=%fused_computation | convolution fusion | flops 3222798336 | bytes 8388608 | tf_op jit(solution)/shard_map/usti,uic->stc/dot_general | solution.py:145
  117.1 60.4 %reduce-scatter.2.cloned.1.call-done = bf16[256,1536]{1,0:T(8,128)(2,1)} async-done(((bf16[1024,1536]{1,0:T(8,128)(2,1)}), bf16[256,1536]{1,0:T(8,128)(2,1)}) %reduce-scatter.2.cloned.1.call-update) | async-done | bytes 786448 | tf_op jit(solution)/shard_map/reduce_scatter | solution.py:152
  (40 shorter events, 1.4 us)
Async XLA Ops:
  6.5 38.8 %all-gather.5.cloned.1.call-start = ((), (), s32[]{:S(2)}) async-start(), calls=%async_computation.2 | async-start | bytes 1331200 | tf_op jit(solution)/shard_map/all_gather | solution.py:91
  10.6 3.8 %copy-start.1 = (bf16[256,1024]{1,0:T(8,128)(2,1)S(1)}, bf16[256,1024]{1,0:T(8,128)(2,1)}, u32[]{:S(2)}) copy-start(bf16[256,1024]{1,0:T(8,128)(2,1)} %param.11) | copy-start | bytes 1572868
  11.9 2.7 %copy-start.2 = (bf16[256,1024]{1,0:T(8,128)(2,1)S(1)}, bf16[256,1024]{1,0:T(8,128)(2,1)}, u32[]{:S(2)}) copy-start(bf16[256,1024]{1,0:T(8,128)(2,1)} %param.14) | copy-start | bytes 1572868
  14.3 95.2 %all-gather.7.cloned.1.call-start = ((), (), s32[]{:S(2)}) async-start(), calls=%async_computation.3 | async-start | bytes 2621440 | tf_op jit(solution)/shard_map/all_gather | solution.py:144
  47.9 2.3 %copy-start.4 = (f32[1024]{0:T(1024)S(1)}, f32[1024]{0:T(1024)}, u32[]{:S(2)}) copy-start(f32[1024]{0:T(1024)} %param.17) | copy-start | bytes 12292
  50.7 32.8 %copy-start.3 = (s32[1536]{0:T(1024)S(1)}, s32[1536]{0:T(1024)}, u32[]{:S(2)}) copy-start(s32[1536]{0:T(1024)} %param.19) | copy-start | bytes 18436
  50.7 32.9 %copy-start = (bf16[1024,1536]{1,0:T(8,128)(2,1)S(1)}, bf16[1024,1536]{1,0:T(8,128)(2,1)}, u32[]{:S(2)}) copy-start(bf16[1024,1536]{1,0:T(8,128)(2,1)} %param.18) | copy-start | bytes 9437188
  51.5 7.0 %collective-permute-start = (bf16[256,256]{0,1:T(8,128)(2,1)}, bf16[256,256]{0,1:T(8,128)(2,1)S(1)}, u32[]{:S(2)}, u32[]{:S(2)}) collective-permute-start(bf16[256,256]{0,1:T(8,128)(2,1)} %get-tuple-element.25), channel_id=1, source_target_pairs={{0,0},{1,4},{2,8},{3,12},{4,1},{5,5},{6,9},{7,13},{8,2},{9,6},{10,... | collective-permute-start | bytes 393224 | tf_op jit(solution)/shard_map/ppermute | solution.py:140
  53.1 22.5 %collective-permute-start.2 = (bf16[256,256]{0,1:T(8,128)(2,1)}, bf16[256,256]{0,1:T(8,128)(2,1)}, u32[]{:S(2)}, u32[]{:S(2)}) collective-permute-start(bf16[256,256]{0,1:T(8,128)(2,1)} %get-tuple-element.26), channel_id=1, source_target_pairs={{0,2},{1,6},{2,10},{3,14},{4,3},{5,7},{6,11},{7,15},{8,0},{9,4},{1... | collective-permute-start | bytes 393224 | tf_op jit(solution)/shard_map/ppermute | solution.py:140
  56.9 18.7 %collective-permute-start.1 = (bf16[256,256]{0,1:T(8,128)(2,1)S(1)}, bf16[256,256]{0,1:T(8,128)(2,1)}, u32[]{:S(2)}, u32[]{:S(2)}) collective-permute-start(bf16[256,256]{0,1:T(8,128)(2,1)S(1)} %get-tuple-element.27), channel_id=1, source_target_pairs={{0,1},{1,5},{2,9},{3,13},{4,2},{5,6},{6,10},{7,14},{8,3},{9,7},{10... | collective-permute-start | bytes 393224 | tf_op jit(solution)/shard_map/ppermute | solution.py:140
  56.9 18.7 %collective-permute-start.3 = (bf16[256,256]{0,1:T(8,128)(2,1)S(1)}, bf16[256,256]{0,1:T(8,128)(2,1)}, u32[]{:S(2)}, u32[]{:S(2)}) collective-permute-start(bf16[256,256]{0,1:T(8,128)(2,1)S(1)} %get-tuple-element.28), channel_id=1, source_target_pairs={{0,3},{1,7},{2,11},{3,15},{4,0},{5,4},{6,8},{7,12},{8,1},{9,5},{10... | collective-permute-start | bytes 393224 | tf_op jit(solution)/shard_map/ppermute | solution.py:140
  83.5 94.0 %reduce-scatter.2.cloned.1.call-start = ((), (), s32[]{:S(2)}) async-start(), calls=%async_computation.1 | async-start | bytes 3932160 | tf_op jit(solution)/shard_map/reduce_scatter | solution.py:152
Sparse Core Ops, SparseCore 0:
  14.4 30.8 all-gather.4
  83.6 25.8 all-gather.6
  117.2 60.2 reduce-scatter.1

commit v3 on v2

--- a/solution.py
+++ b/solution.py
@@ -122,13 +122,11 @@
         jnp.bfloat16
     )
 
-    rows_w = out_weight.shape[0]
+    rows_w, cols_w = weights.shape
     blocks_here = feat_here // rows_w
     piece = rows_w // n_mdl
     s_me = lax.axis_index("seq")
     m_me = lax.axis_index("mdl")
-    pieces = jnp.transpose(attn.reshape(tok_rows, n_seq, piece), (1, 0, 2))
-    pieces = jnp.roll(pieces, -s_me, axis=0)
     received = []
     for k in range(n_seq):
         perm = []
@@ -137,19 +135,45 @@
                 j = (s + k) % n_seq
                 f = m * blocks_here + j // n_mdl
                 perm.append((s * n_mdl + m, f * n_mdl + j % n_mdl))
-        received.append(lax.ppermute(pieces[k], ("seq", "mdl"), perm))
+        j_send = (s_me + k) % n_seq
+        chunk = lax.dynamic_slice_in_dim(attn, j_send * piece, piece, axis=1)
+        received.append(lax.ppermute(chunk, ("seq", "mdl"), perm))
     received = jnp.stack(received)
     j_me = (s_me % blocks_here) * n_mdl + m_me
-    x = jnp.roll(jnp.flip(received, 0), j_me + 1, axis=0)
-    x = lax.all_gather(x, "mdl", axis=0, tiled=False)
-    partial = jnp.einsum(
-        "usti,uic->stc",
-        x,
-        weights.reshape(n_mdl, piece, weights.shape[1]),
-        preferred_element_type=jnp.float32,
-    ).astype(jnp.bfloat16)
-    partial = partial.reshape(n_seq * tok_rows, weights.shape[1])
-    return lax.psum_scatter(partial, "seq", scatter_dimension=0, tiled=True)
+    x = jnp.take(received, (j_me - jnp.arange(n_seq)) % n_seq, axis=0)
+
+    n_x = n_mdl // 2
+    core = m_me % 2
+    xi = m_me // 2
+    got = [x]
+    for d in range(1, n_x):
+        perm = [(mu, ((mu // 2 + d) % n_x) * 2 + mu % 2) for mu in range(n_mdl)]
+        got.append(lax.ppermute(x, "mdl", perm))
+    own = jnp.stack(got)
+    other = lax.ppermute(own, "mdl", [(mu, mu ^ 1) for mu in range(n_mdl)])
+    gathered_x = jnp.stack([own, other], axis=1)
+    d_idx = jnp.arange(n_x)[:, None]
+    e_idx = jnp.arange(2)[None, :]
+    mu_tab = 2 * ((xi - d_idx) % n_x) + jnp.where(e_idx == 0, core, 1 - core)
+    w_perm = jnp.take(
+        weights.reshape(n_mdl, piece, cols_w), mu_tab.reshape(-1), axis=0
+    ).reshape(n_x, 2, piece, cols_w)
+    acc = jnp.einsum(
+        "desti,deic->stc", gathered_x, w_perm, preferred_element_type=jnp.float32
+    )
+
+    for i in range(1, n_seq):
+        t_r = jnp.clip(s_me + n_seq - i, 0, n_seq - 1)
+        t_l = jnp.clip(s_me - n_seq + i, 0, n_seq - 1)
+        send_r = lax.dynamic_index_in_dim(acc, t_r, 0, keepdims=False).astype(jnp.bfloat16)
+        send_l = lax.dynamic_index_in_dim(acc, t_l, 0, keepdims=False).astype(jnp.bfloat16)
+        recv_r = lax.ppermute(send_r, "seq", [(z, z + 1) for z in range(i)])
+        recv_l = lax.ppermute(send_l, "seq", [(z, z - 1) for z in range(n_seq - i, n_seq)])
+        u_r = jnp.clip(s_me - 1 + n_seq - i, 0, n_seq - 1)
+        u_l = jnp.clip(s_me + 1 - n_seq + i, 0, n_seq - 1)
+        acc = acc.at[u_r].add(recv_r.astype(jnp.float32))
+        acc = acc.at[u_l].add(recv_l.astype(jnp.float32))
+    return lax.dynamic_index_in_dim(acc, s_me, 0, keepdims=False).astype(jnp.bfloat16)
 
 
 def solution(mesh):

time: 185 us -> 202 us (1.092)
  waiting for transfers between devices: 129 us -> 104 us
  other arithmetic: 14.9 us -> 33.5 us
  starting transfers between devices: 7.07 us -> 23.5 us
  local copies, waits for them, and re-layouts: 8.14 us -> 14.1 us
    reduce_scatter x1 -> x0, waiting for transfers between devices: 60.4 us -> none  [per_device(): return lax.psum_scatter(partial, 'seq', scatter_dimension=0, tiled=True)]
    ppermute x4 -> x12, waiting for transfers between devices: 17.2 us -> 75.7 us  [the longest x3 43.8 us: per_device(): recv_r = lax.ppermute(send_r, 'seq', [(z, z + 1) for z in range(i)])]
    all_gather x1 -> x0, waiting for transfers between devices: 23.2 us -> none  [per_device(): x = lax.all_gather(x, 'mdl', axis=0, tiled=False)]
    scatter-add x0 -> x6, other arithmetic: none -> 20.4 us  [the longest x3 10.3 us: per_device(): acc = acc.at[u_l].add(recv_l.astype(jnp.float32))]
    ppermute x4 -> x12, starting transfers between devices: 6.99 us -> 23.5 us  [the longest x3 11 us: per_device(): recv_r = lax.ppermute(send_r, 'seq', [(z, z + 1) for z in range(i)])]
    convert_element_type x0 -> x4, local copies, waits for them, and re-layouts: none -> 6.66 us  [the longest x3 4.29 us: per_device(): lax.dynamic_index_in_dim(acc, t_l, 0, keepdims=False).astype(jnp.bfloat16)]
    gather x0 -> x2, local copies, waits for them, and re-layouts: none -> 3 us  [the longest x1 2.41 us: per_device(): jnp.take(weights.reshape(n_mdl, piece, cols_w), mu_tab.reshape(-1), axis=0)]
    another operation x3 -> x6, other arithmetic: 1.36 us -> 4.34 us
  transfers between devices with their start and end apart: 7 -> 13, of which waited for: 4 -> 8; matrix products, arithmetic and copies ran while one was open for 3% -> 9% of each run, Pallas kernels for 0% -> 0%
where the time goes in v3:
time: 202 us; the launch traced here: 201 us
  waiting for transfers between devices  104 us (51%)
  other arithmetic  33.5 us (17%)
  starting transfers between devices  23.5 us (12%)
  local copies, waits for them, and re-layouts  14.1 us (7%)
  between operations  13.8 us (7%)
  matrix products  12.3 us (6%)
    ppermute x3, waiting for transfers between devices, per_device(): recv_r = lax.ppermute(send_r, 'seq', [(z, z + 1) for z in range(i)])  43.8 us
    all_gather x1, waiting for transfers between devices, per_device(): gathered = lax.all_gather(packed, 'seq', axis=0, tiled=False)  28.2 us
    ppermute x4, waiting for transfers between devices, per_device(): received.append(lax.ppermute(chunk, ('seq', 'mdl'), perm))  18 us
    ppermute x1, waiting for transfers between devices, per_device(): got.append(lax.ppermute(x, 'mdl', perm))  13.1 us
    ppermute x3, starting transfers between devices, per_device(): recv_r = lax.ppermute(send_r, 'seq', [(z, z + 1) for z in range(i)])  11 us
    scatter-add x3, other arithmetic, per_device(): acc = acc.at[u_l].add(recv_l.astype(jnp.float32))  10.3 us
    scatter-add x3, other arithmetic, per_device(): acc = acc.at[u_r].add(recv_r.astype(jnp.float32))  10.1 us
    ppermute x4, starting transfers between devices, per_device(): received.append(lax.ppermute(chunk, ('seq', 'mdl'), perm))  8.45 us
  transfers between devices with their start and end apart: 13, of which 8 were waited for; matrix products, arithmetic and copies ran while one was open for 9% of the time, Pallas kernels for 0%

profile of v3, /device:TPU:0, one launch (start us, length us, event | category | flops | bytes accessed | tf_op | source)
XLA Modules:
  0.0 201.2 jit_solution(17433531290872624780)
XLA Ops:
  9.3 1.4 fusion.24
  11.0 1.6 convolution_bitcast_fusion.2
  14.2 2.5 %fusion.14 = f32[1,256,8,128]{1,3,2,0:T(8,128)} fusion(bf16[256,8,128]{0,2,1:T(8,128)(2,1)S(1)} %bitcast.155, f32[8,256]{1,0:T(8,128)S(1)} %bitcast_add_fusion.2, pred[256,256]{1,0:T(8,128)(4,1)S(1)} %iota_compare_fusion, bf16[256,1024]{1,0:T(8,128)(2,1)S(1)} %copy-done.7, f32[1024]{0:T(1024)S(1)} %bitcast.164, bf16[256,1024]{1,0:T(8,128)(2,1)S(1)} %copy-done.6, ...), kind=kOutput, calls=%fused_computation.33 | convolution fusion | flops 276299776 | bytes 2703360 | tf_op jit(solution)/shard_map/hbij,bjhd->bihd/dot_general | solution.py:63
  16.7 28.2 %all-gather.3.cloned.1.call-done = bf16[32,16640]{1,0:T(8,128)(2,1)} async-done(((bf16[8,16640]{1,0:T(8,128)(2,1)}), bf16[32,16640]{1,0:T(8,128)(2,1)}) %all-gather.3.cloned.1.call-update) | async-done | bytes 1064976 | tf_op jit(solution)/shard_map/all_gather | solution.py:91
  45.8 1.6 multiply_reduce_fusion
  47.6 2.3 %multiply_reduce_fusion.1 = (f32[256,8]{0,1:T(8,128)S(1)}, f32[1,256,8,128]{1,3,2,0:T(8,128)S(1)}) fusion(f32[1,256,8,128]{1,3,2,0:T(8,128)} %fusion.14, f32[8,128,128]{1,2,0:T(8,128)S(1)} %copy.45, f32[8]{0:T(128)S(1)} %get-tuple-element.117, f32[256,8]{0,1:T(8,128)S(1)} %get-tuple-element.98, bf16[256,1024]{1,0:T(8,128)(2,1)S(1)} %copy-done.7, ...), kind=kOutput, calls=%fused_computation.53 | convolution fusion | flops 407238656 | bytes 3166240 | tf_op jit(solution)/shard_map/bihd,bhde->bihe/dot_general | solution.py:111
  52.0 2.9 %collective-permute-start.1 = (bf16[256,256]{1,0:T(8,128)(2,1)S(1)}, bf16[256,256]{1,0:T(8,128)(2,1)S(1)}, u32[]{:S(2)}, u32[]{:S(2)}) collective-permute-start(bf16[256,256]{1,0:T(8,128)(2,1)S(1)} %get-tuple-element.111), channel_id=1, source_target_pairs={{0,1},{1,5},{2,9},{3,13},{4,2},{5,6},{6,10},{7,14},{8,3},{9,7},{10... | collective-permute-start | bytes 393224 | tf_op jit(solution)/shard_map/ppermute | solution.py:140
  54.9 3.4 %collective-permute-start.2 = (bf16[256,256]{1,0:T(8,128)(2,1)S(1)}, bf16[256,256]{1,0:T(8,128)(2,1)S(1)}, u32[]{:S(2)}, u32[]{:S(2)}) collective-permute-start(bf16[256,256]{1,0:T(8,128)(2,1)S(1)} %get-tuple-element.110), channel_id=1, source_target_pairs={{0,2},{1,6},{2,10},{3,14},{4,3},{5,7},{6,11},{7,15},{8,0},{9,4},{1... | collective-permute-start | bytes 393224 | tf_op jit(solution)/shard_map/ppermute | solution.py:140
  58.3 1.5 collective-permute-start.3
  59.8 4.6 %collective-permute-done.1 = bf16[256,256]{1,0:T(8,128)(2,1)S(1)} collective-permute-done((bf16[256,256]{1,0:T(8,128)(2,1)S(1)}, bf16[256,256]{1,0:T(8,128)(2,1)S(1)}, u32[]{:S(2)}, u32[]{:S(2)}) %collective-permute-start.1) | collective-permute-done | bytes 131104 | tf_op jit(solution)/shard_map/ppermute | solution.py:140
  64.4 13.4 %collective-permute-done.2 = bf16[256,256]{1,0:T(8,128)(2,1)S(1)} collective-permute-done((bf16[256,256]{1,0:T(8,128)(2,1)S(1)}, bf16[256,256]{1,0:T(8,128)(2,1)S(1)}, u32[]{:S(2)}, u32[]{:S(2)}) %collective-permute-start.2) | collective-permute-done | bytes 131104 | tf_op jit(solution)/shard_map/ppermute | solution.py:140
  78.9 13.1 %collective-permute-done.4 = bf16[4,256,256]{2,1,0:T(8,128)(2,1)S(1)} collective-permute-done((bf16[4,256,256]{2,1,0:T(8,128)(2,1)S(1)}, bf16[4,256,256]{2,1,0:T(8,128)(2,1)S(1)}, u32[]{:S(2)}, u32[]{:S(2)}) %collective-permute-start.4) | collective-permute-done | bytes 524320 | tf_op jit(solution)/shard_map/ppermute | solution.py:151
  92.0 1.5 fusion.107
  94.8 1.4 multiply_convert_fusion
  96.3 2.4 %gather_fusion.1 = bf16[4,256,1536]{2,1,0:T(8,128)(2,1)} fusion(bf16[4,256,1536]{2,1,0:T(8,128)(2,1)S(1)} %bitcast.149, s32[1024]{0:T(1024)S(1)} %pad_clamp_fusion), kind=kCustom, calls=%fused_computation.1 | custom fusion | bytes 6291472 | tf_op jit(solution)/shard_map/jit(_take)/gather | solution.py:158
  98.8 6.0 %convolution_bitcast_fusion = f32[4,256,1536]{2,1,0:T(8,128)S(1)} fusion(bf16[2,2,256,1536]{3,2,1,0:T(8,128)(2,1)} %bitcast.151, pred[2,2]{1,0:T(4,128)(4,1)S(1)} %compare_and_fusion, bf16[2,1,4,256,256]{4,3,1,2,0:T(8,128)(2,1)} %bitcast.34, bf16[2,1,4,256,256]{4,3,1,2,0:T(8,128)(2,1)} %get-tuple-element.106), kind=kOutput, calls=%fused_computation.3 | convolution fusion | flops 3223846912 | bytes 11534340 | tf_op jit(solution)/shard_map/desti,deic->stc/dot_general | solution.py:161
  104.8 2.7 %copy-done = f32[4,256,1536]{2,1,0:T(8,128)} copy-done((f32[4,256,1536]{2,1,0:T(8,128)}, f32[4,256,1536]{2,1,0:T(8,128)S(1)}, u32[]{:S(2)}) %copy-start) | copy-done | bytes 6291480
  107.6 2.1 %collective-permute-start.6 = (bf16[256,1536]{1,0:T(8,128)(2,1)S(1)}, bf16[256,1536]{1,0:T(8,128)(2,1)S(1)}, u32[]{:S(2)}, u32[]{:S(2)}) collective-permute-start(bf16[256,1536]{1,0:T(8,128)(2,1)S(1)} %get-tuple-element.105), channel_id=1, source_target_pairs={{0,4},{1,5},{2,6},{3,7},{16,20},{17,21},{18,22},{19,23}} | collective-permute-start | bytes 2359304 | tf_op jit(solution)/shard_map/ppermute | solution.py:170
  112.0 14.7 %collective-permute-done.6 = bf16[256,1536]{1,0:T(8,128)(2,1)S(1)} collective-permute-done((bf16[256,1536]{1,0:T(8,128)(2,1)S(1)}, bf16[256,1536]{1,0:T(8,128)(2,1)S(1)}, u32[]{:S(2)}, u32[]{:S(2)}) %collective-permute-start.6) | collective-permute-done | bytes 786464 | tf_op jit(solution)/shard_map/ppermute | solution.py:170
  126.6 3.3 %fusion.6 = f32[4,256,1536]{2,1,0:T(8,128)} fusion(f32[4,256,1536]{2,1,0:T(8,128)} %copy-done, s32[]{:T(128)} %min.84, bf16[256,1536]{1,0:T(8,128)(2,1)S(1)} %collective-permute-done.6, pred[]{:T(512)} %and_reduce_fusion.4), kind=kLoop, calls=%fused_computation.18 | loop fusion | flops 1179648 | bytes 3933184 | tf_op jit(solution)/shard_map/scatter-add | solution.py:174
  129.9 3.4 %fusion.7 = f32[4,256,1536]{2,1,0:T(8,128)} fusion(f32[4,256,1536]{2,1,0:T(8,128)} %fusion.6, s32[]{:T(128)} %min.87, bf16[256,1536]{1,0:T(8,128)(2,1)S(1)} %collective-permute-done.7, pred[]{:T(512)} %get-tuple-element.115), kind=kLoop, calls=%fused_computation.19 | loop fusion | flops 1179648 | bytes 3933184 | tf_op jit(solution)/shard_map/scatter-add | solution.py:175
  133.3 2.1 %fusion.32 = (bf16[256,1536]{1,0:T(8,128)(2,1)S(1)}, bf16[256,1536]{1,0:T(8,128)(2,1)S(1)}) fusion(f32[4,256,1536]{2,1,0:T(8,128)} %fusion.7, s32[]{:T(128)} %min.87, s32[]{:T(128)} %min.84), kind=kLoop, calls=%fused_computation.65 | loop fusion | bytes 3145736 | tf_op jit(solution)/shard_map/convert_element_type | solution.py:169
  135.4 4.5 %collective-permute-start.8 = (bf16[256,1536]{1,0:T(8,128)(2,1)S(1)}, bf16[256,1536]{1,0:T(8,128)(2,1)S(1)}, u32[]{:S(2)}, u32[]{:S(2)}) collective-permute-start(bf16[256,1536]{1,0:T(8,128)(2,1)S(1)} %get-tuple-element.103), channel_id=1, source_target_pairs={{0,4},{4,8},{1,5},{5,9},{2,6},{6,10},{3,7},{7,11},{16,20},{20,24},... | collective-permute-start | bytes 2359304 | tf_op jit(solution)/shard_map/ppermute | solution.py:170
  140.6 15.3 %collective-permute-done.8 = bf16[256,1536]{1,0:T(8,128)(2,1)S(1)} collective-permute-done((bf16[256,1536]{1,0:T(8,128)(2,1)S(1)}, bf16[256,1536]{1,0:T(8,128)(2,1)S(1)}, u32[]{:S(2)}, u32[]{:S(2)}) %collective-permute-start.8) | collective-permute-done | bytes 786464 | tf_op jit(solution)/shard_map/ppermute | solution.py:170
  155.9 3.4 %fusion.8 = f32[4,256,1536]{2,1,0:T(8,128)} fusion(f32[4,256,1536]{2,1,0:T(8,128)} %fusion.7, s32[]{:T(128)} %min.90, bf16[256,1536]{1,0:T(8,128)(2,1)S(1)} %collective-permute-done.8, pred[]{:T(512)} %get-tuple-element.116), kind=kLoop, calls=%fused_computation.20 | loop fusion | flops 1179648 | bytes 3933184 | tf_op jit(solution)/shard_map/scatter-add | solution.py:174
  159.3 3.5 %fusion.9 = f32[4,256,1536]{2,1,0:T(8,128)} fusion(f32[4,256,1536]{2,1,0:T(8,128)} %fusion.8, s32[]{:T(128)} %min.92, bf16[256,1536]{1,0:T(8,128)(2,1)S(1)} %collective-permute-done.9, pred[]{:T(512)} %get-tuple-element.95), kind=kLoop, calls=%fused_computation.21 | loop fusion | flops 1179648 | bytes 3933184 | tf_op jit(solution)/shard_map/scatter-add | solution.py:175
  162.8 2.1 %fusion.34 = (bf16[256,1536]{1,0:T(8,128)(2,1)S(1)}, bf16[256,1536]{1,0:T(8,128)(2,1)S(1)}) fusion(f32[4,256,1536]{2,1,0:T(8,128)} %fusion.9, s32[]{:T(128)} %min.92, s32[]{:T(128)} %min.90), kind=kLoop, calls=%fused_computation.67 | loop fusion | bytes 3145736 | tf_op jit(solution)/shard_map/convert_element_type | solution.py:169
  164.9 4.4 %collective-permute-start.10 = (bf16[256,1536]{1,0:T(8,128)(2,1)S(1)}, bf16[256,1536]{1,0:T(8,128)(2,1)S(1)}, u32[]{:S(2)}, u32[]{:S(2)}) collective-permute-start(bf16[256,1536]{1,0:T(8,128)(2,1)S(1)} %get-tuple-element.101), channel_id=1, source_target_pairs={{0,4},{4,8},{8,12},{1,5},{5,9},{9,13},{2,6},{6,10},{10,14},{3,7},{... | collective-permute-start | bytes 2359304 | tf_op jit(solution)/shard_map/ppermute | solution.py:170
  170.6 13.8 %collective-permute-done.10 = bf16[256,1536]{1,0:T(8,128)(2,1)S(1)} collective-permute-done((bf16[256,1536]{1,0:T(8,128)(2,1)S(1)}, bf16[256,1536]{1,0:T(8,128)(2,1)S(1)}, u32[]{:S(2)}, u32[]{:S(2)}) %collective-permute-start.10) | collective-permute-done | bytes 786464 | tf_op jit(solution)/shard_map/ppermute | solution.py:170
  184.4 3.4 %fusion.10 = f32[4,256,1536]{2,1,0:T(8,128)} fusion(f32[4,256,1536]{2,1,0:T(8,128)} %fusion.9, s32[]{:T(128)} %min.94, bf16[256,1536]{1,0:T(8,128)(2,1)S(1)} %collective-permute-done.10, pred[]{:T(512)} %get-tuple-element.94), kind=kLoop, calls=%fused_computation.22 | loop fusion | flops 1179648 | bytes 3933184 | tf_op jit(solution)/shard_map/scatter-add | solution.py:174
  188.6 3.4 %fusion.11 = f32[4,256,1536]{2,1,0:T(8,128)} fusion(f32[4,256,1536]{2,1,0:T(8,128)} %fusion.10, s32[]{:T(128)} %min.94, bf16[256,1536]{1,0:T(8,128)(2,1)S(1)} %collective-permute-done.11, pred[]{:T(512)} %get-tuple-element.94), kind=kLoop, calls=%fused_computation.23 | loop fusion | flops 1179648 | bytes 3933184 | tf_op jit(solution)/shard_map/scatter-add | solution.py:175
  192.0 2.4 %fusion.35 = bf16[256,1536]{1,0:T(8,128)(2,1)} fusion(f32[4,256,1536]{2,1,0:T(8,128)} %fusion.11, s32[]{:T(128)S(6)} %select_n.416), kind=kLoop, calls=%fused_computation.68 | loop fusion | bytes 1572868 | tf_op jit(solution)/shard_map/convert_element_type | solution.py:176
  (74 shorter events, 15.2 us)
Async XLA Ops:
  6.5 38.3 %all-gather.3.cloned.1.call-start = ((), (), s32[]{:S(2)}) async-start(), calls=%async_computation | async-start | bytes 1331200 | tf_op jit(solution)/shard_map/all_gather | solution.py:91
  11.0 3.2 %copy-start.6 = (bf16[256,1024]{1,0:T(8,128)(2,1)S(1)}, bf16[256,1024]{1,0:T(8,128)(2,1)}, u32[]{:S(2)}) copy-start(bf16[256,1024]{1,0:T(8,128)(2,1)} %param.23) | copy-start | bytes 1572868
  11.0 3.2 %copy-start.7 = (bf16[256,1024]{1,0:T(8,128)(2,1)S(1)}, bf16[256,1024]{1,0:T(8,128)(2,1)}, u32[]{:S(2)}) copy-start(bf16[256,1024]{1,0:T(8,128)(2,1)} %param.21) | copy-start | bytes 1572868
  49.9 1.0 copy-start.2
  49.9 1.0 copy-start.4
  50.9 27.8 %copy-start.3 = (s32[1536]{0:T(1024)S(1)}, s32[1536]{0:T(1024)}, u32[]{:S(2)}) copy-start(s32[1536]{0:T(1024)} %param.29) | copy-start | bytes 18436
  51.3 8.5 %collective-permute-start = (bf16[256,256]{1,0:T(8,128)(2,1)S(1)}, bf16[256,256]{1,0:T(8,128)(2,1)S(1)}, u32[]{:S(2)}, u32[]{:S(2)}) collective-permute-start(bf16[256,256]{1,0:T(8,128)(2,1)S(1)} %get-tuple-element.108), channel_id=1, source_target_pairs={{0,0},{1,4},{2,8},{3,12},{4,1},{5,5},{6,9},{7,13},{8,2},{9,6},{10,... | collective-permute-start | bytes 393224 | tf_op jit(solution)/shard_map/ppermute | solution.py:140
  52.0 12.4 %collective-permute-start.1 = (bf16[256,256]{1,0:T(8,128)(2,1)S(1)}, bf16[256,256]{1,0:T(8,128)(2,1)S(1)}, u32[]{:S(2)}, u32[]{:S(2)}) collective-permute-start(bf16[256,256]{1,0:T(8,128)(2,1)S(1)} %get-tuple-element.111), channel_id=1, source_target_pairs={{0,1},{1,5},{2,9},{3,13},{4,2},{5,6},{6,10},{7,14},{8,3},{9,7},{10... | collective-permute-start | bytes 393224 | tf_op jit(solution)/shard_map/ppermute | solution.py:140
  54.9 23.0 %collective-permute-start.2 = (bf16[256,256]{1,0:T(8,128)(2,1)S(1)}, bf16[256,256]{1,0:T(8,128)(2,1)S(1)}, u32[]{:S(2)}, u32[]{:S(2)}) collective-permute-start(bf16[256,256]{1,0:T(8,128)(2,1)S(1)} %get-tuple-element.110), channel_id=1, source_target_pairs={{0,2},{1,6},{2,10},{3,14},{4,3},{5,7},{6,11},{7,15},{8,0},{9,4},{1... | collective-permute-start | bytes 393224 | tf_op jit(solution)/shard_map/ppermute | solution.py:140
  58.3 19.6 %collective-permute-start.3 = (bf16[256,256]{1,0:T(8,128)(2,1)S(1)}, bf16[256,256]{1,0:T(8,128)(2,1)S(1)}, u32[]{:S(2)}, u32[]{:S(2)}) collective-permute-start(bf16[256,256]{1,0:T(8,128)(2,1)S(1)} %get-tuple-element.109), channel_id=1, source_target_pairs={{0,3},{1,7},{2,11},{3,15},{4,0},{5,4},{6,8},{7,12},{8,1},{9,5},{10... | collective-permute-start | bytes 393224 | tf_op jit(solution)/shard_map/ppermute | solution.py:140
  78.6 13.4 %collective-permute-start.4 = (bf16[4,256,256]{2,1,0:T(8,128)(2,1)S(1)}, bf16[4,256,256]{2,1,0:T(8,128)(2,1)S(1)}, u32[]{:S(2)}, u32[]{:S(2)}) collective-permute-start(bf16[4,256,256]{2,1,0:T(8,128)(2,1)S(1)} %broadcast_select_fusion), channel_id=1, source_target_pairs={{0,2},{1,3},{2,0},{3,1},{4,6},{5,7},{6,4},{7,5},{8,10},{9,11},{10,... | collective-permute-start | bytes 1572872 | tf_op jit(solution)/shard_map/ppermute | solution.py:151
  78.8 16.1 %copy-start.1 = (bf16[1024,1536]{1,0:T(8,128)(2,1)S(1)}, bf16[1024,1536]{1,0:T(8,128)(2,1)}, u32[]{:S(2)}) copy-start(bf16[1024,1536]{1,0:T(8,128)(2,1)} %param.28) | copy-start | bytes 9437188
  93.5 5.3 %collective-permute-start.5 = (bf16[2,4,256,256]{3,2,1,0:T(8,128)(2,1)}, bf16[2,4,256,256]{3,2,1,0:T(8,128)(2,1)}, u32[]{:S(2)}, u32[]{:S(2)}) collective-permute-start(bf16[2,4,256,256]{3,2,1,0:T(8,128)(2,1)} %get-tuple-element.107), channel_id=1, source_target_pairs={{0,1},{1,0},{2,3},{3,2},{4,5},{5,4},{6,7},{7,6},{8,9},{9,8},{10,11... | collective-permute-start | bytes 3145736 | tf_op jit(solution)/shard_map/ppermute | solution.py:153
  104.8 2.7 %copy-start = (f32[4,256,1536]{2,1,0:T(8,128)}, f32[4,256,1536]{2,1,0:T(8,128)S(1)}, u32[]{:S(2)}) copy-start(f32[4,256,1536]{2,1,0:T(8,128)S(1)} %convolution_bitcast_fusion) | copy-start | bytes 18874372
  107.5 3.0 %copy-start.5 = (s32[3]{0:T(128)S(1)}, s32[3]{0:T(128)}, u32[]{:S(2)}) copy-start(s32[3]{0:T(128)} %constant.408.clone.1) | copy-start | bytes 40
  107.6 19.0 %collective-permute-start.6 = (bf16[256,1536]{1,0:T(8,128)(2,1)S(1)}, bf16[256,1536]{1,0:T(8,128)(2,1)S(1)}, u32[]{:S(2)}, u32[]{:S(2)}) collective-permute-start(bf16[256,1536]{1,0:T(8,128)(2,1)S(1)} %get-tuple-element.105), channel_id=1, source_target_pairs={{0,4},{1,5},{2,6},{3,7},{16,20},{17,21},{18,22},{19,23}} | collective-permute-start | bytes 2359304 | tf_op jit(solution)/shard_map/ppermute | solution.py:170
  109.7 20.2 %collective-permute-start.7 = (bf16[256,1536]{1,0:T(8,128)(2,1)S(1)}, bf16[256,1536]{1,0:T(8,128)(2,1)S(1)}, u32[]{:S(2)}, u32[]{:S(2)}) collective-permute-start(bf16[256,1536]{1,0:T(8,128)(2,1)S(1)} %get-tuple-element.104), channel_id=1, source_target_pairs={{12,8},{13,9},{14,10},{15,11},{28,24},{29,25},{30,26},{31,27}} | collective-permute-start | bytes 2359304 | tf_op jit(solution)/shard_map/ppermute | solution.py:171
  135.4 20.5 %collective-permute-start.8 = (bf16[256,1536]{1,0:T(8,128)(2,1)S(1)}, bf16[256,1536]{1,0:T(8,128)(2,1)S(1)}, u32[]{:S(2)}, u32[]{:S(2)}) collective-permute-start(bf16[256,1536]{1,0:T(8,128)(2,1)S(1)} %get-tuple-element.103), channel_id=1, source_target_pairs={{0,4},{4,8},{1,5},{5,9},{2,6},{6,10},{3,7},{7,11},{16,20},{20,24},... | collective-permute-start | bytes 2359304 | tf_op jit(solution)/shard_map/ppermute | solution.py:170
  139.9 19.5 %collective-permute-start.9 = (bf16[256,1536]{1,0:T(8,128)(2,1)S(1)}, bf16[256,1536]{1,0:T(8,128)(2,1)S(1)}, u32[]{:S(2)}, u32[]{:S(2)}) collective-permute-start(bf16[256,1536]{1,0:T(8,128)(2,1)S(1)} %get-tuple-element.102), channel_id=1, source_target_pairs={{8,4},{12,8},{9,5},{13,9},{10,6},{14,10},{11,7},{15,11},{24,20},{2... | collective-permute-start | bytes 2359304 | tf_op jit(solution)/shard_map/ppermute | solution.py:171
  164.9 19.6 %collective-permute-start.10 = (bf16[256,1536]{1,0:T(8,128)(2,1)S(1)}, bf16[256,1536]{1,0:T(8,128)(2,1)S(1)}, u32[]{:S(2)}, u32[]{:S(2)}) collective-permute-start(bf16[256,1536]{1,0:T(8,128)(2,1)S(1)} %get-tuple-element.101), channel_id=1, source_target_pairs={{0,4},{4,8},{8,12},{1,5},{5,9},{9,13},{2,6},{6,10},{10,14},{3,7},{... | collective-permute-start | bytes 2359304 | tf_op jit(solution)/shard_map/ppermute | solution.py:170
  169.3 19.3 %collective-permute-start.11 = (bf16[256,1536]{1,0:T(8,128)(2,1)S(1)}, bf16[256,1536]{1,0:T(8,128)(2,1)S(1)}, u32[]{:S(2)}, u32[]{:S(2)}) collective-permute-start(bf16[256,1536]{1,0:T(8,128)(2,1)S(1)} %get-tuple-element.100), channel_id=1, source_target_pairs={{4,0},{8,4},{12,8},{5,1},{9,5},{13,9},{6,2},{10,6},{14,10},{7,3},{... | collective-permute-start | bytes 2359304 | tf_op jit(solution)/shard_map/ppermute | solution.py:171
Sparse Core Ops, SparseCore 0:
  13.9 30.8 all-gather.2

commit v4 on v3

--- a/solution.py
+++ b/solution.py
@@ -158,22 +158,33 @@
     w_perm = jnp.take(
         weights.reshape(n_mdl, piece, cols_w), mu_tab.reshape(-1), axis=0
     ).reshape(n_x, 2, piece, cols_w)
-    acc = jnp.einsum(
-        "desti,deic->stc", gathered_x, w_perm, preferred_element_type=jnp.float32
-    )
-
+
+    def partial_for(target):
+        rows = lax.dynamic_index_in_dim(gathered_x, target, 2, keepdims=False)
+        return jnp.einsum(
+            "deti,deic->tc", rows, w_perm, preferred_element_type=jnp.float32
+        )
+
+    recv_r = None
+    recv_l = None
     for i in range(1, n_seq):
         t_r = jnp.clip(s_me + n_seq - i, 0, n_seq - 1)
         t_l = jnp.clip(s_me - n_seq + i, 0, n_seq - 1)
-        send_r = lax.dynamic_index_in_dim(acc, t_r, 0, keepdims=False).astype(jnp.bfloat16)
-        send_l = lax.dynamic_index_in_dim(acc, t_l, 0, keepdims=False).astype(jnp.bfloat16)
-        recv_r = lax.ppermute(send_r, "seq", [(z, z + 1) for z in range(i)])
-        recv_l = lax.ppermute(send_l, "seq", [(z, z - 1) for z in range(n_seq - i, n_seq)])
-        u_r = jnp.clip(s_me - 1 + n_seq - i, 0, n_seq - 1)
-        u_l = jnp.clip(s_me + 1 - n_seq + i, 0, n_seq - 1)
-        acc = acc.at[u_r].add(recv_r.astype(jnp.float32))
-        acc = acc.at[u_l].add(recv_l.astype(jnp.float32))
-    return lax.dynamic_index_in_dim(acc, s_me, 0, keepdims=False).astype(jnp.bfloat16)
+        send_r = partial_for(t_r)
+        send_l = partial_for(t_l)
+        if recv_r is not None:
+            send_r = send_r + recv_r.astype(jnp.float32)
+            send_l = send_l + recv_l.astype(jnp.float32)
+        recv_r = lax.ppermute(
+            send_r.astype(jnp.bfloat16), "seq", [(z, z + 1) for z in range(i)]
+        )
+        recv_l = lax.ppermute(
+            send_l.astype(jnp.bfloat16), "seq", [(z, z - 1) for z in range(n_seq - i, n_seq)]
+        )
+    total = partial_for(s_me)
+    if recv_r is not None:
+        total = total + recv_r.astype(jnp.float32) + recv_l.astype(jnp.float32)
+    return total.astype(jnp.bfloat16)
 
 
 def solution(mesh):

time: 202 us -> 181 us (0.90)
  other arithmetic: 33.5 us -> 18 us
  local copies, waits for them, and re-layouts: 14.1 us -> 4.92 us
  matrix products: 12.3 us -> 15.2 us
    scatter-add x6 -> x0, other arithmetic: 20.4 us -> none  [the longest x3 10.3 us: per_device(): acc = acc.at[u_l].add(recv_l.astype(jnp.float32))]
    convert_element_type x4 -> x0, local copies, waits for them, and re-layouts: 6.66 us -> none  [the longest x3 4.29 us: per_device(): lax.dynamic_index_in_dim(acc, t_l, 0, keepdims=False).astype(jnp.bfloat16)]
    dot_general x1 -> x7, matrix products: 6.02 us -> 10 us  [partial_for(): jnp.einsum('deti,deic->tc', rows, w_perm, preferred_element_type=jnp.floa...]
    unnamed x16 -> x24, local copies, waits for them, and re-layouts: 3.26 us -> 0.64 us
    select_n x1 -> x2, other arithmetic: 0.01 us -> 2.35 us  [per_device(): jnp.take(weights.reshape(n_mdl, piece, cols_w), mu_tab.reshape(-1), axis=0)]
  transfers between devices with their start and end apart: 13 -> 13, of which waited for: 8 -> 8; matrix products, arithmetic and copies ran while one was open for 9% -> 10% of each run, Pallas kernels for 0% -> 0%
where the time goes in v4:
time: 181 us
  waiting for transfers between devices  105 us (58%)
  starting transfers between devices  23.1 us (13%)
  other arithmetic  18 us (10%)
  matrix products  15.2 us (8%)
  between operations  13.9 us (8%)
  local copies, waits for them, and re-layouts  4.92 us (3%)
    ppermute x3, waiting for transfers between devices, per_device(): lax.ppermute(send_r.astype(jnp.bfloat16), 'seq', [(z, z + 1) for z in ran...  39.5 us
    all_gather x1, waiting for transfers between devices, per_device(): gathered = lax.all_gather(packed, 'seq', axis=0, tiled=False)  28.2 us
    ppermute x4, waiting for transfers between devices, per_device(): received.append(lax.ppermute(chunk, ('seq', 'mdl'), perm))  19.1 us
    ppermute x1, waiting for transfers between devices, per_device(): got.append(lax.ppermute(x, 'mdl', perm))  13.4 us
    ppermute x3, starting transfers between devices, per_device(): lax.ppermute(send_r.astype(jnp.bfloat16), 'seq', [(z, z + 1) for z in ran...  11.8 us
    dot_general x7, matrix products, partial_for(): jnp.einsum('deti,deic->tc', rows, w_perm, preferred_element_type=jnp.floa...  10 us
    ppermute x4, starting transfers between devices, per_device(): received.append(lax.ppermute(chunk, ('seq', 'mdl'), perm))  7.38 us
    ppermute x3, waiting for transfers between devices, per_device(): lax.ppermute(send_l.astype(jnp.bfloat16), 'seq', [(z, z - 1) for z in ran...  5.2 us
  transfers between devices with their start and end apart: 13, of which 8 were waited for; matrix products, arithmetic and copies ran while one was open for 10% of the time, Pallas kernels for 0%

profile of v4, /device:TPU:0, one launch (start us, length us, event | category | flops | bytes accessed | tf_op | source)
XLA Modules:
  0.0 180.6 jit_solution(1216267077964628914)
XLA Ops:
  6.5 1.3 reduce-window.6
  8.4 1.0 fusion.77
  9.4 1.4 fusion.13
  13.2 2.5 %fusion.3 = f32[1,256,8,128]{1,3,2,0:T(8,128)} fusion(bf16[256,8,128]{0,2,1:T(8,128)(2,1)S(1)} %bitcast.189, f32[8,256]{1,0:T(8,128)S(1)} %bitcast_add_fusion.2, pred[256,256]{1,0:T(8,128)(4,1)S(1)} %iota_compare_fusion, bf16[256,1024]{1,0:T(8,128)(2,1)S(1)} %copy-done.11, f32[1024]{0:T(1024)S(1)} %bitcast.198, bf16[256,1024]{1,0:T(8,128)(2,1)S(1)} %copy-done.10, ...), kind=kOutput, calls=%fused_computation.35 | convolution fusion | flops 276299776 | bytes 2703360 | tf_op jit(solution)/shard_map/hbij,bjhd->bihd/dot_general | solution.py:63
  15.6 28.2 %all-gather.3.cloned.1.call-done = bf16[32,16640]{1,0:T(8,128)(2,1)} async-done(((bf16[8,16640]{1,0:T(8,128)(2,1)}), bf16[32,16640]{1,0:T(8,128)(2,1)}) %all-gather.3.cloned.1.call-update) | async-done | bytes 1064976 | tf_op jit(solution)/shard_map/all_gather | solution.py:91
  44.7 1.6 multiply_reduce_fusion
  46.6 2.3 %multiply_reduce_fusion.1 = (f32[256,8]{0,1:T(8,128)S(1)}, f32[1,256,8,128]{1,3,2,0:T(8,128)S(1)}) fusion(f32[1,256,8,128]{1,3,2,0:T(8,128)} %fusion.3, f32[8,128,128]{1,2,0:T(8,128)S(1)} %copy.61, f32[8]{0:T(128)S(1)} %get-tuple-element.39, f32[256,8]{0,1:T(8,128)S(1)} %get-tuple-element.20, bf16[256,1024]{1,0:T(8,128)(2,1)S(1)} %copy-done.11, ...), kind=kOutput, calls=%fused_computation.55 | convolution fusion | flops 407238656 | bytes 3166240 | tf_op jit(solution)/shard_map/bihd,bhde->bihe/dot_general | solution.py:111
  51.0 4.4 %collective-permute-start.3 = (bf16[256,256]{1,0:T(8,128)(2,1)S(1)}, bf16[256,256]{1,0:T(8,128)(2,1)S(1)}, u32[]{:S(2)}, u32[]{:S(2)}) collective-permute-start(bf16[256,256]{1,0:T(8,128)(2,1)S(1)} %get-tuple-element.33), channel_id=1, source_target_pairs={{0,3},{1,7},{2,11},{3,15},{4,0},{5,4},{6,8},{7,12},{8,1},{9,5},{10... | collective-permute-start | bytes 393224 | tf_op jit(solution)/shard_map/ppermute | solution.py:140
  55.9 1.8 collective-permute-start.1
  57.7 5.8 %collective-permute-done.3 = bf16[256,256]{1,0:T(8,128)(2,1)S(1)} collective-permute-done((bf16[256,256]{1,0:T(8,128)(2,1)S(1)}, bf16[256,256]{1,0:T(8,128)(2,1)S(1)}, u32[]{:S(2)}, u32[]{:S(2)}) %collective-permute-start.3) | collective-permute-done | bytes 131104 | tf_op jit(solution)/shard_map/ppermute | solution.py:140
  63.5 13.3 %collective-permute-done.2 = bf16[256,256]{1,0:T(8,128)(2,1)S(1)} collective-permute-done((bf16[256,256]{1,0:T(8,128)(2,1)S(1)}, bf16[256,256]{1,0:T(8,128)(2,1)S(1)}, u32[]{:S(2)}, u32[]{:S(2)}) %collective-permute-start.2) | collective-permute-done | bytes 131104 | tf_op jit(solution)/shard_map/ppermute | solution.py:140
  77.8 13.4 %collective-permute-done.4 = bf16[4,256,256]{2,1,0:T(8,128)(2,1)S(1)} collective-permute-done((bf16[4,256,256]{2,1,0:T(8,128)(2,1)S(1)}, bf16[4,256,256]{2,1,0:T(8,128)(2,1)S(1)}, u32[]{:S(2)}, u32[]{:S(2)}) %collective-permute-start.4) | collective-permute-done | bytes 524320 | tf_op jit(solution)/shard_map/ppermute | solution.py:151
  91.3 1.5 pad_maximum_fusion
  92.7 1.0 collective-permute-start.5
  93.7 1.4 multiply_convert_fusion
  95.3 2.4 %gather_fusion.1 = bf16[4,256,1536]{2,1,0:T(8,128)(2,1)} fusion(bf16[4,256,1536]{2,1,0:T(8,128)(2,1)S(1)} %bitcast.184, s32[1024]{0:T(1024)S(1)} %pad_clamp_fusion), kind=kCustom, calls=%fused_computation.1 | custom fusion | bytes 6291472 | tf_op jit(solution)/shard_map/jit(_take)/gather | solution.py:158
  97.7 2.3 %broadcast_select_fusion = bf16[4,256,1536]{2,1,0:T(8,128)(2,1)S(1)} fusion(bf16[4,256,1536]{2,1,0:T(8,128)(2,1)} %gather_fusion.1, pred[4]{0:T(512)(128)(4,1)S(1)} %get-tuple-element.44), kind=kLoop, calls=%fused_computation.17 | loop fusion | flops 1572864 | bytes 6291460 | tf_op jit(solution)/shard_map/jit(_take)/select_n | solution.py:158
  100.1 2.9 %fusion.22 = (bf16[2,2,1,256,256]{4,3,2,0,1:T(8,128)(2,1)}, bf16[2,2,1,256,256]{4,3,2,0,1:T(8,128)(2,1)}, bf16[2,2,1,256,256]{4,3,2,0,1:T(8,128)(2,1)}, bf16[2,2...) fusion(s32[]{:T(128)S(6)} %min.66, ...), kind=kLoop, calls=%fused_computation.68 | loop fusion | flops 1572864 | bytes 5242904 | tf_op jit(solution)/shard_map/stack | solution.py:154
  103.0 1.9 %fusion = bf16[256,1536]{1,0:T(8,128)(2,1)} fusion(bf16[2,2,256,1536]{3,2,1,0:T(8,128)(2,1)S(1)} %bitcast.177, bf16[2,2,1,256,256]{4,3,2,0,1:T(8,128)(2,1)S(1)} %get-tuple-element.27), kind=kOutput, calls=%fused_computation.25 | convolution fusion | flops 805699584 | bytes 4456448 | tf_op jit(solution)/shard_map/deti,deic->tc/dot_general | solution.py:164
  104.8 2.9 %collective-permute-start.6 = (bf16[256,1536]{1,0:T(8,128)(2,1)}, bf16[256,1536]{1,0:T(8,128)(2,1)}, u32[]{:S(2)}, u32[]{:S(2)}) collective-permute-start(bf16[256,1536]{1,0:T(8,128)(2,1)} %fusion), channel_id=1, source_target_pairs={{0,4},{1,5},{2,6},{3,7},{16,20},{17,21},{18,22},{19,23}} | collective-permute-start | bytes 2359304 | tf_op jit(solution)/shard_map/ppermute | solution.py:178
  107.7 2.1 %fusion.1 = bf16[256,1536]{1,0:T(8,128)(2,1)S(1)} fusion(bf16[2,2,256,1536]{3,2,1,0:T(8,128)(2,1)S(1)} %bitcast.178, s32[]{:T(128)S(6)} %min.71, bf16[2,1,4,256,256]{4,3,2,0,1:T(8,128)(2,1)} %get-tuple-element.31, bf16[2,1,4,256,256]{4,3,2,0,1:T(8,128)(2,1)} %bitcast.33), kind=kOutput, calls=%fused_computation.26 | convolution fusion | flops 805961728 | bytes 6029316 | tf_op jit(solution)/shard_map/deti,deic->tc/dot_general | solution.py:164
  110.5 13.6 %collective-permute-done.6 = bf16[256,1536]{1,0:T(8,128)(2,1)} collective-permute-done((bf16[256,1536]{1,0:T(8,128)(2,1)}, bf16[256,1536]{1,0:T(8,128)(2,1)}, u32[]{:S(2)}, u32[]{:S(2)}) %collective-permute-start.6) | collective-permute-done | bytes 786464 | tf_op jit(solution)/shard_map/ppermute | solution.py:178
  124.1 2.2 %add_convert_fusion.4 = bf16[256,1536]{1,0:T(8,128)(2,1)S(1)} fusion(bf16[256,1536]{1,0:T(8,128)(2,1)} %collective-permute-done.6, bf16[2,2,256,1536]{3,2,1,0:T(8,128)(2,1)S(1)} %bitcast.179, bf16[2,2,1,256,256]{4,3,2,0,1:T(8,128)(2,1)S(1)} %copy-done.7), kind=kOutput, calls=%fused_computation.33 | convolution fusion | flops 806486016 | bytes 5242880 | tf_op jit(solution)/shard_map/deti,deic->tc/dot_general | solution.py:164
  126.3 4.4 %collective-permute-start.7 = (bf16[256,1536]{1,0:T(8,128)(2,1)S(1)}, bf16[256,1536]{1,0:T(8,128)(2,1)S(1)}, u32[]{:S(2)}, u32[]{:S(2)}) collective-permute-start(bf16[256,1536]{1,0:T(8,128)(2,1)S(1)} %add_convert_fusion.4), channel_id=1, source_target_pairs={{0,4},{4,8},{1,5},{5,9},{2,6},{6,10},{3,7},{7,11},{16,20},{20,24},... | collective-permute-start | bytes 2359304 | tf_op jit(solution)/shard_map/ppermute | solution.py:178
  130.8 1.0 add_convert_fusion.2
  132.7 14.1 %collective-permute-done.7 = bf16[256,1536]{1,0:T(8,128)(2,1)S(1)} collective-permute-done((bf16[256,1536]{1,0:T(8,128)(2,1)S(1)}, bf16[256,1536]{1,0:T(8,128)(2,1)S(1)}, u32[]{:S(2)}, u32[]{:S(2)}) %collective-permute-start.7) | collective-permute-done | bytes 786464 | tf_op jit(solution)/shard_map/ppermute | solution.py:178
  147.8 4.4 %collective-permute-start.8 = (bf16[256,1536]{1,0:T(8,128)(2,1)S(1)}, bf16[256,1536]{1,0:T(8,128)(2,1)S(1)}, u32[]{:S(2)}, u32[]{:S(2)}) collective-permute-start(bf16[256,1536]{1,0:T(8,128)(2,1)S(1)} %add_convert_fusion.3), channel_id=1, source_target_pairs={{0,4},{4,8},{8,12},{1,5},{5,9},{9,13},{2,6},{6,10},{10,14},{3,7},{... | collective-permute-start | bytes 2359304 | tf_op jit(solution)/shard_map/ppermute | solution.py:178
  152.3 1.0 add_convert_fusion.1
  153.3 1.3 collective-permute-start.11
  155.5 11.8 %collective-permute-done.8 = bf16[256,1536]{1,0:T(8,128)(2,1)S(1)} collective-permute-done((bf16[256,1536]{1,0:T(8,128)(2,1)S(1)}, bf16[256,1536]{1,0:T(8,128)(2,1)S(1)}, u32[]{:S(2)}, u32[]{:S(2)}) %collective-permute-start.8) | collective-permute-done | bytes 786464 | tf_op jit(solution)/shard_map/ppermute | solution.py:178
  167.4 5.2 %collective-permute-done.11 = bf16[256,1536]{1,0:T(8,128)(2,1)S(1)} collective-permute-done((bf16[256,1536]{1,0:T(8,128)(2,1)S(1)}, bf16[256,1536]{1,0:T(8,128)(2,1)S(1)}, u32[]{:S(2)}, u32[]{:S(2)}) %collective-permute-start.11) | collective-permute-done | bytes 786464 | tf_op jit(solution)/shard_map/ppermute | solution.py:181
  172.5 1.2 add_convert_fusion
  (80 shorter events, 11.2 us)
Async XLA Ops:
  6.5 4.5 %copy-start.10 = (bf16[256,1024]{1,0:T(8,128)(2,1)S(1)}, bf16[256,1024]{1,0:T(8,128)(2,1)}, u32[]{:S(2)}) copy-start(bf16[256,1024]{1,0:T(8,128)(2,1)} %param.11) | copy-start | bytes 1572868
  6.5 37.3 %all-gather.3.cloned.1.call-start = ((), (), s32[]{:S(2)}) async-start(), calls=%async_computation | async-start | bytes 1331200 | tf_op jit(solution)/shard_map/all_gather | solution.py:91
  11.1 2.1 %copy-start.11 = (bf16[256,1024]{1,0:T(8,128)(2,1)S(1)}, bf16[256,1024]{1,0:T(8,128)(2,1)}, u32[]{:S(2)}) copy-start(bf16[256,1024]{1,0:T(8,128)(2,1)} %param.9) | copy-start | bytes 1572868
  48.8 1.0 copy-start.3
  48.8 1.0 copy-start.9
  50.2 27.5 %copy-start.8 = (s32[1536]{0:T(1024)S(1)}, s32[1536]{0:T(1024)}, u32[]{:S(2)}) copy-start(s32[1536]{0:T(1024)} %param.17) | copy-start | bytes 18436
  50.3 7.4 %collective-permute-start = (bf16[256,256]{1,0:T(8,128)(2,1)S(1)}, bf16[256,256]{1,0:T(8,128)(2,1)S(1)}, u32[]{:S(2)}, u32[]{:S(2)}) collective-permute-start(bf16[256,256]{1,0:T(8,128)(2,1)S(1)} %get-tuple-element.32), channel_id=1, source_target_pairs={{0,0},{1,4},{2,8},{3,12},{4,1},{5,5},{6,9},{7,13},{8,2},{9,6},{10,... | collective-permute-start | bytes 393224 | tf_op jit(solution)/shard_map/ppermute | solution.py:140
  51.0 12.5 %collective-permute-start.3 = (bf16[256,256]{1,0:T(8,128)(2,1)S(1)}, bf16[256,256]{1,0:T(8,128)(2,1)S(1)}, u32[]{:S(2)}, u32[]{:S(2)}) collective-permute-start(bf16[256,256]{1,0:T(8,128)(2,1)S(1)} %get-tuple-element.33), channel_id=1, source_target_pairs={{0,3},{1,7},{2,11},{3,15},{4,0},{5,4},{6,8},{7,12},{8,1},{9,5},{10... | collective-permute-start | bytes 393224 | tf_op jit(solution)/shard_map/ppermute | solution.py:140
  55.4 21.5 %collective-permute-start.2 = (bf16[256,256]{1,0:T(8,128)(2,1)S(1)}, bf16[256,256]{1,0:T(8,128)(2,1)S(1)}, u32[]{:S(2)}, u32[]{:S(2)}) collective-permute-start(bf16[256,256]{1,0:T(8,128)(2,1)S(1)} %get-tuple-element.34), channel_id=1, source_target_pairs={{0,2},{1,6},{2,10},{3,14},{4,3},{5,7},{6,11},{7,15},{8,0},{9,4},{1... | collective-permute-start | bytes 393224 | tf_op jit(solution)/shard_map/ppermute | solution.py:140
  55.9 20.9 %collective-permute-start.1 = (bf16[256,256]{1,0:T(8,128)(2,1)S(1)}, bf16[256,256]{1,0:T(8,128)(2,1)S(1)}, u32[]{:S(2)}, u32[]{:S(2)}) collective-permute-start(bf16[256,256]{1,0:T(8,128)(2,1)S(1)} %get-tuple-element.35), channel_id=1, source_target_pairs={{0,1},{1,5},{2,9},{3,13},{4,2},{5,6},{6,10},{7,14},{8,3},{9,7},{10... | collective-permute-start | bytes 393224 | tf_op jit(solution)/shard_map/ppermute | solution.py:140
  77.6 13.7 %collective-permute-start.4 = (bf16[4,256,256]{2,1,0:T(8,128)(2,1)S(1)}, bf16[4,256,256]{2,1,0:T(8,128)(2,1)S(1)}, u32[]{:S(2)}, u32[]{:S(2)}) collective-permute-start(bf16[4,256,256]{2,1,0:T(8,128)(2,1)S(1)} %broadcast_select_fusion.1), channel_id=1, source_target_pairs={{0,2},{1,3},{2,0},{3,1},{4,6},{5,7},{6,4},{7,5},{8,10},{9,11},{10,... | collective-permute-start | bytes 1572872 | tf_op jit(solution)/shard_map/ppermute | solution.py:151
  77.7 16.0 %copy-start.1 = (bf16[1024,1536]{1,0:T(8,128)(2,1)S(1)}, bf16[1024,1536]{1,0:T(8,128)(2,1)}, u32[]{:S(2)}) copy-start(bf16[1024,1536]{1,0:T(8,128)(2,1)} %param.16) | copy-start | bytes 9437188
  92.7 7.3 %collective-permute-start.5 = (bf16[2,4,256,256]{3,2,1,0:T(8,128)(2,1)}, bf16[2,4,256,256]{3,2,1,0:T(8,128)(2,1)}, u32[]{:S(2)}, u32[]{:S(2)}) collective-permute-start(bf16[2,4,256,256]{3,2,1,0:T(8,128)(2,1)} %get-tuple-element.30), channel_id=1, source_target_pairs={{0,1},{1,0},{2,3},{3,2},{4,5},{5,4},{6,7},{7,6},{8,9},{9,8},{10,11... | collective-permute-start | bytes 3145736 | tf_op jit(solution)/shard_map/ppermute | solution.py:153
  97.7 2.4 %copy-start = (bf16[2,1,4,256,256]{4,3,2,0,1:T(8,128)(2,1)S(1)}, bf16[2,1,4,256,256]{4,3,2,0,1:T(8,128)(2,1)}, u32[]{:S(2)}) copy-start(bf16[2,1,4,256,256]{4,3,2,0,1:T(8,128)(2,1)} %get-tuple-element.31) | copy-start | bytes 3145732
  104.8 19.3 %collective-permute-start.6 = (bf16[256,1536]{1,0:T(8,128)(2,1)}, bf16[256,1536]{1,0:T(8,128)(2,1)}, u32[]{:S(2)}, u32[]{:S(2)}) collective-permute-start(bf16[256,1536]{1,0:T(8,128)(2,1)} %fusion), channel_id=1, source_target_pairs={{0,4},{1,5},{2,6},{3,7},{16,20},{17,21},{18,22},{19,23}} | collective-permute-start | bytes 2359304 | tf_op jit(solution)/shard_map/ppermute | solution.py:178
  107.7 16.4 %copy-start.7 = (bf16[2,2,1,256,256]{4,3,2,0,1:T(8,128)(2,1)S(1)}, bf16[2,2,1,256,256]{4,3,2,0,1:T(8,128)(2,1)}, u32[]{:S(2)}) copy-start(bf16[2,2,1,256,256]{4,3,2,0,1:T(8,128)(2,1)} %get-tuple-element.26) | copy-start | bytes 1572868
  109.8 20.9 %collective-permute-start.9 = (bf16[256,1536]{1,0:T(8,128)(2,1)S(1)}, bf16[256,1536]{1,0:T(8,128)(2,1)S(1)}, u32[]{:S(2)}, u32[]{:S(2)}) collective-permute-start(bf16[256,1536]{1,0:T(8,128)(2,1)S(1)} %fusion.1), channel_id=1, source_target_pairs={{12,8},{13,9},{14,10},{15,11},{28,24},{29,25},{30,26},{31,27}} | collective-permute-start | bytes 2359304 | tf_op jit(solution)/shard_map/ppermute | solution.py:181
  124.1 6.6 %copy-start.6 = (bf16[2,2,1,256,256]{4,3,2,0,1:T(8,128)(2,1)S(1)}, bf16[2,2,1,256,256]{4,3,2,0,1:T(8,128)(2,1)}, u32[]{:S(2)}) copy-start(bf16[2,2,1,256,256]{4,3,2,0,1:T(8,128)(2,1)} %get-tuple-element.29) | copy-start | bytes 1572868
  126.3 20.5 %collective-permute-start.7 = (bf16[256,1536]{1,0:T(8,128)(2,1)S(1)}, bf16[256,1536]{1,0:T(8,128)(2,1)S(1)}, u32[]{:S(2)}, u32[]{:S(2)}) collective-permute-start(bf16[256,1536]{1,0:T(8,128)(2,1)S(1)} %add_convert_fusion.4), channel_id=1, source_target_pairs={{0,4},{4,8},{1,5},{5,9},{2,6},{6,10},{3,7},{7,11},{16,20},{20,24},... | collective-permute-start | bytes 2359304 | tf_op jit(solution)/shard_map/ppermute | solution.py:178
  130.8 16.0 %copy-start.5 = (bf16[2,2,1,256,256]{4,3,2,0,1:T(8,128)(2,1)S(1)}, bf16[2,2,1,256,256]{4,3,2,0,1:T(8,128)(2,1)}, u32[]{:S(2)}) copy-start(bf16[2,2,1,256,256]{4,3,2,0,1:T(8,128)(2,1)} %get-tuple-element.24) | copy-start | bytes 1572868
  131.8 20.5 %collective-permute-start.10 = (bf16[256,1536]{1,0:T(8,128)(2,1)S(1)}, bf16[256,1536]{1,0:T(8,128)(2,1)S(1)}, u32[]{:S(2)}, u32[]{:S(2)}) collective-permute-start(bf16[256,1536]{1,0:T(8,128)(2,1)S(1)} %add_convert_fusion.2), channel_id=1, source_target_pairs={{8,4},{12,8},{9,5},{13,9},{10,6},{14,10},{11,7},{15,11},{24,20},{2... | collective-permute-start | bytes 2359304 | tf_op jit(solution)/shard_map/ppermute | solution.py:181
  146.8 5.5 %copy-start.4 = (bf16[2,2,1,256,256]{4,3,2,0,1:T(8,128)(2,1)S(1)}, bf16[2,2,1,256,256]{4,3,2,0,1:T(8,128)(2,1)}, u32[]{:S(2)}) copy-start(bf16[2,2,1,256,256]{4,3,2,0,1:T(8,128)(2,1)} %get-tuple-element.28) | copy-start | bytes 1572868
  147.8 19.6 %collective-permute-start.8 = (bf16[256,1536]{1,0:T(8,128)(2,1)S(1)}, bf16[256,1536]{1,0:T(8,128)(2,1)S(1)}, u32[]{:S(2)}, u32[]{:S(2)}) collective-permute-start(bf16[256,1536]{1,0:T(8,128)(2,1)S(1)} %add_convert_fusion.3), channel_id=1, source_target_pairs={{0,4},{4,8},{8,12},{1,5},{5,9},{9,13},{2,6},{6,10},{10,14},{3,7},{... | collective-permute-start | bytes 2359304 | tf_op jit(solution)/shard_map/ppermute | solution.py:178
  152.2 2.3 %copy-start.2 = (bf16[2,2,1,256,256]{4,3,2,0,1:T(8,128)(2,1)S(1)}, bf16[2,2,1,256,256]{4,3,2,0,1:T(8,128)(2,1)}, u32[]{:S(2)}) copy-start(bf16[2,2,1,256,256]{4,3,2,0,1:T(8,128)(2,1)} %get-tuple-element.25) | copy-start | bytes 1572868
  153.3 19.3 %collective-permute-start.11 = (bf16[256,1536]{1,0:T(8,128)(2,1)S(1)}, bf16[256,1536]{1,0:T(8,128)(2,1)S(1)}, u32[]{:S(2)}, u32[]{:S(2)}) collective-permute-start(bf16[256,1536]{1,0:T(8,128)(2,1)S(1)} %add_convert_fusion.1), channel_id=1, source_target_pairs={{4,0},{8,4},{12,8},{5,1},{9,5},{13,9},{6,2},{10,6},{14,10},{7,3},{... | collective-permute-start | bytes 2359304 | tf_op jit(solution)/shard_map/ppermute | solution.py:181
Sparse Core Ops, SparseCore 0:
  12.9 30.8 all-gather.2

commit v5 on v4

--- a/solution.py
+++ b/solution.py
@@ -165,25 +165,30 @@
             "deti,deic->tc", rows, w_perm, preferred_element_type=jnp.float32
         )
 
-    recv_r = None
-    recv_l = None
-    for i in range(1, n_seq):
-        t_r = jnp.clip(s_me + n_seq - i, 0, n_seq - 1)
-        t_l = jnp.clip(s_me - n_seq + i, 0, n_seq - 1)
-        send_r = partial_for(t_r)
-        send_l = partial_for(t_l)
-        if recv_r is not None:
-            send_r = send_r + recv_r.astype(jnp.float32)
-            send_l = send_l + recv_l.astype(jnp.float32)
-        recv_r = lax.ppermute(
-            send_r.astype(jnp.bfloat16), "seq", [(z, z + 1) for z in range(i)]
+    if n_seq > 8:
+        partial = jnp.concatenate([partial_for(t) for t in range(n_seq)], axis=0)
+        return lax.psum_scatter(
+            partial.astype(jnp.bfloat16), "seq", scatter_dimension=0, tiled=True
         )
-        recv_l = lax.ppermute(
-            send_l.astype(jnp.bfloat16), "seq", [(z, z - 1) for z in range(n_seq - i, n_seq)]
-        )
-    total = partial_for(s_me)
-    if recv_r is not None:
-        total = total + recv_r.astype(jnp.float32) + recv_l.astype(jnp.float32)
+
+    parts = [partial_for(t) for t in range(n_seq)]
+    total = lax.dynamic_index_in_dim(jnp.stack(parts), s_me, 0, keepdims=False)
+    came_r = {}
+    for z in range(n_seq - 1):
+        for t in range(n_seq - 1, z, -1):
+            value = parts[t] if z == 0 else parts[t] + came_r[(z - 1, t)].astype(jnp.float32)
+            came_r[(z, t)] = lax.ppermute(value.astype(jnp.bfloat16), "seq", [(z, z + 1)])
+    came_l = {}
+    for z in range(n_seq - 1, 0, -1):
+        for t in range(z):
+            value = (
+                parts[t] if z == n_seq - 1 else parts[t] + came_l[(z + 1, t)].astype(jnp.float32)
+            )
+            came_l[(z, t)] = lax.ppermute(value.astype(jnp.bfloat16), "seq", [(z, z - 1)])
+    for z in range(1, n_seq):
+        total = total + came_r[(z - 1, z)].astype(jnp.float32)
+    for z in range(n_seq - 1):
+        total = total + came_l[(z + 1, z)].astype(jnp.float32)
     return total.astype(jnp.bfloat16)
 
 

time: 181 us -> 222 us (1.23)
  waiting for transfers between devices: 105 us -> 153 us
  matrix products: 15.2 us -> 9.08 us
    ppermute x6 -> x12, waiting for transfers between devices: 44.7 us -> 93.4 us  [the longest x6 51 us: per_device(): came_l[z, t] = lax.ppermute(value.astype(jnp.bfloat16), 'seq', [(z, z - 1)])]
    dot_general x7 -> x4, matrix products: 10 us -> 3.91 us  [partial_for(): jnp.einsum('deti,deic->tc', rows, w_perm, preferred_element_type=jnp.floa...]
    another operation x4 -> x3, other arithmetic: 4.32 us -> 1.41 us  [the longest x1 2.91 us: per_device(): gathered_x = jnp.stack([own, other], axis=1)]
    ppermute x6 -> x12, starting transfers between devices: 14.7 us -> 11.9 us  [the longest x6 6.88 us: per_device(): came_r[z, t] = lax.ppermute(value.astype(jnp.bfloat16), 'seq', [(z, z + 1)])]
  transfers between devices with their start and end apart: 13 -> 19, of which waited for: 8 -> 7; matrix products, arithmetic and copies ran while one was open for 10% -> 7% of each run, Pallas kernels for 0% -> 0%
where the time goes in v5:
time: 222 us
  waiting for transfers between devices  153 us (69%)
  starting transfers between devices  21.8 us (10%)
  other arithmetic  17.1 us (8%)
  between operations  13.9 us (6%)
  matrix products  9.08 us (4%)
  local copies, waits for them, and re-layouts  6.82 us (3%)
    ppermute x6, waiting for transfers between devices, per_device(): came_l[z, t] = lax.ppermute(value.astype(jnp.bfloat16), 'seq', [(z, z - 1)])  51 us
    ppermute x6, waiting for transfers between devices, per_device(): came_r[z, t] = lax.ppermute(value.astype(jnp.bfloat16), 'seq', [(z, z + 1)])  42.5 us
    all_gather x1, waiting for transfers between devices, per_device(): gathered = lax.all_gather(packed, 'seq', axis=0, tiled=False)  28.2 us
    ppermute x4, waiting for transfers between devices, per_device(): received.append(lax.ppermute(chunk, ('seq', 'mdl'), perm))  18 us
    ppermute x1, waiting for transfers between devices, per_device(): got.append(lax.ppermute(x, 'mdl', perm))  13.1 us
    ppermute x4, starting transfers between devices, per_device(): received.append(lax.ppermute(chunk, ('seq', 'mdl'), perm))  8.44 us
    ppermute x6, starting transfers between devices, per_device(): came_r[z, t] = lax.ppermute(value.astype(jnp.bfloat16), 'seq', [(z, z + 1)])  6.88 us
    ppermute x6, starting transfers between devices, per_device(): came_l[z, t] = lax.ppermute(value.astype(jnp.bfloat16), 'seq', [(z, z - 1)])  5.02 us
  transfers between devices with their start and end apart: 19, of which 7 were waited for; matrix products, arithmetic and copies ran while one was open for 7% of the time, Pallas kernels for 0%

profile of v5, /device:TPU:0, one launch (start us, length us, event | category | flops | bytes accessed | tf_op | source)
XLA Modules:
  0.0 221.5 jit_solution(12766561856259970399)
XLA Ops:
  6.5 1.3 reduce-window.6
  8.4 1.0 fusion.80
  9.4 1.4 fusion.28
  12.0 0.7 pad_maximum_fusion.3
  13.2 2.5 %fusion.18 = f32[1,256,8,128]{1,3,2,0:T(8,128)} fusion(bf16[256,8,128]{0,2,1:T(8,128)(2,1)S(1)} %bitcast.206, f32[8,256]{1,0:T(8,128)S(1)} %bitcast_add_fusion.8, pred[256,256]{1,0:T(8,128)(4,1)S(1)} %iota_compare_fusion, bf16[256,1024]{1,0:T(8,128)(2,1)S(1)} %copy-done.5, f32[1024]{0:T(1024)S(1)} %bitcast.215, bf16[256,1024]{1,0:T(8,128)(2,1)S(1)} %copy-done.4, ...), kind=kOutput, calls=%fused_computation.44 | convolution fusion | flops 276299776 | bytes 2703360 | tf_op jit(solution)/shard_map/hbij,bjhd->bihd/dot_general | solution.py:63
  15.6 28.2 %all-gather.3.cloned.1.call-done = bf16[32,16640]{1,0:T(8,128)(2,1)} async-done(((bf16[8,16640]{1,0:T(8,128)(2,1)}), bf16[32,16640]{1,0:T(8,128)(2,1)}) %all-gather.3.cloned.1.call-update) | async-done | bytes 1064976 | tf_op jit(solution)/shard_map/all_gather | solution.py:91
  43.8 0.8 add_reduce_fusion
  44.7 1.6 multiply_reduce_fusion
  46.5 2.3 %multiply_reduce_fusion.1 = (f32[256,8]{0,1:T(8,128)S(1)}, f32[1,256,8,128]{1,3,2,0:T(8,128)S(1)}) fusion(f32[1,256,8,128]{1,3,2,0:T(8,128)} %fusion.18, f32[8,128,128]{1,2,0:T(8,128)S(1)} %copy.46, f32[8]{0:T(128)S(1)} %get-tuple-element.33, f32[256,8]{0,1:T(8,128)S(1)} %get-tuple-element.20, bf16[256,1024]{1,0:T(8,128)(2,1)S(1)} %copy-done.5, ...), kind=kOutput, calls=%fused_computation.64 | convolution fusion | flops 407238656 | bytes 3166240 | tf_op jit(solution)/shard_map/bihd,bhde->bihe/dot_general | solution.py:111
  51.0 2.9 %collective-permute-start.1 = (bf16[256,256]{1,0:T(8,128)(2,1)S(1)}, bf16[256,256]{1,0:T(8,128)(2,1)S(1)}, u32[]{:S(2)}, u32[]{:S(2)}) collective-permute-start(bf16[256,256]{1,0:T(8,128)(2,1)S(1)} %get-tuple-element.29), channel_id=1, source_target_pairs={{0,1},{1,5},{2,9},{3,13},{4,2},{5,6},{6,10},{7,14},{8,3},{9,7},{10... | collective-permute-start | bytes 393224 | tf_op jit(solution)/shard_map/ppermute | solution.py:140
  53.8 3.4 %collective-permute-start.2 = (bf16[256,256]{1,0:T(8,128)(2,1)S(1)}, bf16[256,256]{1,0:T(8,128)(2,1)S(1)}, u32[]{:S(2)}, u32[]{:S(2)}) collective-permute-start(bf16[256,256]{1,0:T(8,128)(2,1)S(1)} %get-tuple-element.28), channel_id=1, source_target_pairs={{0,2},{1,6},{2,10},{3,14},{4,3},{5,7},{6,11},{7,15},{8,0},{9,4},{1... | collective-permute-start | bytes 393224 | tf_op jit(solution)/shard_map/ppermute | solution.py:140
  57.2 1.5 collective-permute-start.3
  58.8 4.6 %collective-permute-done.1 = bf16[256,256]{1,0:T(8,128)(2,1)S(1)} collective-permute-done((bf16[256,256]{1,0:T(8,128)(2,1)S(1)}, bf16[256,256]{1,0:T(8,128)(2,1)S(1)}, u32[]{:S(2)}, u32[]{:S(2)}) %collective-permute-start.1) | collective-permute-done | bytes 131104 | tf_op jit(solution)/shard_map/ppermute | solution.py:140
  63.4 13.4 %collective-permute-done.2 = bf16[256,256]{1,0:T(8,128)(2,1)S(1)} collective-permute-done((bf16[256,256]{1,0:T(8,128)(2,1)S(1)}, bf16[256,256]{1,0:T(8,128)(2,1)S(1)}, u32[]{:S(2)}, u32[]{:S(2)}) %collective-permute-start.2) | collective-permute-done | bytes 131104 | tf_op jit(solution)/shard_map/ppermute | solution.py:140
  77.8 13.1 %collective-permute-done.4 = bf16[4,256,256]{2,1,0:T(8,128)(2,1)S(1)} collective-permute-done((bf16[4,256,256]{2,1,0:T(8,128)(2,1)S(1)}, bf16[4,256,256]{2,1,0:T(8,128)(2,1)S(1)}, u32[]{:S(2)}, u32[]{:S(2)}) %collective-permute-start.4) | collective-permute-done | bytes 524320 | tf_op jit(solution)/shard_map/ppermute | solution.py:151
  91.1 1.4 collective-permute-start.5
  92.5 2.7 %multiply_convert_fusion = bf16[1024,1536]{1,0:T(8,128)(2,1)} fusion(bf16[1024,1536]{1,0:T(8,128)(2,1)S(1)} %copy-done, f32[1536]{0:T(1024)S(1)} %select_add_fusion), kind=kLoop, calls=%fused_computation.6 | loop fusion | flops 11010048 | bytes 6297600 | tf_op jit(solution)/shard_map/convert_element_type | solution.py:20
  95.3 4.3 %gather_fusion.1 = bf16[4,256,1536]{2,1,0:T(8,128)(2,1)} fusion(bf16[4,256,1536]{2,1,0:T(8,128)(2,1)} %bitcast.201, s32[1024]{0:T(1024)S(1)} %pad_clamp_fusion), kind=kCustom, calls=%fused_computation.1 | custom fusion | bytes 6291472 | tf_op jit(solution)/shard_map/jit(_take)/gather | solution.py:158
  99.6 2.3 %broadcast_select_fusion = bf16[4,256,1536]{2,1,0:T(8,128)(2,1)S(1)} fusion(bf16[4,256,1536]{2,1,0:T(8,128)(2,1)} %gather_fusion.1, pred[4]{0:T(512)(128)(4,1)S(1)} %get-tuple-element.46), kind=kLoop, calls=%fused_computation.7 | loop fusion | flops 1572864 | bytes 6291460 | tf_op jit(solution)/shard_map/jit(_take)/select_n | solution.py:158
  101.8 1.0 bitcast_convert_fusion.2
  102.8 2.1 collective-permute-start.7
  104.9 1.0 bitcast_convert_fusion.3
  106.6 1.3 collective-permute-start.6
  108.7 1.0 bitcast_convert_fusion.1
  109.7 1.3 collective-permute-start.9
  111.0 1.0 bitcast_convert_fusion
  112.0 10.8 %collective-permute-done.7 = bf16[256,1536]{1,0:T(8,128)(2,1)S(1)} collective-permute-done((bf16[256,1536]{1,0:T(8,128)(2,1)S(1)}, bf16[256,1536]{1,0:T(8,128)(2,1)S(1)}, u32[]{:S(2)}, u32[]{:S(2)}) %collective-permute-start.7) | collective-permute-done | bytes 786464 | tf_op jit(solution)/shard_map/ppermute | solution.py:180
  122.8 0.9 collective-permute-start.12
  123.9 31.7 %collective-permute-done.9 = bf16[256,1536]{1,0:T(8,128)(2,1)S(1)} collective-permute-done((bf16[256,1536]{1,0:T(8,128)(2,1)S(1)}, bf16[256,1536]{1,0:T(8,128)(2,1)S(1)}, u32[]{:S(2)}, u32[]{:S(2)}) %collective-permute-start.9) | collective-permute-done | bytes 786464 | tf_op jit(solution)/shard_map/ppermute | solution.py:180
  160.3 1.3 collective-permute-start.14
  161.7 51.0 %collective-permute-done.14 = bf16[256,1536]{1,0:T(8,128)(2,1)S(1)} collective-permute-done((bf16[256,1536]{1,0:T(8,128)(2,1)S(1)}, bf16[256,1536]{1,0:T(8,128)(2,1)S(1)}, u32[]{:S(2)}, u32[]{:S(2)}) %collective-permute-start.14) | collective-permute-done | bytes 786464 | tf_op jit(solution)/shard_map/ppermute | solution.py:187
  212.6 2.1 fusion.16
  (82 shorter events, 12.0 us)
Async XLA Ops:
  6.5 4.5 %copy-start.4 = (bf16[256,1024]{1,0:T(8,128)(2,1)S(1)}, bf16[256,1024]{1,0:T(8,128)(2,1)}, u32[]{:S(2)}) copy-start(bf16[256,1024]{1,0:T(8,128)(2,1)} %param.11) | copy-start | bytes 1572868
  6.5 37.3 %all-gather.3.cloned.1.call-start = ((), (), s32[]{:S(2)}) async-start(), calls=%async_computation | async-start | bytes 1331200 | tf_op jit(solution)/shard_map/all_gather | solution.py:91
  11.1 2.1 copy-start.5
  48.8 1.0 copy-start.1
  48.8 1.0 copy-start.3
  50.2 27.5 %copy-start.2 = (s32[1536]{0:T(1024)S(1)}, s32[1536]{0:T(1024)}, u32[]{:S(2)}) copy-start(s32[1536]{0:T(1024)} %param.17) | copy-start | bytes 18436
  50.3 8.5 %collective-permute-start = (bf16[256,256]{1,0:T(8,128)(2,1)S(1)}, bf16[256,256]{1,0:T(8,128)(2,1)S(1)}, u32[]{:S(2)}, u32[]{:S(2)}) collective-permute-start(bf16[256,256]{1,0:T(8,128)(2,1)S(1)} %get-tuple-element.26), channel_id=1, source_target_pairs={{0,0},{1,4},{2,8},{3,12},{4,1},{5,5},{6,9},{7,13},{8,2},{9,6},{10,... | collective-permute-start | bytes 393224 | tf_op jit(solution)/shard_map/ppermute | solution.py:140
  51.0 12.4 %collective-permute-start.1 = (bf16[256,256]{1,0:T(8,128)(2,1)S(1)}, bf16[256,256]{1,0:T(8,128)(2,1)S(1)}, u32[]{:S(2)}, u32[]{:S(2)}) collective-permute-start(bf16[256,256]{1,0:T(8,128)(2,1)S(1)} %get-tuple-element.29), channel_id=1, source_target_pairs={{0,1},{1,5},{2,9},{3,13},{4,2},{5,6},{6,10},{7,14},{8,3},{9,7},{10... | collective-permute-start | bytes 393224 | tf_op jit(solution)/shard_map/ppermute | solution.py:140
  53.8 23.0 %collective-permute-start.2 = (bf16[256,256]{1,0:T(8,128)(2,1)S(1)}, bf16[256,256]{1,0:T(8,128)(2,1)S(1)}, u32[]{:S(2)}, u32[]{:S(2)}) collective-permute-start(bf16[256,256]{1,0:T(8,128)(2,1)S(1)} %get-tuple-element.28), channel_id=1, source_target_pairs={{0,2},{1,6},{2,10},{3,14},{4,3},{5,7},{6,11},{7,15},{8,0},{9,4},{1... | collective-permute-start | bytes 393224 | tf_op jit(solution)/shard_map/ppermute | solution.py:140
  57.2 19.6 %collective-permute-start.3 = (bf16[256,256]{1,0:T(8,128)(2,1)S(1)}, bf16[256,256]{1,0:T(8,128)(2,1)S(1)}, u32[]{:S(2)}, u32[]{:S(2)}) collective-permute-start(bf16[256,256]{1,0:T(8,128)(2,1)S(1)} %get-tuple-element.27), channel_id=1, source_target_pairs={{0,3},{1,7},{2,11},{3,15},{4,0},{5,4},{6,8},{7,12},{8,1},{9,5},{10... | collective-permute-start | bytes 393224 | tf_op jit(solution)/shard_map/ppermute | solution.py:140
  77.6 13.4 %collective-permute-start.4 = (bf16[4,256,256]{2,1,0:T(8,128)(2,1)S(1)}, bf16[4,256,256]{2,1,0:T(8,128)(2,1)S(1)}, u32[]{:S(2)}, u32[]{:S(2)}) collective-permute-start(bf16[4,256,256]{2,1,0:T(8,128)(2,1)S(1)} %broadcast_select_fusion.1), channel_id=1, source_target_pairs={{0,2},{1,3},{2,0},{3,1},{4,6},{5,7},{6,4},{7,5},{8,10},{9,11},{10,... | collective-permute-start | bytes 1572872 | tf_op jit(solution)/shard_map/ppermute | solution.py:151
  77.7 14.8 %copy-start = (bf16[1024,1536]{1,0:T(8,128)(2,1)S(1)}, bf16[1024,1536]{1,0:T(8,128)(2,1)}, u32[]{:S(2)}) copy-start(bf16[1024,1536]{1,0:T(8,128)(2,1)} %param.16) | copy-start | bytes 9437188
  91.1 10.7 %collective-permute-start.5 = (bf16[2,4,256,256]{3,2,0,1:T(8,128)(2,1)S(1)}, bf16[2,4,256,256]{3,2,0,1:T(8,128)(2,1)S(1)}, u32[]{:S(2)}, u32[]{:S(2)}) collective-permute-start(bf16[2,4,256,256]{3,2,0,1:T(8,128)(2,1)S(1)} %get-tuple-element.24), channel_id=1, source_target_pairs={{0,1},{1,0},{2,3},{3,2},{4,5},{5,4},{6,7},{7,6},{8,9},{9,8},{10,11... | collective-permute-start | bytes 3145736 | tf_op jit(solution)/shard_map/ppermute | solution.py:153
  102.8 19.9 %collective-permute-start.7 = (bf16[256,1536]{1,0:T(8,128)(2,1)S(1)}, bf16[256,1536]{1,0:T(8,128)(2,1)S(1)}, u32[]{:S(2)}, u32[]{:S(2)}) collective-permute-start(bf16[256,1536]{1,0:T(8,128)(2,1)S(1)} %get-tuple-element.38), channel_id=1, source_target_pairs={{0,4},{1,5},{2,6},{3,7},{16,20},{17,21},{18,22},{19,23}} | collective-permute-start | bytes 2359304 | tf_op jit(solution)/shard_map/ppermute | solution.py:180
  105.9 51.6 %collective-permute-start.15 = (bf16[256,1536]{1,0:T(8,128)(2,1)S(1)}, bf16[256,1536]{1,0:T(8,128)(2,1)S(1)}, u32[]{:S(2)}, u32[]{:S(2)}) collective-permute-start(bf16[256,1536]{1,0:T(8,128)(2,1)S(1)} %get-tuple-element.40), channel_id=1, source_target_pairs={{12,8},{13,9},{14,10},{15,11},{28,24},{29,25},{30,26},{31,27}} | collective-permute-start | bytes 2359304 | tf_op jit(solution)/shard_map/ppermute | solution.py:187
  106.6 53.7 %collective-permute-start.6 = (bf16[256,1536]{1,0:T(8,128)(2,1)S(1)}, bf16[256,1536]{1,0:T(8,128)(2,1)S(1)}, u32[]{:S(2)}, u32[]{:S(2)}) collective-permute-start(bf16[256,1536]{1,0:T(8,128)(2,1)S(1)} %get-tuple-element.40), channel_id=1, source_target_pairs={{0,4},{1,5},{2,6},{3,7},{16,20},{17,21},{18,22},{19,23}} | collective-permute-start | bytes 2359304 | tf_op jit(solution)/shard_map/ppermute | solution.py:180
  108.0 53.7 %collective-permute-start.17 = (bf16[256,1536]{1,0:T(8,128)(2,1)S(1)}, bf16[256,1536]{1,0:T(8,128)(2,1)S(1)}, u32[]{:S(2)}, u32[]{:S(2)}) collective-permute-start(bf16[256,1536]{1,0:T(8,128)(2,1)S(1)} %get-tuple-element.38), channel_id=1, source_target_pairs={{12,8},{13,9},{14,10},{15,11},{28,24},{29,25},{30,26},{31,27}} | collective-permute-start | bytes 2359304 | tf_op jit(solution)/shard_map/ppermute | solution.py:187
  109.7 45.9 %collective-permute-start.9 = (bf16[256,1536]{1,0:T(8,128)(2,1)S(1)}, bf16[256,1536]{1,0:T(8,128)(2,1)S(1)}, u32[]{:S(2)}, u32[]{:S(2)}) collective-permute-start(bf16[256,1536]{1,0:T(8,128)(2,1)S(1)} %get-tuple-element.44), channel_id=1, source_target_pairs={{0,4},{1,5},{2,6},{3,7},{16,20},{17,21},{18,22},{19,23}} | collective-permute-start | bytes 2359304 | tf_op jit(solution)/shard_map/ppermute | solution.py:180
  122.8 33.7 %collective-permute-start.12 = (bf16[256,1536]{1,0:T(8,128)(2,1)S(1)}, bf16[256,1536]{1,0:T(8,128)(2,1)S(1)}, u32[]{:S(2)}, u32[]{:S(2)}) collective-permute-start(bf16[256,1536]{1,0:T(8,128)(2,1)S(1)} %get-tuple-element.42), channel_id=1, source_target_pairs={{12,8},{13,9},{14,10},{15,11},{28,24},{29,25},{30,26},{31,27}} | collective-permute-start | bytes 2359304 | tf_op jit(solution)/shard_map/ppermute | solution.py:187
  155.6 6.1 %collective-permute-start.8 = (bf16[256,1536]{1,0:T(8,128)(2,1)S(1)}, bf16[256,1536]{1,0:T(8,128)(2,1)S(1)}, u32[]{:S(2)}, u32[]{:S(2)}) collective-permute-start(bf16[256,1536]{1,0:T(8,128)(2,1)S(1)} %fusion.14), channel_id=1, source_target_pairs={{4,8},{5,9},{6,10},{7,11},{20,24},{21,25},{22,26},{23,27}} | collective-permute-start | bytes 2359304 | tf_op jit(solution)/shard_map/ppermute | solution.py:180
  156.5 1.9 collective-permute-start.10
  157.5 1.9 collective-permute-start.13
  158.4 3.2 %collective-permute-start.16 = (bf16[256,1536]{1,0:T(8,128)(2,1)S(1)}, bf16[256,1536]{1,0:T(8,128)(2,1)S(1)}, u32[]{:S(2)}, u32[]{:S(2)}) collective-permute-start(bf16[256,1536]{1,0:T(8,128)(2,1)S(1)} %fusion.15), channel_id=1, source_target_pairs={{8,4},{9,5},{10,6},{11,7},{24,20},{25,21},{26,22},{27,23}} | collective-permute-start | bytes 2359304 | tf_op jit(solution)/shard_map/ppermute | solution.py:187
  159.4 2.3 %collective-permute-start.11 = (bf16[256,1536]{1,0:T(8,128)(2,1)S(1)}, bf16[256,1536]{1,0:T(8,128)(2,1)S(1)}, u32[]{:S(2)}, u32[]{:S(2)}) collective-permute-start(bf16[256,1536]{1,0:T(8,128)(2,1)S(1)} %fusion.12), channel_id=1, source_target_pairs={{8,12},{9,13},{10,14},{11,15},{24,28},{25,29},{26,30},{27,31}} | collective-permute-start | bytes 2359304 | tf_op jit(solution)/shard_map/ppermute | solution.py:180
  160.3 52.3 %collective-permute-start.14 = (bf16[256,1536]{1,0:T(8,128)(2,1)S(1)}, bf16[256,1536]{1,0:T(8,128)(2,1)S(1)}, u32[]{:S(2)}, u32[]{:S(2)}) collective-permute-start(bf16[256,1536]{1,0:T(8,128)(2,1)S(1)} %fusion.10), channel_id=1, source_target_pairs={{4,0},{5,1},{6,2},{7,3},{20,16},{21,17},{22,18},{23,19}} | collective-permute-start | bytes 2359304 | tf_op jit(solution)/shard_map/ppermute | solution.py:187
Sparse Core Ops, SparseCore 0:
  12.9 30.8 all-gather.2

commit v6 on v4

--- a/solution.py
+++ b/solution.py
@@ -33,7 +33,6 @@
     out_weight,
     weight_exponent,
 ):
-    weights = fake_quant(out_weight, weight_exponent[None, :])
     tok_rows = query_proj.shape[0]
     feat_here = query_proj.shape[1]
     heads_here = log_decay.shape[0]
@@ -63,6 +62,20 @@
     within_block = jnp.einsum(
         "hbij,bjhd->bihd", block_probs, values, preferred_element_type=jnp.float32
     )
+    weights = fake_quant(out_weight, weight_exponent[None, :])
+    rows_w, cols_w = weights.shape
+    piece = rows_w // n_mdl
+    n_x = n_mdl // 2
+    m_me = lax.axis_index("mdl")
+    core = m_me % 2
+    xi = m_me // 2
+    d_idx = jnp.arange(n_x)[:, None]
+    e_idx = jnp.arange(2)[None, :]
+    mu_tab = 2 * ((xi - d_idx) % n_x) + jnp.where(e_idx == 0, core, 1 - core)
+    w_perm = jnp.take(
+        weights.reshape(n_mdl, piece, cols_w), mu_tab.reshape(-1), axis=0
+    ).reshape(n_x, 2, piece, cols_w)
+    within_block, w_perm = lax.optimization_barrier((within_block, w_perm))
     tail_decay = jnp.transpose(jnp.exp(block_total[:, :, None] - decay_cum), (1, 2, 0))
     weighted = (key_feat.astype(jnp.float32) * tail_decay[..., None]).astype(jnp.bfloat16)
     block_states = jnp.einsum(
@@ -122,11 +135,8 @@
         jnp.bfloat16
     )
 
-    rows_w, cols_w = weights.shape
     blocks_here = feat_here // rows_w
-    piece = rows_w // n_mdl
     s_me = lax.axis_index("seq")
-    m_me = lax.axis_index("mdl")
     received = []
     for k in range(n_seq):
         perm = []
@@ -142,27 +152,20 @@
     j_me = (s_me % blocks_here) * n_mdl + m_me
     x = jnp.take(received, (j_me - jnp.arange(n_seq)) % n_seq, axis=0)
 
-    n_x = n_mdl // 2
-    core = m_me % 2
-    xi = m_me // 2
     got = [x]
     for d in range(1, n_x):
         perm = [(mu, ((mu // 2 + d) % n_x) * 2 + mu % 2) for mu in range(n_mdl)]
         got.append(lax.ppermute(x, "mdl", perm))
     own = jnp.stack(got)
     other = lax.ppermute(own, "mdl", [(mu, mu ^ 1) for mu in range(n_mdl)])
-    gathered_x = jnp.stack([own, other], axis=1)
-    d_idx = jnp.arange(n_x)[:, None]
-    e_idx = jnp.arange(2)[None, :]
-    mu_tab = 2 * ((xi - d_idx) % n_x) + jnp.where(e_idx == 0, core, 1 - core)
-    w_perm = jnp.take(
-        weights.reshape(n_mdl, piece, cols_w), mu_tab.reshape(-1), axis=0
-    ).reshape(n_x, 2, piece, cols_w)
 
     def partial_for(target):
-        rows = lax.dynamic_index_in_dim(gathered_x, target, 2, keepdims=False)
+        rows_own = lax.dynamic_index_in_dim(own, target, 1, keepdims=False)
+        rows_other = lax.dynamic_index_in_dim(other, target, 1, keepdims=False)
         return jnp.einsum(
-            "deti,deic->tc", rows, w_perm, preferred_element_type=jnp.float32
+            "dti,dic->tc", rows_own, w_perm[:, 0], preferred_element_type=jnp.float32
+        ) + jnp.einsum(
+            "dti,dic->tc", rows_other, w_perm[:, 1], preferred_element_type=jnp.float32
         )
 
     recv_r = None

time: 181 us -> 189 us (1.044)
  waiting for transfers between devices: 105 us -> 94.6 us
  matrix products: 15.2 us -> 22.7 us
  local copies, waits for them, and re-layouts: 4.92 us -> 10.5 us
  other arithmetic: 18 us -> 22.6 us
    all_gather x1, waiting for transfers between devices: 28.2 us -> 19.6 us  [per_device(): gathered = lax.all_gather(packed, 'seq', axis=0, tiled=False)]
    dot_general x7 -> x14, matrix products: 10 us -> 16.9 us  [the longest x7 11.8 us: partial_for(): jnp.einsum('dti,dic->tc', rows_other, w_perm[:, 1], preferred_element_typ...]
    another operation x4 -> x3, other arithmetic: 4.32 us -> 1.44 us  [the longest x1 2.91 us: per_device(): gathered_x = jnp.stack([own, other], axis=1)]
    reshape x1, local copies, waits for them, and re-layouts: 0.33 us -> 2.61 us  [per_device(): (attended * lax.rsqrt(mean_square + 1e-05)).reshape(tok_rows, heads_here...]
    unnamed x2 -> x3, other arithmetic: 1.65 us -> 3.92 us
    select_n x3, other arithmetic: 0.25 us -> 2.33 us  [per_device(): x = jnp.take(received, (j_me - jnp.arange(n_seq)) % n_seq, axis=0)]
  transfers between devices with their start and end apart: 13 -> 13, of which waited for: 8 -> 9; matrix products, arithmetic and copies ran while one was open for 10% -> 14% of each run, Pallas kernels for 0% -> 0%
where the time goes in v6:
time: 189 us; the launch traced here: 188 us
  waiting for transfers between devices  94.6 us (50%)
  starting transfers between devices  23.7 us (13%)
  matrix products  22.7 us (12%)
  other arithmetic  22.6 us (12%)
  between operations  13.8 us (7%)
  local copies, waits for them, and re-layouts  10.5 us (6%)
    ppermute x3, waiting for transfers between devices, per_device(): lax.ppermute(send_r.astype(jnp.bfloat16), 'seq', [(z, z + 1) for z in ran...  38.7 us
    all_gather x1, waiting for transfers between devices, per_device(): gathered = lax.all_gather(packed, 'seq', axis=0, tiled=False)  19.6 us
    ppermute x4, waiting for transfers between devices, per_device(): received.append(lax.ppermute(chunk, ('seq', 'mdl'), perm))  18.1 us
    ppermute x1, waiting for transfers between devices, per_device(): got.append(lax.ppermute(x, 'mdl', perm))  12.1 us
    dot_general x7, matrix products, partial_for(): jnp.einsum('dti,dic->tc', rows_other, w_perm[:, 1], preferred_element_typ...  11.8 us
    ppermute x3, starting transfers between devices, per_device(): lax.ppermute(send_r.astype(jnp.bfloat16), 'seq', [(z, z + 1) for z in ran...  11 us
    ppermute x4, starting transfers between devices, per_device(): received.append(lax.ppermute(chunk, ('seq', 'mdl'), perm))  8.44 us
    ppermute x3, waiting for transfers between devices, per_device(): lax.ppermute(send_l.astype(jnp.bfloat16), 'seq', [(z, z - 1) for z in ran...  5.75 us
  transfers between devices with their start and end apart: 13, of which 9 were waited for; matrix products, arithmetic and copies ran while one was open for 14% of the time, Pallas kernels for 0%

profile of v6, /device:TPU:0, one launch (start us, length us, event | category | flops | bytes accessed | tf_op | source)
XLA Modules:
  0.0 187.9 jit_solution(12044129260379072238)
XLA Ops:
  14.7 2.8 %multiply_convert_fusion = bf16[1024,1536]{1,0:T(8,128)(2,1)S(1)} fusion(bf16[1024,1536]{1,0:T(8,128)(2,1)} %param.16, f32[1536]{0:T(1024)S(1)} %select_add_fusion), kind=kLoop, calls=%fused_computation.2 | loop fusion | flops 11010048 | bytes 6297600 | tf_op jit(solution)/shard_map/convert_element_type | solution.py:20
  17.5 2.4 %gather_fusion = bf16[4,256,1536]{2,1,0:T(8,128)(2,1)} fusion(bf16[4,256,1536]{2,1,0:T(8,128)(2,1)S(1)} %bitcast.238, s32[1024]{0:T(1024)S(1)} %pad_clamp_fusion.1), kind=kCustom, calls=%fused_computation | custom fusion | bytes 6291472 | tf_op jit(solution)/shard_map/jit(_take)/gather | solution.py:75
  20.0 3.3 %fusion.35 = f32[1,256,8,128]{1,3,2,0:T(8,128)} fusion(bf16[256,8,128]{0,2,1:T(8,128)(2,1)} %bitcast.241, f32[8,256]{1,0:T(8,128)S(1)} %bitcast_add_fusion.2, pred[256,256]{1,0:T(8,128)(4,1)S(1)} %iota_compare_fusion, bf16[32,8,8,128]{3,2,1,0:T(8,128)(2,1)} %get-tuple-element.41, bf16[32,8,8,128]{3,2,1,0:T(8,128)(2,1)} %copy-done.5), kind=kOutput, calls=%fused_computation.70 | convolution fusion | flops 271056896 | bytes 2695168 | tf_op jit(solution)/shard_map/hbij,bjhd->bihd/dot_general | solution.py:62
  23.3 2.4 %copy_select_fusion = bf16[2,2,256,1536]{3,2,0,1:T(8,128)(2,1)S(1)} fusion(bf16[2,2,256,1536]{3,2,1,0:T(8,128)(2,1)} %bitcast.237, pred[2,2]{0,1:T(4,128)(4,1)S(1)} %copy.33), kind=kLoop, calls=%fused_computation.3 | loop fusion | flops 1572864 | bytes 6291460 | tf_op jit(solution)/shard_map/jit(_take)/select_n | solution.py:75
  25.8 19.6 %all-gather.3.cloned.1.call-done = bf16[32,16640]{1,0:T(8,128)(2,1)} async-done(((bf16[8,16640]{1,0:T(8,128)(2,1)}), bf16[32,16640]{1,0:T(8,128)(2,1)}) %all-gather.3.cloned.1.call-update) | async-done | bytes 1064976 | tf_op jit(solution)/shard_map/all_gather | solution.py:104
  46.3 2.4 %multiply_reduce_fusion = f32[8,128,128]{2,0,1:T(8,128)} fusion(bf16[4,8,16640]{2,1,0:T(8,128)(2,1)} %bitcast.243, f32[8,4]{0,1:T(4,128)S(1)} %select_bitcast_fusion), kind=kLoop, calls=%fused_computation.38 | loop fusion | flops 1441792 | bytes 1572992
  48.6 2.0 %copy.45 = f32[8,128,128]{1,2,0:T(8,128)} copy(f32[8,128,128]{2,0,1:T(8,128)} %multiply_reduce_fusion) | data formatting | bytes 1048576 | tf_op jit(solution)/shard_map/nh,nhde->hde/dot_general | solution.py:119
  50.7 2.3 %multiply_reduce_fusion.1 = (f32[256,8]{0,1:T(8,128)S(1)}, f32[1,256,8,128]{1,3,2,0:T(8,128)S(1)}) fusion(f32[1,256,8,128]{1,3,2,0:T(8,128)} %fusion.35, bf16[32,8,8,128]{3,2,1,0:T(8,128)(2,1)} %get-tuple-element.41, f32[8,128,128]{1,2,0:T(8,128)} %copy.45, f32[8]{0:T(128)S(1)} %get-tuple-element.35, f32[256,8]{0,1:T(8,128)S(1)} %get-tuple-element.26), kind=kOutput, calls=%fused_computation.89 | convolution fusion | flops 403830784 | bytes 3162144 | tf_op jit(solution)/shard_map/bihd,bhde->bihe/dot_general | solution.py:124
  54.0 2.6 %copy.38 = f32[256,1024]{1,0:T(8,128)} copy(f32[256,1024]{0,1:T(8,128)} %bitcast.239) | data formatting | bytes 2097152 | tf_op jit(solution)/shard_map/reshape | solution.py:133
  56.6 1.7 multiply_convert_fusion.2
  59.1 2.9 %collective-permute-start.1 = (bf16[256,256]{1,0:T(8,128)(2,1)S(1)}, bf16[256,256]{1,0:T(8,128)(2,1)S(1)}, u32[]{:S(2)}, u32[]{:S(2)}) collective-permute-start(bf16[256,256]{1,0:T(8,128)(2,1)S(1)} %get-tuple-element.31), channel_id=1, source_target_pairs={{0,1},{1,5},{2,9},{3,13},{4,2},{5,6},{6,10},{7,14},{8,3},{9,7},{10... | collective-permute-start | bytes 393224 | tf_op jit(solution)/shard_map/ppermute | solution.py:150
  61.9 3.4 %collective-permute-start.2 = (bf16[256,256]{1,0:T(8,128)(2,1)S(1)}, bf16[256,256]{1,0:T(8,128)(2,1)S(1)}, u32[]{:S(2)}, u32[]{:S(2)}) collective-permute-start(bf16[256,256]{1,0:T(8,128)(2,1)S(1)} %get-tuple-element.30), channel_id=1, source_target_pairs={{0,2},{1,6},{2,10},{3,14},{4,3},{5,7},{6,11},{7,15},{8,0},{9,4},{1... | collective-permute-start | bytes 393224 | tf_op jit(solution)/shard_map/ppermute | solution.py:150
  65.4 1.5 collective-permute-start.3
  66.9 4.6 %collective-permute-done.1 = bf16[256,256]{1,0:T(8,128)(2,1)S(1)} collective-permute-done((bf16[256,256]{1,0:T(8,128)(2,1)S(1)}, bf16[256,256]{1,0:T(8,128)(2,1)S(1)}, u32[]{:S(2)}, u32[]{:S(2)}) %collective-permute-start.1) | collective-permute-done | bytes 131104 | tf_op jit(solution)/shard_map/ppermute | solution.py:150
  71.5 13.4 %collective-permute-done.2 = bf16[256,256]{1,0:T(8,128)(2,1)S(1)} collective-permute-done((bf16[256,256]{1,0:T(8,128)(2,1)S(1)}, bf16[256,256]{1,0:T(8,128)(2,1)S(1)}, u32[]{:S(2)}, u32[]{:S(2)}) %collective-permute-start.2) | collective-permute-done | bytes 131104 | tf_op jit(solution)/shard_map/ppermute | solution.py:150
  85.8 2.4 %gather_fusion.1 = bf16[4,256,256]{2,1,0:T(8,128)(2,1)} fusion(bf16[4,256,256]{2,1,0:T(8,128)(2,1)} %pad_maximum_fusion.1, s32[1024]{0:T(1024)S(1)} %pad_clamp_fusion), kind=kCustom, calls=%fused_computation.1 | custom fusion | bytes 1048592 | tf_op jit(solution)/shard_map/jit(_take)/gather | solution.py:153
  90.6 12.1 %collective-permute-done.4 = bf16[4,256,256]{2,1,0:T(8,128)(2,1)S(1)} collective-permute-done((bf16[4,256,256]{2,1,0:T(8,128)(2,1)S(1)}, bf16[4,256,256]{2,1,0:T(8,128)(2,1)S(1)}, u32[]{:S(2)}, u32[]{:S(2)}) %collective-permute-start.4) | collective-permute-done | bytes 524320 | tf_op jit(solution)/shard_map/ppermute | solution.py:158
  105.3 1.6 convolution_bitcast_fusion.7
  107.9 1.5 fusion.19
  109.4 2.1 %collective-permute-start.6 = (bf16[256,1536]{1,0:T(8,128)(2,1)S(1)}, bf16[256,1536]{1,0:T(8,128)(2,1)S(1)}, u32[]{:S(2)}, u32[]{:S(2)}) collective-permute-start(bf16[256,1536]{1,0:T(8,128)(2,1)S(1)} %fusion.19), channel_id=1, source_target_pairs={{0,4},{1,5},{2,6},{3,7},{16,20},{17,21},{18,22},{19,23}} | collective-permute-start | bytes 2359304 | tf_op jit(solution)/shard_map/ppermute | solution.py:181
  111.5 1.6 fusion.18
  115.0 13.8 %collective-permute-done.6 = bf16[256,1536]{1,0:T(8,128)(2,1)S(1)} collective-permute-done((bf16[256,1536]{1,0:T(8,128)(2,1)S(1)}, bf16[256,1536]{1,0:T(8,128)(2,1)S(1)}, u32[]{:S(2)}, u32[]{:S(2)}) %collective-permute-start.6) | collective-permute-done | bytes 786464 | tf_op jit(solution)/shard_map/ppermute | solution.py:181
  128.8 1.5 fusion.15
  130.3 4.4 %collective-permute-start.7 = (bf16[256,1536]{1,0:T(8,128)(2,1)S(1)}, bf16[256,1536]{1,0:T(8,128)(2,1)S(1)}, u32[]{:S(2)}, u32[]{:S(2)}) collective-permute-start(bf16[256,1536]{1,0:T(8,128)(2,1)S(1)} %fusion.15), channel_id=1, source_target_pairs={{0,4},{4,8},{1,5},{5,9},{2,6},{6,10},{3,7},{7,11},{16,20},{20,24},... | collective-permute-start | bytes 2359304 | tf_op jit(solution)/shard_map/ppermute | solution.py:181
  134.8 1.6 fusion.13
  138.4 12.8 %collective-permute-done.7 = bf16[256,1536]{1,0:T(8,128)(2,1)S(1)} collective-permute-done((bf16[256,1536]{1,0:T(8,128)(2,1)S(1)}, bf16[256,1536]{1,0:T(8,128)(2,1)S(1)}, u32[]{:S(2)}, u32[]{:S(2)}) %collective-permute-start.7) | collective-permute-done | bytes 786464 | tf_op jit(solution)/shard_map/ppermute | solution.py:181
  151.2 1.5 fusion.16
  152.8 4.4 %collective-permute-start.8 = (bf16[256,1536]{1,0:T(8,128)(2,1)S(1)}, bf16[256,1536]{1,0:T(8,128)(2,1)S(1)}, u32[]{:S(2)}, u32[]{:S(2)}) collective-permute-start(bf16[256,1536]{1,0:T(8,128)(2,1)S(1)} %fusion.16), channel_id=1, source_target_pairs={{0,4},{4,8},{8,12},{1,5},{5,9},{9,13},{2,6},{6,10},{10,14},{3,7},{... | collective-permute-start | bytes 2359304 | tf_op jit(solution)/shard_map/ppermute | solution.py:181
  157.3 1.6 fusion.14
  160.7 12.1 %collective-permute-done.8 = bf16[256,1536]{1,0:T(8,128)(2,1)S(1)} collective-permute-done((bf16[256,1536]{1,0:T(8,128)(2,1)S(1)}, bf16[256,1536]{1,0:T(8,128)(2,1)S(1)}, u32[]{:S(2)}, u32[]{:S(2)}) %collective-permute-start.8) | collective-permute-done | bytes 786464 | tf_op jit(solution)/shard_map/ppermute | solution.py:181
  172.8 5.7 %collective-permute-done.11 = bf16[256,1536]{1,0:T(8,128)(2,1)S(1)} collective-permute-done((bf16[256,1536]{1,0:T(8,128)(2,1)S(1)}, bf16[256,1536]{1,0:T(8,128)(2,1)S(1)}, u32[]{:S(2)}, u32[]{:S(2)}) %collective-permute-start.11) | collective-permute-done | bytes 786464 | tf_op jit(solution)/shard_map/ppermute | solution.py:184
  178.5 2.5 %fusion.17 = bf16[256,1536]{1,0:T(8,128)(2,1)} fusion(f32[256,1536]{1,0:T(8,128)S(1)} %convolution_bitcast_fusion.13, bf16[256,1536]{1,0:T(8,128)(2,1)S(1)} %collective-permute-done.11, bf16[256,1536]{1,0:T(8,128)(2,1)S(1)} %collective-permute-done.8, bf16[2,2,256,1536]{3,2,0,1:T(8,128)(2,1)S(1)} %copy_select_fusion, ...), kind=kOutput, calls=%fused_computation.35 | convolution fusion | flops 405012480 | bytes 5767172 | tf_op jit(solution)/shard_map/dti,dic->tc/dot_general | solution.py:167
  (82 shorter events, 23.5 us)
Async XLA Ops:
  6.5 4.6 %copy-start.6 = (bf16[256,1024]{1,0:T(8,128)(2,1)S(1)}, bf16[256,1024]{1,0:T(8,128)(2,1)}, u32[]{:S(2)}) copy-start(bf16[256,1024]{1,0:T(8,128)(2,1)} %param.11) | copy-start | bytes 1572868
  6.5 4.6 %copy-start.7 = (bf16[256,1024]{1,0:T(8,128)(2,1)S(1)}, bf16[256,1024]{1,0:T(8,128)(2,1)}, u32[]{:S(2)}) copy-start(bf16[256,1024]{1,0:T(8,128)(2,1)} %param.9) | copy-start | bytes 1572868
  6.5 38.8 %all-gather.3.cloned.1.call-start = ((), (), s32[]{:S(2)}) async-start(), calls=%async_computation | async-start | bytes 1331200 | tf_op jit(solution)/shard_map/all_gather | solution.py:104
  11.1 1.8 copy-start.4
  12.6 0.8 copy-start.5
  12.6 2.0 %copy-start.8 = (s32[1536]{0:T(1024)S(1)}, s32[1536]{0:T(1024)}, u32[]{:S(2)}) copy-start(s32[1536]{0:T(1024)} %param.17) | copy-start | bytes 18436
  54.0 2.6 %copy-start.9 = (f32[1024]{0:T(1024)S(1)}, f32[1024]{0:T(1024)}, u32[]{:S(2)}) copy-start(f32[1024]{0:T(1024)} %param.15) | copy-start | bytes 12292
  58.4 8.5 %collective-permute-start = (bf16[256,256]{1,0:T(8,128)(2,1)S(1)}, bf16[256,256]{1,0:T(8,128)(2,1)S(1)}, u32[]{:S(2)}, u32[]{:S(2)}) collective-permute-start(bf16[256,256]{1,0:T(8,128)(2,1)S(1)} %get-tuple-element.28), channel_id=1, source_target_pairs={{0,0},{1,4},{2,8},{3,12},{4,1},{5,5},{6,9},{7,13},{8,2},{9,6},{10,... | collective-permute-start | bytes 393224 | tf_op jit(solution)/shard_map/ppermute | solution.py:150
  59.1 12.4 %collective-permute-start.1 = (bf16[256,256]{1,0:T(8,128)(2,1)S(1)}, bf16[256,256]{1,0:T(8,128)(2,1)S(1)}, u32[]{:S(2)}, u32[]{:S(2)}) collective-permute-start(bf16[256,256]{1,0:T(8,128)(2,1)S(1)} %get-tuple-element.31), channel_id=1, source_target_pairs={{0,1},{1,5},{2,9},{3,13},{4,2},{5,6},{6,10},{7,14},{8,3},{9,7},{10... | collective-permute-start | bytes 393224 | tf_op jit(solution)/shard_map/ppermute | solution.py:150
  61.9 23.0 %collective-permute-start.2 = (bf16[256,256]{1,0:T(8,128)(2,1)S(1)}, bf16[256,256]{1,0:T(8,128)(2,1)S(1)}, u32[]{:S(2)}, u32[]{:S(2)}) collective-permute-start(bf16[256,256]{1,0:T(8,128)(2,1)S(1)} %get-tuple-element.30), channel_id=1, source_target_pairs={{0,2},{1,6},{2,10},{3,14},{4,3},{5,7},{6,11},{7,15},{8,0},{9,4},{1... | collective-permute-start | bytes 393224 | tf_op jit(solution)/shard_map/ppermute | solution.py:150
  65.4 19.6 %collective-permute-start.3 = (bf16[256,256]{1,0:T(8,128)(2,1)S(1)}, bf16[256,256]{1,0:T(8,128)(2,1)S(1)}, u32[]{:S(2)}, u32[]{:S(2)}) collective-permute-start(bf16[256,256]{1,0:T(8,128)(2,1)S(1)} %get-tuple-element.29), channel_id=1, source_target_pairs={{0,3},{1,7},{2,11},{3,15},{4,0},{5,4},{6,8},{7,12},{8,1},{9,5},{10... | collective-permute-start | bytes 393224 | tf_op jit(solution)/shard_map/ppermute | solution.py:150
  89.4 13.4 %collective-permute-start.4 = (bf16[4,256,256]{2,1,0:T(8,128)(2,1)S(1)}, bf16[4,256,256]{2,1,0:T(8,128)(2,1)S(1)}, u32[]{:S(2)}, u32[]{:S(2)}) collective-permute-start(bf16[4,256,256]{2,1,0:T(8,128)(2,1)S(1)} %broadcast_select_fusion), channel_id=1, source_target_pairs={{0,2},{1,3},{2,0},{3,1},{4,6},{5,7},{6,4},{7,5},{8,10},{9,11},{10,... | collective-permute-start | bytes 1572872 | tf_op jit(solution)/shard_map/ppermute | solution.py:158
  90.6 12.1 %copy-start = (bf16[1,4,256,256]{3,2,1,0:T(8,128)(2,1)}, bf16[1,4,256,256]{3,2,1,0:T(8,128)(2,1)S(1)}, u32[]{:S(2)}) copy-start(bf16[1,4,256,256]{3,2,1,0:T(8,128)(2,1)S(1)} %bitcast_select_fusion) | copy-start | bytes 1572868
  102.7 1.2 copy-start.2
  103.9 4.0 %collective-permute-start.5 = (bf16[2,4,256,256]{3,2,1,0:T(8,128)(2,1)}, bf16[2,4,256,256]{3,2,1,0:T(8,128)(2,1)}, u32[]{:S(2)}, u32[]{:S(2)}) collective-permute-start(bf16[2,4,256,256]{3,2,1,0:T(8,128)(2,1)} %pad_maximum_fusion), channel_id=1, source_target_pairs={{0,1},{1,0},{2,3},{3,2},{4,5},{5,4},{6,7},{7,6},{8,9},{9,8},{10,11... | collective-permute-start | bytes 3145736 | tf_op jit(solution)/shard_map/ppermute | solution.py:160
  105.2 1.6 copy-start.1
  105.3 1.6 copy-start.3
  109.4 19.4 %collective-permute-start.6 = (bf16[256,1536]{1,0:T(8,128)(2,1)S(1)}, bf16[256,1536]{1,0:T(8,128)(2,1)S(1)}, u32[]{:S(2)}, u32[]{:S(2)}) collective-permute-start(bf16[256,1536]{1,0:T(8,128)(2,1)S(1)} %fusion.19), channel_id=1, source_target_pairs={{0,4},{1,5},{2,6},{3,7},{16,20},{17,21},{18,22},{19,23}} | collective-permute-start | bytes 2359304 | tf_op jit(solution)/shard_map/ppermute | solution.py:181
  113.1 21.7 %collective-permute-start.9 = (bf16[256,1536]{1,0:T(8,128)(2,1)S(1)}, bf16[256,1536]{1,0:T(8,128)(2,1)S(1)}, u32[]{:S(2)}, u32[]{:S(2)}) collective-permute-start(bf16[256,1536]{1,0:T(8,128)(2,1)S(1)} %fusion.18), channel_id=1, source_target_pairs={{12,8},{13,9},{14,10},{15,11},{28,24},{29,25},{30,26},{31,27}} | collective-permute-start | bytes 2359304 | tf_op jit(solution)/shard_map/ppermute | solution.py:184
  130.3 20.9 %collective-permute-start.7 = (bf16[256,1536]{1,0:T(8,128)(2,1)S(1)}, bf16[256,1536]{1,0:T(8,128)(2,1)S(1)}, u32[]{:S(2)}, u32[]{:S(2)}) collective-permute-start(bf16[256,1536]{1,0:T(8,128)(2,1)S(1)} %fusion.15), channel_id=1, source_target_pairs={{0,4},{4,8},{1,5},{5,9},{2,6},{6,10},{3,7},{7,11},{16,20},{20,24},... | collective-permute-start | bytes 2359304 | tf_op jit(solution)/shard_map/ppermute | solution.py:181
  136.4 20.9 %collective-permute-start.10 = (bf16[256,1536]{1,0:T(8,128)(2,1)S(1)}, bf16[256,1536]{1,0:T(8,128)(2,1)S(1)}, u32[]{:S(2)}, u32[]{:S(2)}) collective-permute-start(bf16[256,1536]{1,0:T(8,128)(2,1)S(1)} %fusion.13), channel_id=1, source_target_pairs={{8,4},{12,8},{9,5},{13,9},{10,6},{14,10},{11,7},{15,11},{24,20},{2... | collective-permute-start | bytes 2359304 | tf_op jit(solution)/shard_map/ppermute | solution.py:184
  152.8 20.0 %collective-permute-start.8 = (bf16[256,1536]{1,0:T(8,128)(2,1)S(1)}, bf16[256,1536]{1,0:T(8,128)(2,1)S(1)}, u32[]{:S(2)}, u32[]{:S(2)}) collective-permute-start(bf16[256,1536]{1,0:T(8,128)(2,1)S(1)} %fusion.16), channel_id=1, source_target_pairs={{0,4},{4,8},{8,12},{1,5},{5,9},{9,13},{2,6},{6,10},{10,14},{3,7},{... | collective-permute-start | bytes 2359304 | tf_op jit(solution)/shard_map/ppermute | solution.py:181
  158.8 19.7 %collective-permute-start.11 = (bf16[256,1536]{1,0:T(8,128)(2,1)S(1)}, bf16[256,1536]{1,0:T(8,128)(2,1)S(1)}, u32[]{:S(2)}, u32[]{:S(2)}) collective-permute-start(bf16[256,1536]{1,0:T(8,128)(2,1)S(1)} %fusion.14), channel_id=1, source_target_pairs={{4,0},{8,4},{12,8},{5,1},{9,5},{13,9},{6,2},{10,6},{14,10},{7,3},{... | collective-permute-start | bytes 2359304 | tf_op jit(solution)/shard_map/ppermute | solution.py:184
Sparse Core Ops, SparseCore 0:
  14.4 30.8 all-gather.2

commit v7 on v4

--- a/solution.py
+++ b/solution.py
@@ -88,24 +88,18 @@
         ],
         axis=1,
     )
-    gathered = lax.all_gather(packed, "seq", axis=0, tiled=False)
-    gathered_states = (
-        gathered[:, :, : HDIM * HDIM].astype(jnp.float32).reshape(n_seq, heads_here, HDIM, HDIM)
-    )
-    gathered_logs = gathered[:, :, HDIM * HDIM].astype(jnp.float32) + gathered[
-        :, :, HDIM * HDIM + HDIM
-    ].astype(jnp.float32)
     position = lax.axis_index("seq")
-    end_offsets = jnp.cumsum(gathered_logs, axis=0)
-    start_offsets = end_offsets - gathered_logs
-    own_start = lax.dynamic_index_in_dim(start_offsets, position, 0, keepdims=False)
-    earlier = jnp.arange(gathered_logs.shape[0])[:, None] < position
-    state_weight = jnp.where(
-        earlier, jnp.exp(jnp.minimum(own_start[None, :] - end_offsets, 0.0)), 0.0
-    )
-    incoming = jnp.einsum(
-        "nh,nhde->hde", state_weight, gathered_states, precision=lax.Precision.HIGHEST
-    )
+    incoming = jnp.zeros((heads_here, HDIM, HDIM), jnp.float32)
+    gap = jnp.zeros((heads_here,), jnp.float32)
+    for d in range(1, n_seq):
+        came = lax.ppermute(packed, "seq", [(z, z + d) for z in range(n_seq - d)])
+        came_state = came[:, : HDIM * HDIM].astype(jnp.float32).reshape(heads_here, HDIM, HDIM)
+        came_log = came[:, HDIM * HDIM].astype(jnp.float32) + came[:, HDIM * HDIM + HDIM].astype(
+            jnp.float32
+        )
+        weight = jnp.where(d <= position, jnp.exp(jnp.minimum(gap, 0.0)), 0.0)
+        incoming = incoming + weight[:, None, None] * came_state
+        gap = gap + came_log
     before = jnp.cumsum(block_total, axis=1) - block_total
     entry_state = entry_local + jnp.exp(before).T[:, :, None, None] * incoming[None]
     from_state = jnp.einsum(
@@ -165,25 +159,33 @@
             "deti,deic->tc", rows, w_perm, preferred_element_type=jnp.float32
         )
 
-    recv_r = None
-    recv_l = None
+    halves = 2 if cols_w % 256 == 0 else 1
+    width = cols_w // halves
+    recv_r = [None] * halves
+    recv_l = [None] * halves
     for i in range(1, n_seq):
         t_r = jnp.clip(s_me + n_seq - i, 0, n_seq - 1)
         t_l = jnp.clip(s_me - n_seq + i, 0, n_seq - 1)
-        send_r = partial_for(t_r)
-        send_l = partial_for(t_l)
-        if recv_r is not None:
-            send_r = send_r + recv_r.astype(jnp.float32)
-            send_l = send_l + recv_l.astype(jnp.float32)
-        recv_r = lax.ppermute(
-            send_r.astype(jnp.bfloat16), "seq", [(z, z + 1) for z in range(i)]
+        part_r = partial_for(t_r)
+        part_l = partial_for(t_l)
+        for h in range(halves):
+            send_r = part_r[:, h * width : (h + 1) * width]
+            send_l = part_l[:, h * width : (h + 1) * width]
+            if recv_r[h] is not None:
+                send_r = send_r + recv_r[h].astype(jnp.float32)
+                send_l = send_l + recv_l[h].astype(jnp.float32)
+            recv_r[h] = lax.ppermute(
+                send_r.astype(jnp.bfloat16), "seq", [(z, z + 1) for z in range(i)]
+            )
+            recv_l[h] = lax.ppermute(
+                send_l.astype(jnp.bfloat16), "seq", [(z, z - 1) for z in range(n_seq - i, n_seq)]
+            )
+    total = partial_for(s_me)
+    if recv_r[0] is not None:
+        total = total + jnp.concatenate(
+            [recv_r[h].astype(jnp.float32) + recv_l[h].astype(jnp.float32) for h in range(halves)],
+            axis=1,
         )
-        recv_l = lax.ppermute(
-            send_l.astype(jnp.bfloat16), "seq", [(z, z - 1) for z in range(n_seq - i, n_seq)]
-        )
-    total = partial_for(s_me)
-    if recv_r is not None:
-        total = total + recv_r.astype(jnp.float32) + recv_l.astype(jnp.float32)
     return total.astype(jnp.bfloat16)
 
 

time: 181 us -> 164 us (0.906)
  starting transfers between devices: 23.1 us -> 48.8 us
  waiting for transfers between devices: 105 us -> 79.7 us
  between operations: 13.9 us -> 0.63 us
  other arithmetic: 18 us -> 13.8 us
    all_gather x1 -> x0, waiting for transfers between devices: 28.2 us -> none  [per_device(): gathered = lax.all_gather(packed, 'seq', axis=0, tiled=False)]
    ppermute x3 -> x6, waiting for transfers between devices: 39.5 us -> 26.5 us  [per_device(): lax.ppermute(send_r.astype(jnp.bfloat16), 'seq', [(z, z + 1) for z in ran...]
    ppermute x0 -> x3, starting transfers between devices: none -> 10.7 us  [per_device(): came = lax.ppermute(packed, 'seq', [(z, z + d) for z in range(n_seq - d)])]
    ppermute x0 -> x3, waiting for transfers between devices: none -> 10.2 us  [per_device(): came = lax.ppermute(packed, 'seq', [(z, z + d) for z in range(n_seq - d)])]
    ppermute x3 -> x6, starting transfers between devices: 11.8 us -> 18.9 us  [per_device(): lax.ppermute(send_r.astype(jnp.bfloat16), 'seq', [(z, z + 1) for z in ran...]
    ppermute x4, starting transfers between devices: 7.38 us -> 12.6 us  [per_device(): received.append(lax.ppermute(chunk, ('seq', 'mdl'), perm))]
    ppermute x3 -> x6, waiting for transfers between devices: 5.2 us -> 10 us  [per_device(): lax.ppermute(send_l.astype(jnp.bfloat16), 'seq', [(z, z - 1) for z in ran...]
    ppermute x3 -> x6, starting transfers between devices: 2.89 us -> 5.33 us  [per_device(): lax.ppermute(send_l.astype(jnp.bfloat16), 'seq', [(z, z - 1) for z in ran...]
  transfers between devices with their start and end apart: 13 -> 21, of which waited for: 8 -> 13; matrix products, arithmetic and copies ran while one was open for 10% -> 11% of each run, Pallas kernels for 0% -> 0%
where the time goes in v7:
time: 164 us; the launch traced here: 163 us
  waiting for transfers between devices  79.7 us (49%)
  starting transfers between devices  48.8 us (30%)
  matrix products  15.1 us (9%)
  other arithmetic  13.8 us (8%)
  local copies, waits for them, and re-layouts  5.46 us (3%)
    ppermute x6, waiting for transfers between devices, per_device(): lax.ppermute(send_r.astype(jnp.bfloat16), 'seq', [(z, z + 1) for z in ran...  26.5 us
    ppermute x4, waiting for transfers between devices, per_device(): received.append(lax.ppermute(chunk, ('seq', 'mdl'), perm))  19.7 us
    ppermute x6, starting transfers between devices, per_device(): lax.ppermute(send_r.astype(jnp.bfloat16), 'seq', [(z, z + 1) for z in ran...  18.9 us
    ppermute x1, waiting for transfers between devices, per_device(): got.append(lax.ppermute(x, 'mdl', perm))  13.3 us
    ppermute x4, starting transfers between devices, per_device(): received.append(lax.ppermute(chunk, ('seq', 'mdl'), perm))  12.6 us
    ppermute x3, starting transfers between devices, per_device(): came = lax.ppermute(packed, 'seq', [(z, z + d) for z in range(n_seq - d)])  10.7 us
    ppermute x3, waiting for transfers between devices, per_device(): came = lax.ppermute(packed, 'seq', [(z, z + d) for z in range(n_seq - d)])  10.2 us
    ppermute x6, waiting for transfers between devices, per_device(): lax.ppermute(send_l.astype(jnp.bfloat16), 'seq', [(z, z - 1) for z in ran...  10 us
  transfers between devices with their start and end apart: 21, of which 13 were waited for; matrix products, arithmetic and copies ran while one was open for 11% of the time, Pallas kernels for 0%

profile of v7, /device:TPU:0, one launch (start us, length us, event | category | flops | bytes accessed | tf_op | source)
XLA Modules:
  0.0 163.5 jit_solution(16986932461114033415)
XLA Ops:
  2.8 1.4 fusion.14
  4.5 1.6 convolution_bitcast_fusion.8
  6.6 7.0 %collective-permute-start.2 = (bf16[8,16640]{1,0:T(8,128)(2,1)S(1)}, bf16[8,16640]{1,0:T(8,128)(2,1)S(1)}, u32[]{:S(2)}, u32[]{:S(2)}) collective-permute-start(bf16[8,16640]{1,0:T(8,128)(2,1)S(1)} %pad_maximum_fusion.2), channel_id=1, source_target_pairs={{0,12},{1,13},{2,14},{3,15},{16,28},{17,29},{18,30},{19,31}} | collective-permute-start | bytes 798728 | tf_op jit(solution)/shard_map/ppermute | solution.py:95
  13.5 1.3 collective-permute-start.1
  14.9 2.5 %collective-permute-start = (bf16[8,16640]{1,0:T(8,128)(2,1)S(1)}, bf16[8,16640]{1,0:T(8,128)(2,1)S(1)}, u32[]{:S(2)}, u32[]{:S(2)}) collective-permute-start(bf16[8,16640]{1,0:T(8,128)(2,1)S(1)} %pad_maximum_fusion.2), channel_id=1, source_target_pairs={{0,4},{4,8},{8,12},{1,5},{5,9},{9,13},{2,6},{6,10},{10,14},{3,7},{... | collective-permute-start | bytes 798728 | tf_op jit(solution)/shard_map/ppermute | solution.py:95
  17.5 2.5 %fusion.4 = f32[1,256,8,128]{1,3,2,0:T(8,128)} fusion(bf16[256,8,128]{0,2,1:T(8,128)(2,1)S(1)} %bitcast.176, f32[8,256]{1,0:T(8,128)S(1)} %bitcast_add_fusion.2, pred[256,256]{1,0:T(8,128)(4,1)S(1)} %iota_compare_fusion, bf16[256,1024]{1,0:T(8,128)(2,1)S(1)} %copy-done.6, f32[1024]{0:T(1024)S(1)} %bitcast.185, bf16[256,1024]{1,0:T(8,128)(2,1)S(1)} %copy-done.5, ...), kind=kOutput, calls=%fused_computation.31 | convolution fusion | flops 276299776 | bytes 2703360 | tf_op jit(solution)/shard_map/hbij,bjhd->bihd/dot_general | solution.py:63
  20.7 10.0 %collective-permute-done = bf16[8,16640]{1,0:T(8,128)(2,1)S(1)} collective-permute-done((bf16[8,16640]{1,0:T(8,128)(2,1)S(1)}, bf16[8,16640]{1,0:T(8,128)(2,1)S(1)}, u32[]{:S(2)}, u32[]{:S(2)}) %collective-permute-start) | collective-permute-done | bytes 266272 | tf_op jit(solution)/shard_map/ppermute | solution.py:95
  31.4 2.3 %multiply_reduce_fusion = (f32[256,8]{0,1:T(8,128)S(1)}, f32[1,256,8,128]{1,3,2,0:T(8,128)S(1)}) fusion(f32[1,256,8,128]{1,3,2,0:T(8,128)} %fusion.4, f32[8,128,128]{1,2,0:T(8,128)S(1)} %copy.92, f32[8,128,128]{1,2,0:T(8,128)S(1)} %copy.91, f32[8,128,128]{1,2,0:T(8,128)S(1)} %copy.90, f32[8]{0:T(128)S(1)} %get-tuple-element.14, ...), kind=kOutput, calls=%fused_computation.50 | convolution fusion | flops 407762944 | bytes 4214880 | tf_op jit(solution)/shard_map/bihd,bhde->bihe/dot_general | solution.py:105
  35.8 6.5 %collective-permute-start.6 = (bf16[256,256]{1,0:T(8,128)(2,1)S(1)}, bf16[256,256]{1,0:T(8,128)(2,1)S(1)}, u32[]{:S(2)}, u32[]{:S(2)}) collective-permute-start(bf16[256,256]{1,0:T(8,128)(2,1)S(1)} %get-tuple-element.47), channel_id=1, source_target_pairs={{0,3},{1,7},{2,11},{3,15},{4,0},{5,4},{6,8},{7,12},{8,1},{9,5},{10... | collective-permute-start | bytes 393224 | tf_op jit(solution)/shard_map/ppermute | solution.py:134
  42.4 5.3 %collective-permute-start.5 = (bf16[256,256]{1,0:T(8,128)(2,1)S(1)}, bf16[256,256]{1,0:T(8,128)(2,1)S(1)}, u32[]{:S(2)}, u32[]{:S(2)}) collective-permute-start(bf16[256,256]{1,0:T(8,128)(2,1)S(1)} %get-tuple-element.48), channel_id=1, source_target_pairs={{0,2},{1,6},{2,10},{3,14},{4,3},{5,7},{6,11},{7,15},{8,0},{9,4},{1... | collective-permute-start | bytes 393224 | tf_op jit(solution)/shard_map/ppermute | solution.py:134
  48.8 18.8 %collective-permute-done.5 = bf16[256,256]{1,0:T(8,128)(2,1)S(1)} collective-permute-done((bf16[256,256]{1,0:T(8,128)(2,1)S(1)}, bf16[256,256]{1,0:T(8,128)(2,1)S(1)}, u32[]{:S(2)}, u32[]{:S(2)}) %collective-permute-start.5) | collective-permute-done | bytes 131104 | tf_op jit(solution)/shard_map/ppermute | solution.py:134
  68.6 13.3 %collective-permute-done.7 = bf16[4,256,256]{2,1,0:T(8,128)(2,1)S(1)} collective-permute-done((bf16[4,256,256]{2,1,0:T(8,128)(2,1)S(1)}, bf16[4,256,256]{2,1,0:T(8,128)(2,1)S(1)}, u32[]{:S(2)}, u32[]{:S(2)}) %collective-permute-start.7) | collective-permute-done | bytes 524320 | tf_op jit(solution)/shard_map/ppermute | solution.py:145
  81.9 1.5 pad_maximum_fusion
  84.5 1.4 multiply_convert_fusion
  86.1 2.4 %gather_fusion.1 = bf16[4,256,1536]{2,1,0:T(8,128)(2,1)} fusion(bf16[4,256,1536]{2,1,0:T(8,128)(2,1)S(1)} %bitcast.173, s32[1024]{0:T(1024)S(1)} %pad_clamp_fusion), kind=kCustom, calls=%fused_computation.1 | custom fusion | bytes 6291472 | tf_op jit(solution)/shard_map/jit(_take)/gather | solution.py:152
  88.5 2.3 %broadcast_select_fusion = bf16[4,256,1536]{2,1,0:T(8,128)(2,1)S(1)} fusion(bf16[4,256,1536]{2,1,0:T(8,128)(2,1)} %gather_fusion.1, pred[4]{0:T(512)(128)(4,1)S(1)} %get-tuple-element.58), kind=kLoop, calls=%fused_computation.17 | loop fusion | flops 1572864 | bytes 6291460 | tf_op jit(solution)/shard_map/jit(_take)/select_n | solution.py:152
  90.8 1.9 %fusion.1 = bf16[256,1536]{1,0:T(8,128)(2,1)S(1)} fusion(bf16[2,2,256,1536]{3,2,1,0:T(8,128)(2,1)S(1)} %bitcast.166, s32[]{:T(128)S(6)} %min.84, bf16[2,1,4,256,256]{4,3,2,0,1:T(8,128)(2,1)S(1)} %copy-done, bf16[2,1,4,256,256]{4,3,2,0,1:T(8,128)(2,1)} %bitcast.30), kind=kOutput, calls=%fused_computation.26 | convolution fusion | flops 805961728 | bytes 6029316 | tf_op jit(solution)/shard_map/deti,deic->tc/dot_general | solution.py:158
  94.2 1.8 %fusion.30 = (bf16[2,2,1,256,256]{4,3,2,0,1:T(8,128)(2,1)S(1)}, bf16[2,2,1,256,256]{4,3,2,0,1:T(8,128)(2,1)S(1)}, bf16[2,2,1,256,256]{4,3,2,0,1:T(8,128)(2,1)S(1...) fusion(s32[]{:T(128)S(6)} %select_n.480, ...), kind=kLoop, calls=%fused_computation.80 | loop fusion | flops 1572864 | bytes 5242904 | tf_op jit(solution)/shard_map/stack | solution.py:148
  97.1 2.1 %collective-permute-start.9 = (bf16[256,768]{1,0:T(8,128)(2,1)S(1)}, bf16[256,768]{1,0:T(8,128)(2,1)S(1)}, u32[]{:S(2)}, u32[]{:S(2)}) collective-permute-start(bf16[256,768]{1,0:T(8,128)(2,1)S(1)} %get-tuple-element.42), channel_id=1, source_target_pairs={{0,4},{1,5},{2,6},{3,7},{16,20},{17,21},{18,22},{19,23}} | collective-permute-start | bytes 1179656 | tf_op jit(solution)/shard_map/ppermute | solution.py:177
  99.2 1.5 collective-permute-start.15
  103.7 5.0 %collective-permute-done.9 = bf16[256,768]{1,0:T(8,128)(2,1)S(1)} collective-permute-done((bf16[256,768]{1,0:T(8,128)(2,1)S(1)}, bf16[256,768]{1,0:T(8,128)(2,1)S(1)}, u32[]{:S(2)}, u32[]{:S(2)}) %collective-permute-start.9) | collective-permute-done | bytes 393248 | tf_op jit(solution)/shard_map/ppermute | solution.py:177
  108.7 7.5 %collective-permute-done.15 = bf16[256,768]{1,0:T(8,128)(2,1)S(1)} collective-permute-done((bf16[256,768]{1,0:T(8,128)(2,1)S(1)}, bf16[256,768]{1,0:T(8,128)(2,1)S(1)}, u32[]{:S(2)}, u32[]{:S(2)}) %collective-permute-start.15) | collective-permute-done | bytes 393248 | tf_op jit(solution)/shard_map/ppermute | solution.py:177
  116.4 4.4 %collective-permute-start.10 = (bf16[256,768]{1,0:T(8,128)(2,1)S(1)}, bf16[256,768]{1,0:T(8,128)(2,1)S(1)}, u32[]{:S(2)}, u32[]{:S(2)}) collective-permute-start(bf16[256,768]{1,0:T(8,128)(2,1)S(1)} %get-tuple-element.34), channel_id=1, source_target_pairs={{0,4},{4,8},{1,5},{5,9},{2,6},{6,10},{3,7},{7,11},{16,20},{20,24},... | collective-permute-start | bytes 1179656 | tf_op jit(solution)/shard_map/ppermute | solution.py:177
  120.8 1.9 %collective-permute-start.16 = (bf16[256,768]{1,0:T(8,128)(2,1)S(1)}, bf16[256,768]{1,0:T(8,128)(2,1)S(1)}, u32[]{:S(2)}, u32[]{:S(2)}) collective-permute-start(bf16[256,768]{1,0:T(8,128)(2,1)S(1)} %get-tuple-element.35), channel_id=1, source_target_pairs={{0,4},{4,8},{1,5},{5,9},{2,6},{6,10},{3,7},{7,11},{16,20},{20,24},... | collective-permute-start | bytes 1179656 | tf_op jit(solution)/shard_map/ppermute | solution.py:177
  125.3 5.0 %collective-permute-done.10 = bf16[256,768]{1,0:T(8,128)(2,1)S(1)} collective-permute-done((bf16[256,768]{1,0:T(8,128)(2,1)S(1)}, bf16[256,768]{1,0:T(8,128)(2,1)S(1)}, u32[]{:S(2)}, u32[]{:S(2)}) %collective-permute-start.10) | collective-permute-done | bytes 393248 | tf_op jit(solution)/shard_map/ppermute | solution.py:177
  130.3 6.5 %collective-permute-done.16 = bf16[256,768]{1,0:T(8,128)(2,1)S(1)} collective-permute-done((bf16[256,768]{1,0:T(8,128)(2,1)S(1)}, bf16[256,768]{1,0:T(8,128)(2,1)S(1)}, u32[]{:S(2)}, u32[]{:S(2)}) %collective-permute-start.16) | collective-permute-done | bytes 393248 | tf_op jit(solution)/shard_map/ppermute | solution.py:177
  137.1 4.4 %collective-permute-start.11 = (bf16[256,768]{1,0:T(8,128)(2,1)S(1)}, bf16[256,768]{1,0:T(8,128)(2,1)S(1)}, u32[]{:S(2)}, u32[]{:S(2)}) collective-permute-start(bf16[256,768]{1,0:T(8,128)(2,1)S(1)} %get-tuple-element.32), channel_id=1, source_target_pairs={{0,4},{4,8},{8,12},{1,5},{5,9},{9,13},{2,6},{6,10},{10,14},{3,7},{... | collective-permute-start | bytes 1179656 | tf_op jit(solution)/shard_map/ppermute | solution.py:177
  143.1 4.6 %collective-permute-start.17 = (bf16[256,768]{1,0:T(8,128)(2,1)S(1)}, bf16[256,768]{1,0:T(8,128)(2,1)S(1)}, u32[]{:S(2)}, u32[]{:S(2)}) collective-permute-start(bf16[256,768]{1,0:T(8,128)(2,1)S(1)} %get-tuple-element.33), channel_id=1, source_target_pairs={{0,4},{4,8},{8,12},{1,5},{5,9},{9,13},{2,6},{6,10},{10,14},{3,7},{... | collective-permute-start | bytes 1179656 | tf_op jit(solution)/shard_map/ppermute | solution.py:177
  148.9 1.6 collective-permute-done.11
  150.5 5.2 %collective-permute-done.14 = bf16[256,768]{1,0:T(8,128)(2,1)S(1)} collective-permute-done((bf16[256,768]{1,0:T(8,128)(2,1)S(1)}, bf16[256,768]{1,0:T(8,128)(2,1)S(1)}, u32[]{:S(2)}, u32[]{:S(2)}) %collective-permute-start.14) | collective-permute-done | bytes 393248 | tf_op jit(solution)/shard_map/ppermute | solution.py:180
  156.7 4.9 %collective-permute-done.20 = bf16[256,768]{1,0:T(8,128)(2,1)S(1)} collective-permute-done((bf16[256,768]{1,0:T(8,128)(2,1)S(1)}, bf16[256,768]{1,0:T(8,128)(2,1)S(1)}, u32[]{:S(2)}, u32[]{:S(2)}) %collective-permute-start.20) | collective-permute-done | bytes 393248 | tf_op jit(solution)/shard_map/ppermute | solution.py:180
  161.6 1.9 %fusion.2 = bf16[256,1536]{1,0:T(8,128)(2,1)} fusion(f32[256,768]{1,0:T(8,128)S(1)} %convert_add_fusion, f32[256,768]{1,0:T(8,128)S(1)} %convert_add_fusion.1, bf16[2,2,256,1536]{3,2,1,0:T(8,128)(2,1)S(1)} %bitcast.172, bf16[2,2,1,256,256]{4,3,2,0,1:T(8,128)(2,1)S(1)} %get-tuple-element.26), kind=kOutput, calls=%fused_computation.29 | convolution fusion | flops 806486016 | bytes 6029312 | tf_op jit(solution)/shard_map/deti,deic->tc/dot_general | solution.py:158
  (91 shorter events, 22.5 us)
Async XLA Ops:
  4.5 13.0 %copy-start.5 = (bf16[256,1024]{1,0:T(8,128)(2,1)S(1)}, bf16[256,1024]{1,0:T(8,128)(2,1)}, u32[]{:S(2)}) copy-start(bf16[256,1024]{1,0:T(8,128)(2,1)} %param.11) | copy-start | bytes 1572868
  4.5 13.0 %copy-start.6 = (bf16[256,1024]{1,0:T(8,128)(2,1)S(1)}, bf16[256,1024]{1,0:T(8,128)(2,1)}, u32[]{:S(2)}) copy-start(bf16[256,1024]{1,0:T(8,128)(2,1)} %param.9) | copy-start | bytes 1572868
  6.6 13.8 %collective-permute-start.2 = (bf16[8,16640]{1,0:T(8,128)(2,1)S(1)}, bf16[8,16640]{1,0:T(8,128)(2,1)S(1)}, u32[]{:S(2)}, u32[]{:S(2)}) collective-permute-start(bf16[8,16640]{1,0:T(8,128)(2,1)S(1)} %pad_maximum_fusion.2), channel_id=1, source_target_pairs={{0,12},{1,13},{2,14},{3,15},{16,28},{17,29},{18,30},{19,31}} | collective-permute-start | bytes 798728 | tf_op jit(solution)/shard_map/ppermute | solution.py:95
  13.5 17.4 %collective-permute-start.1 = (bf16[8,16640]{1,0:T(8,128)(2,1)S(1)}, bf16[8,16640]{1,0:T(8,128)(2,1)S(1)}, u32[]{:S(2)}, u32[]{:S(2)}) collective-permute-start(bf16[8,16640]{1,0:T(8,128)(2,1)S(1)} %pad_maximum_fusion.2), channel_id=1, source_target_pairs={{0,8},{4,12},{1,9},{5,13},{2,10},{6,14},{3,11},{7,15},{16,24},{20,... | collective-permute-start | bytes 798728 | tf_op jit(solution)/shard_map/ppermute | solution.py:95
  14.9 15.8 %collective-permute-start = (bf16[8,16640]{1,0:T(8,128)(2,1)S(1)}, bf16[8,16640]{1,0:T(8,128)(2,1)S(1)}, u32[]{:S(2)}, u32[]{:S(2)}) collective-permute-start(bf16[8,16640]{1,0:T(8,128)(2,1)S(1)} %pad_maximum_fusion.2), channel_id=1, source_target_pairs={{0,4},{4,8},{8,12},{1,5},{5,9},{9,13},{2,6},{6,10},{10,14},{3,7},{... | collective-permute-start | bytes 798728 | tf_op jit(solution)/shard_map/ppermute | solution.py:95
  33.7 1.0 copy-start.2
  33.7 1.0 copy-start.4
  34.7 33.7 %copy-start.3 = (s32[1536]{0:T(1024)S(1)}, s32[1536]{0:T(1024)}, u32[]{:S(2)}) copy-start(s32[1536]{0:T(1024)} %param.17) | copy-start | bytes 18436
  35.2 12.6 %collective-permute-start.3 = (bf16[256,256]{1,0:T(8,128)(2,1)S(1)}, bf16[256,256]{1,0:T(8,128)(2,1)S(1)}, u32[]{:S(2)}, u32[]{:S(2)}) collective-permute-start(bf16[256,256]{1,0:T(8,128)(2,1)S(1)} %get-tuple-element.46), channel_id=1, source_target_pairs={{0,0},{1,4},{2,8},{3,12},{4,1},{5,5},{6,9},{7,13},{8,2},{9,6},{10,... | collective-permute-start | bytes 393224 | tf_op jit(solution)/shard_map/ppermute | solution.py:134
  35.8 13.0 %collective-permute-start.6 = (bf16[256,256]{1,0:T(8,128)(2,1)S(1)}, bf16[256,256]{1,0:T(8,128)(2,1)S(1)}, u32[]{:S(2)}, u32[]{:S(2)}) collective-permute-start(bf16[256,256]{1,0:T(8,128)(2,1)S(1)} %get-tuple-element.47), channel_id=1, source_target_pairs={{0,3},{1,7},{2,11},{3,15},{4,0},{5,4},{6,8},{7,12},{8,1},{9,5},{10... | collective-permute-start | bytes 393224 | tf_op jit(solution)/shard_map/ppermute | solution.py:134
  42.4 25.2 %collective-permute-start.5 = (bf16[256,256]{1,0:T(8,128)(2,1)S(1)}, bf16[256,256]{1,0:T(8,128)(2,1)S(1)}, u32[]{:S(2)}, u32[]{:S(2)}) collective-permute-start(bf16[256,256]{1,0:T(8,128)(2,1)S(1)} %get-tuple-element.48), channel_id=1, source_target_pairs={{0,2},{1,6},{2,10},{3,14},{4,3},{5,7},{6,11},{7,15},{8,0},{9,4},{1... | collective-permute-start | bytes 393224 | tf_op jit(solution)/shard_map/ppermute | solution.py:134
  47.7 19.8 %collective-permute-start.4 = (bf16[256,256]{1,0:T(8,128)(2,1)S(1)}, bf16[256,256]{1,0:T(8,128)(2,1)S(1)}, u32[]{:S(2)}, u32[]{:S(2)}) collective-permute-start(bf16[256,256]{1,0:T(8,128)(2,1)S(1)} %get-tuple-element.49), channel_id=1, source_target_pairs={{0,1},{1,5},{2,9},{3,13},{4,2},{5,6},{6,10},{7,14},{8,3},{9,7},{10... | collective-permute-start | bytes 393224 | tf_op jit(solution)/shard_map/ppermute | solution.py:134
  68.2 16.3 %copy-start.1 = (bf16[1024,1536]{1,0:T(8,128)(2,1)S(1)}, bf16[1024,1536]{1,0:T(8,128)(2,1)}, u32[]{:S(2)}) copy-start(bf16[1024,1536]{1,0:T(8,128)(2,1)} %param.16) | copy-start | bytes 9437188
  68.3 13.6 %collective-permute-start.7 = (bf16[4,256,256]{2,1,0:T(8,128)(2,1)S(1)}, bf16[4,256,256]{2,1,0:T(8,128)(2,1)S(1)}, u32[]{:S(2)}, u32[]{:S(2)}) collective-permute-start(bf16[4,256,256]{2,1,0:T(8,128)(2,1)S(1)} %broadcast_select_fusion.1), channel_id=1, source_target_pairs={{0,2},{1,3},{2,0},{3,1},{4,6},{5,7},{6,4},{7,5},{8,10},{9,11},{10,... | collective-permute-start | bytes 1572872 | tf_op jit(solution)/shard_map/ppermute | solution.py:145
  83.4 7.4 %collective-permute-start.8 = (bf16[2,4,256,256]{3,2,1,0:T(8,128)(2,1)}, bf16[2,4,256,256]{3,2,1,0:T(8,128)(2,1)}, u32[]{:S(2)}, u32[]{:S(2)}) collective-permute-start(bf16[2,4,256,256]{3,2,1,0:T(8,128)(2,1)} %get-tuple-element.40), channel_id=1, source_target_pairs={{0,1},{1,0},{2,3},{3,2},{4,5},{5,4},{6,7},{7,6},{8,9},{9,8},{10,11... | collective-permute-start | bytes 3145736 | tf_op jit(solution)/shard_map/ppermute | solution.py:147
  88.5 2.4 %copy-start = (bf16[2,1,4,256,256]{4,3,2,0,1:T(8,128)(2,1)S(1)}, bf16[2,1,4,256,256]{4,3,2,0,1:T(8,128)(2,1)}, u32[]{:S(2)}) copy-start(bf16[2,1,4,256,256]{4,3,2,0,1:T(8,128)(2,1)} %get-tuple-element.41) | copy-start | bytes 3145732
  92.9 29.9 %collective-permute-start.12 = (bf16[256,768]{1,0:T(8,128)(2,1)S(1)}, bf16[256,768]{1,0:T(8,128)(2,1)S(1)}, u32[]{:S(2)}, u32[]{:S(2)}) collective-permute-start(bf16[256,768]{1,0:T(8,128)(2,1)S(1)} %get-tuple-element.44), channel_id=1, source_target_pairs={{12,8},{13,9},{14,10},{15,11},{28,24},{29,25},{30,26},{31,27}} | collective-permute-start | bytes 1179656 | tf_op jit(solution)/shard_map/ppermute | solution.py:180
  93.5 29.2 %collective-permute-start.18 = (bf16[256,768]{1,0:T(8,128)(2,1)S(1)}, bf16[256,768]{1,0:T(8,128)(2,1)S(1)}, u32[]{:S(2)}, u32[]{:S(2)}) collective-permute-start(bf16[256,768]{1,0:T(8,128)(2,1)S(1)} %get-tuple-element.45), channel_id=1, source_target_pairs={{12,8},{13,9},{14,10},{15,11},{28,24},{29,25},{30,26},{31,27}} | collective-permute-start | bytes 1179656 | tf_op jit(solution)/shard_map/ppermute | solution.py:180
  97.1 11.6 %collective-permute-start.9 = (bf16[256,768]{1,0:T(8,128)(2,1)S(1)}, bf16[256,768]{1,0:T(8,128)(2,1)S(1)}, u32[]{:S(2)}, u32[]{:S(2)}) collective-permute-start(bf16[256,768]{1,0:T(8,128)(2,1)S(1)} %get-tuple-element.42), channel_id=1, source_target_pairs={{0,4},{1,5},{2,6},{3,7},{16,20},{17,21},{18,22},{19,23}} | collective-permute-start | bytes 1179656 | tf_op jit(solution)/shard_map/ppermute | solution.py:177
  99.2 16.9 %collective-permute-start.15 = (bf16[256,768]{1,0:T(8,128)(2,1)S(1)}, bf16[256,768]{1,0:T(8,128)(2,1)S(1)}, u32[]{:S(2)}, u32[]{:S(2)}) collective-permute-start(bf16[256,768]{1,0:T(8,128)(2,1)S(1)} %get-tuple-element.43), channel_id=1, source_target_pairs={{0,4},{1,5},{2,6},{3,7},{16,20},{17,21},{18,22},{19,23}} | collective-permute-start | bytes 1179656 | tf_op jit(solution)/shard_map/ppermute | solution.py:177
  116.4 13.9 %collective-permute-start.10 = (bf16[256,768]{1,0:T(8,128)(2,1)S(1)}, bf16[256,768]{1,0:T(8,128)(2,1)S(1)}, u32[]{:S(2)}, u32[]{:S(2)}) collective-permute-start(bf16[256,768]{1,0:T(8,128)(2,1)S(1)} %get-tuple-element.34), channel_id=1, source_target_pairs={{0,4},{4,8},{1,5},{5,9},{2,6},{6,10},{3,7},{7,11},{16,20},{20,24},... | collective-permute-start | bytes 1179656 | tf_op jit(solution)/shard_map/ppermute | solution.py:177
  120.8 16.1 %collective-permute-start.16 = (bf16[256,768]{1,0:T(8,128)(2,1)S(1)}, bf16[256,768]{1,0:T(8,128)(2,1)S(1)}, u32[]{:S(2)}, u32[]{:S(2)}) collective-permute-start(bf16[256,768]{1,0:T(8,128)(2,1)S(1)} %get-tuple-element.35), channel_id=1, source_target_pairs={{0,4},{4,8},{1,5},{5,9},{2,6},{6,10},{3,7},{7,11},{16,20},{20,24},... | collective-permute-start | bytes 1179656 | tf_op jit(solution)/shard_map/ppermute | solution.py:177
  123.0 18.5 %collective-permute-start.13 = (bf16[256,768]{1,0:T(8,128)(2,1)S(1)}, bf16[256,768]{1,0:T(8,128)(2,1)S(1)}, u32[]{:S(2)}, u32[]{:S(2)}) collective-permute-start(bf16[256,768]{1,0:T(8,128)(2,1)S(1)} %get-tuple-element.38), channel_id=1, source_target_pairs={{8,4},{12,8},{9,5},{13,9},{10,6},{14,10},{11,7},{15,11},{24,20},{2... | collective-permute-start | bytes 1179656 | tf_op jit(solution)/shard_map/ppermute | solution.py:180
  123.7 17.9 %collective-permute-start.19 = (bf16[256,768]{1,0:T(8,128)(2,1)S(1)}, bf16[256,768]{1,0:T(8,128)(2,1)S(1)}, u32[]{:S(2)}, u32[]{:S(2)}) collective-permute-start(bf16[256,768]{1,0:T(8,128)(2,1)S(1)} %get-tuple-element.39), channel_id=1, source_target_pairs={{8,4},{12,8},{9,5},{13,9},{10,6},{14,10},{11,7},{15,11},{24,20},{2... | collective-permute-start | bytes 1179656 | tf_op jit(solution)/shard_map/ppermute | solution.py:180
  137.1 13.5 %collective-permute-start.11 = (bf16[256,768]{1,0:T(8,128)(2,1)S(1)}, bf16[256,768]{1,0:T(8,128)(2,1)S(1)}, u32[]{:S(2)}, u32[]{:S(2)}) collective-permute-start(bf16[256,768]{1,0:T(8,128)(2,1)S(1)} %get-tuple-element.32), channel_id=1, source_target_pairs={{0,4},{4,8},{8,12},{1,5},{5,9},{9,13},{2,6},{6,10},{10,14},{3,7},{... | collective-permute-start | bytes 1179656 | tf_op jit(solution)/shard_map/ppermute | solution.py:177
  141.8 13.9 %collective-permute-start.14 = (bf16[256,768]{1,0:T(8,128)(2,1)S(1)}, bf16[256,768]{1,0:T(8,128)(2,1)S(1)}, u32[]{:S(2)}, u32[]{:S(2)}) collective-permute-start(bf16[256,768]{1,0:T(8,128)(2,1)S(1)} %get-tuple-element.36), channel_id=1, source_target_pairs={{4,0},{8,4},{12,8},{5,1},{9,5},{13,9},{6,2},{10,6},{14,10},{7,3},{... | collective-permute-start | bytes 1179656 | tf_op jit(solution)/shard_map/ppermute | solution.py:180
  143.1 13.6 %collective-permute-start.17 = (bf16[256,768]{1,0:T(8,128)(2,1)S(1)}, bf16[256,768]{1,0:T(8,128)(2,1)S(1)}, u32[]{:S(2)}, u32[]{:S(2)}) collective-permute-start(bf16[256,768]{1,0:T(8,128)(2,1)S(1)} %get-tuple-element.33), channel_id=1, source_target_pairs={{0,4},{4,8},{8,12},{1,5},{5,9},{9,13},{2,6},{6,10},{10,14},{3,7},{... | collective-permute-start | bytes 1179656 | tf_op jit(solution)/shard_map/ppermute | solution.py:177
  147.6 13.9 %collective-permute-start.20 = (bf16[256,768]{1,0:T(8,128)(2,1)S(1)}, bf16[256,768]{1,0:T(8,128)(2,1)S(1)}, u32[]{:S(2)}, u32[]{:S(2)}) collective-permute-start(bf16[256,768]{1,0:T(8,128)(2,1)S(1)} %get-tuple-element.37), channel_id=1, source_target_pairs={{4,0},{8,4},{12,8},{5,1},{9,5},{13,9},{6,2},{10,6},{14,10},{7,3},{... | collective-permute-start | bytes 1179656 | tf_op jit(solution)/shard_map/ppermute | solution.py:180

commit v8 on v7

--- a/solution.py
+++ b/solution.py
@@ -121,20 +121,41 @@
     piece = rows_w // n_mdl
     s_me = lax.axis_index("seq")
     m_me = lax.axis_index("mdl")
-    received = []
-    for k in range(n_seq):
-        perm = []
-        for s in range(n_seq):
-            for m in range(n_mdl):
-                j = (s + k) % n_seq
-                f = m * blocks_here + j // n_mdl
-                perm.append((s * n_mdl + m, f * n_mdl + j % n_mdl))
-        j_send = (s_me + k) % n_seq
-        chunk = lax.dynamic_slice_in_dim(attn, j_send * piece, piece, axis=1)
-        received.append(lax.ppermute(chunk, ("seq", "mdl"), perm))
-    received = jnp.stack(received)
-    j_me = (s_me % blocks_here) * n_mdl + m_me
-    x = jnp.take(received, (j_me - jnp.arange(n_seq)) % n_seq, axis=0)
+    if n_seq == 4 and n_mdl == 4:
+        x_me = m_me // 2
+        own_pieces = attn.reshape(tok_rows, n_mdl, piece)
+        keep = lax.dynamic_slice_in_dim(own_pieces, 2 * x_me, 2, axis=1)
+        away = lax.dynamic_slice_in_dim(own_pieces, 2 * (1 - x_me), 2, axis=1)
+        came = lax.ppermute(away, "mdl", [(mu, mu ^ 2) for mu in range(n_mdl)])
+        items = jnp.transpose(jnp.concatenate([keep, came], axis=1), (1, 0, 2))
+        received = []
+        for k in range(n_seq):
+            perm = []
+            for s in range(n_seq):
+                for mu in range(n_mdl):
+                    r = (s + k) % n_seq
+                    f = mu if r // 2 == 0 else mu ^ 2
+                    perm.append((s * n_mdl + mu, f * n_mdl + 2 * (mu // 2) + r % 2))
+            item = lax.dynamic_index_in_dim(items, (s_me + k) % n_seq, 0, keepdims=False)
+            received.append(lax.ppermute(item, ("seq", "mdl"), perm))
+        received = jnp.stack(received)
+        r_me = 2 * ((s_me // 2) != (m_me // 2)).astype(jnp.int32) + m_me % 2
+        x = jnp.take(received, (r_me - jnp.arange(n_seq)) % n_seq, axis=0)
+    else:
+        received = []
+        for k in range(n_seq):
+            perm = []
+            for s in range(n_seq):
+                for m in range(n_mdl):
+                    j = (s + k) % n_seq
+                    f = m * blocks_here + j // n_mdl
+                    perm.append((s * n_mdl + m, f * n_mdl + j % n_mdl))
+            j_send = (s_me + k) % n_seq
+            chunk = lax.dynamic_slice_in_dim(attn, j_send * piece, piece, axis=1)
+            received.append(lax.ppermute(chunk, ("seq", "mdl"), perm))
+        received = jnp.stack(received)
+        j_me = (s_me % blocks_here) * n_mdl + m_me
+        x = jnp.take(received, (j_me - jnp.arange(n_seq)) % n_seq, axis=0)
 
     n_x = n_mdl // 2
     core = m_me % 2

time: 164 us -> 164 us (level)
  waiting for transfers between devices: 79.7 us -> 70.6 us
  starting transfers between devices: 48.8 us -> 54.8 us
  other arithmetic: 13.8 us -> 16.4 us
  local copies, waits for them, and re-layouts: 5.46 us -> 7.66 us
  matrix products: 15.1 us -> 12.9 us
    ppermute x4 -> x5, waiting for transfers between devices: 19.7 us -> 12.7 us  [the longest x4 7.24 us: per_device(): received.append(lax.ppermute(item, ('seq', 'mdl'), perm))]
    ppermute x1, starting transfers between devices: 0.07 us -> 3.8 us  [per_device(): got.append(lax.ppermute(x, 'mdl', perm))]
    ppermute x4 -> x5, starting transfers between devices: 12.6 us -> 16 us  [the longest x4 14.5 us: per_device(): received.append(lax.ppermute(item, ('seq', 'mdl'), perm))]
    ppermute x6, waiting for transfers between devices: 26.5 us -> 29.1 us  [per_device(): lax.ppermute(send_r.astype(jnp.bfloat16), 'seq', [(z, z + 1) for z in ran...]
    ppermute x1, waiting for transfers between devices: 13.3 us -> 10.9 us  [per_device(): got.append(lax.ppermute(x, 'mdl', perm))]
    unnamed x14 -> x16, local copies, waits for them, and re-layouts: 0.61 us -> 2.99 us
    ppermute x3, waiting for transfers between devices: 10.2 us -> 8.35 us  [per_device(): came = lax.ppermute(packed, 'seq', [(z, z + d) for z in range(n_seq - d)])]
  transfers between devices with their start and end apart: 21 -> 22, of which waited for: 13 -> 12; matrix products, arithmetic and copies ran while one was open for 11% -> 12% of each run, Pallas kernels for 0% -> 0%
where the time goes in v8:
time: 164 us; the launch traced here: 163 us
  waiting for transfers between devices  70.6 us (43%)
  starting transfers between devices  54.8 us (33%)
  other arithmetic  16.4 us (10%)
  matrix products  12.9 us (8%)
  local copies, waits for them, and re-layouts  7.66 us (5%)
    ppermute x6, waiting for transfers between devices, per_device(): lax.ppermute(send_r.astype(jnp.bfloat16), 'seq', [(z, z + 1) for z in ran...  29.1 us
    ppermute x6, starting transfers between devices, per_device(): lax.ppermute(send_r.astype(jnp.bfloat16), 'seq', [(z, z + 1) for z in ran...  18.2 us
    ppermute x4, starting transfers between devices, per_device(): received.append(lax.ppermute(item, ('seq', 'mdl'), perm))  14.5 us
    ppermute x3, starting transfers between devices, per_device(): came = lax.ppermute(packed, 'seq', [(z, z + d) for z in range(n_seq - d)])  11.4 us
    ppermute x1, waiting for transfers between devices, per_device(): got.append(lax.ppermute(x, 'mdl', perm))  10.9 us
    ppermute x6, waiting for transfers between devices, per_device(): lax.ppermute(send_l.astype(jnp.bfloat16), 'seq', [(z, z - 1) for z in ran...  9.48 us
    dot_general x7, matrix products, partial_for(): jnp.einsum('deti,deic->tc', rows, w_perm, preferred_element_type=jnp.floa...  8.67 us
    ppermute x3, waiting for transfers between devices, per_device(): came = lax.ppermute(packed, 'seq', [(z, z + d) for z in range(n_seq - d)])  8.35 us
  transfers between devices with their start and end apart: 22, of which 12 were waited for; matrix products, arithmetic and copies ran while one was open for 12% of the time, Pallas kernels for 0%

profile of v8, /device:TPU:0, one launch (start us, length us, event | category | flops | bytes accessed | tf_op | source)
XLA Modules:
  0.0 162.9 jit_solution(5869320701319545650)
XLA Ops:
  7.0 7.7 %collective-permute-start.2 = (bf16[8,16640]{1,0:T(8,128)(2,1)S(1)}, bf16[8,16640]{1,0:T(8,128)(2,1)}, u32[]{:S(2)}, u32[]{:S(2)}) collective-permute-start(bf16[8,16640]{1,0:T(8,128)(2,1)S(1)} %pad_maximum_fusion.2), channel_id=1, source_target_pairs={{0,12},{1,13},{2,14},{3,15},{16,28},{17,29},{18,30},{19,31}} | collective-permute-start | bytes 798728 | tf_op jit(solution)/shard_map/ppermute | solution.py:95
  16.0 2.5 %collective-permute-start = (bf16[8,16640]{1,0:T(8,128)(2,1)S(1)}, bf16[8,16640]{1,0:T(8,128)(2,1)}, u32[]{:S(2)}, u32[]{:S(2)}) collective-permute-start(bf16[8,16640]{1,0:T(8,128)(2,1)S(1)} %pad_maximum_fusion.2), channel_id=1, source_target_pairs={{0,4},{4,8},{8,12},{1,5},{5,9},{9,13},{2,6},{6,10},{10,14},{3,7},{... | collective-permute-start | bytes 798728 | tf_op jit(solution)/shard_map/ppermute | solution.py:95
  19.3 1.9 %fusion.4 = f32[1,256,8,128]{1,3,2,0:T(8,128)} fusion(bf16[256,8,128]{0,2,1:T(8,128)(2,1)S(1)} %bitcast.169, bf16[256,8,128]{0,2,1:T(8,128)(2,1)S(1)} %bitcast.164, bf16[256,8,128]{0,2,1:T(8,128)(2,1)S(1)} %bitcast.167, f32[8,256]{1,0:T(8,128)S(1)} %bitcast_add_fusion.2, pred[256,256]{1,0:T(8,128)(4,1)S(1)} %iota_compare_fusion), kind=kOutput, calls=%fused_computation.31 | convolution fusion | flops 271056896 | bytes 2695168 | tf_op jit(solution)/shard_map/hbij,bjhd->bihd/dot_general | solution.py:63
  22.8 8.3 %collective-permute-done = bf16[8,16640]{1,0:T(8,128)(2,1)} collective-permute-done((bf16[8,16640]{1,0:T(8,128)(2,1)S(1)}, bf16[8,16640]{1,0:T(8,128)(2,1)}, u32[]{:S(2)}, u32[]{:S(2)}) %collective-permute-start) | collective-permute-done | bytes 266272 | tf_op jit(solution)/shard_map/ppermute | solution.py:95
  33.5 2.0 %multiply_reduce_fusion = (f32[256,8]{0,1:T(8,128)S(1)}, f32[1,256,8,128]{1,3,2,0:T(8,128)S(1)}) fusion(f32[1,256,8,128]{1,3,2,0:T(8,128)} %fusion.4, bf16[256,8,128]{0,2,1:T(8,128)(2,1)S(1)} %bitcast.165, f32[8,128,128]{1,2,0:T(8,128)S(1)} %copy.98, f32[8,128,128]{1,2,0:T(8,128)S(1)} %copy.97, f32[8,128,128]{1,2,0:T(8,128)S(1)} %copy.96, ...), kind=kOutput, calls=%fused_computation.52 | convolution fusion | flops 404355072 | bytes 4210784 | tf_op jit(solution)/shard_map/bihd,bhde->bihe/dot_general | solution.py:105
  36.0 1.6 collective-permute-start.3
  37.7 5.5 %collective-permute-done.3 = bf16[256,2,256]{0,2,1:T(8,128)(2,1)S(1)} collective-permute-done((bf16[256,2,256]{0,2,1:T(8,128)(2,1)S(1)}, bf16[256,2,256]{0,2,1:T(8,128)(2,1)S(1)}, u32[]{:S(2)}, u32[]{:S(2)}) %collective-permute-start.3) | collective-permute-done | bytes 262176 | tf_op jit(solution)/shard_map/ppermute | solution.py:129
  43.8 9.0 %collective-permute-start.7 = (bf16[256,256]{1,0:T(8,128)(2,1)S(1)}, bf16[256,256]{1,0:T(8,128)(2,1)S(1)}, u32[]{:S(2)}, u32[]{:S(2)}) collective-permute-start(bf16[256,256]{1,0:T(8,128)(2,1)S(1)} %bitcast.175), channel_id=1, source_target_pairs={{0,9},{1,13},{2,3},{3,7},{4,0},{5,4},{6,10},{7,14},{8,1},{9,5},{10... | collective-permute-start | bytes 393224 | tf_op jit(solution)/shard_map/ppermute | solution.py:140
  52.9 3.1 %collective-permute-start.6 = (bf16[256,256]{1,0:T(8,128)(2,1)S(1)}, bf16[256,256]{1,0:T(8,128)(2,1)S(1)}, u32[]{:S(2)}, u32[]{:S(2)}) collective-permute-start(bf16[256,256]{1,0:T(8,128)(2,1)S(1)} %bitcast.174), channel_id=1, source_target_pairs={{0,8},{1,12},{2,2},{3,6},{4,9},{5,13},{6,3},{7,7},{8,0},{9,4},{10,... | collective-permute-start | bytes 393224 | tf_op jit(solution)/shard_map/ppermute | solution.py:140
  56.0 1.6 collective-permute-start.5
  58.4 7.2 %collective-permute-done.6 = bf16[256,256]{1,0:T(8,128)(2,1)S(1)} collective-permute-done((bf16[256,256]{1,0:T(8,128)(2,1)S(1)}, bf16[256,256]{1,0:T(8,128)(2,1)S(1)}, u32[]{:S(2)}, u32[]{:S(2)}) %collective-permute-start.6) | collective-permute-done | bytes 131104 | tf_op jit(solution)/shard_map/ppermute | solution.py:140
  66.4 3.8 %collective-permute-start.8 = (bf16[4,256,256]{2,1,0:T(8,128)(2,1)S(1)}, bf16[4,256,256]{2,1,0:T(8,128)(2,1)S(1)}, u32[]{:S(2)}, u32[]{:S(2)}) collective-permute-start(bf16[4,256,256]{2,1,0:T(8,128)(2,1)S(1)} %broadcast_select_fusion.1), channel_id=1, source_target_pairs={{0,2},{1,3},{2,0},{3,1},{4,6},{5,7},{6,4},{7,5},{8,10},{9,11},{10,... | collective-permute-start | bytes 1572872 | tf_op jit(solution)/shard_map/ppermute | solution.py:166
  70.3 10.9 %collective-permute-done.8 = bf16[4,256,256]{2,1,0:T(8,128)(2,1)S(1)} collective-permute-done((bf16[4,256,256]{2,1,0:T(8,128)(2,1)S(1)}, bf16[4,256,256]{2,1,0:T(8,128)(2,1)S(1)}, u32[]{:S(2)}, u32[]{:S(2)}) %collective-permute-start.8) | collective-permute-done | bytes 524320 | tf_op jit(solution)/shard_map/ppermute | solution.py:166
  81.2 1.5 pad_maximum_fusion
  84.3 2.4 %gather_fusion.1 = bf16[4,256,1536]{2,1,0:T(8,128)(2,1)} fusion(bf16[4,256,1536]{2,1,0:T(8,128)(2,1)S(1)} %bitcast.163, s32[1024]{0:T(1024)S(1)} %pad_clamp_fusion), kind=kCustom, calls=%fused_computation.1 | custom fusion | bytes 6291472 | tf_op jit(solution)/shard_map/jit(_take)/gather | solution.py:173
  86.7 2.3 %broadcast_select_fusion = bf16[4,256,1536]{2,1,0:T(8,128)(2,1)S(1)} fusion(bf16[4,256,1536]{2,1,0:T(8,128)(2,1)} %gather_fusion.1, pred[4]{0:T(512)(128)(4,1)S(1)} %get-tuple-element.60), kind=kLoop, calls=%fused_computation.17 | loop fusion | flops 1572864 | bytes 6291460 | tf_op jit(solution)/shard_map/jit(_take)/select_n | solution.py:173
  89.0 1.9 %fusion.1 = bf16[256,1536]{1,0:T(8,128)(2,1)S(1)} fusion(bf16[2,2,256,1536]{3,2,1,0:T(8,128)(2,1)S(1)} %bitcast.156, s32[]{:T(128)S(6)} %min.84, bf16[2,1,4,256,256]{4,3,2,0,1:T(8,128)(2,1)S(1)} %copy-done, bf16[2,1,4,256,256]{4,3,2,0,1:T(8,128)(2,1)} %bitcast.38), kind=kOutput, calls=%fused_computation.26 | convolution fusion | flops 805961728 | bytes 6029316 | tf_op jit(solution)/shard_map/deti,deic->tc/dot_general | solution.py:179
  92.4 1.8 %fusion.30 = (bf16[2,2,1,256,256]{4,3,2,0,1:T(8,128)(2,1)S(1)}, bf16[2,2,1,256,256]{4,3,2,0,1:T(8,128)(2,1)S(1)}, bf16[2,2,1,256,256]{4,3,2,0,1:T(8,128)(2,1)S(1...) fusion(s32[]{:T(128)S(6)} %select_n.497, ...), kind=kLoop, calls=%fused_computation.88 | loop fusion | flops 1572864 | bytes 5242904 | tf_op jit(solution)/shard_map/stack | solution.py:169
  96.7 1.5 collective-permute-start.16
  101.1 5.0 %collective-permute-done.10 = bf16[256,768]{1,0:T(8,128)(2,1)S(1)} collective-permute-done((bf16[256,768]{1,0:T(8,128)(2,1)S(1)}, bf16[256,768]{1,0:T(8,128)(2,1)S(1)}, u32[]{:S(2)}, u32[]{:S(2)}) %collective-permute-start.10) | collective-permute-done | bytes 393248 | tf_op jit(solution)/shard_map/ppermute | solution.py:198
  106.1 8.1 %collective-permute-done.16 = bf16[256,768]{1,0:T(8,128)(2,1)S(1)} collective-permute-done((bf16[256,768]{1,0:T(8,128)(2,1)S(1)}, bf16[256,768]{1,0:T(8,128)(2,1)S(1)}, u32[]{:S(2)}, u32[]{:S(2)}) %collective-permute-start.16) | collective-permute-done | bytes 393248 | tf_op jit(solution)/shard_map/ppermute | solution.py:198
  114.5 4.4 %collective-permute-start.11 = (bf16[256,768]{1,0:T(8,128)(2,1)S(1)}, bf16[256,768]{1,0:T(8,128)(2,1)S(1)}, u32[]{:S(2)}, u32[]{:S(2)}) collective-permute-start(bf16[256,768]{1,0:T(8,128)(2,1)S(1)} %get-tuple-element.34), channel_id=1, source_target_pairs={{0,4},{4,8},{1,5},{5,9},{2,6},{6,10},{3,7},{7,11},{16,20},{20,24},... | collective-permute-start | bytes 1179656 | tf_op jit(solution)/shard_map/ppermute | solution.py:198
  118.9 1.9 %collective-permute-start.17 = (bf16[256,768]{1,0:T(8,128)(2,1)S(1)}, bf16[256,768]{1,0:T(8,128)(2,1)S(1)}, u32[]{:S(2)}, u32[]{:S(2)}) collective-permute-start(bf16[256,768]{1,0:T(8,128)(2,1)S(1)} %get-tuple-element.35), channel_id=1, source_target_pairs={{0,4},{4,8},{1,5},{5,9},{2,6},{6,10},{3,7},{7,11},{16,20},{20,24},... | collective-permute-start | bytes 1179656 | tf_op jit(solution)/shard_map/ppermute | solution.py:198
  123.4 5.0 %collective-permute-done.11 = bf16[256,768]{1,0:T(8,128)(2,1)S(1)} collective-permute-done((bf16[256,768]{1,0:T(8,128)(2,1)S(1)}, bf16[256,768]{1,0:T(8,128)(2,1)S(1)}, u32[]{:S(2)}, u32[]{:S(2)}) %collective-permute-start.11) | collective-permute-done | bytes 393248 | tf_op jit(solution)/shard_map/ppermute | solution.py:198
  128.4 7.3 %collective-permute-done.17 = bf16[256,768]{1,0:T(8,128)(2,1)S(1)} collective-permute-done((bf16[256,768]{1,0:T(8,128)(2,1)S(1)}, bf16[256,768]{1,0:T(8,128)(2,1)S(1)}, u32[]{:S(2)}, u32[]{:S(2)}) %collective-permute-start.17) | collective-permute-done | bytes 393248 | tf_op jit(solution)/shard_map/ppermute | solution.py:198
  135.9 4.4 %collective-permute-start.12 = (bf16[256,768]{1,0:T(8,128)(2,1)S(1)}, bf16[256,768]{1,0:T(8,128)(2,1)S(1)}, u32[]{:S(2)}, u32[]{:S(2)}) collective-permute-start(bf16[256,768]{1,0:T(8,128)(2,1)S(1)} %get-tuple-element.32), channel_id=1, source_target_pairs={{0,4},{4,8},{8,12},{1,5},{5,9},{9,13},{2,6},{6,10},{10,14},{3,7},{... | collective-permute-start | bytes 1179656 | tf_op jit(solution)/shard_map/ppermute | solution.py:198
  141.8 4.6 %collective-permute-start.18 = (bf16[256,768]{1,0:T(8,128)(2,1)S(1)}, bf16[256,768]{1,0:T(8,128)(2,1)S(1)}, u32[]{:S(2)}, u32[]{:S(2)}) collective-permute-start(bf16[256,768]{1,0:T(8,128)(2,1)S(1)} %get-tuple-element.33), channel_id=1, source_target_pairs={{0,4},{4,8},{8,12},{1,5},{5,9},{9,13},{2,6},{6,10},{10,14},{3,7},{... | collective-permute-start | bytes 1179656 | tf_op jit(solution)/shard_map/ppermute | solution.py:198
  147.7 2.1 %collective-permute-done.12 = bf16[256,768]{1,0:T(8,128)(2,1)S(1)} collective-permute-done((bf16[256,768]{1,0:T(8,128)(2,1)S(1)}, bf16[256,768]{1,0:T(8,128)(2,1)S(1)}, u32[]{:S(2)}, u32[]{:S(2)}) %collective-permute-start.12) | collective-permute-done | bytes 393248 | tf_op jit(solution)/shard_map/ppermute | solution.py:198
  149.8 4.7 %collective-permute-done.15 = bf16[256,768]{1,0:T(8,128)(2,1)S(1)} collective-permute-done((bf16[256,768]{1,0:T(8,128)(2,1)S(1)}, bf16[256,768]{1,0:T(8,128)(2,1)S(1)}, u32[]{:S(2)}, u32[]{:S(2)}) %collective-permute-start.15) | collective-permute-done | bytes 393248 | tf_op jit(solution)/shard_map/ppermute | solution.py:201
  154.5 1.6 collective-permute-done.18
  156.2 4.8 %collective-permute-done.21 = bf16[256,768]{1,0:T(8,128)(2,1)S(1)} collective-permute-done((bf16[256,768]{1,0:T(8,128)(2,1)S(1)}, bf16[256,768]{1,0:T(8,128)(2,1)S(1)}, u32[]{:S(2)}, u32[]{:S(2)}) %collective-permute-start.21) | collective-permute-done | bytes 393248 | tf_op jit(solution)/shard_map/ppermute | solution.py:201
  161.1 1.9 %fusion.2 = bf16[256,1536]{1,0:T(8,128)(2,1)} fusion(f32[256,768]{1,0:T(8,128)S(1)} %convert_add_fusion, f32[256,768]{1,0:T(8,128)S(1)} %convert_add_fusion.1, bf16[2,2,256,1536]{3,2,1,0:T(8,128)(2,1)S(1)} %bitcast.162, bf16[2,2,1,256,256]{4,3,2,0,1:T(8,128)(2,1)S(1)} %get-tuple-element.26), kind=kOutput, calls=%fused_computation.29 | convolution fusion | flops 806486016 | bytes 6029312 | tf_op jit(solution)/shard_map/deti,deic->tc/dot_general | solution.py:179
  (100 shorter events, 29.9 us)
Async XLA Ops:
  4.1 14.5 %copy-start.2 = (bf16[256,1024]{1,0:T(8,128)(2,1)S(1)}, bf16[256,1024]{1,0:T(8,128)(2,1)}, u32[]{:S(2)}) copy-start(bf16[256,1024]{1,0:T(8,128)(2,1)} %param.9) | copy-start | bytes 1572868
  7.0 14.5 %collective-permute-start.2 = (bf16[8,16640]{1,0:T(8,128)(2,1)S(1)}, bf16[8,16640]{1,0:T(8,128)(2,1)}, u32[]{:S(2)}, u32[]{:S(2)}) collective-permute-start(bf16[8,16640]{1,0:T(8,128)(2,1)S(1)} %pad_maximum_fusion.2), channel_id=1, source_target_pairs={{0,12},{1,13},{2,14},{3,15},{16,28},{17,29},{18,30},{19,31}} | collective-permute-start | bytes 798728 | tf_op jit(solution)/shard_map/ppermute | solution.py:95
  14.7 17.7 %collective-permute-start.1 = (bf16[8,16640]{1,0:T(8,128)(2,1)S(1)}, bf16[8,16640]{1,0:T(8,128)(2,1)S(1)}, u32[]{:S(2)}, u32[]{:S(2)}) collective-permute-start(bf16[8,16640]{1,0:T(8,128)(2,1)S(1)} %pad_maximum_fusion.2), channel_id=1, source_target_pairs={{0,8},{4,12},{1,9},{5,13},{2,10},{6,14},{3,11},{7,15},{16,24},{20,... | collective-permute-start | bytes 798728 | tf_op jit(solution)/shard_map/ppermute | solution.py:95
  16.0 15.1 %collective-permute-start = (bf16[8,16640]{1,0:T(8,128)(2,1)S(1)}, bf16[8,16640]{1,0:T(8,128)(2,1)}, u32[]{:S(2)}, u32[]{:S(2)}) collective-permute-start(bf16[8,16640]{1,0:T(8,128)(2,1)S(1)} %pad_maximum_fusion.2), channel_id=1, source_target_pairs={{0,4},{4,8},{8,12},{1,5},{5,9},{9,13},{2,6},{6,10},{10,14},{3,7},{... | collective-permute-start | bytes 798728 | tf_op jit(solution)/shard_map/ppermute | solution.py:95
  18.8 2.5 %copy-start.3 = (bf16[256,1024]{1,0:T(8,128)(2,1)S(1)}, bf16[256,1024]{1,0:T(8,128)(2,1)}, u32[]{:S(2)}) copy-start(bf16[256,1024]{1,0:T(8,128)(2,1)} %param.12) | copy-start | bytes 1572868
  33.5 2.1 %copy-start.5 = (f32[1024]{0:T(1024)S(1)}, f32[1024]{0:T(1024)}, u32[]{:S(2)}) copy-start(f32[1024]{0:T(1024)} %param.15) | copy-start | bytes 12292
  35.9 34.3 %copy-start.4 = (s32[1536]{0:T(1024)S(1)}, s32[1536]{0:T(1024)}, u32[]{:S(2)}) copy-start(s32[1536]{0:T(1024)} %param.17) | copy-start | bytes 18436
  36.0 7.2 %collective-permute-start.3 = (bf16[256,2,256]{0,2,1:T(8,128)(2,1)S(1)}, bf16[256,2,256]{0,2,1:T(8,128)(2,1)S(1)}, u32[]{:S(2)}, u32[]{:S(2)}) collective-permute-start(bf16[256,2,256]{0,2,1:T(8,128)(2,1)S(1)} %get-tuple-element.50), channel_id=1, source_target_pairs={{0,2},{1,3},{2,0},{3,1},{4,6},{5,7},{6,4},{7,5},{8,10},{9,11},{10,... | collective-permute-start | bytes 786440 | tf_op jit(solution)/shard_map/ppermute | solution.py:129
  43.8 14.5 %collective-permute-start.7 = (bf16[256,256]{1,0:T(8,128)(2,1)S(1)}, bf16[256,256]{1,0:T(8,128)(2,1)S(1)}, u32[]{:S(2)}, u32[]{:S(2)}) collective-permute-start(bf16[256,256]{1,0:T(8,128)(2,1)S(1)} %bitcast.175), channel_id=1, source_target_pairs={{0,9},{1,13},{2,3},{3,7},{4,0},{5,4},{6,10},{7,14},{8,1},{9,5},{10... | collective-permute-start | bytes 393224 | tf_op jit(solution)/shard_map/ppermute | solution.py:140
  52.9 12.7 %collective-permute-start.6 = (bf16[256,256]{1,0:T(8,128)(2,1)S(1)}, bf16[256,256]{1,0:T(8,128)(2,1)S(1)}, u32[]{:S(2)}, u32[]{:S(2)}) collective-permute-start(bf16[256,256]{1,0:T(8,128)(2,1)S(1)} %bitcast.174), channel_id=1, source_target_pairs={{0,8},{1,12},{2,2},{3,6},{4,9},{5,13},{6,3},{7,7},{8,0},{9,4},{10,... | collective-permute-start | bytes 393224 | tf_op jit(solution)/shard_map/ppermute | solution.py:140
  56.0 9.6 %collective-permute-start.5 = (bf16[256,256]{1,0:T(8,128)(2,1)S(1)}, bf16[256,256]{1,0:T(8,128)(2,1)S(1)}, u32[]{:S(2)}, u32[]{:S(2)}) collective-permute-start(bf16[256,256]{1,0:T(8,128)(2,1)S(1)} %bitcast.173), channel_id=1, source_target_pairs={{0,1},{1,5},{2,11},{3,15},{4,8},{5,12},{6,2},{7,6},{8,9},{9,13},{1... | collective-permute-start | bytes 393224 | tf_op jit(solution)/shard_map/ppermute | solution.py:140
  57.7 7.9 %collective-permute-start.4 = (bf16[256,256]{1,0:T(8,128)(2,1)S(1)}, bf16[256,256]{1,0:T(8,128)(2,1)S(1)}, u32[]{:S(2)}, u32[]{:S(2)}) collective-permute-start(bf16[256,256]{1,0:T(8,128)(2,1)S(1)} %bitcast.172), channel_id=1, source_target_pairs={{0,0},{1,4},{2,10},{3,14},{4,1},{5,5},{6,11},{7,15},{8,8},{9,12},{... | collective-permute-start | bytes 393224 | tf_op jit(solution)/shard_map/ppermute | solution.py:140
  66.3 16.4 %copy-start.1 = (bf16[1024,1536]{1,0:T(8,128)(2,1)S(1)}, bf16[1024,1536]{1,0:T(8,128)(2,1)}, u32[]{:S(2)}) copy-start(bf16[1024,1536]{1,0:T(8,128)(2,1)} %param.16) | copy-start | bytes 9437188
  66.4 14.8 %collective-permute-start.8 = (bf16[4,256,256]{2,1,0:T(8,128)(2,1)S(1)}, bf16[4,256,256]{2,1,0:T(8,128)(2,1)S(1)}, u32[]{:S(2)}, u32[]{:S(2)}) collective-permute-start(bf16[4,256,256]{2,1,0:T(8,128)(2,1)S(1)} %broadcast_select_fusion.1), channel_id=1, source_target_pairs={{0,2},{1,3},{2,0},{3,1},{4,6},{5,7},{6,4},{7,5},{8,10},{9,11},{10,... | collective-permute-start | bytes 1572872 | tf_op jit(solution)/shard_map/ppermute | solution.py:166
  82.7 6.3 %collective-permute-start.9 = (bf16[2,4,256,256]{3,2,1,0:T(8,128)(2,1)}, bf16[2,4,256,256]{3,2,1,0:T(8,128)(2,1)}, u32[]{:S(2)}, u32[]{:S(2)}) collective-permute-start(bf16[2,4,256,256]{3,2,1,0:T(8,128)(2,1)} %get-tuple-element.40), channel_id=1, source_target_pairs={{0,1},{1,0},{2,3},{3,2},{4,5},{5,4},{6,7},{7,6},{8,9},{9,8},{10,11... | collective-permute-start | bytes 3145736 | tf_op jit(solution)/shard_map/ppermute | solution.py:168
  86.6 2.4 %copy-start = (bf16[2,1,4,256,256]{4,3,2,0,1:T(8,128)(2,1)S(1)}, bf16[2,1,4,256,256]{4,3,2,0,1:T(8,128)(2,1)}, u32[]{:S(2)}) copy-start(bf16[2,1,4,256,256]{4,3,2,0,1:T(8,128)(2,1)} %get-tuple-element.41) | copy-start | bytes 3145732
  91.0 29.8 %collective-permute-start.13 = (bf16[256,768]{1,0:T(8,128)(2,1)S(1)}, bf16[256,768]{1,0:T(8,128)(2,1)S(1)}, u32[]{:S(2)}, u32[]{:S(2)}) collective-permute-start(bf16[256,768]{1,0:T(8,128)(2,1)S(1)} %get-tuple-element.44), channel_id=1, source_target_pairs={{12,8},{13,9},{14,10},{15,11},{28,24},{29,25},{30,26},{31,27}} | collective-permute-start | bytes 1179656 | tf_op jit(solution)/shard_map/ppermute | solution.py:201
  91.7 29.1 %collective-permute-start.19 = (bf16[256,768]{1,0:T(8,128)(2,1)S(1)}, bf16[256,768]{1,0:T(8,128)(2,1)S(1)}, u32[]{:S(2)}, u32[]{:S(2)}) collective-permute-start(bf16[256,768]{1,0:T(8,128)(2,1)S(1)} %get-tuple-element.45), channel_id=1, source_target_pairs={{12,8},{13,9},{14,10},{15,11},{28,24},{29,25},{30,26},{31,27}} | collective-permute-start | bytes 1179656 | tf_op jit(solution)/shard_map/ppermute | solution.py:201
  95.2 10.9 %collective-permute-start.10 = (bf16[256,768]{1,0:T(8,128)(2,1)S(1)}, bf16[256,768]{1,0:T(8,128)(2,1)S(1)}, u32[]{:S(2)}, u32[]{:S(2)}) collective-permute-start(bf16[256,768]{1,0:T(8,128)(2,1)S(1)} %get-tuple-element.42), channel_id=1, source_target_pairs={{0,4},{1,5},{2,6},{3,7},{16,20},{17,21},{18,22},{19,23}} | collective-permute-start | bytes 1179656 | tf_op jit(solution)/shard_map/ppermute | solution.py:198
  96.7 17.6 %collective-permute-start.16 = (bf16[256,768]{1,0:T(8,128)(2,1)S(1)}, bf16[256,768]{1,0:T(8,128)(2,1)S(1)}, u32[]{:S(2)}, u32[]{:S(2)}) collective-permute-start(bf16[256,768]{1,0:T(8,128)(2,1)S(1)} %get-tuple-element.43), channel_id=1, source_target_pairs={{0,4},{1,5},{2,6},{3,7},{16,20},{17,21},{18,22},{19,23}} | collective-permute-start | bytes 1179656 | tf_op jit(solution)/shard_map/ppermute | solution.py:198
  114.5 13.9 %collective-permute-start.11 = (bf16[256,768]{1,0:T(8,128)(2,1)S(1)}, bf16[256,768]{1,0:T(8,128)(2,1)S(1)}, u32[]{:S(2)}, u32[]{:S(2)}) collective-permute-start(bf16[256,768]{1,0:T(8,128)(2,1)S(1)} %get-tuple-element.34), channel_id=1, source_target_pairs={{0,4},{4,8},{1,5},{5,9},{2,6},{6,10},{3,7},{7,11},{16,20},{20,24},... | collective-permute-start | bytes 1179656 | tf_op jit(solution)/shard_map/ppermute | solution.py:198
  118.9 16.7 %collective-permute-start.17 = (bf16[256,768]{1,0:T(8,128)(2,1)S(1)}, bf16[256,768]{1,0:T(8,128)(2,1)S(1)}, u32[]{:S(2)}, u32[]{:S(2)}) collective-permute-start(bf16[256,768]{1,0:T(8,128)(2,1)S(1)} %get-tuple-element.35), channel_id=1, source_target_pairs={{0,4},{4,8},{1,5},{5,9},{2,6},{6,10},{3,7},{7,11},{16,20},{20,24},... | collective-permute-start | bytes 1179656 | tf_op jit(solution)/shard_map/ppermute | solution.py:198
  121.0 19.2 %collective-permute-start.14 = (bf16[256,768]{1,0:T(8,128)(2,1)S(1)}, bf16[256,768]{1,0:T(8,128)(2,1)S(1)}, u32[]{:S(2)}, u32[]{:S(2)}) collective-permute-start(bf16[256,768]{1,0:T(8,128)(2,1)S(1)} %get-tuple-element.38), channel_id=1, source_target_pairs={{8,4},{12,8},{9,5},{13,9},{10,6},{14,10},{11,7},{15,11},{24,20},{2... | collective-permute-start | bytes 1179656 | tf_op jit(solution)/shard_map/ppermute | solution.py:201
  121.7 18.6 %collective-permute-start.20 = (bf16[256,768]{1,0:T(8,128)(2,1)S(1)}, bf16[256,768]{1,0:T(8,128)(2,1)S(1)}, u32[]{:S(2)}, u32[]{:S(2)}) collective-permute-start(bf16[256,768]{1,0:T(8,128)(2,1)S(1)} %get-tuple-element.39), channel_id=1, source_target_pairs={{8,4},{12,8},{9,5},{13,9},{10,6},{14,10},{11,7},{15,11},{24,20},{2... | collective-permute-start | bytes 1179656 | tf_op jit(solution)/shard_map/ppermute | solution.py:201
  135.9 13.9 %collective-permute-start.12 = (bf16[256,768]{1,0:T(8,128)(2,1)S(1)}, bf16[256,768]{1,0:T(8,128)(2,1)S(1)}, u32[]{:S(2)}, u32[]{:S(2)}) collective-permute-start(bf16[256,768]{1,0:T(8,128)(2,1)S(1)} %get-tuple-element.32), channel_id=1, source_target_pairs={{0,4},{4,8},{8,12},{1,5},{5,9},{9,13},{2,6},{6,10},{10,14},{3,7},{... | collective-permute-start | bytes 1179656 | tf_op jit(solution)/shard_map/ppermute | solution.py:198
  140.5 13.9 %collective-permute-start.15 = (bf16[256,768]{1,0:T(8,128)(2,1)S(1)}, bf16[256,768]{1,0:T(8,128)(2,1)S(1)}, u32[]{:S(2)}, u32[]{:S(2)}) collective-permute-start(bf16[256,768]{1,0:T(8,128)(2,1)S(1)} %get-tuple-element.36), channel_id=1, source_target_pairs={{4,0},{8,4},{12,8},{5,1},{9,5},{13,9},{6,2},{10,6},{14,10},{7,3},{... | collective-permute-start | bytes 1179656 | tf_op jit(solution)/shard_map/ppermute | solution.py:201
  141.8 14.3 %collective-permute-start.18 = (bf16[256,768]{1,0:T(8,128)(2,1)S(1)}, bf16[256,768]{1,0:T(8,128)(2,1)S(1)}, u32[]{:S(2)}, u32[]{:S(2)}) collective-permute-start(bf16[256,768]{1,0:T(8,128)(2,1)S(1)} %get-tuple-element.33), channel_id=1, source_target_pairs={{0,4},{4,8},{8,12},{1,5},{5,9},{9,13},{2,6},{6,10},{10,14},{3,7},{... | collective-permute-start | bytes 1179656 | tf_op jit(solution)/shard_map/ppermute | solution.py:198
  146.4 14.6 %collective-permute-start.21 = (bf16[256,768]{1,0:T(8,128)(2,1)S(1)}, bf16[256,768]{1,0:T(8,128)(2,1)S(1)}, u32[]{:S(2)}, u32[]{:S(2)}) collective-permute-start(bf16[256,768]{1,0:T(8,128)(2,1)S(1)} %get-tuple-element.37), channel_id=1, source_target_pairs={{4,0},{8,4},{12,8},{5,1},{9,5},{13,9},{6,2},{10,6},{14,10},{7,3},{... | collective-permute-start | bytes 1179656 | tf_op jit(solution)/shard_map/ppermute | solution.py:201

commit v9 on v8

--- a/solution.py
+++ b/solution.py
@@ -33,7 +33,6 @@
     out_weight,
     weight_exponent,
 ):
-    weights = fake_quant(out_weight, weight_exponent[None, :])
     tok_rows = query_proj.shape[0]
     feat_here = query_proj.shape[1]
     heads_here = log_decay.shape[0]
@@ -78,6 +77,19 @@
         advance, jnp.zeros((heads_here, HDIM, HDIM), jnp.float32), (block_gain, block_states)
     )
     device_log = jnp.sum(block_total, axis=1)
+    weights = fake_quant(out_weight, weight_exponent[None, :])
+    rows_w, cols_w = weights.shape
+    piece = rows_w // n_mdl
+    n_x = n_mdl // 2
+    m_me = lax.axis_index("mdl")
+    core = m_me % 2
+    xi = m_me // 2
+    d_idx = jnp.arange(n_x)[:, None]
+    e_idx = jnp.arange(2)[None, :]
+    mu_tab = 2 * ((xi - d_idx) % n_x) + jnp.where(e_idx == 0, core, 1 - core)
+    w_perm = jnp.take(
+        weights.reshape(n_mdl, piece, cols_w), mu_tab.reshape(-1), axis=0
+    ).reshape(n_x, 2, piece, cols_w)
     log_hi = device_log.astype(jnp.bfloat16)
     log_lo = (device_log - log_hi.astype(jnp.float32)).astype(jnp.bfloat16)
     packed = jnp.concatenate(
@@ -93,6 +105,8 @@
     gap = jnp.zeros((heads_here,), jnp.float32)
     for d in range(1, n_seq):
         came = lax.ppermute(packed, "seq", [(z, z + d) for z in range(n_seq - d)])
+        if d == 1:
+            came, w_perm = lax.optimization_barrier((came, w_perm))
         came_state = came[:, : HDIM * HDIM].astype(jnp.float32).reshape(heads_here, HDIM, HDIM)
         came_log = came[:, HDIM * HDIM].astype(jnp.float32) + came[:, HDIM * HDIM + HDIM].astype(
             jnp.float32
@@ -116,11 +130,8 @@
         jnp.bfloat16
     )
 
-    rows_w, cols_w = weights.shape
     blocks_here = feat_here // rows_w
-    piece = rows_w // n_mdl
     s_me = lax.axis_index("seq")
-    m_me = lax.axis_index("mdl")
     if n_seq == 4 and n_mdl == 4:
         x_me = m_me // 2
         own_pieces = attn.reshape(tok_rows, n_mdl, piece)
@@ -167,13 +178,6 @@
     own = jnp.stack(got)
     other = lax.ppermute(own, "mdl", [(mu, mu ^ 1) for mu in range(n_mdl)])
     gathered_x = jnp.stack([own, other], axis=1)
-    d_idx = jnp.arange(n_x)[:, None]
-    e_idx = jnp.arange(2)[None, :]
-    mu_tab = 2 * ((xi - d_idx) % n_x) + jnp.where(e_idx == 0, core, 1 - core)
-    w_perm = jnp.take(
-        weights.reshape(n_mdl, piece, cols_w), mu_tab.reshape(-1), axis=0
-    ).reshape(n_x, 2, piece, cols_w)
-
     def partial_for(target):
         rows = lax.dynamic_index_in_dim(gathered_x, target, 2, keepdims=False)
         return jnp.einsum(

time: 164 us -> 176 us (1.073)
  local copies, waits for them, and re-layouts: 7.66 us -> 21.4 us
  other arithmetic: 16.4 us -> 26.1 us
  starting transfers between devices: 54.8 us -> 47.5 us
  waiting for transfers between devices: 70.6 us -> 64 us
  matrix products: 12.9 us -> 15.1 us
    ppermute x4, starting transfers between devices: 14.5 us -> 5.42 us  [per_device(): received.append(lax.ppermute(item, ('seq', 'mdl'), perm))]
    ppermute x3, waiting for transfers between devices: 8.35 us -> 0.01 us  [per_device(): came = lax.ppermute(packed, 'seq', [(z, z + d) for z in range(n_seq - d)])]
    another operation x5, local copies, waits for them, and re-layouts: 0.4 us -> 4.43 us
    reshape x2, local copies, waits for them, and re-layouts: 0.45 us -> 4.09 us  [per_device(): came[:, :HDIM * HDIM].astype(jnp.float32).reshape(heads_here, HDIM, HDIM)]
    ppermute x1, waiting for transfers between devices: 0.01 us -> 3 us  [per_device(): other = lax.ppermute(own, 'mdl', [(mu, mu ^ 1) for mu in range(n_mdl)])]
    ppermute x6, starting transfers between devices: 18.2 us -> 20.7 us  [per_device(): lax.ppermute(send_r.astype(jnp.bfloat16), 'seq', [(z, z + 1) for z in ran...]
    select_n x3, other arithmetic: 0.24 us -> 2.32 us  [per_device(): x = jnp.take(received, (r_me - jnp.arange(n_seq)) % n_seq, axis=0)]
    ppermute x6, waiting for transfers between devices: 29.1 us -> 27.2 us  [per_device(): lax.ppermute(send_r.astype(jnp.bfloat16), 'seq', [(z, z + 1) for z in ran...]
  transfers between devices with their start and end apart: 22 -> 22, of which waited for: 12 -> 13; matrix products, arithmetic and copies ran while one was open for 12% -> 17% of each run, Pallas kernels for 0% -> 0%
where the time goes in v9:
time: 176 us; the launch traced here: 175 us
  waiting for transfers between devices  64 us (36%)
  starting transfers between devices  47.5 us (27%)
  other arithmetic  26.1 us (15%)
  local copies, waits for them, and re-layouts  21.4 us (12%)
  matrix products  15.1 us (9%)
    ppermute x6, waiting for transfers between devices, per_device(): lax.ppermute(send_r.astype(jnp.bfloat16), 'seq', [(z, z + 1) for z in ran...  27.2 us
    ppermute x6, starting transfers between devices, per_device(): lax.ppermute(send_r.astype(jnp.bfloat16), 'seq', [(z, z + 1) for z in ran...  20.7 us
    ppermute x3, starting transfers between devices, per_device(): came = lax.ppermute(packed, 'seq', [(z, z + d) for z in range(n_seq - d)])  11.5 us
    ppermute x6, waiting for transfers between devices, per_device(): lax.ppermute(send_l.astype(jnp.bfloat16), 'seq', [(z, z - 1) for z in ran...  9.77 us
    ppermute x1, waiting for transfers between devices, per_device(): got.append(lax.ppermute(x, 'mdl', perm))  8.95 us
    dot_general x7, matrix products, partial_for(): jnp.einsum('deti,deic->tc', rows, w_perm, preferred_element_type=jnp.floa...  8.82 us
    ppermute x4, waiting for transfers between devices, per_device(): received.append(lax.ppermute(item, ('seq', 'mdl'), perm))  8.78 us
    ppermute x1, waiting for transfers between devices, per_device(): came = lax.ppermute(away, 'mdl', [(mu, mu ^ 2) for mu in range(n_mdl)])  6.3 us
  transfers between devices with their start and end apart: 22, of which 13 were waited for; matrix products, arithmetic and copies ran while one was open for 17% of the time, Pallas kernels for 0%

profile of v9, /device:TPU:0, one launch (start us, length us, event | category | flops | bytes accessed | tf_op | source)
XLA Modules:
  0.0 174.5 jit_solution(15740739800137939172)
XLA Ops:
  7.8 7.6 %collective-permute-start.2 = (bf16[8,16640]{1,0:T(8,128)(2,1)}, bf16[8,16640]{1,0:T(8,128)(2,1)}, u32[]{:S(2)}, u32[]{:S(2)}) collective-permute-start(bf16[8,16640]{1,0:T(8,128)(2,1)} %pad_maximum_fusion.2), channel_id=1, source_target_pairs={{0,12},{1,13},{2,14},{3,15},{16,28},{17,29},{18,30},{19,31}} | collective-permute-start | bytes 798728 | tf_op jit(solution)/shard_map/ppermute | solution.py:107
  16.7 2.5 %collective-permute-start = (bf16[8,16640]{1,0:T(8,128)(2,1)}, bf16[8,16640]{1,0:T(8,128)(2,1)}, u32[]{:S(2)}, u32[]{:S(2)}) collective-permute-start(bf16[8,16640]{1,0:T(8,128)(2,1)} %pad_maximum_fusion.2), channel_id=1, source_target_pairs={{0,4},{4,8},{8,12},{1,5},{5,9},{9,13},{2,6},{6,10},{10,14},{3,7},{... | collective-permute-start | bytes 798728 | tf_op jit(solution)/shard_map/ppermute | solution.py:107
  21.2 2.8 %multiply_convert_fusion = bf16[1024,1536]{1,0:T(8,128)(2,1)S(1)} fusion(bf16[1024,1536]{1,0:T(8,128)(2,1)} %param.16, f32[1536]{0:T(1024)S(1)} %select_add_fusion), kind=kLoop, calls=%fused_computation.2 | loop fusion | flops 11010048 | bytes 6297600 | tf_op jit(solution)/shard_map/convert_element_type | solution.py:20
  24.0 2.4 %gather_fusion = bf16[4,256,1536]{2,1,0:T(8,128)(2,1)} fusion(bf16[4,256,1536]{2,1,0:T(8,128)(2,1)S(1)} %bitcast.157, s32[1024]{0:T(1024)S(1)} %pad_clamp_fusion.1), kind=kCustom, calls=%fused_computation | custom fusion | bytes 6291472 | tf_op jit(solution)/shard_map/jit(_take)/gather | solution.py:90
  26.4 2.3 %broadcast_select_fusion = bf16[2,2,256,1536]{3,2,1,0:T(8,128)(2,1)S(1)} fusion(bf16[2,2,256,1536]{3,2,1,0:T(8,128)(2,1)} %bitcast.156, pred[2,2]{1,0:T(4,128)(4,1)S(1)} %compare_and_fusion), kind=kLoop, calls=%fused_computation.17 | loop fusion | flops 1572864 | bytes 6291460 | tf_op jit(solution)/shard_map/jit(_take)/select_n | solution.py:90
  28.7 3.3 %fusion.5 = f32[1,256,8,128]{1,3,2,0:T(8,128)} fusion(bf16[256,8,128]{0,2,1:T(8,128)(2,1)} %bitcast.161, bf16[256,8,128]{0,2,1:T(8,128)(2,1)} %bitcast.162, bf16[256,8,128]{0,2,1:T(8,128)(2,1)} %bitcast.159, f32[8,256]{1,0:T(8,128)S(1)} %bitcast_add_fusion.2, pred[256,256]{1,0:T(8,128)(4,1)S(1)} %iota_compare_fusion), kind=kOutput, calls=%fused_computation.31 | convolution fusion | flops 271056896 | bytes 2695168 | tf_op jit(solution)/shard_map/hbij,bjhd->bihd/dot_general | solution.py:62
  32.0 2.0 %copy.100 = bf16[256,1024]{0,1:T(8,128)(2,1)} copy(bf16[256,1024]{1,0:T(8,128)(2,1)} %param.12) | data formatting | bytes 1048576 | tf_op args[3]
  35.8 2.1 %copy.98 = f32[8,128,128]{1,2,0:T(8,128)} copy(f32[8,128,128]{2,0,1:T(8,128)} %fusion.58) | data formatting | bytes 1048576 | tf_op jit(solution)/shard_map/reshape | solution.py:110
  38.7 2.0 %copy.96 = f32[8,128,128]{1,2,0:T(8,128)} copy(f32[8,128,128]{2,0,1:T(8,128)} %fusion.59) | data formatting | bytes 1048576 | tf_op jit(solution)/shard_map/reshape | solution.py:110
  42.5 2.0 %copy.97 = f32[8,128,128]{1,2,0:T(8,128)} copy(f32[8,128,128]{2,0,1:T(8,128)} %multiply_bitcast_fusion) | data formatting | bytes 1048576 | tf_op jit(solution)/shard_map/mul | solution.py:115
  45.4 2.7 %multiply_reduce_fusion = (f32[256,8]{0,1:T(8,128)S(1)}, f32[1,256,8,128]{1,3,2,0:T(8,128)S(1)}) fusion(f32[1,256,8,128]{1,3,2,0:T(8,128)} %fusion.5, bf16[256,8,128]{0,2,1:T(8,128)(2,1)} %bitcast.163, f32[8,128,128]{1,2,0:T(8,128)} %copy.98, f32[8,128,128]{1,2,0:T(8,128)} %copy.97, f32[8,128,128]{1,2,0:T(8,128)} %copy.96, f32[8]{0:T(128)S(1)} %get-tuple-element.25, ...), kind=kOutput, calls=%fused_computation.52 | convolution fusion | flops 404355072 | bytes 4210784 | tf_op jit(solution)/shard_map/bihd,bhde->bihe/dot_general | solution.py:119
  50.8 6.3 %collective-permute-done.3 = bf16[256,2,256]{0,2,1:T(8,128)(2,1)} collective-permute-done((bf16[256,2,256]{0,2,1:T(8,128)(2,1)}, bf16[256,2,256]{0,2,1:T(8,128)(2,1)}, u32[]{:S(2)}, u32[]{:S(2)}) %collective-permute-start.3) | collective-permute-done | bytes 262176 | tf_op jit(solution)/shard_map/ppermute | solution.py:140
  57.1 1.8 %fusion.64 = (bf16[256,1,256]{0,2,1:T(8,128)(2,1)}, bf16[256,1,256]{0,2,1:T(8,128)(2,1)}, bf16[256,1,256]{0,2,1:T(8,128)(2,1)}, bf16[256,1,256]{0,2,1:T(8,128)(2,1)S(1)}) fusion(s32[]{:T(128)S(6)} %select_n.475, bf16[256,2,256]{0,2,1:T(8,128)(2,1)S(1)} %get-tuple-element.55, bf16[256,2,256]{0,2,1:T(8,128)(2,1)} %collective-permute-done.3, ...), kind=kLoop, calls=%fused_computation.131 | loop fusion | flops 262144 | bytes 1048592 | tf_op jit(solution)/shard_map/concatenate | solution.py:141
  63.4 3.1 %collective-permute-start.6 = (bf16[256,256]{1,0:T(8,128)(2,1)}, bf16[256,256]{1,0:T(8,128)(2,1)S(1)}, u32[]{:S(2)}, u32[]{:S(2)}) collective-permute-start(bf16[256,256]{1,0:T(8,128)(2,1)} %bitcast.168), channel_id=1, source_target_pairs={{0,8},{1,12},{2,2},{3,6},{4,9},{5,13},{6,3},{7,7},{8,0},{9,4},{10,... | collective-permute-start | bytes 393224 | tf_op jit(solution)/shard_map/ppermute | solution.py:151
  69.1 8.5 %collective-permute-done.6 = bf16[256,256]{1,0:T(8,128)(2,1)S(1)} collective-permute-done((bf16[256,256]{1,0:T(8,128)(2,1)}, bf16[256,256]{1,0:T(8,128)(2,1)S(1)}, u32[]{:S(2)}, u32[]{:S(2)}) %collective-permute-start.6) | collective-permute-done | bytes 131104 | tf_op jit(solution)/shard_map/ppermute | solution.py:151
  78.5 2.4 %gather_fusion.1 = bf16[4,256,256]{2,1,0:T(8,128)(2,1)} fusion(bf16[4,256,256]{2,1,0:T(8,128)(2,1)} %pad_maximum_fusion.1, s32[1024]{0:T(1024)S(1)} %pad_clamp_fusion), kind=kCustom, calls=%fused_computation.1 | custom fusion | bytes 1048592 | tf_op jit(solution)/shard_map/jit(_take)/gather | solution.py:154
  82.1 3.1 %collective-permute-start.8 = (bf16[4,256,256]{2,1,0:T(8,128)(2,1)S(1)}, bf16[4,256,256]{2,1,0:T(8,128)(2,1)S(1)}, u32[]{:S(2)}, u32[]{:S(2)}) collective-permute-start(bf16[4,256,256]{2,1,0:T(8,128)(2,1)S(1)} %broadcast_select_fusion.1), channel_id=1, source_target_pairs={{0,2},{1,3},{2,0},{3,1},{4,6},{5,7},{6,4},{7,5},{8,10},{9,11},{10,... | collective-permute-start | bytes 1572872 | tf_op jit(solution)/shard_map/ppermute | solution.py:177
  86.3 8.9 %collective-permute-done.8 = bf16[4,256,256]{2,1,0:T(8,128)(2,1)S(1)} collective-permute-done((bf16[4,256,256]{2,1,0:T(8,128)(2,1)S(1)}, bf16[4,256,256]{2,1,0:T(8,128)(2,1)S(1)}, u32[]{:S(2)}, u32[]{:S(2)}) %collective-permute-start.8) | collective-permute-done | bytes 524320 | tf_op jit(solution)/shard_map/ppermute | solution.py:177
  96.7 3.0 %collective-permute-done.9 = bf16[2,4,256,256]{3,2,1,0:T(8,128)(2,1)} collective-permute-done((bf16[2,4,256,256]{3,2,1,0:T(8,128)(2,1)}, bf16[2,4,256,256]{3,2,1,0:T(8,128)(2,1)}, u32[]{:S(2)}, u32[]{:S(2)}) %collective-permute-start.9) | collective-permute-done | bytes 1048608 | tf_op jit(solution)/shard_map/ppermute | solution.py:179
  99.7 2.1 %fusion.3 = bf16[256,1536]{1,0:T(8,128)(2,1)S(1)} fusion(bf16[2,2,256,1536]{3,2,1,0:T(8,128)(2,1)S(1)} %broadcast_select_fusion, s32[]{:T(128)S(6)} %min.84, bf16[2,1,4,256,256]{4,3,2,0,1:T(8,128)(2,1)} %get-tuple-element.45, bf16[2,1,4,256,256]{4,3,2,0,1:T(8,128)(2,1)} %bitcast.41), kind=kOutput, calls=%fused_computation.28 | convolution fusion | flops 805961728 | bytes 6029316 | tf_op jit(solution)/shard_map/deti,deic->tc/dot_general | solution.py:183
  105.9 3.9 %collective-permute-start.10 = (bf16[256,768]{1,0:T(8,128)(2,1)S(1)}, bf16[256,768]{1,0:T(8,128)(2,1)S(1)}, u32[]{:S(2)}, u32[]{:S(2)}) collective-permute-start(bf16[256,768]{1,0:T(8,128)(2,1)S(1)} %get-tuple-element.46), channel_id=1, source_target_pairs={{0,4},{1,5},{2,6},{3,7},{16,20},{17,21},{18,22},{19,23}} | collective-permute-start | bytes 1179656 | tf_op jit(solution)/shard_map/ppermute | solution.py:202
  114.3 5.0 %collective-permute-done.10 = bf16[256,768]{1,0:T(8,128)(2,1)S(1)} collective-permute-done((bf16[256,768]{1,0:T(8,128)(2,1)S(1)}, bf16[256,768]{1,0:T(8,128)(2,1)S(1)}, u32[]{:S(2)}, u32[]{:S(2)}) %collective-permute-start.10) | collective-permute-done | bytes 393248 | tf_op jit(solution)/shard_map/ppermute | solution.py:202
  119.3 7.6 %collective-permute-done.16 = bf16[256,768]{1,0:T(8,128)(2,1)S(1)} collective-permute-done((bf16[256,768]{1,0:T(8,128)(2,1)S(1)}, bf16[256,768]{1,0:T(8,128)(2,1)S(1)}, u32[]{:S(2)}, u32[]{:S(2)}) %collective-permute-start.16) | collective-permute-done | bytes 393248 | tf_op jit(solution)/shard_map/ppermute | solution.py:202
  127.2 4.4 %collective-permute-start.11 = (bf16[256,768]{1,0:T(8,128)(2,1)S(1)}, bf16[256,768]{1,0:T(8,128)(2,1)S(1)}, u32[]{:S(2)}, u32[]{:S(2)}) collective-permute-start(bf16[256,768]{1,0:T(8,128)(2,1)S(1)} %get-tuple-element.38), channel_id=1, source_target_pairs={{0,4},{4,8},{1,5},{5,9},{2,6},{6,10},{3,7},{7,11},{16,20},{20,24},... | collective-permute-start | bytes 1179656 | tf_op jit(solution)/shard_map/ppermute | solution.py:202
  131.6 1.9 %collective-permute-start.17 = (bf16[256,768]{1,0:T(8,128)(2,1)S(1)}, bf16[256,768]{1,0:T(8,128)(2,1)S(1)}, u32[]{:S(2)}, u32[]{:S(2)}) collective-permute-start(bf16[256,768]{1,0:T(8,128)(2,1)S(1)} %get-tuple-element.39), channel_id=1, source_target_pairs={{0,4},{4,8},{1,5},{5,9},{2,6},{6,10},{3,7},{7,11},{16,20},{20,24},... | collective-permute-start | bytes 1179656 | tf_op jit(solution)/shard_map/ppermute | solution.py:202
  136.1 5.0 %collective-permute-done.11 = bf16[256,768]{1,0:T(8,128)(2,1)S(1)} collective-permute-done((bf16[256,768]{1,0:T(8,128)(2,1)S(1)}, bf16[256,768]{1,0:T(8,128)(2,1)S(1)}, u32[]{:S(2)}, u32[]{:S(2)}) %collective-permute-start.11) | collective-permute-done | bytes 393248 | tf_op jit(solution)/shard_map/ppermute | solution.py:202
  141.1 6.7 %collective-permute-done.17 = bf16[256,768]{1,0:T(8,128)(2,1)S(1)} collective-permute-done((bf16[256,768]{1,0:T(8,128)(2,1)S(1)}, bf16[256,768]{1,0:T(8,128)(2,1)S(1)}, u32[]{:S(2)}, u32[]{:S(2)}) %collective-permute-start.17) | collective-permute-done | bytes 393248 | tf_op jit(solution)/shard_map/ppermute | solution.py:202
  148.0 4.4 %collective-permute-start.12 = (bf16[256,768]{1,0:T(8,128)(2,1)S(1)}, bf16[256,768]{1,0:T(8,128)(2,1)S(1)}, u32[]{:S(2)}, u32[]{:S(2)}) collective-permute-start(bf16[256,768]{1,0:T(8,128)(2,1)S(1)} %get-tuple-element.36), channel_id=1, source_target_pairs={{0,4},{4,8},{8,12},{1,5},{5,9},{9,13},{2,6},{6,10},{10,14},{3,7},{... | collective-permute-start | bytes 1179656 | tf_op jit(solution)/shard_map/ppermute | solution.py:202
  154.0 4.6 %collective-permute-start.18 = (bf16[256,768]{1,0:T(8,128)(2,1)S(1)}, bf16[256,768]{1,0:T(8,128)(2,1)S(1)}, u32[]{:S(2)}, u32[]{:S(2)}) collective-permute-start(bf16[256,768]{1,0:T(8,128)(2,1)S(1)} %get-tuple-element.37), channel_id=1, source_target_pairs={{0,4},{4,8},{8,12},{1,5},{5,9},{9,13},{2,6},{6,10},{10,14},{3,7},{... | collective-permute-start | bytes 1179656 | tf_op jit(solution)/shard_map/ppermute | solution.py:202
  161.7 4.9 %collective-permute-done.15 = bf16[256,768]{1,0:T(8,128)(2,1)S(1)} collective-permute-done((bf16[256,768]{1,0:T(8,128)(2,1)S(1)}, bf16[256,768]{1,0:T(8,128)(2,1)S(1)}, u32[]{:S(2)}, u32[]{:S(2)}) %collective-permute-start.15) | collective-permute-done | bytes 393248 | tf_op jit(solution)/shard_map/ppermute | solution.py:205
  167.8 4.8 %collective-permute-done.21 = bf16[256,768]{1,0:T(8,128)(2,1)S(1)} collective-permute-done((bf16[256,768]{1,0:T(8,128)(2,1)S(1)}, bf16[256,768]{1,0:T(8,128)(2,1)S(1)}, u32[]{:S(2)}, u32[]{:S(2)}) %collective-permute-start.21) | collective-permute-done | bytes 393248 | tf_op jit(solution)/shard_map/ppermute | solution.py:205
  172.7 1.9 %fusion.1 = bf16[256,1536]{1,0:T(8,128)(2,1)} fusion(bf16[2,2,256,1536]{3,2,1,0:T(8,128)(2,1)S(1)} %broadcast_select_fusion, f32[256,768]{1,0:T(8,128)S(1)} %convert_add_fusion, f32[256,768]{1,0:T(8,128)S(1)} %convert_add_fusion.1, bf16[2,2,1,256,256]{4,3,2,0,1:T(8,128)(2,1)S(1)} %get-tuple-element.30), kind=kOutput, calls=%fused_computation.26 | convolution fusion | flops 806486016 | bytes 6029312 | tf_op jit(solution)/shard_map/deti,deic->tc/dot_general | solution.py:183
  (101 shorter events, 47.9 us)
Async XLA Ops:
  4.1 15.6 %copy-start.5 = (s32[1536]{0:T(1024)S(1)}, s32[1536]{0:T(1024)}, u32[]{:S(2)}) copy-start(s32[1536]{0:T(1024)} %param.17) | copy-start | bytes 18436
  4.1 15.6 %copy-start.4 = (bf16[256,1024]{1,0:T(8,128)(2,1)S(1)}, bf16[256,1024]{1,0:T(8,128)(2,1)}, u32[]{:S(2)}) copy-start(bf16[256,1024]{1,0:T(8,128)(2,1)} %param.9) | copy-start | bytes 1572868
  5.9 13.9 %copy-start.1 = (bf16[256,1024]{0,1:T(8,128)(2,1)}, bf16[256,1024]{0,1:T(8,128)(2,1)S(1)}, u32[]{:S(2)}) copy-start(bf16[256,1024]{0,1:T(8,128)(2,1)S(1)} %fusion.15) | copy-start | bytes 1572868
  6.3 13.6 %copy-start.2 = (bf16[256,1024]{0,1:T(8,128)(2,1)}, bf16[256,1024]{0,1:T(8,128)(2,1)S(1)}, u32[]{:S(2)}) copy-start(bf16[256,1024]{0,1:T(8,128)(2,1)S(1)} %multiply_convert_fusion.5) | copy-start | bytes 1572868
  7.8 26.3 %collective-permute-start.2 = (bf16[8,16640]{1,0:T(8,128)(2,1)}, bf16[8,16640]{1,0:T(8,128)(2,1)}, u32[]{:S(2)}, u32[]{:S(2)}) collective-permute-start(bf16[8,16640]{1,0:T(8,128)(2,1)} %pad_maximum_fusion.2), channel_id=1, source_target_pairs={{0,12},{1,13},{2,14},{3,15},{16,28},{17,29},{18,30},{19,31}} | collective-permute-start | bytes 798728 | tf_op jit(solution)/shard_map/ppermute | solution.py:107
  15.4 22.4 %collective-permute-start.1 = (bf16[8,16640]{1,0:T(8,128)(2,1)}, bf16[8,16640]{1,0:T(8,128)(2,1)S(1)}, u32[]{:S(2)}, u32[]{:S(2)}) collective-permute-start(bf16[8,16640]{1,0:T(8,128)(2,1)} %pad_maximum_fusion.2), channel_id=1, source_target_pairs={{0,8},{4,12},{1,9},{5,13},{2,10},{6,14},{3,11},{7,15},{16,24},{20,... | collective-permute-start | bytes 798728 | tf_op jit(solution)/shard_map/ppermute | solution.py:107
  16.7 24.0 %collective-permute-start = (bf16[8,16640]{1,0:T(8,128)(2,1)}, bf16[8,16640]{1,0:T(8,128)(2,1)}, u32[]{:S(2)}, u32[]{:S(2)}) collective-permute-start(bf16[8,16640]{1,0:T(8,128)(2,1)} %pad_maximum_fusion.2), channel_id=1, source_target_pairs={{0,4},{4,8},{8,12},{1,5},{5,9},{9,13},{2,6},{6,10},{10,14},{3,7},{... | collective-permute-start | bytes 798728 | tf_op jit(solution)/shard_map/ppermute | solution.py:107
  45.4 2.8 %copy-start.3 = (bf16[256,1024]{0,1:T(8,128)(2,1)S(1)}, bf16[256,1024]{0,1:T(8,128)(2,1)}, u32[]{:S(2)}) copy-start(bf16[256,1024]{0,1:T(8,128)(2,1)} %copy.100) | copy-start | bytes 1572868
  45.4 2.8 %copy-start.6 = (f32[1024]{0:T(1024)S(1)}, f32[1024]{0:T(1024)}, u32[]{:S(2)}) copy-start(f32[1024]{0:T(1024)} %param.15) | copy-start | bytes 12292
  49.3 7.8 %collective-permute-start.3 = (bf16[256,2,256]{0,2,1:T(8,128)(2,1)}, bf16[256,2,256]{0,2,1:T(8,128)(2,1)}, u32[]{:S(2)}, u32[]{:S(2)}) collective-permute-start(bf16[256,2,256]{0,2,1:T(8,128)(2,1)} %get-tuple-element.54), channel_id=1, source_target_pairs={{0,2},{1,3},{2,0},{3,1},{4,6},{5,7},{6,4},{7,5},{8,10},{9,11},{10,... | collective-permute-start | bytes 786440 | tf_op jit(solution)/shard_map/ppermute | solution.py:140
  63.4 5.8 %collective-permute-start.7 = (bf16[256,256]{1,0:T(8,128)(2,1)}, bf16[256,256]{1,0:T(8,128)(2,1)S(1)}, u32[]{:S(2)}, u32[]{:S(2)}) collective-permute-start(bf16[256,256]{1,0:T(8,128)(2,1)} %bitcast.169), channel_id=1, source_target_pairs={{0,9},{1,13},{2,3},{3,7},{4,0},{5,4},{6,10},{7,14},{8,1},{9,5},{10... | collective-permute-start | bytes 393224 | tf_op jit(solution)/shard_map/ppermute | solution.py:151
  63.4 14.2 %collective-permute-start.6 = (bf16[256,256]{1,0:T(8,128)(2,1)}, bf16[256,256]{1,0:T(8,128)(2,1)S(1)}, u32[]{:S(2)}, u32[]{:S(2)}) collective-permute-start(bf16[256,256]{1,0:T(8,128)(2,1)} %bitcast.168), channel_id=1, source_target_pairs={{0,8},{1,12},{2,2},{3,6},{4,9},{5,13},{6,3},{7,7},{8,0},{9,4},{10,... | collective-permute-start | bytes 393224 | tf_op jit(solution)/shard_map/ppermute | solution.py:151
  66.5 11.1 %collective-permute-start.5 = (bf16[256,256]{1,0:T(8,128)(2,1)S(1)}, bf16[256,256]{1,0:T(8,128)(2,1)S(1)}, u32[]{:S(2)}, u32[]{:S(2)}) collective-permute-start(bf16[256,256]{1,0:T(8,128)(2,1)S(1)} %bitcast.167), channel_id=1, source_target_pairs={{0,1},{1,5},{2,11},{3,15},{4,8},{5,12},{6,2},{7,6},{8,9},{9,13},{1... | collective-permute-start | bytes 393224 | tf_op jit(solution)/shard_map/ppermute | solution.py:151
  68.1 9.5 %collective-permute-start.4 = (bf16[256,256]{1,0:T(8,128)(2,1)S(1)}, bf16[256,256]{1,0:T(8,128)(2,1)S(1)}, u32[]{:S(2)}, u32[]{:S(2)}) collective-permute-start(bf16[256,256]{1,0:T(8,128)(2,1)S(1)} %bitcast.166), channel_id=1, source_target_pairs={{0,0},{1,4},{2,10},{3,14},{4,1},{5,5},{6,11},{7,15},{8,8},{9,12},{... | collective-permute-start | bytes 393224 | tf_op jit(solution)/shard_map/ppermute | solution.py:151
  82.1 13.2 %collective-permute-start.8 = (bf16[4,256,256]{2,1,0:T(8,128)(2,1)S(1)}, bf16[4,256,256]{2,1,0:T(8,128)(2,1)S(1)}, u32[]{:S(2)}, u32[]{:S(2)}) collective-permute-start(bf16[4,256,256]{2,1,0:T(8,128)(2,1)S(1)} %broadcast_select_fusion.1), channel_id=1, source_target_pairs={{0,2},{1,3},{2,0},{3,1},{4,6},{5,7},{6,4},{7,5},{8,10},{9,11},{10,... | collective-permute-start | bytes 1572872 | tf_op jit(solution)/shard_map/ppermute | solution.py:177
  96.7 3.0 %collective-permute-start.9 = (bf16[2,4,256,256]{3,2,1,0:T(8,128)(2,1)}, bf16[2,4,256,256]{3,2,1,0:T(8,128)(2,1)}, u32[]{:S(2)}, u32[]{:S(2)}) collective-permute-start(bf16[2,4,256,256]{3,2,1,0:T(8,128)(2,1)} %get-tuple-element.44), channel_id=1, source_target_pairs={{0,1},{1,0},{2,3},{3,2},{4,5},{5,4},{6,7},{7,6},{8,9},{9,8},{10,11... | collective-permute-start | bytes 3145736 | tf_op jit(solution)/shard_map/ppermute | solution.py:179
  99.7 3.6 %copy-start = (bf16[2,1,4,256,256]{4,3,2,0,1:T(8,128)(2,1)S(1)}, bf16[2,1,4,256,256]{4,3,2,0,1:T(8,128)(2,1)}, u32[]{:S(2)}) copy-start(bf16[2,1,4,256,256]{4,3,2,0,1:T(8,128)(2,1)} %get-tuple-element.45) | copy-start | bytes 3145732
  101.8 31.7 %collective-permute-start.13 = (bf16[256,768]{1,0:T(8,128)(2,1)S(1)}, bf16[256,768]{1,0:T(8,128)(2,1)S(1)}, u32[]{:S(2)}, u32[]{:S(2)}) collective-permute-start(bf16[256,768]{1,0:T(8,128)(2,1)S(1)} %get-tuple-element.48), channel_id=1, source_target_pairs={{12,8},{13,9},{14,10},{15,11},{28,24},{29,25},{30,26},{31,27}} | collective-permute-start | bytes 1179656 | tf_op jit(solution)/shard_map/ppermute | solution.py:205
  102.5 31.0 %collective-permute-start.19 = (bf16[256,768]{1,0:T(8,128)(2,1)S(1)}, bf16[256,768]{1,0:T(8,128)(2,1)S(1)}, u32[]{:S(2)}, u32[]{:S(2)}) collective-permute-start(bf16[256,768]{1,0:T(8,128)(2,1)S(1)} %get-tuple-element.49), channel_id=1, source_target_pairs={{12,8},{13,9},{14,10},{15,11},{28,24},{29,25},{30,26},{31,27}} | collective-permute-start | bytes 1179656 | tf_op jit(solution)/shard_map/ppermute | solution.py:205
  105.9 13.4 %collective-permute-start.10 = (bf16[256,768]{1,0:T(8,128)(2,1)S(1)}, bf16[256,768]{1,0:T(8,128)(2,1)S(1)}, u32[]{:S(2)}, u32[]{:S(2)}) collective-permute-start(bf16[256,768]{1,0:T(8,128)(2,1)S(1)} %get-tuple-element.46), channel_id=1, source_target_pairs={{0,4},{1,5},{2,6},{3,7},{16,20},{17,21},{18,22},{19,23}} | collective-permute-start | bytes 1179656 | tf_op jit(solution)/shard_map/ppermute | solution.py:202
  109.9 17.1 %collective-permute-start.16 = (bf16[256,768]{1,0:T(8,128)(2,1)S(1)}, bf16[256,768]{1,0:T(8,128)(2,1)S(1)}, u32[]{:S(2)}, u32[]{:S(2)}) collective-permute-start(bf16[256,768]{1,0:T(8,128)(2,1)S(1)} %get-tuple-element.47), channel_id=1, source_target_pairs={{0,4},{1,5},{2,6},{3,7},{16,20},{17,21},{18,22},{19,23}} | collective-permute-start | bytes 1179656 | tf_op jit(solution)/shard_map/ppermute | solution.py:202
  127.2 13.9 %collective-permute-start.11 = (bf16[256,768]{1,0:T(8,128)(2,1)S(1)}, bf16[256,768]{1,0:T(8,128)(2,1)S(1)}, u32[]{:S(2)}, u32[]{:S(2)}) collective-permute-start(bf16[256,768]{1,0:T(8,128)(2,1)S(1)} %get-tuple-element.38), channel_id=1, source_target_pairs={{0,4},{4,8},{1,5},{5,9},{2,6},{6,10},{3,7},{7,11},{16,20},{20,24},... | collective-permute-start | bytes 1179656 | tf_op jit(solution)/shard_map/ppermute | solution.py:202
  131.6 16.2 %collective-permute-start.17 = (bf16[256,768]{1,0:T(8,128)(2,1)S(1)}, bf16[256,768]{1,0:T(8,128)(2,1)S(1)}, u32[]{:S(2)}, u32[]{:S(2)}) collective-permute-start(bf16[256,768]{1,0:T(8,128)(2,1)S(1)} %get-tuple-element.39), channel_id=1, source_target_pairs={{0,4},{4,8},{1,5},{5,9},{2,6},{6,10},{3,7},{7,11},{16,20},{20,24},... | collective-permute-start | bytes 1179656 | tf_op jit(solution)/shard_map/ppermute | solution.py:202
  133.8 18.7 %collective-permute-start.14 = (bf16[256,768]{1,0:T(8,128)(2,1)S(1)}, bf16[256,768]{1,0:T(8,128)(2,1)S(1)}, u32[]{:S(2)}, u32[]{:S(2)}) collective-permute-start(bf16[256,768]{1,0:T(8,128)(2,1)S(1)} %get-tuple-element.42), channel_id=1, source_target_pairs={{8,4},{12,8},{9,5},{13,9},{10,6},{14,10},{11,7},{15,11},{24,20},{2... | collective-permute-start | bytes 1179656 | tf_op jit(solution)/shard_map/ppermute | solution.py:205
  134.4 18.0 %collective-permute-start.20 = (bf16[256,768]{1,0:T(8,128)(2,1)S(1)}, bf16[256,768]{1,0:T(8,128)(2,1)S(1)}, u32[]{:S(2)}, u32[]{:S(2)}) collective-permute-start(bf16[256,768]{1,0:T(8,128)(2,1)S(1)} %get-tuple-element.43), channel_id=1, source_target_pairs={{8,4},{12,8},{9,5},{13,9},{10,6},{14,10},{11,7},{15,11},{24,20},{2... | collective-permute-start | bytes 1179656 | tf_op jit(solution)/shard_map/ppermute | solution.py:205
  148.0 13.6 %collective-permute-start.12 = (bf16[256,768]{1,0:T(8,128)(2,1)S(1)}, bf16[256,768]{1,0:T(8,128)(2,1)S(1)}, u32[]{:S(2)}, u32[]{:S(2)}) collective-permute-start(bf16[256,768]{1,0:T(8,128)(2,1)S(1)} %get-tuple-element.36), channel_id=1, source_target_pairs={{0,4},{4,8},{8,12},{1,5},{5,9},{9,13},{2,6},{6,10},{10,14},{3,7},{... | collective-permute-start | bytes 1179656 | tf_op jit(solution)/shard_map/ppermute | solution.py:202
  152.7 13.9 %collective-permute-start.15 = (bf16[256,768]{1,0:T(8,128)(2,1)S(1)}, bf16[256,768]{1,0:T(8,128)(2,1)S(1)}, u32[]{:S(2)}, u32[]{:S(2)}) collective-permute-start(bf16[256,768]{1,0:T(8,128)(2,1)S(1)} %get-tuple-element.40), channel_id=1, source_target_pairs={{4,0},{8,4},{12,8},{5,1},{9,5},{13,9},{6,2},{10,6},{14,10},{7,3},{... | collective-permute-start | bytes 1179656 | tf_op jit(solution)/shard_map/ppermute | solution.py:205
  154.0 13.8 %collective-permute-start.18 = (bf16[256,768]{1,0:T(8,128)(2,1)S(1)}, bf16[256,768]{1,0:T(8,128)(2,1)S(1)}, u32[]{:S(2)}, u32[]{:S(2)}) collective-permute-start(bf16[256,768]{1,0:T(8,128)(2,1)S(1)} %get-tuple-element.37), channel_id=1, source_target_pairs={{0,4},{4,8},{8,12},{1,5},{5,9},{9,13},{2,6},{6,10},{10,14},{3,7},{... | collective-permute-start | bytes 1179656 | tf_op jit(solution)/shard_map/ppermute | solution.py:202
  158.5 14.0 %collective-permute-start.21 = (bf16[256,768]{1,0:T(8,128)(2,1)S(1)}, bf16[256,768]{1,0:T(8,128)(2,1)S(1)}, u32[]{:S(2)}, u32[]{:S(2)}) collective-permute-start(bf16[256,768]{1,0:T(8,128)(2,1)S(1)} %get-tuple-element.41), channel_id=1, source_target_pairs={{4,0},{8,4},{12,8},{5,1},{9,5},{13,9},{6,2},{10,6},{14,10},{7,3},{... | collective-permute-start | bytes 1179656 | tf_op jit(solution)/shard_map/ppermute | solution.py:205

commit v10 on v8

--- a/solution.py
+++ b/solution.py
@@ -180,6 +180,33 @@
             "deti,deic->tc", rows, w_perm, preferred_element_type=jnp.float32
         )
 
+    if n_seq == 4:
+        def bf(v):
+            return v.astype(jnp.bfloat16)
+
+        near_r = lax.ppermute(
+            bf(partial_for(jnp.clip(s_me + 2, 0, 3))), "seq", [(0, 1), (1, 2)]
+        )
+        far_r = lax.ppermute(bf(partial_for(jnp.int32(3))), "seq", [(0, 3)])
+        near_l = lax.ppermute(
+            bf(partial_for(jnp.clip(s_me - 2, 0, 3))), "seq", [(3, 2), (2, 1)]
+        )
+        far_l = lax.ppermute(bf(partial_for(jnp.int32(0))), "seq", [(3, 0)])
+        last_r = lax.ppermute(
+            bf(partial_for(jnp.clip(s_me + 1, 0, 3)) + near_r.astype(jnp.float32)),
+            "seq",
+            [(0, 1), (1, 2), (2, 3)],
+        )
+        last_l = lax.ppermute(
+            bf(partial_for(jnp.clip(s_me - 1, 0, 3)) + near_l.astype(jnp.float32)),
+            "seq",
+            [(3, 2), (2, 1), (1, 0)],
+        )
+        total = partial_for(s_me)
+        for came in (last_r, far_r, last_l, far_l):
+            total = total + came.astype(jnp.float32)
+        return total.astype(jnp.bfloat16)
+
     halves = 2 if cols_w % 256 == 0 else 1
     width = cols_w // halves
     recv_r = [None] * halves

time: 164 us -> 162 us (0.988)
  waiting for transfers between devices: 70.6 us -> 53.9 us
  matrix products: 12.9 us -> 23.5 us
  starting transfers between devices: 54.8 us -> 61.7 us
  other arithmetic: 16.4 us -> 13.6 us
    ppermute x12 -> x6, waiting for transfers between devices: 38.6 us -> 21.9 us  [the longest x1 13.6 us: per_device(): lax.ppermute(bf(partial_for(jnp.clip(s_me - 1, 0, 3)) + near_l.astype(jnp...]
    dot_general x7, matrix products: 8.67 us -> 19.3 us  [partial_for(): jnp.einsum('deti,deic->tc', rows, w_perm, preferred_element_type=jnp.floa...]
    ppermute x12 -> x6, starting transfers between devices: 23.6 us -> 32.2 us  [the longest x1 20.1 us: per_device(): lax.ppermute(bf(partial_for(jnp.clip(s_me + 1, 0, 3)) + near_r.astype(jnp...]
    ppermute x1, starting transfers between devices: 3.8 us -> 0.07 us  [per_device(): got.append(lax.ppermute(x, 'mdl', perm))]
    ppermute x3, waiting for transfers between devices: 8.35 us -> 6.02 us  [per_device(): came = lax.ppermute(packed, 'seq', [(z, z + d) for z in range(n_seq - d)])]
    ppermute x1, waiting for transfers between devices: 10.9 us -> 13 us  [per_device(): got.append(lax.ppermute(x, 'mdl', perm))]
  transfers between devices with their start and end apart: 22 -> 16, of which waited for: 12 -> 9; matrix products, arithmetic and copies ran while one was open for 12% -> 15% of each run, Pallas kernels for 0% -> 0%
where the time goes in v10:
time: 162 us; the launch traced here: 161 us
  starting transfers between devices  61.7 us (38%)
  waiting for transfers between devices  53.9 us (33%)
  matrix products  23.5 us (15%)
  other arithmetic  13.6 us (8%)
  local copies, waits for them, and re-layouts  7.54 us (5%)
    ppermute x1, starting transfers between devices, per_device(): lax.ppermute(bf(partial_for(jnp.clip(s_me + 1, 0, 3)) + near_r.astype(jnp...  20.1 us
    dot_general x7, matrix products, partial_for(): jnp.einsum('deti,deic->tc', rows, w_perm, preferred_element_type=jnp.floa...  19.3 us
    ppermute x4, starting transfers between devices, per_device(): received.append(lax.ppermute(item, ('seq', 'mdl'), perm))  15 us
    ppermute x1, waiting for transfers between devices, per_device(): lax.ppermute(bf(partial_for(jnp.clip(s_me - 1, 0, 3)) + near_l.astype(jnp...  13.6 us
    ppermute x1, waiting for transfers between devices, per_device(): got.append(lax.ppermute(x, 'mdl', perm))  13 us
    ppermute x3, starting transfers between devices, per_device(): came = lax.ppermute(packed, 'seq', [(z, z + d) for z in range(n_seq - d)])  11.4 us
    ppermute x4, waiting for transfers between devices, per_device(): received.append(lax.ppermute(item, ('seq', 'mdl'), perm))  7.49 us
    ppermute x3, waiting for transfers between devices, per_device(): came = lax.ppermute(packed, 'seq', [(z, z + d) for z in range(n_seq - d)])  6.02 us
  transfers between devices with their start and end apart: 16, of which 9 were waited for; matrix products, arithmetic and copies ran while one was open for 15% of the time, Pallas kernels for 0%

profile of v10, /device:TPU:0, one launch (start us, length us, event | category | flops | bytes accessed | tf_op | source)
XLA Modules:
  0.0 160.8 jit_solution(4991839880963452223)
XLA Ops:
  7.0 5.7 %collective-permute-start = (bf16[8,16640]{1,0:T(8,128)(2,1)S(1)}, bf16[8,16640]{1,0:T(8,128)(2,1)}, u32[]{:S(2)}, u32[]{:S(2)}) collective-permute-start(bf16[8,16640]{1,0:T(8,128)(2,1)S(1)} %pad_maximum_fusion.3), channel_id=1, source_target_pairs={{0,4},{4,8},{8,12},{1,5},{5,9},{9,13},{2,6},{6,10},{10,14},{3,7},{... | collective-permute-start | bytes 798728 | tf_op jit(solution)/shard_map/ppermute | solution.py:95
  12.7 3.8 %collective-permute-start.1 = (bf16[8,16640]{1,0:T(8,128)(2,1)S(1)}, bf16[8,16640]{1,0:T(8,128)(2,1)S(1)}, u32[]{:S(2)}, u32[]{:S(2)}) collective-permute-start(bf16[8,16640]{1,0:T(8,128)(2,1)S(1)} %pad_maximum_fusion.3), channel_id=1, source_target_pairs={{0,8},{4,12},{1,9},{5,13},{2,10},{6,14},{3,11},{7,15},{16,24},{20,... | collective-permute-start | bytes 798728 | tf_op jit(solution)/shard_map/ppermute | solution.py:95
  16.5 2.0 %collective-permute-start.2 = (bf16[8,16640]{1,0:T(8,128)(2,1)S(1)}, bf16[8,16640]{1,0:T(8,128)(2,1)}, u32[]{:S(2)}, u32[]{:S(2)}) collective-permute-start(bf16[8,16640]{1,0:T(8,128)(2,1)S(1)} %pad_maximum_fusion.3), channel_id=1, source_target_pairs={{0,12},{1,13},{2,14},{3,15},{16,28},{17,29},{18,30},{19,31}} | collective-permute-start | bytes 798728 | tf_op jit(solution)/shard_map/ppermute | solution.py:95
  19.3 1.9 %fusion.14 = f32[1,256,8,128]{1,3,2,0:T(8,128)} fusion(bf16[256,8,128]{0,2,1:T(8,128)(2,1)S(1)} %bitcast.191, bf16[256,8,128]{0,2,1:T(8,128)(2,1)S(1)} %bitcast.188, bf16[256,8,128]{0,2,1:T(8,128)(2,1)S(1)} %bitcast.193, f32[8,256]{1,0:T(8,128)S(1)} %bitcast_add_fusion.2, pred[256,256]{1,0:T(8,128)(4,1)S(1)} %iota_compare_fusion), kind=kOutput, calls=%fused_computation.38 | convolution fusion | flops 271056896 | bytes 2695168 | tf_op jit(solution)/shard_map/hbij,bjhd->bihd/dot_general | solution.py:63
  22.8 1.7 %collective-permute-done.1 = bf16[8,16640]{1,0:T(8,128)(2,1)S(1)} collective-permute-done((bf16[8,16640]{1,0:T(8,128)(2,1)S(1)}, bf16[8,16640]{1,0:T(8,128)(2,1)S(1)}, u32[]{:S(2)}, u32[]{:S(2)}) %collective-permute-start.1) | collective-permute-done | bytes 266272 | tf_op jit(solution)/shard_map/ppermute | solution.py:95
  24.8 4.3 %collective-permute-done.2 = bf16[8,16640]{1,0:T(8,128)(2,1)} collective-permute-done((bf16[8,16640]{1,0:T(8,128)(2,1)S(1)}, bf16[8,16640]{1,0:T(8,128)(2,1)}, u32[]{:S(2)}, u32[]{:S(2)}) %collective-permute-start.2) | collective-permute-done | bytes 266272 | tf_op jit(solution)/shard_map/ppermute | solution.py:95
  31.1 2.0 %multiply_reduce_fusion = (f32[256,8]{0,1:T(8,128)S(1)}, f32[1,256,8,128]{1,3,2,0:T(8,128)S(1)}) fusion(f32[1,256,8,128]{1,3,2,0:T(8,128)} %fusion.14, bf16[256,8,128]{0,2,1:T(8,128)(2,1)S(1)} %bitcast.189, f32[8,128,128]{1,2,0:T(8,128)S(1)} %copy.83, f32[8,128,128]{1,2,0:T(8,128)S(1)} %copy.82, f32[8,128,128]{1,2,0:T(8,128)S(1)} %copy.81, ...), kind=kOutput, calls=%fused_computation.59 | convolution fusion | flops 404355072 | bytes 4210784 | tf_op jit(solution)/shard_map/bihd,bhde->bihe/dot_general | solution.py:105
  33.6 1.6 collective-permute-start.3
  35.4 5.5 %collective-permute-done.3 = bf16[256,2,256]{0,2,1:T(8,128)(2,1)S(1)} collective-permute-done((bf16[256,2,256]{0,2,1:T(8,128)(2,1)S(1)}, bf16[256,2,256]{0,2,1:T(8,128)(2,1)S(1)}, u32[]{:S(2)}, u32[]{:S(2)}) %collective-permute-start.3) | collective-permute-done | bytes 262176 | tf_op jit(solution)/shard_map/ppermute | solution.py:129
  42.0 8.9 %collective-permute-start.5 = (bf16[256,256]{1,0:T(8,128)(2,1)S(1)}, bf16[256,256]{1,0:T(8,128)(2,1)S(1)}, u32[]{:S(2)}, u32[]{:S(2)}) collective-permute-start(bf16[256,256]{1,0:T(8,128)(2,1)S(1)} %bitcast.197), channel_id=1, source_target_pairs={{0,1},{1,5},{2,11},{3,15},{4,8},{5,12},{6,2},{7,6},{8,9},{9,13},{1... | collective-permute-start | bytes 393224 | tf_op jit(solution)/shard_map/ppermute | solution.py:140
  51.0 5.3 %collective-permute-start.6 = (bf16[256,256]{1,0:T(8,128)(2,1)S(1)}, bf16[256,256]{1,0:T(8,128)(2,1)S(1)}, u32[]{:S(2)}, u32[]{:S(2)}) collective-permute-start(bf16[256,256]{1,0:T(8,128)(2,1)S(1)} %bitcast.198), channel_id=1, source_target_pairs={{0,8},{1,12},{2,2},{3,6},{4,9},{5,13},{6,3},{7,7},{8,0},{9,4},{10,... | collective-permute-start | bytes 393224 | tf_op jit(solution)/shard_map/ppermute | solution.py:140
  56.5 1.9 %collective-permute-done.5 = bf16[256,256]{1,0:T(8,128)(2,1)S(1)} collective-permute-done((bf16[256,256]{1,0:T(8,128)(2,1)S(1)}, bf16[256,256]{1,0:T(8,128)(2,1)S(1)}, u32[]{:S(2)}, u32[]{:S(2)}) %collective-permute-start.5) | collective-permute-done | bytes 131104 | tf_op jit(solution)/shard_map/ppermute | solution.py:140
  58.4 5.6 %collective-permute-done.6 = bf16[256,256]{1,0:T(8,128)(2,1)S(1)} collective-permute-done((bf16[256,256]{1,0:T(8,128)(2,1)S(1)}, bf16[256,256]{1,0:T(8,128)(2,1)S(1)}, u32[]{:S(2)}, u32[]{:S(2)}) %collective-permute-start.6) | collective-permute-done | bytes 131104 | tf_op jit(solution)/shard_map/ppermute | solution.py:140
  65.0 13.0 %collective-permute-done.8 = bf16[4,256,256]{2,1,0:T(8,128)(2,1)S(1)} collective-permute-done((bf16[4,256,256]{2,1,0:T(8,128)(2,1)S(1)}, bf16[4,256,256]{2,1,0:T(8,128)(2,1)S(1)}, u32[]{:S(2)}, u32[]{:S(2)}) %collective-permute-start.8) | collective-permute-done | bytes 524320 | tf_op jit(solution)/shard_map/ppermute | solution.py:166
  78.0 1.5 fusion.133
  79.5 1.5 collective-permute-start.9
  81.0 1.4 multiply_convert_fusion
  82.5 2.4 %gather_fusion.1 = bf16[4,256,1536]{2,1,0:T(8,128)(2,1)} fusion(bf16[4,256,1536]{2,1,0:T(8,128)(2,1)S(1)} %bitcast.187, s32[1024]{0:T(1024)S(1)} %pad_clamp_fusion), kind=kCustom, calls=%fused_computation.1 | custom fusion | bytes 6291472 | tf_op jit(solution)/shard_map/jit(_take)/gather | solution.py:173
  84.9 2.3 %broadcast_select_fusion = bf16[4,256,1536]{2,1,0:T(8,128)(2,1)S(1)} fusion(bf16[4,256,1536]{2,1,0:T(8,128)(2,1)} %gather_fusion.1, pred[4]{0:T(512)(128)(4,1)S(1)} %get-tuple-element.42), kind=kLoop, calls=%fused_computation.15 | loop fusion | flops 1572864 | bytes 6291460 | tf_op jit(solution)/shard_map/jit(_take)/select_n | solution.py:173
  87.3 1.9 %fusion.9 = bf16[256,1536]{1,0:T(8,128)(2,1)S(1)} fusion(bf16[2,2,256,1536]{3,2,1,0:T(8,128)(2,1)S(1)} %bitcast.180, s32[]{:T(128)S(6)} %min.74, bf16[2,1,4,256,256]{4,3,1,0,2:T(8,128)(2,1)S(1)} %copy-done, bf16[2,1,4,256,256]{4,3,1,0,2:T(8,128)(2,1)} %bitcast.40), kind=kOutput, calls=%fused_computation.32 | convolution fusion | flops 805961728 | bytes 6029316 | tf_op jit(solution)/shard_map/deti,deic->tc/dot_general | solution.py:179
  89.2 3.1 %collective-permute-start.10 = (bf16[256,1536]{1,0:T(8,128)(2,1)S(1)}, bf16[256,1536]{1,0:T(8,128)(2,1)S(1)}, u32[]{:S(2)}, u32[]{:S(2)}) collective-permute-start(bf16[256,1536]{1,0:T(8,128)(2,1)S(1)} %fusion.9), channel_id=1, source_target_pairs={{0,4},{4,8},{1,5},{5,9},{2,6},{6,10},{3,7},{7,11},{16,20},{20,24},... | collective-permute-start | bytes 2359304 | tf_op jit(solution)/shard_map/ppermute | solution.py:187
  92.3 1.9 %fusion.11 = bf16[256,1536]{1,0:T(8,128)(2,1)S(1)} fusion(bf16[2,2,256,1536]{3,2,1,0:T(8,128)(2,1)S(1)} %bitcast.181, s32[]{:T(128)S(6)} %min.76, bf16[2,1,4,256,256]{4,3,1,0,2:T(8,128)(2,1)S(1)} %copy-done, bf16[2,1,4,256,256]{4,3,1,0,2:T(8,128)(2,1)} %bitcast.40), kind=kOutput, calls=%fused_computation.34 | convolution fusion | flops 805961728 | bytes 6029316 | tf_op jit(solution)/shard_map/deti,deic->tc/dot_general | solution.py:179
  95.0 2.9 %fusion.10 = bf16[256,1536]{1,0:T(8,128)(2,1)} fusion(bf16[2,2,256,1536]{3,2,1,0:T(8,128)(2,1)S(1)} %bitcast.182, bf16[2,1,4,256,256]{4,3,1,0,2:T(8,128)(2,1)S(1)} %copy-done, bf16[2,1,4,256,256]{4,3,1,0,2:T(8,128)(2,1)} %bitcast.40), kind=kOutput, calls=%fused_computation.33 | convolution fusion | flops 805961728 | bytes 6029312 | tf_op jit(solution)/shard_map/deti,deic->tc/dot_general | solution.py:179
  97.8 5.8 %collective-permute-start.12 = (bf16[256,1536]{1,0:T(8,128)(2,1)}, bf16[256,1536]{1,0:T(8,128)(2,1)}, u32[]{:S(2)}, u32[]{:S(2)}) collective-permute-start(bf16[256,1536]{1,0:T(8,128)(2,1)} %fusion.10), channel_id=1, source_target_pairs={{0,12},{1,13},{2,14},{3,15},{16,28},{17,29},{18,30},{19,31}} | collective-permute-start | bytes 2359304 | tf_op jit(solution)/shard_map/ppermute | solution.py:190
  103.6 2.8 %fusion.12 = bf16[256,1536]{1,0:T(8,128)(2,1)} fusion(bf16[2,2,256,1536]{3,2,1,0:T(8,128)(2,1)S(1)} %bitcast.183, bf16[2,1,4,256,256]{4,3,1,0,2:T(8,128)(2,1)} %bitcast.40, bf16[2,1,4,256,256]{4,3,1,0,2:T(8,128)(2,1)S(1)} %copy-done), kind=kOutput, calls=%fused_computation.35 | convolution fusion | flops 805961728 | bytes 6029312 | tf_op jit(solution)/shard_map/deti,deic->tc/dot_general | solution.py:179
  107.7 2.4 %collective-permute-done.10 = bf16[256,1536]{1,0:T(8,128)(2,1)S(1)} collective-permute-done((bf16[256,1536]{1,0:T(8,128)(2,1)S(1)}, bf16[256,1536]{1,0:T(8,128)(2,1)S(1)}, u32[]{:S(2)}, u32[]{:S(2)}) %collective-permute-start.10) | collective-permute-done | bytes 786464 | tf_op jit(solution)/shard_map/ppermute | solution.py:187
  110.2 2.8 %fusion.7 = bf16[256,1536]{1,0:T(8,128)(2,1)} fusion(bf16[2,2,256,1536]{3,2,1,0:T(8,128)(2,1)S(1)} %bitcast.184, bf16[256,1536]{1,0:T(8,128)(2,1)S(1)} %collective-permute-done.10, s32[]{:T(128)S(6)} %min.73, bf16[2,1,4,256,256]{4,3,1,0,2:T(8,128)(2,1)S(1)} %copy-done, bf16[2,1,4,256,256]{4,3,1,0,2:T(8,128)(2,1)} %bitcast.40), kind=kOutput, calls=%fused_computation.30 | convolution fusion | flops 806748160 | bytes 6815748 | tf_op jit(solution)/shard_map/deti,deic->tc/dot_general | solution.py:179
  113.0 20.1 %collective-permute-start.11 = (bf16[256,1536]{1,0:T(8,128)(2,1)}, bf16[256,1536]{1,0:T(8,128)(2,1)}, u32[]{:S(2)}, u32[]{:S(2)}) collective-permute-start(bf16[256,1536]{1,0:T(8,128)(2,1)} %fusion.7), channel_id=1, source_target_pairs={{0,4},{4,8},{8,12},{1,5},{5,9},{9,13},{2,6},{6,10},{10,14},{3,7},{... | collective-permute-start | bytes 2359304 | tf_op jit(solution)/shard_map/ppermute | solution.py:195
  133.1 2.8 %fusion.6 = bf16[256,1536]{1,0:T(8,128)(2,1)} fusion(bf16[2,2,256,1536]{3,2,1,0:T(8,128)(2,1)S(1)} %bitcast.185, bf16[256,1536]{1,0:T(8,128)(2,1)S(1)} %collective-permute-done.13, s32[]{:T(128)S(6)} %min.75, bf16[2,1,4,256,256]{4,3,1,0,2:T(8,128)(2,1)S(1)} %copy-done, bf16[2,1,4,256,256]{4,3,1,0,2:T(8,128)(2,1)} %bitcast.40), kind=kOutput, calls=%fused_computation.29 | convolution fusion | flops 806748160 | bytes 6815748 | tf_op jit(solution)/shard_map/deti,deic->tc/dot_general | solution.py:179
  137.2 5.8 %collective-permute-done.11 = bf16[256,1536]{1,0:T(8,128)(2,1)} collective-permute-done((bf16[256,1536]{1,0:T(8,128)(2,1)}, bf16[256,1536]{1,0:T(8,128)(2,1)}, u32[]{:S(2)}, u32[]{:S(2)}) %collective-permute-start.11) | collective-permute-done | bytes 786464 | tf_op jit(solution)/shard_map/ppermute | solution.py:195
  143.1 13.6 %collective-permute-done.14 = bf16[256,1536]{1,0:T(8,128)(2,1)} collective-permute-done((bf16[256,1536]{1,0:T(8,128)(2,1)}, bf16[256,1536]{1,0:T(8,128)(2,1)}, u32[]{:S(2)}, u32[]{:S(2)}) %collective-permute-start.14) | collective-permute-done | bytes 786464 | tf_op jit(solution)/shard_map/ppermute | solution.py:200
  156.6 4.1 %fusion.8 = bf16[256,1536]{1,0:T(8,128)(2,1)} fusion(bf16[2,2,256,1536]{3,2,1,0:T(8,128)(2,1)S(1)} %bitcast.186, bf16[256,1536]{1,0:T(8,128)(2,1)} %collective-permute-done.15, bf16[256,1536]{1,0:T(8,128)(2,1)} %collective-permute-done.14, bf16[256,1536]{1,0:T(8,128)(2,1)} %collective-permute-done.12, bf16[256,1536]{1,0:T(8,128)(2,1)} %collective-permute-done.11, ...), kind=kOutput, calls=%fused_computation.31 | convolution fusion | flops 809107456 | bytes 9175044 | tf_op jit(solution)/shard_map/deti,deic->tc/dot_general | solution.py:179
  (79 shorter events, 17.9 us)
Async XLA Ops:
  4.1 14.5 %copy-start.2 = (bf16[256,1024]{1,0:T(8,128)(2,1)S(1)}, bf16[256,1024]{1,0:T(8,128)(2,1)}, u32[]{:S(2)}) copy-start(bf16[256,1024]{1,0:T(8,128)(2,1)} %param.9) | copy-start | bytes 1572868
  7.0 14.5 %collective-permute-start = (bf16[8,16640]{1,0:T(8,128)(2,1)S(1)}, bf16[8,16640]{1,0:T(8,128)(2,1)}, u32[]{:S(2)}, u32[]{:S(2)}) collective-permute-start(bf16[8,16640]{1,0:T(8,128)(2,1)S(1)} %pad_maximum_fusion.3), channel_id=1, source_target_pairs={{0,4},{4,8},{8,12},{1,5},{5,9},{9,13},{2,6},{6,10},{10,14},{3,7},{... | collective-permute-start | bytes 798728 | tf_op jit(solution)/shard_map/ppermute | solution.py:95
  12.7 11.8 %collective-permute-start.1 = (bf16[8,16640]{1,0:T(8,128)(2,1)S(1)}, bf16[8,16640]{1,0:T(8,128)(2,1)S(1)}, u32[]{:S(2)}, u32[]{:S(2)}) collective-permute-start(bf16[8,16640]{1,0:T(8,128)(2,1)S(1)} %pad_maximum_fusion.3), channel_id=1, source_target_pairs={{0,8},{4,12},{1,9},{5,13},{2,10},{6,14},{3,11},{7,15},{16,24},{20,... | collective-permute-start | bytes 798728 | tf_op jit(solution)/shard_map/ppermute | solution.py:95
  16.5 12.6 %collective-permute-start.2 = (bf16[8,16640]{1,0:T(8,128)(2,1)S(1)}, bf16[8,16640]{1,0:T(8,128)(2,1)}, u32[]{:S(2)}, u32[]{:S(2)}) collective-permute-start(bf16[8,16640]{1,0:T(8,128)(2,1)S(1)} %pad_maximum_fusion.3), channel_id=1, source_target_pairs={{0,12},{1,13},{2,14},{3,15},{16,28},{17,29},{18,30},{19,31}} | collective-permute-start | bytes 798728 | tf_op jit(solution)/shard_map/ppermute | solution.py:95
  18.8 2.5 %copy-start.3 = (bf16[256,1024]{1,0:T(8,128)(2,1)S(1)}, bf16[256,1024]{1,0:T(8,128)(2,1)}, u32[]{:S(2)}) copy-start(bf16[256,1024]{1,0:T(8,128)(2,1)} %param.12) | copy-start | bytes 1572868
  31.1 2.1 %copy-start.5 = (f32[1024]{0:T(1024)S(1)}, f32[1024]{0:T(1024)}, u32[]{:S(2)}) copy-start(f32[1024]{0:T(1024)} %param.15) | copy-start | bytes 12292
  33.6 31.3 %copy-start.4 = (s32[1536]{0:T(1024)S(1)}, s32[1536]{0:T(1024)}, u32[]{:S(2)}) copy-start(s32[1536]{0:T(1024)} %param.17) | copy-start | bytes 18436
  33.6 7.2 %collective-permute-start.3 = (bf16[256,2,256]{0,2,1:T(8,128)(2,1)S(1)}, bf16[256,2,256]{0,2,1:T(8,128)(2,1)S(1)}, u32[]{:S(2)}, u32[]{:S(2)}) collective-permute-start(bf16[256,2,256]{0,2,1:T(8,128)(2,1)S(1)} %get-tuple-element.32), channel_id=1, source_target_pairs={{0,2},{1,3},{2,0},{3,1},{4,6},{5,7},{6,4},{7,5},{8,10},{9,11},{10,... | collective-permute-start | bytes 786440 | tf_op jit(solution)/shard_map/ppermute | solution.py:129
  41.2 15.3 %collective-permute-start.4 = (bf16[256,256]{1,0:T(8,128)(2,1)S(1)}, bf16[256,256]{1,0:T(8,128)(2,1)S(1)}, u32[]{:S(2)}, u32[]{:S(2)}) collective-permute-start(bf16[256,256]{1,0:T(8,128)(2,1)S(1)} %bitcast.196), channel_id=1, source_target_pairs={{0,0},{1,4},{2,10},{3,14},{4,1},{5,5},{6,11},{7,15},{8,8},{9,12},{... | collective-permute-start | bytes 393224 | tf_op jit(solution)/shard_map/ppermute | solution.py:140
  42.0 16.5 %collective-permute-start.5 = (bf16[256,256]{1,0:T(8,128)(2,1)S(1)}, bf16[256,256]{1,0:T(8,128)(2,1)S(1)}, u32[]{:S(2)}, u32[]{:S(2)}) collective-permute-start(bf16[256,256]{1,0:T(8,128)(2,1)S(1)} %bitcast.197), channel_id=1, source_target_pairs={{0,1},{1,5},{2,11},{3,15},{4,8},{5,12},{6,2},{7,6},{8,9},{9,13},{1... | collective-permute-start | bytes 393224 | tf_op jit(solution)/shard_map/ppermute | solution.py:140
  51.0 13.0 %collective-permute-start.6 = (bf16[256,256]{1,0:T(8,128)(2,1)S(1)}, bf16[256,256]{1,0:T(8,128)(2,1)S(1)}, u32[]{:S(2)}, u32[]{:S(2)}) collective-permute-start(bf16[256,256]{1,0:T(8,128)(2,1)S(1)} %bitcast.198), channel_id=1, source_target_pairs={{0,8},{1,12},{2,2},{3,6},{4,9},{5,13},{6,3},{7,7},{8,0},{9,4},{10,... | collective-permute-start | bytes 393224 | tf_op jit(solution)/shard_map/ppermute | solution.py:140
  56.4 7.6 %collective-permute-start.7 = (bf16[256,256]{1,0:T(8,128)(2,1)S(1)}, bf16[256,256]{1,0:T(8,128)(2,1)S(1)}, u32[]{:S(2)}, u32[]{:S(2)}) collective-permute-start(bf16[256,256]{1,0:T(8,128)(2,1)S(1)} %bitcast.199), channel_id=1, source_target_pairs={{0,9},{1,13},{2,3},{3,7},{4,0},{5,4},{6,10},{7,14},{8,1},{9,5},{10... | collective-permute-start | bytes 393224 | tf_op jit(solution)/shard_map/ppermute | solution.py:140
  64.7 16.3 %copy-start.1 = (bf16[1024,1536]{1,0:T(8,128)(2,1)S(1)}, bf16[1024,1536]{1,0:T(8,128)(2,1)}, u32[]{:S(2)}) copy-start(bf16[1024,1536]{1,0:T(8,128)(2,1)} %param.16) | copy-start | bytes 9437188
  64.8 13.2 %collective-permute-start.8 = (bf16[4,256,256]{2,1,0:T(8,128)(2,1)S(1)}, bf16[4,256,256]{2,1,0:T(8,128)(2,1)S(1)}, u32[]{:S(2)}, u32[]{:S(2)}) collective-permute-start(bf16[4,256,256]{2,1,0:T(8,128)(2,1)S(1)} %broadcast_select_fusion.1), channel_id=1, source_target_pairs={{0,2},{1,3},{2,0},{3,1},{4,6},{5,7},{6,4},{7,5},{8,10},{9,11},{10,... | collective-permute-start | bytes 1572872 | tf_op jit(solution)/shard_map/ppermute | solution.py:166
  79.5 7.8 %collective-permute-start.9 = (bf16[2,4,256,256]{3,2,0,1:T(8,128)(2,1)}, bf16[2,4,256,256]{3,2,0,1:T(8,128)(2,1)}, u32[]{:S(2)}, u32[]{:S(2)}) collective-permute-start(bf16[2,4,256,256]{3,2,0,1:T(8,128)(2,1)} %get-tuple-element.27), channel_id=1, source_target_pairs={{0,1},{1,0},{2,3},{3,2},{4,5},{5,4},{6,7},{7,6},{8,9},{9,8},{10,11... | collective-permute-start | bytes 3145736 | tf_op jit(solution)/shard_map/ppermute | solution.py:168
  84.9 2.4 %copy-start = (bf16[2,1,4,256,256]{4,3,1,0,2:T(8,128)(2,1)S(1)}, bf16[2,1,4,256,256]{4,3,1,0,2:T(8,128)(2,1)}, u32[]{:S(2)}) copy-start(bf16[2,1,4,256,256]{4,3,1,0,2:T(8,128)(2,1)} %get-tuple-element.26) | copy-start | bytes 3145732
  89.2 20.9 %collective-permute-start.10 = (bf16[256,1536]{1,0:T(8,128)(2,1)S(1)}, bf16[256,1536]{1,0:T(8,128)(2,1)S(1)}, u32[]{:S(2)}, u32[]{:S(2)}) collective-permute-start(bf16[256,1536]{1,0:T(8,128)(2,1)S(1)} %fusion.9), channel_id=1, source_target_pairs={{0,4},{4,8},{1,5},{5,9},{2,6},{6,10},{3,7},{7,11},{16,20},{20,24},... | collective-permute-start | bytes 2359304 | tf_op jit(solution)/shard_map/ppermute | solution.py:187
  94.2 38.9 %collective-permute-start.13 = (bf16[256,1536]{1,0:T(8,128)(2,1)S(1)}, bf16[256,1536]{1,0:T(8,128)(2,1)S(1)}, u32[]{:S(2)}, u32[]{:S(2)}) collective-permute-start(bf16[256,1536]{1,0:T(8,128)(2,1)S(1)} %fusion.11), channel_id=1, source_target_pairs={{12,8},{8,4},{13,9},{9,5},{14,10},{10,6},{15,11},{11,7},{28,24},{2... | collective-permute-start | bytes 2359304 | tf_op jit(solution)/shard_map/ppermute | solution.py:191
  97.8 39.4 %collective-permute-start.12 = (bf16[256,1536]{1,0:T(8,128)(2,1)}, bf16[256,1536]{1,0:T(8,128)(2,1)}, u32[]{:S(2)}, u32[]{:S(2)}) collective-permute-start(bf16[256,1536]{1,0:T(8,128)(2,1)} %fusion.10), channel_id=1, source_target_pairs={{0,12},{1,13},{2,14},{3,15},{16,28},{17,29},{18,30},{19,31}} | collective-permute-start | bytes 2359304 | tf_op jit(solution)/shard_map/ppermute | solution.py:190
  106.4 30.8 %collective-permute-start.15 = (bf16[256,1536]{1,0:T(8,128)(2,1)}, bf16[256,1536]{1,0:T(8,128)(2,1)}, u32[]{:S(2)}, u32[]{:S(2)}) collective-permute-start(bf16[256,1536]{1,0:T(8,128)(2,1)} %fusion.12), channel_id=1, source_target_pairs={{12,0},{13,1},{14,2},{15,3},{28,16},{29,17},{30,18},{31,19}} | collective-permute-start | bytes 2359304 | tf_op jit(solution)/shard_map/ppermute | solution.py:194
  113.0 30.1 %collective-permute-start.11 = (bf16[256,1536]{1,0:T(8,128)(2,1)}, bf16[256,1536]{1,0:T(8,128)(2,1)}, u32[]{:S(2)}, u32[]{:S(2)}) collective-permute-start(bf16[256,1536]{1,0:T(8,128)(2,1)} %fusion.7), channel_id=1, source_target_pairs={{0,4},{4,8},{8,12},{1,5},{5,9},{9,13},{2,6},{6,10},{10,14},{3,7},{... | collective-permute-start | bytes 2359304 | tf_op jit(solution)/shard_map/ppermute | solution.py:195
  135.9 20.7 %collective-permute-start.14 = (bf16[256,1536]{1,0:T(8,128)(2,1)}, bf16[256,1536]{1,0:T(8,128)(2,1)}, u32[]{:S(2)}, u32[]{:S(2)}) collective-permute-start(bf16[256,1536]{1,0:T(8,128)(2,1)} %fusion.6), channel_id=1, source_target_pairs={{12,8},{8,4},{4,0},{13,9},{9,5},{5,1},{14,10},{10,6},{6,2},{15,11}... | collective-permute-start | bytes 2359304 | tf_op jit(solution)/shard_map/ppermute | solution.py:200

commit v11 on v10

--- a/solution.py
+++ b/solution.py
@@ -174,11 +174,21 @@
         weights.reshape(n_mdl, piece, cols_w), mu_tab.reshape(-1), axis=0
     ).reshape(n_x, 2, piece, cols_w)
 
-    def partial_for(target):
-        rows = lax.dynamic_index_in_dim(gathered_x, target, 2, keepdims=False)
-        return jnp.einsum(
-            "deti,deic->tc", rows, w_perm, preferred_element_type=jnp.float32
-        )
+    if n_seq == 4:
+        all_partials = jnp.einsum(
+            "desti,deic->stc", gathered_x, w_perm, preferred_element_type=jnp.float32
+        )
+
+        def partial_for(target):
+            return lax.dynamic_index_in_dim(all_partials, target, 0, keepdims=False)
+
+    else:
+
+        def partial_for(target):
+            rows = lax.dynamic_index_in_dim(gathered_x, target, 2, keepdims=False)
+            return jnp.einsum(
+                "deti,deic->tc", rows, w_perm, preferred_element_type=jnp.float32
+            )
 
     if n_seq == 4:
         def bf(v):

time: 162 us -> 168 us (1.037)
  matrix products: 23.5 us -> 10.2 us
  waiting for transfers between devices: 53.9 us -> 60.1 us
  local copies, waits for them, and re-layouts: 7.54 us -> 12.7 us
  other arithmetic: 13.6 us -> 18.1 us
  starting transfers between devices: 61.7 us -> 65.7 us
    dot_general x7 -> x1, matrix products: 19.3 us -> 6.02 us  [per_device(): jnp.einsum('desti,deic->stc', gathered_x, w_perm, preferred_element_type=...]
    ppermute x1, waiting for transfers between devices: 13.6 us -> 3.95 us  [per_device(): lax.ppermute(bf(partial_for(jnp.clip(s_me - 1, 0, 3)) + near_l.astype(jnp...]
    ppermute x1, waiting for transfers between devices: 5.83 us -> 15.3 us  [per_device(): lax.ppermute(bf(partial_for(jnp.clip(s_me + 1, 0, 3)) + near_r.astype(jnp...]
    convert_element_type x0 -> x2, other arithmetic: none -> 6.77 us  [the longest x1 3.74 us: bf(): return v.astype(jnp.bfloat16)]
    ppermute x1, waiting for transfers between devices: 2.45 us -> 9.02 us  [per_device(): lax.ppermute(bf(partial_for(jnp.clip(s_me + 2, 0, 3))), 'seq', [(0, 1), (...]
    ppermute x1, starting transfers between devices: 20.1 us -> 24 us  [per_device(): lax.ppermute(bf(partial_for(jnp.clip(s_me + 1, 0, 3)) + near_r.astype(jnp...]
    convert_element_type x0 -> x2, local copies, waits for them, and re-layouts: none -> 2.64 us  [bf(): return v.astype(jnp.bfloat16)]
    unnamed x16, local copies, waits for them, and re-layouts: 2.99 us -> 5.63 us
  transfers between devices with their start and end apart: 16 -> 16, of which waited for: 9 -> 9; matrix products, arithmetic and copies ran while one was open for 15% -> 8% of each run, Pallas kernels for 0% -> 0%
where the time goes in v11:
time: 168 us; the launch traced here: 167 us
  starting transfers between devices  65.7 us (39%)
  waiting for transfers between devices  60.1 us (36%)
  other arithmetic  18.1 us (11%)
  local copies, waits for them, and re-layouts  12.7 us (8%)
  matrix products  10.2 us (6%)
    ppermute x1, starting transfers between devices, per_device(): lax.ppermute(bf(partial_for(jnp.clip(s_me + 1, 0, 3)) + near_r.astype(jnp...  24 us
    ppermute x1, waiting for transfers between devices, per_device(): lax.ppermute(bf(partial_for(jnp.clip(s_me + 1, 0, 3)) + near_r.astype(jnp...  15.3 us
    ppermute x4, starting transfers between devices, per_device(): received.append(lax.ppermute(item, ('seq', 'mdl'), perm))  15 us
    ppermute x1, waiting for transfers between devices, per_device(): got.append(lax.ppermute(x, 'mdl', perm))  12.9 us
    ppermute x3, starting transfers between devices, per_device(): came = lax.ppermute(packed, 'seq', [(z, z + d) for z in range(n_seq - d)])  11.5 us
    ppermute x1, waiting for transfers between devices, per_device(): lax.ppermute(bf(partial_for(jnp.clip(s_me + 2, 0, 3))), 'seq', [(0, 1), (...  9.02 us
    ppermute x4, waiting for transfers between devices, per_device(): received.append(lax.ppermute(item, ('seq', 'mdl'), perm))  7.49 us
    dot_general x1, matrix products, per_device(): jnp.einsum('desti,deic->stc', gathered_x, w_perm, preferred_element_type=...  6.02 us
  transfers between devices with their start and end apart: 16, of which 9 were waited for; matrix products, arithmetic and copies ran while one was open for 8% of the time, Pallas kernels for 0%

profile of v11, /device:TPU:0, one launch (start us, length us, event | category | flops | bytes accessed | tf_op | source)
XLA Modules:
  0.0 167.5 jit_solution(2654323862242080029)
XLA Ops:
  4.1 1.3 copy.74
  7.0 5.7 %collective-permute-start = (bf16[8,16640]{1,0:T(8,128)(2,1)S(1)}, bf16[8,16640]{1,0:T(8,128)(2,1)}, u32[]{:S(2)}, u32[]{:S(2)}) collective-permute-start(bf16[8,16640]{1,0:T(8,128)(2,1)S(1)} %pad_maximum_fusion.2), channel_id=1, source_target_pairs={{0,4},{4,8},{8,12},{1,5},{5,9},{9,13},{2,6},{6,10},{10,14},{3,7},{... | collective-permute-start | bytes 798728 | tf_op jit(solution)/shard_map/ppermute | solution.py:95
  12.7 3.8 %collective-permute-start.1 = (bf16[8,16640]{1,0:T(8,128)(2,1)S(1)}, bf16[8,16640]{1,0:T(8,128)(2,1)S(1)}, u32[]{:S(2)}, u32[]{:S(2)}) collective-permute-start(bf16[8,16640]{1,0:T(8,128)(2,1)S(1)} %pad_maximum_fusion.2), channel_id=1, source_target_pairs={{0,8},{4,12},{1,9},{5,13},{2,10},{6,14},{3,11},{7,15},{16,24},{20,... | collective-permute-start | bytes 798728 | tf_op jit(solution)/shard_map/ppermute | solution.py:95
  16.5 2.0 %collective-permute-start.2 = (bf16[8,16640]{1,0:T(8,128)(2,1)S(1)}, bf16[8,16640]{1,0:T(8,128)(2,1)}, u32[]{:S(2)}, u32[]{:S(2)}) collective-permute-start(bf16[8,16640]{1,0:T(8,128)(2,1)S(1)} %pad_maximum_fusion.2), channel_id=1, source_target_pairs={{0,12},{1,13},{2,14},{3,15},{16,28},{17,29},{18,30},{19,31}} | collective-permute-start | bytes 798728 | tf_op jit(solution)/shard_map/ppermute | solution.py:95
  19.4 1.9 %fusion.14 = f32[1,256,8,128]{1,3,2,0:T(8,128)} fusion(bf16[256,8,128]{0,2,1:T(8,128)(2,1)S(1)} %bitcast.136, bf16[256,8,128]{0,2,1:T(8,128)(2,1)S(1)} %bitcast.133, bf16[256,8,128]{0,2,1:T(8,128)(2,1)S(1)} %bitcast.138, f32[8,256]{1,0:T(8,128)S(1)} %bitcast_add_fusion.5, pred[256,256]{1,0:T(8,128)(4,1)S(1)} %iota_compare_fusion), kind=kOutput, calls=%fused_computation.24 | convolution fusion | flops 271056896 | bytes 2695168 | tf_op jit(solution)/shard_map/hbij,bjhd->bihd/dot_general | solution.py:63
  22.9 1.6 collective-permute-done.1
  24.8 4.3 %collective-permute-done.2 = bf16[8,16640]{1,0:T(8,128)(2,1)} collective-permute-done((bf16[8,16640]{1,0:T(8,128)(2,1)S(1)}, bf16[8,16640]{1,0:T(8,128)(2,1)}, u32[]{:S(2)}, u32[]{:S(2)}) %collective-permute-start.2) | collective-permute-done | bytes 266272 | tf_op jit(solution)/shard_map/ppermute | solution.py:95
  31.1 2.0 %multiply_reduce_fusion = (f32[256,8]{0,1:T(8,128)S(1)}, f32[1,256,8,128]{1,3,2,0:T(8,128)S(1)}) fusion(f32[1,256,8,128]{1,3,2,0:T(8,128)} %fusion.14, bf16[256,8,128]{0,2,1:T(8,128)(2,1)S(1)} %bitcast.134, f32[8,128,128]{1,2,0:T(8,128)S(1)} %copy.81, f32[8,128,128]{1,2,0:T(8,128)S(1)} %copy.80, f32[8,128,128]{1,2,0:T(8,128)S(1)} %copy.79, ...), kind=kOutput, calls=%fused_computation.45 | convolution fusion | flops 404355072 | bytes 4210784 | tf_op jit(solution)/shard_map/bihd,bhde->bihe/dot_general | solution.py:105
  33.6 1.6 collective-permute-start.3
  35.3 5.5 %collective-permute-done.3 = bf16[256,2,256]{0,2,1:T(8,128)(2,1)S(1)} collective-permute-done((bf16[256,2,256]{0,2,1:T(8,128)(2,1)S(1)}, bf16[256,2,256]{0,2,1:T(8,128)(2,1)S(1)}, u32[]{:S(2)}, u32[]{:S(2)}) %collective-permute-start.3) | collective-permute-done | bytes 262176 | tf_op jit(solution)/shard_map/ppermute | solution.py:129
  41.9 8.9 %collective-permute-start.5 = (bf16[256,256]{1,0:T(8,128)(2,1)S(1)}, bf16[256,256]{1,0:T(8,128)(2,1)S(1)}, u32[]{:S(2)}, u32[]{:S(2)}) collective-permute-start(bf16[256,256]{1,0:T(8,128)(2,1)S(1)} %bitcast.142), channel_id=1, source_target_pairs={{0,1},{1,5},{2,11},{3,15},{4,8},{5,12},{6,2},{7,6},{8,9},{9,13},{1... | collective-permute-start | bytes 393224 | tf_op jit(solution)/shard_map/ppermute | solution.py:140
  51.0 5.3 %collective-permute-start.6 = (bf16[256,256]{1,0:T(8,128)(2,1)S(1)}, bf16[256,256]{1,0:T(8,128)(2,1)S(1)}, u32[]{:S(2)}, u32[]{:S(2)}) collective-permute-start(bf16[256,256]{1,0:T(8,128)(2,1)S(1)} %bitcast.143), channel_id=1, source_target_pairs={{0,8},{1,12},{2,2},{3,6},{4,9},{5,13},{6,3},{7,7},{8,0},{9,4},{10,... | collective-permute-start | bytes 393224 | tf_op jit(solution)/shard_map/ppermute | solution.py:140
  56.5 1.9 %collective-permute-done.5 = bf16[256,256]{1,0:T(8,128)(2,1)S(1)} collective-permute-done((bf16[256,256]{1,0:T(8,128)(2,1)S(1)}, bf16[256,256]{1,0:T(8,128)(2,1)S(1)}, u32[]{:S(2)}, u32[]{:S(2)}) %collective-permute-start.5) | collective-permute-done | bytes 131104 | tf_op jit(solution)/shard_map/ppermute | solution.py:140
  58.4 5.6 %collective-permute-done.6 = bf16[256,256]{1,0:T(8,128)(2,1)S(1)} collective-permute-done((bf16[256,256]{1,0:T(8,128)(2,1)S(1)}, bf16[256,256]{1,0:T(8,128)(2,1)S(1)}, u32[]{:S(2)}, u32[]{:S(2)}) %collective-permute-start.6) | collective-permute-done | bytes 131104 | tf_op jit(solution)/shard_map/ppermute | solution.py:140
  65.1 12.9 %collective-permute-done.8 = bf16[4,256,256]{2,1,0:T(8,128)(2,1)S(1)} collective-permute-done((bf16[4,256,256]{2,1,0:T(8,128)(2,1)S(1)}, bf16[4,256,256]{2,1,0:T(8,128)(2,1)S(1)}, u32[]{:S(2)}, u32[]{:S(2)}) %collective-permute-start.8) | collective-permute-done | bytes 524320 | tf_op jit(solution)/shard_map/ppermute | solution.py:166
  78.0 1.5 fusion.103
  79.5 1.5 collective-permute-start.9
  81.0 1.4 multiply_convert_fusion
  82.4 2.4 %gather_fusion.1 = bf16[4,256,1536]{2,1,0:T(8,128)(2,1)} fusion(bf16[4,256,1536]{2,1,0:T(8,128)(2,1)S(1)} %bitcast.131, s32[1024]{0:T(1024)S(1)} %pad_clamp_fusion), kind=kCustom, calls=%fused_computation.1 | custom fusion | bytes 6291472 | tf_op jit(solution)/shard_map/jit(_take)/gather | solution.py:173
  84.9 6.0 %fusion.104 = (bf16[4,256,1536]{2,1,0:T(8,128)(2,1)S(1)}, f32[4,256,1536]{2,1,0:T(8,128)S(1)}) fusion(bf16[2,2,256,1536]{3,2,1,0:T(8,128)(2,1)} %bitcast.132, pred[2,2]{1,0:T(4,128)(4,1)S(1)} %compare_and_fusion, bf16[2,1,4,256,256]{4,3,1,2,0:T(8,128)(2,1)} %bitcast.39, bf16[2,1,4,256,256]{4,3,1,2,0:T(8,128)(2,1)} %get-tuple-element.32), kind=kOutput, calls=%fused_computation.231 | convolution fusion | flops 3225419776 | bytes 14680068 | tf_op jit(solution)/shard_map/desti,deic->stc/dot_general | solution.py:178
  90.9 2.6 %copy-done = f32[4,256,1536]{2,1,0:T(8,128)} copy-done((f32[4,256,1536]{2,1,0:T(8,128)}, f32[4,256,1536]{2,1,0:T(8,128)S(1)}, u32[]{:S(2)}) %copy-start) | copy-done | bytes 6291480
  93.6 1.4 fusion.31
  94.9 3.9 %collective-permute-start.10 = (bf16[256,1536]{1,0:T(8,128)(2,1)}, bf16[256,1536]{1,0:T(8,128)(2,1)}, u32[]{:S(2)}, u32[]{:S(2)}) collective-permute-start(bf16[256,1536]{1,0:T(8,128)(2,1)} %get-tuple-element.28), channel_id=1, source_target_pairs={{0,4},{4,8},{1,5},{5,9},{2,6},{6,10},{3,7},{7,11},{16,20},{20,24},... | collective-permute-start | bytes 2359304 | tf_op jit(solution)/shard_map/ppermute | solution.py:197
  98.8 1.6 collective-permute-start.13
  101.7 4.1 %collective-permute-start.12 = (bf16[256,1536]{1,0:T(8,128)(2,1)}, bf16[256,1536]{1,0:T(8,128)(2,1)S(1)}, u32[]{:S(2)}, u32[]{:S(2)}) collective-permute-start(bf16[256,1536]{1,0:T(8,128)(2,1)} %get-tuple-element.30), channel_id=1, source_target_pairs={{0,12},{1,13},{2,14},{3,15},{16,28},{17,29},{18,30},{19,31}} | collective-permute-start | bytes 2359304 | tf_op jit(solution)/shard_map/ppermute | solution.py:200
  105.9 1.3 collective-permute-start.15
  107.2 9.0 %collective-permute-done.10 = bf16[256,1536]{1,0:T(8,128)(2,1)} collective-permute-done((bf16[256,1536]{1,0:T(8,128)(2,1)}, bf16[256,1536]{1,0:T(8,128)(2,1)}, u32[]{:S(2)}, u32[]{:S(2)}) %collective-permute-start.10) | collective-permute-done | bytes 786464 | tf_op jit(solution)/shard_map/ppermute | solution.py:197
  116.2 3.7 %fusion.7 = (bf16[256,1536]{1,0:T(8,128)(2,1)}, bf16[256,1536]{1,0:T(8,128)(2,1)S(1)}) fusion(bf16[256,1536]{1,0:T(8,128)(2,1)} %collective-permute-done.10, f32[4,256,1536]{2,1,0:T(8,128)} %copy-done, s32[]{:T(128)S(6)} %min.73, bf16[256,1536]{1,0:T(8,128)(2,1)} %collective-permute-done.13, s32[]{:T(128)S(6)} %min.75), kind=kLoop, calls=%fused_computation.14 | loop fusion | flops 2359296 | bytes 6291464 | tf_op jit(solution)/shard_map/convert_element_type | solution.py:195
  119.9 24.0 %collective-permute-start.11 = (bf16[256,1536]{1,0:T(8,128)(2,1)}, bf16[256,1536]{1,0:T(8,128)(2,1)S(1)}, u32[]{:S(2)}, u32[]{:S(2)}) collective-permute-start(bf16[256,1536]{1,0:T(8,128)(2,1)} %get-tuple-element.26), channel_id=1, source_target_pairs={{0,4},{4,8},{8,12},{1,5},{5,9},{9,13},{2,6},{6,10},{10,14},{3,7},{... | collective-permute-start | bytes 2359304 | tf_op jit(solution)/shard_map/ppermute | solution.py:205
  145.2 15.3 %collective-permute-done.11 = bf16[256,1536]{1,0:T(8,128)(2,1)S(1)} collective-permute-done((bf16[256,1536]{1,0:T(8,128)(2,1)}, bf16[256,1536]{1,0:T(8,128)(2,1)S(1)}, u32[]{:S(2)}, u32[]{:S(2)}) %collective-permute-start.11) | collective-permute-done | bytes 786464 | tf_op jit(solution)/shard_map/ppermute | solution.py:205
  160.5 4.0 %collective-permute-done.14 = bf16[256,1536]{1,0:T(8,128)(2,1)} collective-permute-done((bf16[256,1536]{1,0:T(8,128)(2,1)S(1)}, bf16[256,1536]{1,0:T(8,128)(2,1)}, u32[]{:S(2)}, u32[]{:S(2)}) %collective-permute-start.14) | collective-permute-done | bytes 786464 | tf_op jit(solution)/shard_map/ppermute | solution.py:210
  164.5 3.0 %fusion.11 = bf16[256,1536]{1,0:T(8,128)(2,1)} fusion(bf16[256,1536]{1,0:T(8,128)(2,1)S(1)} %collective-permute-done.15, bf16[256,1536]{1,0:T(8,128)(2,1)} %collective-permute-done.14, bf16[256,1536]{1,0:T(8,128)(2,1)S(1)} %collective-permute-done.12, bf16[256,1536]{1,0:T(8,128)(2,1)S(1)} %collective-permute-done.11, f32[4,256,1536]{2,1,0:T(8,128)} %copy-done, ...), kind=kLoop, calls=%fused_computation.19 | loop fusion | flops 3538944 | bytes 5505028 | tf_op jit(solution)/shard_map/convert_element_type | solution.py:218
  (75 shorter events, 15.8 us)
Async XLA Ops:
  4.1 14.6 %copy-start.2 = (bf16[256,1024]{1,0:T(8,128)(2,1)S(1)}, bf16[256,1024]{1,0:T(8,128)(2,1)}, u32[]{:S(2)}) copy-start(bf16[256,1024]{1,0:T(8,128)(2,1)} %param.9) | copy-start | bytes 1572868
  7.0 14.6 %collective-permute-start = (bf16[8,16640]{1,0:T(8,128)(2,1)S(1)}, bf16[8,16640]{1,0:T(8,128)(2,1)}, u32[]{:S(2)}, u32[]{:S(2)}) collective-permute-start(bf16[8,16640]{1,0:T(8,128)(2,1)S(1)} %pad_maximum_fusion.2), channel_id=1, source_target_pairs={{0,4},{4,8},{8,12},{1,5},{5,9},{9,13},{2,6},{6,10},{10,14},{3,7},{... | collective-permute-start | bytes 798728 | tf_op jit(solution)/shard_map/ppermute | solution.py:95
  12.7 11.8 %collective-permute-start.1 = (bf16[8,16640]{1,0:T(8,128)(2,1)S(1)}, bf16[8,16640]{1,0:T(8,128)(2,1)S(1)}, u32[]{:S(2)}, u32[]{:S(2)}) collective-permute-start(bf16[8,16640]{1,0:T(8,128)(2,1)S(1)} %pad_maximum_fusion.2), channel_id=1, source_target_pairs={{0,8},{4,12},{1,9},{5,13},{2,10},{6,14},{3,11},{7,15},{16,24},{20,... | collective-permute-start | bytes 798728 | tf_op jit(solution)/shard_map/ppermute | solution.py:95
  16.5 12.6 %collective-permute-start.2 = (bf16[8,16640]{1,0:T(8,128)(2,1)S(1)}, bf16[8,16640]{1,0:T(8,128)(2,1)}, u32[]{:S(2)}, u32[]{:S(2)}) collective-permute-start(bf16[8,16640]{1,0:T(8,128)(2,1)S(1)} %pad_maximum_fusion.2), channel_id=1, source_target_pairs={{0,12},{1,13},{2,14},{3,15},{16,28},{17,29},{18,30},{19,31}} | collective-permute-start | bytes 798728 | tf_op jit(solution)/shard_map/ppermute | solution.py:95
  18.8 2.6 %copy-start.3 = (bf16[256,1024]{1,0:T(8,128)(2,1)S(1)}, bf16[256,1024]{1,0:T(8,128)(2,1)}, u32[]{:S(2)}) copy-start(bf16[256,1024]{1,0:T(8,128)(2,1)} %param.12) | copy-start | bytes 1572868
  31.1 2.1 %copy-start.5 = (f32[1024]{0:T(1024)S(1)}, f32[1024]{0:T(1024)}, u32[]{:S(2)}) copy-start(f32[1024]{0:T(1024)} %param.15) | copy-start | bytes 12292
  33.6 31.3 %copy-start.4 = (s32[1536]{0:T(1024)S(1)}, s32[1536]{0:T(1024)}, u32[]{:S(2)}) copy-start(s32[1536]{0:T(1024)} %param.17) | copy-start | bytes 18436
  33.6 7.2 %collective-permute-start.3 = (bf16[256,2,256]{0,2,1:T(8,128)(2,1)S(1)}, bf16[256,2,256]{0,2,1:T(8,128)(2,1)S(1)}, u32[]{:S(2)}, u32[]{:S(2)}) collective-permute-start(bf16[256,2,256]{0,2,1:T(8,128)(2,1)S(1)} %get-tuple-element.38), channel_id=1, source_target_pairs={{0,2},{1,3},{2,0},{3,1},{4,6},{5,7},{6,4},{7,5},{8,10},{9,11},{10,... | collective-permute-start | bytes 786440 | tf_op jit(solution)/shard_map/ppermute | solution.py:129
  41.2 15.3 %collective-permute-start.4 = (bf16[256,256]{1,0:T(8,128)(2,1)S(1)}, bf16[256,256]{1,0:T(8,128)(2,1)S(1)}, u32[]{:S(2)}, u32[]{:S(2)}) collective-permute-start(bf16[256,256]{1,0:T(8,128)(2,1)S(1)} %bitcast.141), channel_id=1, source_target_pairs={{0,0},{1,4},{2,10},{3,14},{4,1},{5,5},{6,11},{7,15},{8,8},{9,12},{... | collective-permute-start | bytes 393224 | tf_op jit(solution)/shard_map/ppermute | solution.py:140
  41.9 16.5 %collective-permute-start.5 = (bf16[256,256]{1,0:T(8,128)(2,1)S(1)}, bf16[256,256]{1,0:T(8,128)(2,1)S(1)}, u32[]{:S(2)}, u32[]{:S(2)}) collective-permute-start(bf16[256,256]{1,0:T(8,128)(2,1)S(1)} %bitcast.142), channel_id=1, source_target_pairs={{0,1},{1,5},{2,11},{3,15},{4,8},{5,12},{6,2},{7,6},{8,9},{9,13},{1... | collective-permute-start | bytes 393224 | tf_op jit(solution)/shard_map/ppermute | solution.py:140
  51.0 13.0 %collective-permute-start.6 = (bf16[256,256]{1,0:T(8,128)(2,1)S(1)}, bf16[256,256]{1,0:T(8,128)(2,1)S(1)}, u32[]{:S(2)}, u32[]{:S(2)}) collective-permute-start(bf16[256,256]{1,0:T(8,128)(2,1)S(1)} %bitcast.143), channel_id=1, source_target_pairs={{0,8},{1,12},{2,2},{3,6},{4,9},{5,13},{6,3},{7,7},{8,0},{9,4},{10,... | collective-permute-start | bytes 393224 | tf_op jit(solution)/shard_map/ppermute | solution.py:140
  56.4 7.6 %collective-permute-start.7 = (bf16[256,256]{1,0:T(8,128)(2,1)S(1)}, bf16[256,256]{1,0:T(8,128)(2,1)S(1)}, u32[]{:S(2)}, u32[]{:S(2)}) collective-permute-start(bf16[256,256]{1,0:T(8,128)(2,1)S(1)} %bitcast.144), channel_id=1, source_target_pairs={{0,9},{1,13},{2,3},{3,7},{4,0},{5,4},{6,10},{7,14},{8,1},{9,5},{10... | collective-permute-start | bytes 393224 | tf_op jit(solution)/shard_map/ppermute | solution.py:140
  64.8 13.2 %collective-permute-start.8 = (bf16[4,256,256]{2,1,0:T(8,128)(2,1)S(1)}, bf16[4,256,256]{2,1,0:T(8,128)(2,1)S(1)}, u32[]{:S(2)}, u32[]{:S(2)}) collective-permute-start(bf16[4,256,256]{2,1,0:T(8,128)(2,1)S(1)} %broadcast_select_fusion), channel_id=1, source_target_pairs={{0,2},{1,3},{2,0},{3,1},{4,6},{5,7},{6,4},{7,5},{8,10},{9,11},{10,... | collective-permute-start | bytes 1572872 | tf_op jit(solution)/shard_map/ppermute | solution.py:166
  64.9 16.1 %copy-start.1 = (bf16[1024,1536]{1,0:T(8,128)(2,1)S(1)}, bf16[1024,1536]{1,0:T(8,128)(2,1)}, u32[]{:S(2)}) copy-start(bf16[1024,1536]{1,0:T(8,128)(2,1)} %param.16) | copy-start | bytes 9437188
  79.5 5.4 %collective-permute-start.9 = (bf16[2,4,256,256]{3,2,1,0:T(8,128)(2,1)}, bf16[2,4,256,256]{3,2,1,0:T(8,128)(2,1)}, u32[]{:S(2)}, u32[]{:S(2)}) collective-permute-start(bf16[2,4,256,256]{3,2,1,0:T(8,128)(2,1)} %get-tuple-element.33), channel_id=1, source_target_pairs={{0,1},{1,0},{2,3},{3,2},{4,5},{5,4},{6,7},{7,6},{8,9},{9,8},{10,11... | collective-permute-start | bytes 3145736 | tf_op jit(solution)/shard_map/ppermute | solution.py:168
  90.9 2.7 %copy-start = (f32[4,256,1536]{2,1,0:T(8,128)}, f32[4,256,1536]{2,1,0:T(8,128)S(1)}, u32[]{:S(2)}) copy-start(f32[4,256,1536]{2,1,0:T(8,128)S(1)} %get-tuple-element.49) | copy-start | bytes 18874372
  94.9 21.2 %collective-permute-start.10 = (bf16[256,1536]{1,0:T(8,128)(2,1)}, bf16[256,1536]{1,0:T(8,128)(2,1)}, u32[]{:S(2)}, u32[]{:S(2)}) collective-permute-start(bf16[256,1536]{1,0:T(8,128)(2,1)} %get-tuple-element.28), channel_id=1, source_target_pairs={{0,4},{4,8},{1,5},{5,9},{2,6},{6,10},{3,7},{7,11},{16,20},{20,24},... | collective-permute-start | bytes 2359304 | tf_op jit(solution)/shard_map/ppermute | solution.py:197
  98.8 17.3 %collective-permute-start.13 = (bf16[256,1536]{1,0:T(8,128)(2,1)}, bf16[256,1536]{1,0:T(8,128)(2,1)}, u32[]{:S(2)}, u32[]{:S(2)}) collective-permute-start(bf16[256,1536]{1,0:T(8,128)(2,1)} %get-tuple-element.29), channel_id=1, source_target_pairs={{12,8},{8,4},{13,9},{9,5},{14,10},{10,6},{15,11},{11,7},{28,24},{2... | collective-permute-start | bytes 2359304 | tf_op jit(solution)/shard_map/ppermute | solution.py:201
  101.7 43.5 %collective-permute-start.12 = (bf16[256,1536]{1,0:T(8,128)(2,1)}, bf16[256,1536]{1,0:T(8,128)(2,1)S(1)}, u32[]{:S(2)}, u32[]{:S(2)}) collective-permute-start(bf16[256,1536]{1,0:T(8,128)(2,1)} %get-tuple-element.30), channel_id=1, source_target_pairs={{0,12},{1,13},{2,14},{3,15},{16,28},{17,29},{18,30},{19,31}} | collective-permute-start | bytes 2359304 | tf_op jit(solution)/shard_map/ppermute | solution.py:200
  105.9 39.4 %collective-permute-start.15 = (bf16[256,1536]{1,0:T(8,128)(2,1)}, bf16[256,1536]{1,0:T(8,128)(2,1)S(1)}, u32[]{:S(2)}, u32[]{:S(2)}) collective-permute-start(bf16[256,1536]{1,0:T(8,128)(2,1)} %get-tuple-element.31), channel_id=1, source_target_pairs={{12,0},{13,1},{14,2},{15,3},{28,16},{29,17},{30,18},{31,19}} | collective-permute-start | bytes 2359304 | tf_op jit(solution)/shard_map/ppermute | solution.py:204
  119.9 40.6 %collective-permute-start.11 = (bf16[256,1536]{1,0:T(8,128)(2,1)}, bf16[256,1536]{1,0:T(8,128)(2,1)S(1)}, u32[]{:S(2)}, u32[]{:S(2)}) collective-permute-start(bf16[256,1536]{1,0:T(8,128)(2,1)} %get-tuple-element.26), channel_id=1, source_target_pairs={{0,4},{4,8},{8,12},{1,5},{5,9},{9,13},{2,6},{6,10},{10,14},{3,7},{... | collective-permute-start | bytes 2359304 | tf_op jit(solution)/shard_map/ppermute | solution.py:205
  143.9 20.6 %collective-permute-start.14 = (bf16[256,1536]{1,0:T(8,128)(2,1)S(1)}, bf16[256,1536]{1,0:T(8,128)(2,1)}, u32[]{:S(2)}, u32[]{:S(2)}) collective-permute-start(bf16[256,1536]{1,0:T(8,128)(2,1)S(1)} %get-tuple-element.27), channel_id=1, source_target_pairs={{12,8},{8,4},{4,0},{13,9},{9,5},{5,1},{14,10},{10,6},{6,2},{15,11}... | collective-permute-start | bytes 2359304 | tf_op jit(solution)/shard_map/ppermute | solution.py:210

commit v12 on v11

--- a/solution.py
+++ b/solution.py
@@ -122,12 +122,14 @@
     s_me = lax.axis_index("seq")
     m_me = lax.axis_index("mdl")
     if n_seq == 4 and n_mdl == 4:
-        x_me = m_me // 2
-        own_pieces = attn.reshape(tok_rows, n_mdl, piece)
-        keep = lax.dynamic_slice_in_dim(own_pieces, 2 * x_me, 2, axis=1)
-        away = lax.dynamic_slice_in_dim(own_pieces, 2 * (1 - x_me), 2, axis=1)
-        came = lax.ppermute(away, "mdl", [(mu, mu ^ 2) for mu in range(n_mdl)])
-        items = jnp.transpose(jnp.concatenate([keep, came], axis=1), (1, 0, 2))
+        b_me = m_me % 2
+        partner_attn = lax.ppermute(attn, "mdl", [(mu, mu ^ 2) for mu in range(n_mdl)])
+        pair = 2 * piece
+        items = []
+        for blk in (attn, partner_attn):
+            halves_of = blk.reshape(tok_rows, 2, pair)
+            items.append(jnp.transpose(halves_of, (1, 0, 2)))
+        items = jnp.concatenate(items, axis=0)
         received = []
         for k in range(n_seq):
             perm = []
@@ -139,8 +141,19 @@
             item = lax.dynamic_index_in_dim(items, (s_me + k) % n_seq, 0, keepdims=False)
             received.append(lax.ppermute(item, ("seq", "mdl"), perm))
         received = jnp.stack(received)
-        r_me = 2 * ((s_me // 2) != (m_me // 2)).astype(jnp.int32) + m_me % 2
-        x = jnp.take(received, (r_me - jnp.arange(n_seq)) % n_seq, axis=0)
+        r_me = 2 * ((s_me // 2) != (m_me // 2)).astype(jnp.int32) + b_me
+        mine = jnp.take(received, (r_me - jnp.arange(n_seq)) % n_seq, axis=0)
+        theirs = lax.ppermute(mine, "mdl", [(mu, mu ^ 1) for mu in range(n_mdl)])
+        w_mine = lax.dynamic_slice_in_dim(weights, b_me * pair, pair, axis=0)
+        w_theirs = lax.dynamic_slice_in_dim(weights, (1 - b_me) * pair, pair, axis=0)
+
+        def partial_for(target):
+            rows_mine = lax.dynamic_index_in_dim(mine, target, 0, keepdims=False)
+            rows_theirs = lax.dynamic_index_in_dim(theirs, target, 0, keepdims=False)
+            return jnp.dot(rows_mine, w_mine, preferred_element_type=jnp.float32) + jnp.dot(
+                rows_theirs, w_theirs, preferred_element_type=jnp.float32
+            )
+
     else:
         received = []
         for k in range(n_seq):
@@ -157,32 +170,22 @@
         j_me = (s_me % blocks_here) * n_mdl + m_me
         x = jnp.take(received, (j_me - jnp.arange(n_seq)) % n_seq, axis=0)
 
-    n_x = n_mdl // 2
-    core = m_me % 2
-    xi = m_me // 2
-    got = [x]
-    for d in range(1, n_x):
-        perm = [(mu, ((mu // 2 + d) % n_x) * 2 + mu % 2) for mu in range(n_mdl)]
-        got.append(lax.ppermute(x, "mdl", perm))
-    own = jnp.stack(got)
-    other = lax.ppermute(own, "mdl", [(mu, mu ^ 1) for mu in range(n_mdl)])
-    gathered_x = jnp.stack([own, other], axis=1)
-    d_idx = jnp.arange(n_x)[:, None]
-    e_idx = jnp.arange(2)[None, :]
-    mu_tab = 2 * ((xi - d_idx) % n_x) + jnp.where(e_idx == 0, core, 1 - core)
-    w_perm = jnp.take(
-        weights.reshape(n_mdl, piece, cols_w), mu_tab.reshape(-1), axis=0
-    ).reshape(n_x, 2, piece, cols_w)
-
-    if n_seq == 4:
-        all_partials = jnp.einsum(
-            "desti,deic->stc", gathered_x, w_perm, preferred_element_type=jnp.float32
-        )
-
-        def partial_for(target):
-            return lax.dynamic_index_in_dim(all_partials, target, 0, keepdims=False)
-
-    else:
+        n_x = n_mdl // 2
+        core = m_me % 2
+        xi = m_me // 2
+        got = [x]
+        for d in range(1, n_x):
+            perm = [(mu, ((mu // 2 + d) % n_x) * 2 + mu % 2) for mu in range(n_mdl)]
+            got.append(lax.ppermute(x, "mdl", perm))
+        own = jnp.stack(got)
+        other = lax.ppermute(own, "mdl", [(mu, mu ^ 1) for mu in range(n_mdl)])
+        gathered_x = jnp.stack([own, other], axis=1)
+        d_idx = jnp.arange(n_x)[:, None]
+        e_idx = jnp.arange(2)[None, :]
+        mu_tab = 2 * ((xi - d_idx) % n_x) + jnp.where(e_idx == 0, core, 1 - core)
+        w_perm = jnp.take(
+            weights.reshape(n_mdl, piece, cols_w), mu_tab.reshape(-1), axis=0
+        ).reshape(n_x, 2, piece, cols_w)
 
         def partial_for(target):
             rows = lax.dynamic_index_in_dim(gathered_x, target, 2, keepdims=False)

time: 168 us -> 164 us (0.976)
  starting transfers between devices: 65.7 us -> 48.5 us
  matrix products: 10.2 us -> 19.9 us
  waiting for transfers between devices: 60.1 us -> 63.4 us
  other arithmetic: 18.1 us -> 15.9 us
  local copies, waits for them, and re-layouts: 12.7 us -> 14.7 us
    ppermute x1, starting transfers between devices: 24 us -> 5.27 us  [per_device(): lax.ppermute(bf(partial_for(jnp.clip(s_me + 1, 0, 3)) + near_r.astype(jnp...]
    dot_general x1 -> x14, matrix products: 6.02 us -> 15.7 us  [the longest x7 10.8 us: partial_for(): jnp.dot(rows_theirs, w_theirs, preferred_element_type=jnp.float32)]
    ppermute x3 -> x2, waiting for transfers between devices: 18.5 us -> 10.1 us  [the longest x1 10.1 us: per_device(): lax.ppermute(attn, 'mdl', [(mu, mu ^ 2) for mu in range(n_mdl)])]
    ppermute x4, waiting for transfers between devices: 7.49 us -> 14.5 us  [per_device(): received.append(lax.ppermute(item, ('seq', 'mdl'), perm))]
    convert_element_type x2 -> x0, other arithmetic: 6.77 us -> none  [the longest x1 3.74 us: bf(): return v.astype(jnp.bfloat16)]
    dynamic_slice x1 -> x4, local copies, waits for them, and re-layouts: 0.04 us -> 6.22 us  [per_device(): lax.dynamic_index_in_dim(items, (s_me + k) % n_seq, 0, keepdims=False)]
    ppermute x1, waiting for transfers between devices: 0.01 us -> 5.93 us  [per_device(): far_r = lax.ppermute(bf(partial_for(jnp.int32(3))), 'seq', [(0, 3)])]
    ppermute x3 -> x2, starting transfers between devices: 3.11 us -> 6.82 us  [the longest x1 5.33 us: per_device(): theirs = lax.ppermute(mine, 'mdl', [(mu, mu ^ 1) for mu in range(n_mdl)])]
  transfers between devices with their start and end apart: 16 -> 15, of which waited for: 9 -> 10; matrix products, arithmetic and copies ran while one was open for 8% -> 14% of each run, Pallas kernels for 0% -> 0%
where the time goes in v12:
time: 164 us; the launch traced here: 163 us
  waiting for transfers between devices  63.4 us (39%)
  starting transfers between devices  48.5 us (30%)
  matrix products  19.9 us (12%)
  other arithmetic  15.9 us (10%)
  local copies, waits for them, and re-layouts  14.7 us (9%)
    ppermute x4, starting transfers between devices, per_device(): received.append(lax.ppermute(item, ('seq', 'mdl'), perm))  14.8 us
    ppermute x4, waiting for transfers between devices, per_device(): received.append(lax.ppermute(item, ('seq', 'mdl'), perm))  14.5 us
    ppermute x1, waiting for transfers between devices, per_device(): lax.ppermute(bf(partial_for(jnp.clip(s_me + 1, 0, 3)) + near_r.astype(jnp...  12.5 us
    ppermute x3, starting transfers between devices, per_device(): came = lax.ppermute(packed, 'seq', [(z, z + d) for z in range(n_seq - d)])  11.4 us
    dot_general x7, matrix products, partial_for(): jnp.dot(rows_theirs, w_theirs, preferred_element_type=jnp.float32)  10.8 us
    ppermute x1, waiting for transfers between devices, per_device(): lax.ppermute(attn, 'mdl', [(mu, mu ^ 2) for mu in range(n_mdl)])  10.1 us
    ppermute x1, waiting for transfers between devices, per_device(): lax.ppermute(bf(partial_for(jnp.clip(s_me + 2, 0, 3))), 'seq', [(0, 1), (...  7.85 us
    dynamic_slice x4, local copies, waits for them, and re-layouts, per_device(): lax.dynamic_index_in_dim(items, (s_me + k) % n_seq, 0, keepdims=False)  6.22 us
  transfers between devices with their start and end apart: 15, of which 10 were waited for; matrix products, arithmetic and copies ran while one was open for 14% of the time, Pallas kernels for 0%

profile of v12, /device:TPU:0, one launch (start us, length us, event | category | flops | bytes accessed | tf_op | source)
XLA Modules:
  0.0 162.9 jit_solution(5822822575588856207)
XLA Ops:
  7.0 5.6 %collective-permute-start = (bf16[8,16640]{1,0:T(8,128)(2,1)S(1)}, bf16[8,16640]{1,0:T(8,128)(2,1)}, u32[]{:S(2)}, u32[]{:S(2)}) collective-permute-start(bf16[8,16640]{1,0:T(8,128)(2,1)S(1)} %pad_maximum_fusion.1), channel_id=1, source_target_pairs={{0,4},{4,8},{8,12},{1,5},{5,9},{9,13},{2,6},{6,10},{10,14},{3,7},{... | collective-permute-start | bytes 798728 | tf_op jit(solution)/shard_map/ppermute | solution.py:95
  12.6 3.8 %collective-permute-start.1 = (bf16[8,16640]{1,0:T(8,128)(2,1)S(1)}, bf16[8,16640]{1,0:T(8,128)(2,1)S(1)}, u32[]{:S(2)}, u32[]{:S(2)}) collective-permute-start(bf16[8,16640]{1,0:T(8,128)(2,1)S(1)} %pad_maximum_fusion.1), channel_id=1, source_target_pairs={{0,8},{4,12},{1,9},{5,13},{2,10},{6,14},{3,11},{7,15},{16,24},{20,... | collective-permute-start | bytes 798728 | tf_op jit(solution)/shard_map/ppermute | solution.py:95
  16.4 2.0 %collective-permute-start.2 = (bf16[8,16640]{1,0:T(8,128)(2,1)S(1)}, bf16[8,16640]{1,0:T(8,128)(2,1)}, u32[]{:S(2)}, u32[]{:S(2)}) collective-permute-start(bf16[8,16640]{1,0:T(8,128)(2,1)S(1)} %pad_maximum_fusion.1), channel_id=1, source_target_pairs={{0,12},{1,13},{2,14},{3,15},{16,28},{17,29},{18,30},{19,31}} | collective-permute-start | bytes 798728 | tf_op jit(solution)/shard_map/ppermute | solution.py:95
  19.3 1.9 %fusion.14 = f32[1,256,8,128]{1,3,2,0:T(8,128)} fusion(bf16[256,8,128]{0,2,1:T(8,128)(2,1)S(1)} %bitcast.132, bf16[256,8,128]{0,2,1:T(8,128)(2,1)S(1)} %bitcast.129, bf16[256,8,128]{0,2,1:T(8,128)(2,1)S(1)} %bitcast.134, f32[8,256]{1,0:T(8,128)S(1)} %bitcast_add_fusion.2, pred[256,256]{1,0:T(8,128)(4,1)S(1)} %iota_compare_fusion), kind=kOutput, calls=%fused_computation.32 | convolution fusion | flops 271056896 | bytes 2695168 | tf_op jit(solution)/shard_map/hbij,bjhd->bihd/dot_general | solution.py:63
  24.7 4.3 %collective-permute-done.2 = bf16[8,16640]{1,0:T(8,128)(2,1)} collective-permute-done((bf16[8,16640]{1,0:T(8,128)(2,1)S(1)}, bf16[8,16640]{1,0:T(8,128)(2,1)}, u32[]{:S(2)}, u32[]{:S(2)}) %collective-permute-start.2) | collective-permute-done | bytes 266272 | tf_op jit(solution)/shard_map/ppermute | solution.py:95
  31.1 2.0 %multiply_reduce_fusion = (f32[256,8]{0,1:T(8,128)S(1)}, f32[1,256,8,128]{1,3,2,0:T(8,128)S(1)}) fusion(f32[1,256,8,128]{1,3,2,0:T(8,128)} %fusion.14, bf16[256,8,128]{0,2,1:T(8,128)(2,1)S(1)} %bitcast.130, f32[8,128,128]{1,2,0:T(8,128)S(1)} %copy.75, f32[8,128,128]{1,2,0:T(8,128)S(1)} %copy.74, f32[8,128,128]{1,2,0:T(8,128)S(1)} %copy.73, ...), kind=kOutput, calls=%fused_computation.53 | convolution fusion | flops 404355072 | bytes 4210784 | tf_op jit(solution)/shard_map/bihd,bhde->bihe/dot_general | solution.py:105
  35.2 1.5 collective-permute-start.3
  38.2 10.1 %collective-permute-done.3 = bf16[256,1024]{0,1:T(8,128)(2,1)} collective-permute-done((bf16[256,1024]{0,1:T(8,128)(2,1)}, bf16[256,1024]{0,1:T(8,128)(2,1)}, u32[]{:S(2)}, u32[]{:S(2)}) %collective-permute-start.3) | collective-permute-done | bytes 524320 | tf_op jit(solution)/shard_map/ppermute | solution.py:126
  48.3 2.4 %fusion.60 = (bf16[1,256,512]{1,2,0:T(8,128)(2,1)}, bf16[1,256,512]{1,2,0:T(8,128)(2,1)}, bf16[1,256,512]{1,2,0:T(8,128)(2,1)}, bf16[1,256,512]{1,2,0:T(8,128)(2,1)S(1)}) fusion(s32[]{:T(128)S(6)} %select_n.404, bf16[2,256,512]{1,2,0:T(8,128)(2,1)} %bitcast.26, bf16[2,256,512]{1,2,0:T(8,128)(2,1)} %bitcast.28, s32[]{:T(128)S(6)} %select_n.406, ...), kind=kLoop, calls=%fused_computation.96 | loop fusion | flops 524288 | bytes 2097168 | tf_op jit(solution)/shard_map/concatenate | solution.py:132
  50.7 1.8 %copy.78 = bf16[1,256,512]{2,1,0:T(8,128)(2,1)} copy(bf16[1,256,512]{1,2,0:T(8,128)(2,1)} %get-tuple-element.26) | data formatting | bytes 524288 | tf_op jit(solution)/shard_map/jit(dynamic_index_in_dim)/dynamic_slice | solution.py:141
  52.5 3.6 %collective-permute-start.4 = (bf16[256,512]{1,0:T(8,128)(2,1)}, bf16[256,512]{1,0:T(8,128)(2,1)}, u32[]{:S(2)}, u32[]{:S(2)}) collective-permute-start(bf16[256,512]{1,0:T(8,128)(2,1)} %bitcast.135), channel_id=1, source_target_pairs={{0,0},{1,4},{2,10},{3,14},{4,1},{5,5},{6,11},{7,15},{8,8},{9,12},{... | collective-permute-start | bytes 786440 | tf_op jit(solution)/shard_map/ppermute | solution.py:142
  56.1 1.8 %copy.79 = bf16[1,256,512]{2,1,0:T(8,128)(2,1)} copy(bf16[1,256,512]{1,2,0:T(8,128)(2,1)} %get-tuple-element.27) | data formatting | bytes 524288 | tf_op jit(solution)/shard_map/jit(dynamic_index_in_dim)/dynamic_slice | solution.py:141
  57.9 5.9 %collective-permute-start.5 = (bf16[256,512]{1,0:T(8,128)(2,1)}, bf16[256,512]{1,0:T(8,128)(2,1)}, u32[]{:S(2)}, u32[]{:S(2)}) collective-permute-start(bf16[256,512]{1,0:T(8,128)(2,1)} %bitcast.136), channel_id=1, source_target_pairs={{0,1},{1,5},{2,11},{3,15},{4,8},{5,12},{6,2},{7,6},{8,9},{9,13},{1... | collective-permute-start | bytes 786440 | tf_op jit(solution)/shard_map/ppermute | solution.py:142
  63.8 1.8 %copy.80 = bf16[1,256,512]{2,1,0:T(8,128)(2,1)} copy(bf16[1,256,512]{1,2,0:T(8,128)(2,1)} %get-tuple-element.28) | data formatting | bytes 524288 | tf_op jit(solution)/shard_map/jit(dynamic_index_in_dim)/dynamic_slice | solution.py:141
  65.6 5.3 %collective-permute-start.6 = (bf16[256,512]{1,0:T(8,128)(2,1)}, bf16[256,512]{1,0:T(8,128)(2,1)}, u32[]{:S(2)}, u32[]{:S(2)}) collective-permute-start(bf16[256,512]{1,0:T(8,128)(2,1)} %bitcast.137), channel_id=1, source_target_pairs={{0,8},{1,12},{2,2},{3,6},{4,9},{5,13},{6,3},{7,7},{8,0},{9,4},{10,... | collective-permute-start | bytes 786440 | tf_op jit(solution)/shard_map/ppermute | solution.py:142
  71.8 4.1 %collective-permute-done.5 = bf16[256,512]{1,0:T(8,128)(2,1)} collective-permute-done((bf16[256,512]{1,0:T(8,128)(2,1)}, bf16[256,512]{1,0:T(8,128)(2,1)}, u32[]{:S(2)}, u32[]{:S(2)}) %collective-permute-start.5) | collective-permute-done | bytes 262176 | tf_op jit(solution)/shard_map/ppermute | solution.py:142
  75.9 10.4 %collective-permute-done.6 = bf16[256,512]{1,0:T(8,128)(2,1)} collective-permute-done((bf16[256,512]{1,0:T(8,128)(2,1)}, bf16[256,512]{1,0:T(8,128)(2,1)}, u32[]{:S(2)}, u32[]{:S(2)}) %collective-permute-start.6) | collective-permute-done | bytes 262176 | tf_op jit(solution)/shard_map/ppermute | solution.py:142
  86.3 2.2 %pad_maximum_fusion = bf16[4,256,512]{2,1,0:T(8,128)(2,1)} fusion(bf16[1,256,512]{2,1,0:T(8,128)(2,1)S(1)} %bitcast.139, bf16[1,256,512]{2,1,0:T(8,128)(2,1)} %bitcast.34, bf16[1,256,512]{2,1,0:T(8,128)(2,1)} %bitcast.32, bf16[1,256,512]{2,1,0:T(8,128)(2,1)} %bitcast.30), kind=kLoop, calls=%fused_computation.49 | loop fusion | flops 1572864 | bytes 2097152 | tf_op jit(solution)/shard_map/stack | solution.py:143
  88.5 2.9 %gather_fusion = bf16[4,256,512]{2,1,0:T(8,128)(2,1)} fusion(bf16[4,256,512]{2,1,0:T(8,128)(2,1)} %pad_maximum_fusion, s32[1024]{0:T(1024)S(1)} %pad_clamp_fusion), kind=kCustom, calls=%fused_computation | custom fusion | bytes 2097168 | tf_op jit(solution)/shard_map/jit(_take)/gather | solution.py:145
  92.8 5.3 %collective-permute-start.8 = (bf16[4,256,512]{2,1,0:T(8,128)(2,1)S(1)}, bf16[4,256,512]{2,1,0:T(8,128)(2,1)S(1)}, u32[]{:S(2)}, u32[]{:S(2)}) collective-permute-start(bf16[4,256,512]{2,1,0:T(8,128)(2,1)S(1)} %broadcast_select_fusion), channel_id=1, source_target_pairs={{0,1},{1,0},{2,3},{3,2},{4,5},{5,4},{6,7},{7,6},{8,9},{9,8},{10,11... | collective-permute-start | bytes 3145736 | tf_op jit(solution)/shard_map/ppermute | solution.py:146
  102.2 2.6 %collective-permute-start.9 = (bf16[256,1536]{1,0:T(8,128)(2,1)S(1)}, bf16[256,1536]{1,0:T(8,128)(2,1)S(1)}, u32[]{:S(2)}, u32[]{:S(2)}) collective-permute-start(bf16[256,1536]{1,0:T(8,128)(2,1)S(1)} %fusion.9), channel_id=1, source_target_pairs={{0,4},{4,8},{1,5},{5,9},{2,6},{6,10},{3,7},{7,11},{16,20},{20,24},... | collective-permute-start | bytes 2359304 | tf_op jit(solution)/shard_map/ppermute | solution.py:200
  106.2 1.5 fusion.10
  107.7 4.2 %collective-permute-start.11 = (bf16[256,1536]{1,0:T(8,128)(2,1)}, bf16[256,1536]{1,0:T(8,128)(2,1)}, u32[]{:S(2)}, u32[]{:S(2)}) collective-permute-start(bf16[256,1536]{1,0:T(8,128)(2,1)} %fusion.10), channel_id=1, source_target_pairs={{0,12},{1,13},{2,14},{3,15},{16,28},{17,29},{18,30},{19,31}} | collective-permute-start | bytes 2359304 | tf_op jit(solution)/shard_map/ppermute | solution.py:203
  114.7 7.8 %collective-permute-done.9 = bf16[256,1536]{1,0:T(8,128)(2,1)S(1)} collective-permute-done((bf16[256,1536]{1,0:T(8,128)(2,1)S(1)}, bf16[256,1536]{1,0:T(8,128)(2,1)S(1)}, u32[]{:S(2)}, u32[]{:S(2)}) %collective-permute-start.9) | collective-permute-done | bytes 786464 | tf_op jit(solution)/shard_map/ppermute | solution.py:200
  122.5 1.5 fusion.6
  124.0 5.3 %collective-permute-start.10 = (bf16[256,1536]{1,0:T(8,128)(2,1)}, bf16[256,1536]{1,0:T(8,128)(2,1)}, u32[]{:S(2)}, u32[]{:S(2)}) collective-permute-start(bf16[256,1536]{1,0:T(8,128)(2,1)} %fusion.6), channel_id=1, source_target_pairs={{0,4},{4,8},{8,12},{1,5},{5,9},{9,13},{2,6},{6,10},{10,14},{3,7},{... | collective-permute-start | bytes 2359304 | tf_op jit(solution)/shard_map/ppermute | solution.py:208
  132.1 1.5 fusion.57
  133.6 5.9 %collective-permute-done.11 = bf16[256,1536]{1,0:T(8,128)(2,1)} collective-permute-done((bf16[256,1536]{1,0:T(8,128)(2,1)}, bf16[256,1536]{1,0:T(8,128)(2,1)}, u32[]{:S(2)}, u32[]{:S(2)}) %collective-permute-start.11) | collective-permute-done | bytes 786464 | tf_op jit(solution)/shard_map/ppermute | solution.py:203
  139.5 3.4 %collective-permute-done.14 = bf16[256,1536]{1,0:T(8,128)(2,1)} collective-permute-done((bf16[256,1536]{1,0:T(8,128)(2,1)}, bf16[256,1536]{1,0:T(8,128)(2,1)}, u32[]{:S(2)}, u32[]{:S(2)}) %collective-permute-start.14) | collective-permute-done | bytes 786464 | tf_op jit(solution)/shard_map/ppermute | solution.py:207
  142.9 12.5 %collective-permute-done.10 = bf16[256,1536]{1,0:T(8,128)(2,1)} collective-permute-done((bf16[256,1536]{1,0:T(8,128)(2,1)}, bf16[256,1536]{1,0:T(8,128)(2,1)}, u32[]{:S(2)}, u32[]{:S(2)}) %collective-permute-start.10) | collective-permute-done | bytes 786464 | tf_op jit(solution)/shard_map/ppermute | solution.py:208
  155.4 3.9 %collective-permute-done.13 = bf16[256,1536]{1,0:T(8,128)(2,1)} collective-permute-done((bf16[256,1536]{1,0:T(8,128)(2,1)}, bf16[256,1536]{1,0:T(8,128)(2,1)}, u32[]{:S(2)}, u32[]{:S(2)}) %collective-permute-start.13) | collective-permute-done | bytes 786464 | tf_op jit(solution)/shard_map/ppermute | solution.py:213
  159.3 3.6 %fusion.8 = bf16[256,1536]{1,0:T(8,128)(2,1)} fusion(f32[256,1536]{1,0:T(8,128)S(1)} %fusion.57, bf16[256,1536]{1,0:T(8,128)(2,1)} %collective-permute-done.14, bf16[256,1536]{1,0:T(8,128)(2,1)} %collective-permute-done.13, bf16[256,1536]{1,0:T(8,128)(2,1)} %collective-permute-done.11, bf16[256,1536]{1,0:T(8,128)(2,1)} %collective-permute-done.10, ...), kind=kOutput, calls=%fused_computation.17 | convolution fusion | flops 406585344 | bytes 7340040 | tf_op jit(solution)/shard_map/dot_general | solution.py:153
  (76 shorter events, 29.9 us)
Async XLA Ops:
  6.2 12.3 %copy-start.4 = (bf16[256,1024]{1,0:T(8,128)(2,1)S(1)}, bf16[256,1024]{1,0:T(8,128)(2,1)}, u32[]{:S(2)}) copy-start(bf16[256,1024]{1,0:T(8,128)(2,1)} %param.9) | copy-start | bytes 1572868
  7.0 15.3 %collective-permute-start = (bf16[8,16640]{1,0:T(8,128)(2,1)S(1)}, bf16[8,16640]{1,0:T(8,128)(2,1)}, u32[]{:S(2)}, u32[]{:S(2)}) collective-permute-start(bf16[8,16640]{1,0:T(8,128)(2,1)S(1)} %pad_maximum_fusion.1), channel_id=1, source_target_pairs={{0,4},{4,8},{8,12},{1,5},{5,9},{9,13},{2,6},{6,10},{10,14},{3,7},{... | collective-permute-start | bytes 798728 | tf_op jit(solution)/shard_map/ppermute | solution.py:95
  12.6 11.8 %collective-permute-start.1 = (bf16[8,16640]{1,0:T(8,128)(2,1)S(1)}, bf16[8,16640]{1,0:T(8,128)(2,1)S(1)}, u32[]{:S(2)}, u32[]{:S(2)}) collective-permute-start(bf16[8,16640]{1,0:T(8,128)(2,1)S(1)} %pad_maximum_fusion.1), channel_id=1, source_target_pairs={{0,8},{4,12},{1,9},{5,13},{2,10},{6,14},{3,11},{7,15},{16,24},{20,... | collective-permute-start | bytes 798728 | tf_op jit(solution)/shard_map/ppermute | solution.py:95
  16.4 12.6 %collective-permute-start.2 = (bf16[8,16640]{1,0:T(8,128)(2,1)S(1)}, bf16[8,16640]{1,0:T(8,128)(2,1)}, u32[]{:S(2)}, u32[]{:S(2)}) collective-permute-start(bf16[8,16640]{1,0:T(8,128)(2,1)S(1)} %pad_maximum_fusion.1), channel_id=1, source_target_pairs={{0,12},{1,13},{2,14},{3,15},{16,28},{17,29},{18,30},{19,31}} | collective-permute-start | bytes 798728 | tf_op jit(solution)/shard_map/ppermute | solution.py:95
  19.3 1.9 %copy-start.6 = (s32[1536]{0:T(1024)S(1)}, s32[1536]{0:T(1024)}, u32[]{:S(2)}) copy-start(s32[1536]{0:T(1024)} %param.17) | copy-start | bytes 18436
  19.3 2.0 %copy-start.5 = (bf16[256,1024]{1,0:T(8,128)(2,1)S(1)}, bf16[256,1024]{1,0:T(8,128)(2,1)}, u32[]{:S(2)}) copy-start(bf16[256,1024]{1,0:T(8,128)(2,1)} %param.12) | copy-start | bytes 1572868
  33.1 1.0 copy-start.3
  33.1 1.0 copy-start.7
  33.1 3.6 %copy-start.2 = (bf16[1024,1536]{1,0:T(8,128)(2,1)S(1)}, bf16[1024,1536]{1,0:T(8,128)(2,1)}, u32[]{:S(2)}) copy-start(bf16[1024,1536]{1,0:T(8,128)(2,1)} %param.16) | copy-start | bytes 9437188
  35.2 13.1 %collective-permute-start.3 = (bf16[256,1024]{0,1:T(8,128)(2,1)}, bf16[256,1024]{0,1:T(8,128)(2,1)}, u32[]{:S(2)}, u32[]{:S(2)}) collective-permute-start(bf16[256,1024]{0,1:T(8,128)(2,1)} %fusion.26), channel_id=1, source_target_pairs={{0,2},{1,3},{2,0},{3,1},{4,6},{5,7},{6,4},{7,5},{8,10},{9,11},{10,... | collective-permute-start | bytes 1572872 | tf_op jit(solution)/shard_map/ppermute | solution.py:126
  52.5 19.3 %collective-permute-start.4 = (bf16[256,512]{1,0:T(8,128)(2,1)}, bf16[256,512]{1,0:T(8,128)(2,1)}, u32[]{:S(2)}, u32[]{:S(2)}) collective-permute-start(bf16[256,512]{1,0:T(8,128)(2,1)} %bitcast.135), channel_id=1, source_target_pairs={{0,0},{1,4},{2,10},{3,14},{4,1},{5,5},{6,11},{7,15},{8,8},{9,12},{... | collective-permute-start | bytes 786440 | tf_op jit(solution)/shard_map/ppermute | solution.py:142
  57.9 18.1 %collective-permute-start.5 = (bf16[256,512]{1,0:T(8,128)(2,1)}, bf16[256,512]{1,0:T(8,128)(2,1)}, u32[]{:S(2)}, u32[]{:S(2)}) collective-permute-start(bf16[256,512]{1,0:T(8,128)(2,1)} %bitcast.136), channel_id=1, source_target_pairs={{0,1},{1,5},{2,11},{3,15},{4,8},{5,12},{6,2},{7,6},{8,9},{9,13},{1... | collective-permute-start | bytes 786440 | tf_op jit(solution)/shard_map/ppermute | solution.py:142
  65.6 20.7 %collective-permute-start.6 = (bf16[256,512]{1,0:T(8,128)(2,1)}, bf16[256,512]{1,0:T(8,128)(2,1)}, u32[]{:S(2)}, u32[]{:S(2)}) collective-permute-start(bf16[256,512]{1,0:T(8,128)(2,1)} %bitcast.137), channel_id=1, source_target_pairs={{0,8},{1,12},{2,2},{3,6},{4,9},{5,13},{6,3},{7,7},{8,0},{9,4},{10,... | collective-permute-start | bytes 786440 | tf_op jit(solution)/shard_map/ppermute | solution.py:142
  71.7 14.6 %collective-permute-start.7 = (bf16[256,512]{1,0:T(8,128)(2,1)}, bf16[256,512]{1,0:T(8,128)(2,1)S(1)}, u32[]{:S(2)}, u32[]{:S(2)}) collective-permute-start(bf16[256,512]{1,0:T(8,128)(2,1)} %bitcast.138), channel_id=1, source_target_pairs={{0,9},{1,13},{2,3},{3,7},{4,0},{5,4},{6,10},{7,14},{8,1},{9,5},{10... | collective-permute-start | bytes 786440 | tf_op jit(solution)/shard_map/ppermute | solution.py:142
  92.7 8.2 %copy-start = (bf16[4,256,512]{2,1,0:T(8,128)(2,1)}, bf16[4,256,512]{2,1,0:T(8,128)(2,1)S(1)}, u32[]{:S(2)}) copy-start(bf16[4,256,512]{2,1,0:T(8,128)(2,1)S(1)} %broadcast_select_fusion) | copy-start | bytes 3145732
  92.8 8.8 %collective-permute-start.8 = (bf16[4,256,512]{2,1,0:T(8,128)(2,1)S(1)}, bf16[4,256,512]{2,1,0:T(8,128)(2,1)S(1)}, u32[]{:S(2)}, u32[]{:S(2)}) collective-permute-start(bf16[4,256,512]{2,1,0:T(8,128)(2,1)S(1)} %broadcast_select_fusion), channel_id=1, source_target_pairs={{0,1},{1,0},{2,3},{3,2},{4,5},{5,4},{6,7},{7,6},{8,9},{9,8},{10,11... | collective-permute-start | bytes 3145736 | tf_op jit(solution)/shard_map/ppermute | solution.py:146
  101.6 27.7 %copy-start.1 = (bf16[4,256,512]{2,1,0:T(8,128)(2,1)}, bf16[4,256,512]{2,1,0:T(8,128)(2,1)S(1)}, u32[]{:S(2)}) copy-start(bf16[4,256,512]{2,1,0:T(8,128)(2,1)S(1)} %collective-permute-done.8) | copy-start | bytes 3145732
  102.2 20.3 %collective-permute-start.9 = (bf16[256,1536]{1,0:T(8,128)(2,1)S(1)}, bf16[256,1536]{1,0:T(8,128)(2,1)S(1)}, u32[]{:S(2)}, u32[]{:S(2)}) collective-permute-start(bf16[256,1536]{1,0:T(8,128)(2,1)S(1)} %fusion.9), channel_id=1, source_target_pairs={{0,4},{4,8},{1,5},{5,9},{2,6},{6,10},{3,7},{7,11},{16,20},{20,24},... | collective-permute-start | bytes 2359304 | tf_op jit(solution)/shard_map/ppermute | solution.py:200
  105.5 23.8 %collective-permute-start.12 = (bf16[256,1536]{1,0:T(8,128)(2,1)S(1)}, bf16[256,1536]{1,0:T(8,128)(2,1)S(1)}, u32[]{:S(2)}, u32[]{:S(2)}) collective-permute-start(bf16[256,1536]{1,0:T(8,128)(2,1)S(1)} %fusion.11), channel_id=1, source_target_pairs={{12,8},{8,4},{13,9},{9,5},{14,10},{10,6},{15,11},{11,7},{28,24},{2... | collective-permute-start | bytes 2359304 | tf_op jit(solution)/shard_map/ppermute | solution.py:204
  107.7 31.8 %collective-permute-start.11 = (bf16[256,1536]{1,0:T(8,128)(2,1)}, bf16[256,1536]{1,0:T(8,128)(2,1)}, u32[]{:S(2)}, u32[]{:S(2)}) collective-permute-start(bf16[256,1536]{1,0:T(8,128)(2,1)} %fusion.10), channel_id=1, source_target_pairs={{0,12},{1,13},{2,14},{3,15},{16,28},{17,29},{18,30},{19,31}} | collective-permute-start | bytes 2359304 | tf_op jit(solution)/shard_map/ppermute | solution.py:203
  113.4 29.5 %collective-permute-start.14 = (bf16[256,1536]{1,0:T(8,128)(2,1)}, bf16[256,1536]{1,0:T(8,128)(2,1)}, u32[]{:S(2)}, u32[]{:S(2)}) collective-permute-start(bf16[256,1536]{1,0:T(8,128)(2,1)} %fusion.12), channel_id=1, source_target_pairs={{12,0},{13,1},{14,2},{15,3},{28,16},{29,17},{30,18},{31,19}} | collective-permute-start | bytes 2359304 | tf_op jit(solution)/shard_map/ppermute | solution.py:207
  124.0 31.4 %collective-permute-start.10 = (bf16[256,1536]{1,0:T(8,128)(2,1)}, bf16[256,1536]{1,0:T(8,128)(2,1)}, u32[]{:S(2)}, u32[]{:S(2)}) collective-permute-start(bf16[256,1536]{1,0:T(8,128)(2,1)} %fusion.6), channel_id=1, source_target_pairs={{0,4},{4,8},{8,12},{1,5},{5,9},{9,13},{2,6},{6,10},{10,14},{3,7},{... | collective-permute-start | bytes 2359304 | tf_op jit(solution)/shard_map/ppermute | solution.py:208
  130.8 28.5 %collective-permute-start.13 = (bf16[256,1536]{1,0:T(8,128)(2,1)}, bf16[256,1536]{1,0:T(8,128)(2,1)}, u32[]{:S(2)}, u32[]{:S(2)}) collective-permute-start(bf16[256,1536]{1,0:T(8,128)(2,1)} %fusion.7), channel_id=1, source_target_pairs={{12,8},{8,4},{4,0},{13,9},{9,5},{5,1},{14,10},{10,6},{6,2},{15,11}... | collective-permute-start | bytes 2359304 | tf_op jit(solution)/shard_map/ppermute | solution.py:213

commit v13 on v10

--- a/solution.py
+++ b/solution.py
@@ -187,11 +187,15 @@
         near_r = lax.ppermute(
             bf(partial_for(jnp.clip(s_me + 2, 0, 3))), "seq", [(0, 1), (1, 2)]
         )
-        far_r = lax.ppermute(bf(partial_for(jnp.int32(3))), "seq", [(0, 3)])
         near_l = lax.ppermute(
             bf(partial_for(jnp.clip(s_me - 2, 0, 3))), "seq", [(3, 2), (2, 1)]
         )
-        far_l = lax.ppermute(bf(partial_for(jnp.int32(0))), "seq", [(3, 0)])
+        far_r = lax.ppermute(
+            bf(partial_for(jnp.int32(3))) + near_r * jnp.bfloat16(0), "seq", [(0, 3)]
+        )
+        far_l = lax.ppermute(
+            bf(partial_for(jnp.int32(0))) + near_l * jnp.bfloat16(0), "seq", [(3, 0)]
+        )
         last_r = lax.ppermute(
             bf(partial_for(jnp.clip(s_me + 1, 0, 3)) + near_r.astype(jnp.float32)),
             "seq",

time: 162 us -> 172 us (1.062)
  waiting for transfers between devices: 53.9 us -> 78.6 us
  starting transfers between devices: 61.7 us -> 44.6 us
  matrix products: 23.5 us -> 26.5 us
    ppermute x1, starting transfers between devices: 20.1 us -> 4.63 us  [per_device(): lax.ppermute(bf(partial_for(jnp.clip(s_me + 1, 0, 3)) + near_r.astype(jnp...]
    ppermute x1, waiting for transfers between devices: 5.83 us -> 16 us  [per_device(): lax.ppermute(bf(partial_for(jnp.clip(s_me + 1, 0, 3)) + near_r.astype(jnp...]
    ppermute x1, waiting for transfers between devices: 2.45 us -> 12.5 us  [per_device(): lax.ppermute(bf(partial_for(jnp.clip(s_me + 2, 0, 3))), 'seq', [(0, 1), (...]
    ppermute x1, starting transfers between devices: 0.07 us -> 3.8 us  [per_device(): got.append(lax.ppermute(x, 'mdl', perm))]
    ppermute x2, starting transfers between devices: 7.08 us -> 3.45 us  [the longest x1 2.17 us: per_device(): lax.ppermute(bf(partial_for(jnp.int32(3))) + near_r * jnp.bfloat16(0), 's...]
    dot_general x7, matrix products: 19.3 us -> 22.3 us  [partial_for(): jnp.einsum('deti,deic->tc', rows, w_perm, preferred_element_type=jnp.floa...]
    ppermute x2, waiting for transfers between devices: 0.01 us -> 2.89 us  [the longest x1 2.01 us: per_device(): lax.ppermute(bf(partial_for(jnp.int32(0))) + near_l * jnp.bfloat16(0), 's...]
    ppermute x3, waiting for transfers between devices: 6.02 us -> 8.35 us  [per_device(): came = lax.ppermute(packed, 'seq', [(z, z + d) for z in range(n_seq - d)])]
  transfers between devices with their start and end apart: 16 -> 16, of which waited for: 9 -> 9; matrix products, arithmetic and copies ran while one was open for 15% -> 16% of each run, Pallas kernels for 0% -> 0%
where the time goes in v13:
time: 172 us; the launch traced here: 171 us
  waiting for transfers between devices  78.6 us (46%)
  starting transfers between devices  44.6 us (26%)
  matrix products  26.5 us (15%)
  other arithmetic  13.6 us (8%)
  local copies, waits for them, and re-layouts  7.54 us (4%)
    dot_general x7, matrix products, partial_for(): jnp.einsum('deti,deic->tc', rows, w_perm, preferred_element_type=jnp.floa...  22.3 us
    ppermute x1, waiting for transfers between devices, per_device(): lax.ppermute(bf(partial_for(jnp.clip(s_me + 1, 0, 3)) + near_r.astype(jnp...  16 us
    ppermute x1, waiting for transfers between devices, per_device(): lax.ppermute(bf(partial_for(jnp.clip(s_me - 1, 0, 3)) + near_l.astype(jnp...  15.3 us
    ppermute x4, starting transfers between devices, per_device(): received.append(lax.ppermute(item, ('seq', 'mdl'), perm))  14.5 us
    ppermute x1, waiting for transfers between devices, per_device(): lax.ppermute(bf(partial_for(jnp.clip(s_me + 2, 0, 3))), 'seq', [(0, 1), (...  12.5 us
    ppermute x3, starting transfers between devices, per_device(): came = lax.ppermute(packed, 'seq', [(z, z + d) for z in range(n_seq - d)])  11.5 us
    ppermute x1, waiting for transfers between devices, per_device(): got.append(lax.ppermute(x, 'mdl', perm))  10.9 us
    ppermute x3, waiting for transfers between devices, per_device(): came = lax.ppermute(packed, 'seq', [(z, z + d) for z in range(n_seq - d)])  8.35 us
  transfers between devices with their start and end apart: 16, of which 9 were waited for; matrix products, arithmetic and copies ran while one was open for 16% of the time, Pallas kernels for 0%

profile of v13, /device:TPU:0, one launch (start us, length us, event | category | flops | bytes accessed | tf_op | source)
XLA Modules:
  0.0 171.2 jit_solution(9154627103227871133)
XLA Ops:
  7.0 7.7 %collective-permute-start.2 = (bf16[8,16640]{1,0:T(8,128)(2,1)S(1)}, bf16[8,16640]{1,0:T(8,128)(2,1)}, u32[]{:S(2)}, u32[]{:S(2)}) collective-permute-start(bf16[8,16640]{1,0:T(8,128)(2,1)S(1)} %pad_maximum_fusion.3), channel_id=1, source_target_pairs={{0,12},{1,13},{2,14},{3,15},{16,28},{17,29},{18,30},{19,31}} | collective-permute-start | bytes 798728 | tf_op jit(solution)/shard_map/ppermute | solution.py:95
  16.0 2.5 %collective-permute-start = (bf16[8,16640]{1,0:T(8,128)(2,1)S(1)}, bf16[8,16640]{1,0:T(8,128)(2,1)}, u32[]{:S(2)}, u32[]{:S(2)}) collective-permute-start(bf16[8,16640]{1,0:T(8,128)(2,1)S(1)} %pad_maximum_fusion.3), channel_id=1, source_target_pairs={{0,4},{4,8},{8,12},{1,5},{5,9},{9,13},{2,6},{6,10},{10,14},{3,7},{... | collective-permute-start | bytes 798728 | tf_op jit(solution)/shard_map/ppermute | solution.py:95
  19.4 1.9 %fusion.16 = f32[1,256,8,128]{1,3,2,0:T(8,128)} fusion(bf16[256,8,128]{0,2,1:T(8,128)(2,1)S(1)} %bitcast.197, bf16[256,8,128]{0,2,1:T(8,128)(2,1)S(1)} %bitcast.192, bf16[256,8,128]{0,2,1:T(8,128)(2,1)S(1)} %bitcast.195, f32[8,256]{1,0:T(8,128)S(1)} %bitcast_add_fusion.2, pred[256,256]{1,0:T(8,128)(4,1)S(1)} %iota_compare_fusion), kind=kOutput, calls=%fused_computation.40 | convolution fusion | flops 271056896 | bytes 2695168 | tf_op jit(solution)/shard_map/hbij,bjhd->bihd/dot_general | solution.py:63
  22.8 8.3 %collective-permute-done = bf16[8,16640]{1,0:T(8,128)(2,1)} collective-permute-done((bf16[8,16640]{1,0:T(8,128)(2,1)S(1)}, bf16[8,16640]{1,0:T(8,128)(2,1)}, u32[]{:S(2)}, u32[]{:S(2)}) %collective-permute-start) | collective-permute-done | bytes 266272 | tf_op jit(solution)/shard_map/ppermute | solution.py:95
  33.5 2.0 %multiply_reduce_fusion = (f32[256,8]{0,1:T(8,128)S(1)}, f32[1,256,8,128]{1,3,2,0:T(8,128)S(1)}) fusion(f32[1,256,8,128]{1,3,2,0:T(8,128)} %fusion.16, bf16[256,8,128]{0,2,1:T(8,128)(2,1)S(1)} %bitcast.193, f32[8,128,128]{1,2,0:T(8,128)S(1)} %copy.83, f32[8,128,128]{1,2,0:T(8,128)S(1)} %copy.82, f32[8,128,128]{1,2,0:T(8,128)S(1)} %copy.81, ...), kind=kOutput, calls=%fused_computation.61 | convolution fusion | flops 404355072 | bytes 4210784 | tf_op jit(solution)/shard_map/bihd,bhde->bihe/dot_general | solution.py:105
  36.0 1.6 collective-permute-start.3
  37.7 5.5 %collective-permute-done.3 = bf16[256,2,256]{0,2,1:T(8,128)(2,1)S(1)} collective-permute-done((bf16[256,2,256]{0,2,1:T(8,128)(2,1)S(1)}, bf16[256,2,256]{0,2,1:T(8,128)(2,1)S(1)}, u32[]{:S(2)}, u32[]{:S(2)}) %collective-permute-start.3) | collective-permute-done | bytes 262176 | tf_op jit(solution)/shard_map/ppermute | solution.py:129
  43.8 9.0 %collective-permute-start.7 = (bf16[256,256]{1,0:T(8,128)(2,1)S(1)}, bf16[256,256]{1,0:T(8,128)(2,1)S(1)}, u32[]{:S(2)}, u32[]{:S(2)}) collective-permute-start(bf16[256,256]{1,0:T(8,128)(2,1)S(1)} %bitcast.203), channel_id=1, source_target_pairs={{0,9},{1,13},{2,3},{3,7},{4,0},{5,4},{6,10},{7,14},{8,1},{9,5},{10... | collective-permute-start | bytes 393224 | tf_op jit(solution)/shard_map/ppermute | solution.py:140
  52.9 3.1 %collective-permute-start.6 = (bf16[256,256]{1,0:T(8,128)(2,1)S(1)}, bf16[256,256]{1,0:T(8,128)(2,1)S(1)}, u32[]{:S(2)}, u32[]{:S(2)}) collective-permute-start(bf16[256,256]{1,0:T(8,128)(2,1)S(1)} %bitcast.202), channel_id=1, source_target_pairs={{0,8},{1,12},{2,2},{3,6},{4,9},{5,13},{6,3},{7,7},{8,0},{9,4},{10,... | collective-permute-start | bytes 393224 | tf_op jit(solution)/shard_map/ppermute | solution.py:140
  56.0 1.6 collective-permute-start.5
  58.3 7.2 %collective-permute-done.6 = bf16[256,256]{1,0:T(8,128)(2,1)S(1)} collective-permute-done((bf16[256,256]{1,0:T(8,128)(2,1)S(1)}, bf16[256,256]{1,0:T(8,128)(2,1)S(1)}, u32[]{:S(2)}, u32[]{:S(2)}) %collective-permute-start.6) | collective-permute-done | bytes 131104 | tf_op jit(solution)/shard_map/ppermute | solution.py:140
  66.4 3.8 %collective-permute-start.8 = (bf16[4,256,256]{2,1,0:T(8,128)(2,1)S(1)}, bf16[4,256,256]{2,1,0:T(8,128)(2,1)S(1)}, u32[]{:S(2)}, u32[]{:S(2)}) collective-permute-start(bf16[4,256,256]{2,1,0:T(8,128)(2,1)S(1)} %broadcast_select_fusion.1), channel_id=1, source_target_pairs={{0,2},{1,3},{2,0},{3,1},{4,6},{5,7},{6,4},{7,5},{8,10},{9,11},{10,... | collective-permute-start | bytes 1572872 | tf_op jit(solution)/shard_map/ppermute | solution.py:166
  70.3 10.9 %collective-permute-done.8 = bf16[4,256,256]{2,1,0:T(8,128)(2,1)S(1)} collective-permute-done((bf16[4,256,256]{2,1,0:T(8,128)(2,1)S(1)}, bf16[4,256,256]{2,1,0:T(8,128)(2,1)S(1)}, u32[]{:S(2)}, u32[]{:S(2)}) %collective-permute-start.8) | collective-permute-done | bytes 524320 | tf_op jit(solution)/shard_map/ppermute | solution.py:166
  81.2 1.5 pad_maximum_fusion
  82.6 1.4 multiply_convert_fusion
  84.2 2.4 %gather_fusion.1 = bf16[4,256,1536]{2,1,0:T(8,128)(2,1)} fusion(bf16[4,256,1536]{2,1,0:T(8,128)(2,1)S(1)} %bitcast.191, s32[1024]{0:T(1024)S(1)} %pad_clamp_fusion), kind=kCustom, calls=%fused_computation.1 | custom fusion | bytes 6291472 | tf_op jit(solution)/shard_map/jit(_take)/gather | solution.py:173
  86.6 2.3 %broadcast_select_fusion = bf16[4,256,1536]{2,1,0:T(8,128)(2,1)S(1)} fusion(bf16[4,256,1536]{2,1,0:T(8,128)(2,1)} %gather_fusion.1, pred[4]{0:T(512)(128)(4,1)S(1)} %get-tuple-element.42), kind=kLoop, calls=%fused_computation.15 | loop fusion | flops 1572864 | bytes 6291460 | tf_op jit(solution)/shard_map/jit(_take)/select_n | solution.py:173
  88.9 2.8 %fusion.9 = bf16[256,1536]{1,0:T(8,128)(2,1)} fusion(bf16[2,2,256,1536]{3,2,1,0:T(8,128)(2,1)S(1)} %bitcast.184, s32[]{:T(128)S(6)} %min.74, bf16[2,1,4,256,256]{4,3,1,0,2:T(8,128)(2,1)S(1)} %copy-done, bf16[2,1,4,256,256]{4,3,1,0,2:T(8,128)(2,1)} %bitcast.40), kind=kOutput, calls=%fused_computation.32 | convolution fusion | flops 805961728 | bytes 6029316 | tf_op jit(solution)/shard_map/deti,deic->tc/dot_general | solution.py:179
  91.8 2.4 %collective-permute-start.10 = (bf16[256,1536]{1,0:T(8,128)(2,1)}, bf16[256,1536]{1,0:T(8,128)(2,1)}, u32[]{:S(2)}, u32[]{:S(2)}) collective-permute-start(bf16[256,1536]{1,0:T(8,128)(2,1)} %fusion.9), channel_id=1, source_target_pairs={{0,4},{4,8},{1,5},{5,9},{2,6},{6,10},{3,7},{7,11},{16,20},{20,24},... | collective-permute-start | bytes 2359304 | tf_op jit(solution)/shard_map/ppermute | solution.py:187
  94.2 2.9 %fusion.11 = bf16[256,1536]{1,0:T(8,128)(2,1)} fusion(bf16[2,2,256,1536]{3,2,1,0:T(8,128)(2,1)S(1)} %bitcast.185, s32[]{:T(128)S(6)} %min.76, bf16[2,1,4,256,256]{4,3,1,0,2:T(8,128)(2,1)} %get-tuple-element.27, bf16[2,1,4,256,256]{4,3,1,0,2:T(8,128)(2,1)} %bitcast.40), kind=kOutput, calls=%fused_computation.34 | convolution fusion | flops 805961728 | bytes 6029316 | tf_op jit(solution)/shard_map/deti,deic->tc/dot_general | solution.py:179
  97.1 1.5 collective-permute-start.13
  98.6 12.5 %collective-permute-done.10 = bf16[256,1536]{1,0:T(8,128)(2,1)} collective-permute-done((bf16[256,1536]{1,0:T(8,128)(2,1)}, bf16[256,1536]{1,0:T(8,128)(2,1)}, u32[]{:S(2)}, u32[]{:S(2)}) %collective-permute-start.10) | collective-permute-done | bytes 786464 | tf_op jit(solution)/shard_map/ppermute | solution.py:187
  111.1 3.2 %fusion.14 = bf16[256,1536]{1,0:T(8,128)(2,1)} fusion(bf16[2,2,256,1536]{3,2,1,0:T(8,128)(2,1)S(1)} %bitcast.186, bf16[256,1536]{1,0:T(8,128)(2,1)} %collective-permute-done.10, bf16[2,1,4,256,256]{4,3,1,0,2:T(8,128)(2,1)} %get-tuple-element.27, bf16[2,1,4,256,256]{4,3,1,0,2:T(8,128)(2,1)} %bitcast.40), kind=kOutput, calls=%fused_computation.37 | convolution fusion | flops 806748160 | bytes 6815744 | tf_op jit(solution)/shard_map/deti,deic->tc/dot_general | solution.py:179
  114.3 2.2 %collective-permute-start.12 = (bf16[256,1536]{1,0:T(8,128)(2,1)}, bf16[256,1536]{1,0:T(8,128)(2,1)}, u32[]{:S(2)}, u32[]{:S(2)}) collective-permute-start(bf16[256,1536]{1,0:T(8,128)(2,1)} %fusion.14), channel_id=1, source_target_pairs={{0,12},{1,13},{2,14},{3,15},{16,28},{17,29},{18,30},{19,31}} | collective-permute-start | bytes 2359304 | tf_op jit(solution)/shard_map/ppermute | solution.py:193
  116.5 3.1 %fusion.7 = bf16[256,1536]{1,0:T(8,128)(2,1)} fusion(bf16[2,2,256,1536]{3,2,1,0:T(8,128)(2,1)S(1)} %bitcast.187, bf16[256,1536]{1,0:T(8,128)(2,1)} %collective-permute-done.10, s32[]{:T(128)S(6)} %min.73, bf16[2,1,4,256,256]{4,3,1,0,2:T(8,128)(2,1)S(1)} %copy-done.1, bf16[2,1,4,256,256]{4,3,1,0,2:T(8,128)(2,1)} %bitcast.40), kind=kOutput, calls=%fused_computation.30 | convolution fusion | flops 806748160 | bytes 6815748 | tf_op jit(solution)/shard_map/deti,deic->tc/dot_general | solution.py:179
  119.6 4.6 %collective-permute-start.11 = (bf16[256,1536]{1,0:T(8,128)(2,1)}, bf16[256,1536]{1,0:T(8,128)(2,1)}, u32[]{:S(2)}, u32[]{:S(2)}) collective-permute-start(bf16[256,1536]{1,0:T(8,128)(2,1)} %fusion.7), channel_id=1, source_target_pairs={{0,4},{4,8},{8,12},{1,5},{5,9},{9,13},{2,6},{6,10},{10,14},{3,7},{... | collective-permute-start | bytes 2359304 | tf_op jit(solution)/shard_map/ppermute | solution.py:199
  124.2 3.1 %fusion.13 = bf16[256,1536]{1,0:T(8,128)(2,1)} fusion(bf16[2,2,256,1536]{3,2,1,0:T(8,128)(2,1)S(1)} %bitcast.188, bf16[256,1536]{1,0:T(8,128)(2,1)} %collective-permute-done.13, bf16[2,1,4,256,256]{4,3,1,0,2:T(8,128)(2,1)} %bitcast.40, bf16[2,1,4,256,256]{4,3,1,0,2:T(8,128)(2,1)S(1)} %copy-done.1), kind=kOutput, calls=%fused_computation.36 | convolution fusion | flops 806748160 | bytes 6815744 | tf_op jit(solution)/shard_map/deti,deic->tc/dot_general | solution.py:179
  128.6 3.1 %fusion.6 = bf16[256,1536]{1,0:T(8,128)(2,1)} fusion(bf16[2,2,256,1536]{3,2,1,0:T(8,128)(2,1)S(1)} %bitcast.189, bf16[256,1536]{1,0:T(8,128)(2,1)} %collective-permute-done.13, s32[]{:T(128)S(6)} %min.75, bf16[2,1,4,256,256]{4,3,1,0,2:T(8,128)(2,1)S(1)} %copy-done.1, bf16[2,1,4,256,256]{4,3,1,0,2:T(8,128)(2,1)} %bitcast.40), kind=kOutput, calls=%fused_computation.29 | convolution fusion | flops 806748160 | bytes 6815748 | tf_op jit(solution)/shard_map/deti,deic->tc/dot_general | solution.py:179
  133.8 16.0 %collective-permute-done.11 = bf16[256,1536]{1,0:T(8,128)(2,1)} collective-permute-done((bf16[256,1536]{1,0:T(8,128)(2,1)}, bf16[256,1536]{1,0:T(8,128)(2,1)}, u32[]{:S(2)}, u32[]{:S(2)}) %collective-permute-start.11) | collective-permute-done | bytes 786464 | tf_op jit(solution)/shard_map/ppermute | solution.py:199
  149.8 2.0 %collective-permute-done.15 = bf16[256,1536]{1,0:T(8,128)(2,1)} collective-permute-done((bf16[256,1536]{1,0:T(8,128)(2,1)}, bf16[256,1536]{1,0:T(8,128)(2,1)}, u32[]{:S(2)}, u32[]{:S(2)}) %collective-permute-start.15) | collective-permute-done | bytes 786464 | tf_op jit(solution)/shard_map/ppermute | solution.py:196
  151.8 15.3 %collective-permute-done.14 = bf16[256,1536]{1,0:T(8,128)(2,1)} collective-permute-done((bf16[256,1536]{1,0:T(8,128)(2,1)}, bf16[256,1536]{1,0:T(8,128)(2,1)}, u32[]{:S(2)}, u32[]{:S(2)}) %collective-permute-start.14) | collective-permute-done | bytes 786464 | tf_op jit(solution)/shard_map/ppermute | solution.py:204
  167.1 4.1 %fusion.8 = bf16[256,1536]{1,0:T(8,128)(2,1)} fusion(bf16[2,2,256,1536]{3,2,1,0:T(8,128)(2,1)S(1)} %bitcast.190, bf16[256,1536]{1,0:T(8,128)(2,1)} %collective-permute-done.15, bf16[256,1536]{1,0:T(8,128)(2,1)} %collective-permute-done.14, bf16[256,1536]{1,0:T(8,128)(2,1)} %collective-permute-done.12, bf16[256,1536]{1,0:T(8,128)(2,1)} %collective-permute-done.11, ...), kind=kOutput, calls=%fused_computation.31 | convolution fusion | flops 809107456 | bytes 9175044 | tf_op jit(solution)/shard_map/deti,deic->tc/dot_general | solution.py:179
  (81 shorter events, 19.2 us)
Async XLA Ops:
  4.1 14.5 %copy-start.3 = (bf16[256,1024]{1,0:T(8,128)(2,1)S(1)}, bf16[256,1024]{1,0:T(8,128)(2,1)}, u32[]{:S(2)}) copy-start(bf16[256,1024]{1,0:T(8,128)(2,1)} %param.9) | copy-start | bytes 1572868
  7.0 14.5 %collective-permute-start.2 = (bf16[8,16640]{1,0:T(8,128)(2,1)S(1)}, bf16[8,16640]{1,0:T(8,128)(2,1)}, u32[]{:S(2)}, u32[]{:S(2)}) collective-permute-start(bf16[8,16640]{1,0:T(8,128)(2,1)S(1)} %pad_maximum_fusion.3), channel_id=1, source_target_pairs={{0,12},{1,13},{2,14},{3,15},{16,28},{17,29},{18,30},{19,31}} | collective-permute-start | bytes 798728 | tf_op jit(solution)/shard_map/ppermute | solution.py:95
  14.7 17.6 %collective-permute-start.1 = (bf16[8,16640]{1,0:T(8,128)(2,1)S(1)}, bf16[8,16640]{1,0:T(8,128)(2,1)S(1)}, u32[]{:S(2)}, u32[]{:S(2)}) collective-permute-start(bf16[8,16640]{1,0:T(8,128)(2,1)S(1)} %pad_maximum_fusion.3), channel_id=1, source_target_pairs={{0,8},{4,12},{1,9},{5,13},{2,10},{6,14},{3,11},{7,15},{16,24},{20,... | collective-permute-start | bytes 798728 | tf_op jit(solution)/shard_map/ppermute | solution.py:95
  16.0 15.1 %collective-permute-start = (bf16[8,16640]{1,0:T(8,128)(2,1)S(1)}, bf16[8,16640]{1,0:T(8,128)(2,1)}, u32[]{:S(2)}, u32[]{:S(2)}) collective-permute-start(bf16[8,16640]{1,0:T(8,128)(2,1)S(1)} %pad_maximum_fusion.3), channel_id=1, source_target_pairs={{0,4},{4,8},{8,12},{1,5},{5,9},{9,13},{2,6},{6,10},{10,14},{3,7},{... | collective-permute-start | bytes 798728 | tf_op jit(solution)/shard_map/ppermute | solution.py:95
  18.8 2.5 %copy-start.4 = (bf16[256,1024]{1,0:T(8,128)(2,1)S(1)}, bf16[256,1024]{1,0:T(8,128)(2,1)}, u32[]{:S(2)}) copy-start(bf16[256,1024]{1,0:T(8,128)(2,1)} %param.12) | copy-start | bytes 1572868
  33.5 2.1 %copy-start.6 = (f32[1024]{0:T(1024)S(1)}, f32[1024]{0:T(1024)}, u32[]{:S(2)}) copy-start(f32[1024]{0:T(1024)} %param.15) | copy-start | bytes 12292
  35.9 34.3 %copy-start.5 = (s32[1536]{0:T(1024)S(1)}, s32[1536]{0:T(1024)}, u32[]{:S(2)}) copy-start(s32[1536]{0:T(1024)} %param.17) | copy-start | bytes 18436
  36.0 7.2 %collective-permute-start.3 = (bf16[256,2,256]{0,2,1:T(8,128)(2,1)S(1)}, bf16[256,2,256]{0,2,1:T(8,128)(2,1)S(1)}, u32[]{:S(2)}, u32[]{:S(2)}) collective-permute-start(bf16[256,2,256]{0,2,1:T(8,128)(2,1)S(1)} %get-tuple-element.32), channel_id=1, source_target_pairs={{0,2},{1,3},{2,0},{3,1},{4,6},{5,7},{6,4},{7,5},{8,10},{9,11},{10,... | collective-permute-start | bytes 786440 | tf_op jit(solution)/shard_map/ppermute | solution.py:129
  43.8 14.5 %collective-permute-start.7 = (bf16[256,256]{1,0:T(8,128)(2,1)S(1)}, bf16[256,256]{1,0:T(8,128)(2,1)S(1)}, u32[]{:S(2)}, u32[]{:S(2)}) collective-permute-start(bf16[256,256]{1,0:T(8,128)(2,1)S(1)} %bitcast.203), channel_id=1, source_target_pairs={{0,9},{1,13},{2,3},{3,7},{4,0},{5,4},{6,10},{7,14},{8,1},{9,5},{10... | collective-permute-start | bytes 393224 | tf_op jit(solution)/shard_map/ppermute | solution.py:140
  52.9 12.7 %collective-permute-start.6 = (bf16[256,256]{1,0:T(8,128)(2,1)S(1)}, bf16[256,256]{1,0:T(8,128)(2,1)S(1)}, u32[]{:S(2)}, u32[]{:S(2)}) collective-permute-start(bf16[256,256]{1,0:T(8,128)(2,1)S(1)} %bitcast.202), channel_id=1, source_target_pairs={{0,8},{1,12},{2,2},{3,6},{4,9},{5,13},{6,3},{7,7},{8,0},{9,4},{10,... | collective-permute-start | bytes 393224 | tf_op jit(solution)/shard_map/ppermute | solution.py:140
  56.0 9.6 %collective-permute-start.5 = (bf16[256,256]{1,0:T(8,128)(2,1)S(1)}, bf16[256,256]{1,0:T(8,128)(2,1)S(1)}, u32[]{:S(2)}, u32[]{:S(2)}) collective-permute-start(bf16[256,256]{1,0:T(8,128)(2,1)S(1)} %bitcast.201), channel_id=1, source_target_pairs={{0,1},{1,5},{2,11},{3,15},{4,8},{5,12},{6,2},{7,6},{8,9},{9,13},{1... | collective-permute-start | bytes 393224 | tf_op jit(solution)/shard_map/ppermute | solution.py:140
  57.6 7.9 %collective-permute-start.4 = (bf16[256,256]{1,0:T(8,128)(2,1)S(1)}, bf16[256,256]{1,0:T(8,128)(2,1)S(1)}, u32[]{:S(2)}, u32[]{:S(2)}) collective-permute-start(bf16[256,256]{1,0:T(8,128)(2,1)S(1)} %bitcast.200), channel_id=1, source_target_pairs={{0,0},{1,4},{2,10},{3,14},{4,1},{5,5},{6,11},{7,15},{8,8},{9,12},{... | collective-permute-start | bytes 393224 | tf_op jit(solution)/shard_map/ppermute | solution.py:140
  66.2 16.4 %copy-start.2 = (bf16[1024,1536]{1,0:T(8,128)(2,1)S(1)}, bf16[1024,1536]{1,0:T(8,128)(2,1)}, u32[]{:S(2)}) copy-start(bf16[1024,1536]{1,0:T(8,128)(2,1)} %param.16) | copy-start | bytes 9437188
  66.4 14.8 %collective-permute-start.8 = (bf16[4,256,256]{2,1,0:T(8,128)(2,1)S(1)}, bf16[4,256,256]{2,1,0:T(8,128)(2,1)S(1)}, u32[]{:S(2)}, u32[]{:S(2)}) collective-permute-start(bf16[4,256,256]{2,1,0:T(8,128)(2,1)S(1)} %broadcast_select_fusion.1), channel_id=1, source_target_pairs={{0,2},{1,3},{2,0},{3,1},{4,6},{5,7},{6,4},{7,5},{8,10},{9,11},{10,... | collective-permute-start | bytes 1572872 | tf_op jit(solution)/shard_map/ppermute | solution.py:166
  82.6 6.3 %collective-permute-start.9 = (bf16[2,4,256,256]{3,2,0,1:T(8,128)(2,1)}, bf16[2,4,256,256]{3,2,0,1:T(8,128)(2,1)}, u32[]{:S(2)}, u32[]{:S(2)}) collective-permute-start(bf16[2,4,256,256]{3,2,0,1:T(8,128)(2,1)} %get-tuple-element.26), channel_id=1, source_target_pairs={{0,1},{1,0},{2,3},{3,2},{4,5},{5,4},{6,7},{7,6},{8,9},{9,8},{10,11... | collective-permute-start | bytes 3145736 | tf_op jit(solution)/shard_map/ppermute | solution.py:168
  86.6 2.4 %copy-start = (bf16[2,1,4,256,256]{4,3,1,0,2:T(8,128)(2,1)S(1)}, bf16[2,1,4,256,256]{4,3,1,0,2:T(8,128)(2,1)}, u32[]{:S(2)}) copy-start(bf16[2,1,4,256,256]{4,3,1,0,2:T(8,128)(2,1)} %get-tuple-element.27) | copy-start | bytes 3145732
  91.8 19.3 %collective-permute-start.10 = (bf16[256,1536]{1,0:T(8,128)(2,1)}, bf16[256,1536]{1,0:T(8,128)(2,1)}, u32[]{:S(2)}, u32[]{:S(2)}) collective-permute-start(bf16[256,1536]{1,0:T(8,128)(2,1)} %fusion.9), channel_id=1, source_target_pairs={{0,4},{4,8},{1,5},{5,9},{2,6},{6,10},{3,7},{7,11},{16,20},{20,24},... | collective-permute-start | bytes 2359304 | tf_op jit(solution)/shard_map/ppermute | solution.py:187
  97.1 27.1 %collective-permute-start.13 = (bf16[256,1536]{1,0:T(8,128)(2,1)}, bf16[256,1536]{1,0:T(8,128)(2,1)}, u32[]{:S(2)}, u32[]{:S(2)}) collective-permute-start(bf16[256,1536]{1,0:T(8,128)(2,1)} %fusion.11), channel_id=1, source_target_pairs={{12,8},{8,4},{13,9},{9,5},{14,10},{10,6},{15,11},{11,7},{28,24},{2... | collective-permute-start | bytes 2359304 | tf_op jit(solution)/shard_map/ppermute | solution.py:190
  98.6 17.8 %copy-start.1 = (bf16[2,1,4,256,256]{4,3,1,0,2:T(8,128)(2,1)S(1)}, bf16[2,1,4,256,256]{4,3,1,0,2:T(8,128)(2,1)}, u32[]{:S(2)}) copy-start(bf16[2,1,4,256,256]{4,3,1,0,2:T(8,128)(2,1)} %get-tuple-element.27) | copy-start | bytes 3145732
  114.3 19.5 %collective-permute-start.12 = (bf16[256,1536]{1,0:T(8,128)(2,1)}, bf16[256,1536]{1,0:T(8,128)(2,1)}, u32[]{:S(2)}, u32[]{:S(2)}) collective-permute-start(bf16[256,1536]{1,0:T(8,128)(2,1)} %fusion.14), channel_id=1, source_target_pairs={{0,12},{1,13},{2,14},{3,15},{16,28},{17,29},{18,30},{19,31}} | collective-permute-start | bytes 2359304 | tf_op jit(solution)/shard_map/ppermute | solution.py:193
  119.6 30.2 %collective-permute-start.11 = (bf16[256,1536]{1,0:T(8,128)(2,1)}, bf16[256,1536]{1,0:T(8,128)(2,1)}, u32[]{:S(2)}, u32[]{:S(2)}) collective-permute-start(bf16[256,1536]{1,0:T(8,128)(2,1)} %fusion.7), channel_id=1, source_target_pairs={{0,4},{4,8},{8,12},{1,5},{5,9},{9,13},{2,6},{6,10},{10,14},{3,7},{... | collective-permute-start | bytes 2359304 | tf_op jit(solution)/shard_map/ppermute | solution.py:199
  127.3 24.5 %collective-permute-start.15 = (bf16[256,1536]{1,0:T(8,128)(2,1)}, bf16[256,1536]{1,0:T(8,128)(2,1)}, u32[]{:S(2)}, u32[]{:S(2)}) collective-permute-start(bf16[256,1536]{1,0:T(8,128)(2,1)} %fusion.13), channel_id=1, source_target_pairs={{12,0},{13,1},{14,2},{15,3},{28,16},{29,17},{30,18},{31,19}} | collective-permute-start | bytes 2359304 | tf_op jit(solution)/shard_map/ppermute | solution.py:196
  131.7 35.4 %collective-permute-start.14 = (bf16[256,1536]{1,0:T(8,128)(2,1)}, bf16[256,1536]{1,0:T(8,128)(2,1)}, u32[]{:S(2)}, u32[]{:S(2)}) collective-permute-start(bf16[256,1536]{1,0:T(8,128)(2,1)} %fusion.6), channel_id=1, source_target_pairs={{12,8},{8,4},{4,0},{13,9},{9,5},{5,1},{14,10},{10,6},{6,2},{15,11}... | collective-permute-start | bytes 2359304 | tf_op jit(solution)/shard_map/ppermute | solution.py:204

commit v14 on v10

--- a/solution.py
+++ b/solution.py
@@ -192,8 +192,13 @@
             bf(partial_for(jnp.clip(s_me - 2, 0, 3))), "seq", [(3, 2), (2, 1)]
         )
         far_l = lax.ppermute(bf(partial_for(jnp.int32(0))), "seq", [(3, 0)])
+        own_part = partial_for(s_me)
         last_r = lax.ppermute(
-            bf(partial_for(jnp.clip(s_me + 1, 0, 3)) + near_r.astype(jnp.float32)),
+            bf(
+                partial_for(jnp.clip(s_me + 1, 0, 3))
+                + near_r.astype(jnp.float32)
+                + own_part * 0.0
+            ),
             "seq",
             [(0, 1), (1, 2), (2, 3)],
         )
@@ -202,7 +207,7 @@
             "seq",
             [(3, 2), (2, 1), (1, 0)],
         )
-        total = partial_for(s_me)
+        total = own_part
         for came in (last_r, far_r, last_l, far_l):
             total = total + came.astype(jnp.float32)
         return total.astype(jnp.bfloat16)

time: 162 us -> 157 us (0.969)
  matrix products: 23.5 us -> 11.1 us
  waiting for transfers between devices: 53.9 us -> 59.4 us
  local copies, waits for them, and re-layouts: 7.54 us -> 9.99 us
    dot_general x7, matrix products: 19.3 us -> 6.89 us  [partial_for(): jnp.einsum('deti,deic->tc', rows, w_perm, preferred_element_type=jnp.floa...]
    ppermute x1, waiting for transfers between devices: 2.45 us -> 7.71 us  [per_device(): lax.ppermute(bf(partial_for(jnp.clip(s_me + 2, 0, 3))), 'seq', [(0, 1), (...]
    ppermute x1, waiting for transfers between devices: 5.83 us -> 9.94 us  [per_device(): lax.ppermute(bf(partial_for(jnp.clip(s_me + 1, 0, 3)) + near_r.astype(jnp...]
    ppermute x1, waiting for transfers between devices: 13.6 us -> 9.74 us  [per_device(): lax.ppermute(bf(partial_for(jnp.clip(s_me - 1, 0, 3)) + near_l.astype(jnp...]
    gather x1, local copies, waits for them, and re-layouts: 2.39 us -> 4.31 us  [per_device(): jnp.take(weights.reshape(n_mdl, piece, cols_w), mu_tab.reshape(-1), axis=0)]
    unnamed x16 -> x14, local copies, waits for them, and re-layouts: 2.99 us -> 3.51 us
  transfers between devices with their start and end apart: 16 -> 16, of which waited for: 9 -> 9; matrix products, arithmetic and copies ran while one was open for 15% -> 12% of each run, Pallas kernels for 0% -> 0%
where the time goes in v14:
time: 157 us; the launch traced here: 156 us
  starting transfers between devices  60.7 us (39%)
  waiting for transfers between devices  59.4 us (38%)
  other arithmetic  14.7 us (9%)
  matrix products  11.1 us (7%)
  local copies, waits for them, and re-layouts  9.99 us (6%)
    ppermute x1, starting transfers between devices, per_device(): lax.ppermute(bf(partial_for(jnp.clip(s_me + 1, 0, 3)) + near_r.astype(jnp...  19.6 us
    ppermute x4, starting transfers between devices, per_device(): received.append(lax.ppermute(item, ('seq', 'mdl'), perm))  15 us
    ppermute x1, waiting for transfers between devices, per_device(): got.append(lax.ppermute(x, 'mdl', perm))  13 us
    ppermute x3, starting transfers between devices, per_device(): came = lax.ppermute(packed, 'seq', [(z, z + d) for z in range(n_seq - d)])  11.5 us
    ppermute x1, waiting for transfers between devices, per_device(): lax.ppermute(bf(partial_for(jnp.clip(s_me + 1, 0, 3)) + near_r.astype(jnp...  9.94 us
    ppermute x1, waiting for transfers between devices, per_device(): lax.ppermute(bf(partial_for(jnp.clip(s_me - 1, 0, 3)) + near_l.astype(jnp...  9.74 us
    ppermute x1, waiting for transfers between devices, per_device(): lax.ppermute(bf(partial_for(jnp.clip(s_me + 2, 0, 3))), 'seq', [(0, 1), (...  7.71 us
    ppermute x4, waiting for transfers between devices, per_device(): received.append(lax.ppermute(item, ('seq', 'mdl'), perm))  7.49 us
  transfers between devices with their start and end apart: 16, of which 9 were waited for; matrix products, arithmetic and copies ran while one was open for 12% of the time, Pallas kernels for 0%

profile of v14, /device:TPU:0, one launch (start us, length us, event | category | flops | bytes accessed | tf_op | source)
XLA Modules:
  0.0 156.4 jit_solution(9074033525232990642)
XLA Ops:
  0.0 1.2 reduce-window.6
  1.8 1.0 fusion.114
  2.8 1.2 copy.74
  4.1 1.2 copy.76
  7.0 5.6 %collective-permute-start = (bf16[8,16640]{1,0:T(8,128)(2,1)S(1)}, bf16[8,16640]{1,0:T(8,128)(2,1)}, u32[]{:S(2)}, u32[]{:S(2)}) collective-permute-start(bf16[8,16640]{1,0:T(8,128)(2,1)S(1)} %pad_maximum_fusion.3), channel_id=1, source_target_pairs={{0,4},{4,8},{8,12},{1,5},{5,9},{9,13},{2,6},{6,10},{10,14},{3,7},{... | collective-permute-start | bytes 798728 | tf_op jit(solution)/shard_map/ppermute | solution.py:95
  12.6 3.8 %collective-permute-start.1 = (bf16[8,16640]{1,0:T(8,128)(2,1)S(1)}, bf16[8,16640]{1,0:T(8,128)(2,1)S(1)}, u32[]{:S(2)}, u32[]{:S(2)}) collective-permute-start(bf16[8,16640]{1,0:T(8,128)(2,1)S(1)} %pad_maximum_fusion.3), channel_id=1, source_target_pairs={{0,8},{4,12},{1,9},{5,13},{2,10},{6,14},{3,11},{7,15},{16,24},{20,... | collective-permute-start | bytes 798728 | tf_op jit(solution)/shard_map/ppermute | solution.py:95
  16.4 2.0 %collective-permute-start.2 = (bf16[8,16640]{1,0:T(8,128)(2,1)S(1)}, bf16[8,16640]{1,0:T(8,128)(2,1)}, u32[]{:S(2)}, u32[]{:S(2)}) collective-permute-start(bf16[8,16640]{1,0:T(8,128)(2,1)S(1)} %pad_maximum_fusion.3), channel_id=1, source_target_pairs={{0,12},{1,13},{2,14},{3,15},{16,28},{17,29},{18,30},{19,31}} | collective-permute-start | bytes 798728 | tf_op jit(solution)/shard_map/ppermute | solution.py:95
  19.3 1.9 %fusion.10 = f32[1,256,8,128]{1,3,2,0:T(8,128)} fusion(bf16[256,8,128]{0,2,1:T(8,128)(2,1)S(1)} %bitcast.190, bf16[256,8,128]{0,2,1:T(8,128)(2,1)S(1)} %bitcast.187, bf16[256,8,128]{0,2,1:T(8,128)(2,1)S(1)} %bitcast.192, f32[8,256]{1,0:T(8,128)S(1)} %bitcast_add_fusion.2, pred[256,256]{1,0:T(8,128)(4,1)S(1)} %iota_compare_fusion), kind=kOutput, calls=%fused_computation.35 | convolution fusion | flops 271056896 | bytes 2695168 | tf_op jit(solution)/shard_map/hbij,bjhd->bihd/dot_general | solution.py:63
  22.7 1.7 %collective-permute-done.1 = bf16[8,16640]{1,0:T(8,128)(2,1)S(1)} collective-permute-done((bf16[8,16640]{1,0:T(8,128)(2,1)S(1)}, bf16[8,16640]{1,0:T(8,128)(2,1)S(1)}, u32[]{:S(2)}, u32[]{:S(2)}) %collective-permute-start.1) | collective-permute-done | bytes 266272 | tf_op jit(solution)/shard_map/ppermute | solution.py:95
  24.7 4.3 %collective-permute-done.2 = bf16[8,16640]{1,0:T(8,128)(2,1)} collective-permute-done((bf16[8,16640]{1,0:T(8,128)(2,1)S(1)}, bf16[8,16640]{1,0:T(8,128)(2,1)}, u32[]{:S(2)}, u32[]{:S(2)}) %collective-permute-start.2) | collective-permute-done | bytes 266272 | tf_op jit(solution)/shard_map/ppermute | solution.py:95
  31.1 2.0 %multiply_reduce_fusion = (f32[256,8]{0,1:T(8,128)S(1)}, f32[1,256,8,128]{1,3,2,0:T(8,128)S(1)}) fusion(f32[1,256,8,128]{1,3,2,0:T(8,128)} %fusion.10, bf16[256,8,128]{0,2,1:T(8,128)(2,1)S(1)} %bitcast.188, f32[8,128,128]{1,2,0:T(8,128)S(1)} %copy.83, f32[8,128,128]{1,2,0:T(8,128)S(1)} %copy.82, f32[8,128,128]{1,2,0:T(8,128)S(1)} %copy.81, ...), kind=kOutput, calls=%fused_computation.56 | convolution fusion | flops 404355072 | bytes 4210784 | tf_op jit(solution)/shard_map/bihd,bhde->bihe/dot_general | solution.py:105
  34.1 1.6 collective-permute-start.3
  35.8 5.5 %collective-permute-done.3 = bf16[256,2,256]{0,2,1:T(8,128)(2,1)S(1)} collective-permute-done((bf16[256,2,256]{0,2,1:T(8,128)(2,1)S(1)}, bf16[256,2,256]{0,2,1:T(8,128)(2,1)S(1)}, u32[]{:S(2)}, u32[]{:S(2)}) %collective-permute-start.3) | collective-permute-done | bytes 262176 | tf_op jit(solution)/shard_map/ppermute | solution.py:129
  42.5 8.9 %collective-permute-start.5 = (bf16[256,256]{1,0:T(8,128)(2,1)S(1)}, bf16[256,256]{1,0:T(8,128)(2,1)S(1)}, u32[]{:S(2)}, u32[]{:S(2)}) collective-permute-start(bf16[256,256]{1,0:T(8,128)(2,1)S(1)} %bitcast.196), channel_id=1, source_target_pairs={{0,1},{1,5},{2,11},{3,15},{4,8},{5,12},{6,2},{7,6},{8,9},{9,13},{1... | collective-permute-start | bytes 393224 | tf_op jit(solution)/shard_map/ppermute | solution.py:140
  51.5 5.3 %collective-permute-start.6 = (bf16[256,256]{1,0:T(8,128)(2,1)S(1)}, bf16[256,256]{1,0:T(8,128)(2,1)S(1)}, u32[]{:S(2)}, u32[]{:S(2)}) collective-permute-start(bf16[256,256]{1,0:T(8,128)(2,1)S(1)} %bitcast.197), channel_id=1, source_target_pairs={{0,8},{1,12},{2,2},{3,6},{4,9},{5,13},{6,3},{7,7},{8,0},{9,4},{10,... | collective-permute-start | bytes 393224 | tf_op jit(solution)/shard_map/ppermute | solution.py:140
  57.0 1.9 %collective-permute-done.5 = bf16[256,256]{1,0:T(8,128)(2,1)S(1)} collective-permute-done((bf16[256,256]{1,0:T(8,128)(2,1)S(1)}, bf16[256,256]{1,0:T(8,128)(2,1)S(1)}, u32[]{:S(2)}, u32[]{:S(2)}) %collective-permute-start.5) | collective-permute-done | bytes 131104 | tf_op jit(solution)/shard_map/ppermute | solution.py:140
  58.9 5.6 %collective-permute-done.6 = bf16[256,256]{1,0:T(8,128)(2,1)S(1)} collective-permute-done((bf16[256,256]{1,0:T(8,128)(2,1)S(1)}, bf16[256,256]{1,0:T(8,128)(2,1)S(1)}, u32[]{:S(2)}, u32[]{:S(2)}) %collective-permute-start.6) | collective-permute-done | bytes 131104 | tf_op jit(solution)/shard_map/ppermute | solution.py:140
  65.5 13.0 %collective-permute-done.8 = bf16[4,256,256]{2,1,0:T(8,128)(2,1)S(1)} collective-permute-done((bf16[4,256,256]{2,1,0:T(8,128)(2,1)S(1)}, bf16[4,256,256]{2,1,0:T(8,128)(2,1)S(1)}, u32[]{:S(2)}, u32[]{:S(2)}) %collective-permute-start.8) | collective-permute-done | bytes 524320 | tf_op jit(solution)/shard_map/ppermute | solution.py:166
  78.6 1.5 collective-permute-start.9
  80.2 2.6 %multiply_convert_fusion = bf16[1024,1536]{1,0:T(8,128)(2,1)} fusion(bf16[1024,1536]{1,0:T(8,128)(2,1)S(1)} %copy-done, f32[1536]{0:T(1024)S(1)} %select_add_fusion), kind=kLoop, calls=%fused_computation.2 | loop fusion | flops 11010048 | bytes 6297600 | tf_op jit(solution)/shard_map/convert_element_type | solution.py:20
  82.9 4.3 %gather_fusion.1 = bf16[4,256,1536]{2,1,0:T(8,128)(2,1)} fusion(bf16[4,256,1536]{2,1,0:T(8,128)(2,1)} %bitcast.186, s32[1024]{0:T(1024)S(1)} %pad_clamp_fusion), kind=kCustom, calls=%fused_computation.1 | custom fusion | bytes 6291472 | tf_op jit(solution)/shard_map/jit(_take)/gather | solution.py:173
  87.2 2.3 %broadcast_select_fusion = bf16[4,256,1536]{2,1,0:T(8,128)(2,1)S(1)} fusion(bf16[4,256,1536]{2,1,0:T(8,128)(2,1)} %gather_fusion.1, pred[4]{0:T(512)(128)(4,1)S(1)} %get-tuple-element.42), kind=kLoop, calls=%fused_computation.15 | loop fusion | flops 1572864 | bytes 6291460 | tf_op jit(solution)/shard_map/jit(_take)/select_n | solution.py:173
  91.5 3.1 %collective-permute-start.10 = (bf16[256,1536]{1,0:T(8,128)(2,1)S(1)}, bf16[256,1536]{1,0:T(8,128)(2,1)S(1)}, u32[]{:S(2)}, u32[]{:S(2)}) collective-permute-start(bf16[256,1536]{1,0:T(8,128)(2,1)S(1)} %fusion.5), channel_id=1, source_target_pairs={{0,4},{4,8},{1,5},{5,9},{2,6},{6,10},{3,7},{7,11},{16,20},{20,24},... | collective-permute-start | bytes 2359304 | tf_op jit(solution)/shard_map/ppermute | solution.py:187
  97.4 5.0 %collective-permute-start.12 = (bf16[256,1536]{1,0:T(8,128)(2,1)S(1)}, bf16[256,1536]{1,0:T(8,128)(2,1)S(1)}, u32[]{:S(2)}, u32[]{:S(2)}) collective-permute-start(bf16[256,1536]{1,0:T(8,128)(2,1)S(1)} %fusion.6), channel_id=1, source_target_pairs={{0,12},{1,13},{2,14},{3,15},{16,28},{17,29},{18,30},{19,31}} | collective-permute-start | bytes 2359304 | tf_op jit(solution)/shard_map/ppermute | solution.py:190
  102.4 1.3 collective-permute-start.15
  104.7 7.7 %collective-permute-done.10 = bf16[256,1536]{1,0:T(8,128)(2,1)S(1)} collective-permute-done((bf16[256,1536]{1,0:T(8,128)(2,1)S(1)}, bf16[256,1536]{1,0:T(8,128)(2,1)S(1)}, u32[]{:S(2)}, u32[]{:S(2)}) %collective-permute-start.10) | collective-permute-done | bytes 786464 | tf_op jit(solution)/shard_map/ppermute | solution.py:187
  112.4 1.0 fusion.4
  113.4 19.6 %collective-permute-start.11 = (bf16[256,1536]{1,0:T(8,128)(2,1)S(1)}, bf16[256,1536]{1,0:T(8,128)(2,1)S(1)}, u32[]{:S(2)}, u32[]{:S(2)}) collective-permute-start(bf16[256,1536]{1,0:T(8,128)(2,1)S(1)} %fusion.4), channel_id=1, source_target_pairs={{0,4},{4,8},{8,12},{1,5},{5,9},{9,13},{2,6},{6,10},{10,14},{3,7},{... | collective-permute-start | bytes 2359304 | tf_op jit(solution)/shard_map/ppermute | solution.py:196
  134.0 1.3 collective-permute-start.14
  135.3 9.9 %collective-permute-done.11 = bf16[256,1536]{1,0:T(8,128)(2,1)S(1)} collective-permute-done((bf16[256,1536]{1,0:T(8,128)(2,1)S(1)}, bf16[256,1536]{1,0:T(8,128)(2,1)S(1)}, u32[]{:S(2)}, u32[]{:S(2)}) %collective-permute-start.11) | collective-permute-done | bytes 786464 | tf_op jit(solution)/shard_map/ppermute | solution.py:196
  145.3 9.7 %collective-permute-done.14 = bf16[256,1536]{1,0:T(8,128)(2,1)S(1)} collective-permute-done((bf16[256,1536]{1,0:T(8,128)(2,1)S(1)}, bf16[256,1536]{1,0:T(8,128)(2,1)S(1)}, u32[]{:S(2)}, u32[]{:S(2)}) %collective-permute-start.14) | collective-permute-done | bytes 786464 | tf_op jit(solution)/shard_map/ppermute | solution.py:205
  155.0 1.4 add_convert_fusion
  (78 shorter events, 17.3 us)
Async XLA Ops:
  5.6 12.9 %copy-start.1 = (bf16[256,1024]{1,0:T(8,128)(2,1)S(1)}, bf16[256,1024]{1,0:T(8,128)(2,1)}, u32[]{:S(2)}) copy-start(bf16[256,1024]{1,0:T(8,128)(2,1)} %param.9) | copy-start | bytes 1572868
  7.0 14.5 %collective-permute-start = (bf16[8,16640]{1,0:T(8,128)(2,1)S(1)}, bf16[8,16640]{1,0:T(8,128)(2,1)}, u32[]{:S(2)}, u32[]{:S(2)}) collective-permute-start(bf16[8,16640]{1,0:T(8,128)(2,1)S(1)} %pad_maximum_fusion.3), channel_id=1, source_target_pairs={{0,4},{4,8},{8,12},{1,5},{5,9},{9,13},{2,6},{6,10},{10,14},{3,7},{... | collective-permute-start | bytes 798728 | tf_op jit(solution)/shard_map/ppermute | solution.py:95
  12.6 11.8 %collective-permute-start.1 = (bf16[8,16640]{1,0:T(8,128)(2,1)S(1)}, bf16[8,16640]{1,0:T(8,128)(2,1)S(1)}, u32[]{:S(2)}, u32[]{:S(2)}) collective-permute-start(bf16[8,16640]{1,0:T(8,128)(2,1)S(1)} %pad_maximum_fusion.3), channel_id=1, source_target_pairs={{0,8},{4,12},{1,9},{5,13},{2,10},{6,14},{3,11},{7,15},{16,24},{20,... | collective-permute-start | bytes 798728 | tf_op jit(solution)/shard_map/ppermute | solution.py:95
  16.4 12.6 %collective-permute-start.2 = (bf16[8,16640]{1,0:T(8,128)(2,1)S(1)}, bf16[8,16640]{1,0:T(8,128)(2,1)}, u32[]{:S(2)}, u32[]{:S(2)}) collective-permute-start(bf16[8,16640]{1,0:T(8,128)(2,1)S(1)} %pad_maximum_fusion.3), channel_id=1, source_target_pairs={{0,12},{1,13},{2,14},{3,15},{16,28},{17,29},{18,30},{19,31}} | collective-permute-start | bytes 798728 | tf_op jit(solution)/shard_map/ppermute | solution.py:95
  19.3 2.0 %copy-start.2 = (bf16[256,1024]{1,0:T(8,128)(2,1)S(1)}, bf16[256,1024]{1,0:T(8,128)(2,1)}, u32[]{:S(2)}) copy-start(bf16[256,1024]{1,0:T(8,128)(2,1)} %param.12) | copy-start | bytes 1572868
  33.1 0.7 copy-start.4
  34.1 7.2 %collective-permute-start.3 = (bf16[256,2,256]{0,2,1:T(8,128)(2,1)S(1)}, bf16[256,2,256]{0,2,1:T(8,128)(2,1)S(1)}, u32[]{:S(2)}, u32[]{:S(2)}) collective-permute-start(bf16[256,2,256]{0,2,1:T(8,128)(2,1)S(1)} %get-tuple-element.32), channel_id=1, source_target_pairs={{0,2},{1,3},{2,0},{3,1},{4,6},{5,7},{6,4},{7,5},{8,10},{9,11},{10,... | collective-permute-start | bytes 786440 | tf_op jit(solution)/shard_map/ppermute | solution.py:129
  41.6 23.8 %copy-start.3 = (s32[1536]{0:T(1024)S(1)}, s32[1536]{0:T(1024)}, u32[]{:S(2)}) copy-start(s32[1536]{0:T(1024)} %param.17) | copy-start | bytes 18436
  41.7 15.3 %collective-permute-start.4 = (bf16[256,256]{1,0:T(8,128)(2,1)S(1)}, bf16[256,256]{1,0:T(8,128)(2,1)S(1)}, u32[]{:S(2)}, u32[]{:S(2)}) collective-permute-start(bf16[256,256]{1,0:T(8,128)(2,1)S(1)} %bitcast.195), channel_id=1, source_target_pairs={{0,0},{1,4},{2,10},{3,14},{4,1},{5,5},{6,11},{7,15},{8,8},{9,12},{... | collective-permute-start | bytes 393224 | tf_op jit(solution)/shard_map/ppermute | solution.py:140
  42.5 16.5 %collective-permute-start.5 = (bf16[256,256]{1,0:T(8,128)(2,1)S(1)}, bf16[256,256]{1,0:T(8,128)(2,1)S(1)}, u32[]{:S(2)}, u32[]{:S(2)}) collective-permute-start(bf16[256,256]{1,0:T(8,128)(2,1)S(1)} %bitcast.196), channel_id=1, source_target_pairs={{0,1},{1,5},{2,11},{3,15},{4,8},{5,12},{6,2},{7,6},{8,9},{9,13},{1... | collective-permute-start | bytes 393224 | tf_op jit(solution)/shard_map/ppermute | solution.py:140
  51.5 13.0 %collective-permute-start.6 = (bf16[256,256]{1,0:T(8,128)(2,1)S(1)}, bf16[256,256]{1,0:T(8,128)(2,1)S(1)}, u32[]{:S(2)}, u32[]{:S(2)}) collective-permute-start(bf16[256,256]{1,0:T(8,128)(2,1)S(1)} %bitcast.197), channel_id=1, source_target_pairs={{0,8},{1,12},{2,2},{3,6},{4,9},{5,13},{6,3},{7,7},{8,0},{9,4},{10,... | collective-permute-start | bytes 393224 | tf_op jit(solution)/shard_map/ppermute | solution.py:140
  56.9 7.6 %collective-permute-start.7 = (bf16[256,256]{1,0:T(8,128)(2,1)S(1)}, bf16[256,256]{1,0:T(8,128)(2,1)S(1)}, u32[]{:S(2)}, u32[]{:S(2)}) collective-permute-start(bf16[256,256]{1,0:T(8,128)(2,1)S(1)} %bitcast.198), channel_id=1, source_target_pairs={{0,9},{1,13},{2,3},{3,7},{4,0},{5,4},{6,10},{7,14},{8,1},{9,5},{10... | collective-permute-start | bytes 393224 | tf_op jit(solution)/shard_map/ppermute | solution.py:140
  65.3 13.2 %collective-permute-start.8 = (bf16[4,256,256]{2,1,0:T(8,128)(2,1)S(1)}, bf16[4,256,256]{2,1,0:T(8,128)(2,1)S(1)}, u32[]{:S(2)}, u32[]{:S(2)}) collective-permute-start(bf16[4,256,256]{2,1,0:T(8,128)(2,1)S(1)} %broadcast_select_fusion.1), channel_id=1, source_target_pairs={{0,2},{1,3},{2,0},{3,1},{4,6},{5,7},{6,4},{7,5},{8,10},{9,11},{10,... | collective-permute-start | bytes 1572872 | tf_op jit(solution)/shard_map/ppermute | solution.py:166
  65.4 14.8 %copy-start = (bf16[1024,1536]{1,0:T(8,128)(2,1)S(1)}, bf16[1024,1536]{1,0:T(8,128)(2,1)}, u32[]{:S(2)}) copy-start(bf16[1024,1536]{1,0:T(8,128)(2,1)} %param.16) | copy-start | bytes 9437188
  78.6 10.9 %collective-permute-start.9 = (bf16[2,4,256,256]{3,2,0,1:T(8,128)(2,1)S(1)}, bf16[2,4,256,256]{3,2,0,1:T(8,128)(2,1)S(1)}, u32[]{:S(2)}, u32[]{:S(2)}) collective-permute-start(bf16[2,4,256,256]{3,2,0,1:T(8,128)(2,1)S(1)} %get-tuple-element.27), channel_id=1, source_target_pairs={{0,1},{1,0},{2,3},{3,2},{4,5},{5,4},{6,7},{7,6},{8,9},{9,8},{10,11... | collective-permute-start | bytes 3145736 | tf_op jit(solution)/shard_map/ppermute | solution.py:168
  91.5 20.9 %collective-permute-start.10 = (bf16[256,1536]{1,0:T(8,128)(2,1)S(1)}, bf16[256,1536]{1,0:T(8,128)(2,1)S(1)}, u32[]{:S(2)}, u32[]{:S(2)}) collective-permute-start(bf16[256,1536]{1,0:T(8,128)(2,1)S(1)} %fusion.5), channel_id=1, source_target_pairs={{0,4},{4,8},{1,5},{5,9},{2,6},{6,10},{3,7},{7,11},{16,20},{20,24},... | collective-permute-start | bytes 2359304 | tf_op jit(solution)/shard_map/ppermute | solution.py:187
  95.5 37.5 %collective-permute-start.13 = (bf16[256,1536]{1,0:T(8,128)(2,1)S(1)}, bf16[256,1536]{1,0:T(8,128)(2,1)S(1)}, u32[]{:S(2)}, u32[]{:S(2)}) collective-permute-start(bf16[256,1536]{1,0:T(8,128)(2,1)S(1)} %fusion.7), channel_id=1, source_target_pairs={{12,8},{8,4},{13,9},{9,5},{14,10},{10,6},{15,11},{11,7},{28,24},{2... | collective-permute-start | bytes 2359304 | tf_op jit(solution)/shard_map/ppermute | solution.py:191
  97.4 37.9 %collective-permute-start.12 = (bf16[256,1536]{1,0:T(8,128)(2,1)S(1)}, bf16[256,1536]{1,0:T(8,128)(2,1)S(1)}, u32[]{:S(2)}, u32[]{:S(2)}) collective-permute-start(bf16[256,1536]{1,0:T(8,128)(2,1)S(1)} %fusion.6), channel_id=1, source_target_pairs={{0,12},{1,13},{2,14},{3,15},{16,28},{17,29},{18,30},{19,31}} | collective-permute-start | bytes 2359304 | tf_op jit(solution)/shard_map/ppermute | solution.py:190
  102.4 32.9 %collective-permute-start.15 = (bf16[256,1536]{1,0:T(8,128)(2,1)S(1)}, bf16[256,1536]{1,0:T(8,128)(2,1)S(1)}, u32[]{:S(2)}, u32[]{:S(2)}) collective-permute-start(bf16[256,1536]{1,0:T(8,128)(2,1)S(1)} %fusion.8), channel_id=1, source_target_pairs={{12,0},{13,1},{14,2},{15,3},{28,16},{29,17},{30,18},{31,19}} | collective-permute-start | bytes 2359304 | tf_op jit(solution)/shard_map/ppermute | solution.py:194
  113.4 31.8 %collective-permute-start.11 = (bf16[256,1536]{1,0:T(8,128)(2,1)S(1)}, bf16[256,1536]{1,0:T(8,128)(2,1)S(1)}, u32[]{:S(2)}, u32[]{:S(2)}) collective-permute-start(bf16[256,1536]{1,0:T(8,128)(2,1)S(1)} %fusion.4), channel_id=1, source_target_pairs={{0,4},{4,8},{8,12},{1,5},{5,9},{9,13},{2,6},{6,10},{10,14},{3,7},{... | collective-permute-start | bytes 2359304 | tf_op jit(solution)/shard_map/ppermute | solution.py:196
  134.0 21.0 %collective-permute-start.14 = (bf16[256,1536]{1,0:T(8,128)(2,1)S(1)}, bf16[256,1536]{1,0:T(8,128)(2,1)S(1)}, u32[]{:S(2)}, u32[]{:S(2)}) collective-permute-start(bf16[256,1536]{1,0:T(8,128)(2,1)S(1)} %fusion.3), channel_id=1, source_target_pairs={{12,8},{8,4},{4,0},{13,9},{9,5},{5,1},{14,10},{10,6},{6,2},{15,11}... | collective-permute-start | bytes 2359304 | tf_op jit(solution)/shard_map/ppermute | solution.py:205

commit v15 on v14

--- a/solution.py
+++ b/solution.py
@@ -160,6 +160,14 @@
     n_x = n_mdl // 2
     core = m_me % 2
     xi = m_me // 2
+    d_idx = jnp.arange(n_x)[:, None]
+    e_idx = jnp.arange(2)[None, :]
+    mu_tab = 2 * ((xi - d_idx) % n_x) + jnp.where(e_idx == 0, core, 1 - core)
+    w_perm = jnp.take(
+        weights.reshape(n_mdl, piece, cols_w), mu_tab.reshape(-1), axis=0
+    ).reshape(n_x, 2, piece, cols_w)
+    if n_seq == 4 and n_mdl == 4:
+        x = x + w_perm[0, 0, 0, 0] * jnp.bfloat16(0)
     got = [x]
     for d in range(1, n_x):
         perm = [(mu, ((mu // 2 + d) % n_x) * 2 + mu % 2) for mu in range(n_mdl)]
@@ -167,12 +175,6 @@
     own = jnp.stack(got)
     other = lax.ppermute(own, "mdl", [(mu, mu ^ 1) for mu in range(n_mdl)])
     gathered_x = jnp.stack([own, other], axis=1)
-    d_idx = jnp.arange(n_x)[:, None]
-    e_idx = jnp.arange(2)[None, :]
-    mu_tab = 2 * ((xi - d_idx) % n_x) + jnp.where(e_idx == 0, core, 1 - core)
-    w_perm = jnp.take(
-        weights.reshape(n_mdl, piece, cols_w), mu_tab.reshape(-1), axis=0
-    ).reshape(n_x, 2, piece, cols_w)
 
     def partial_for(target):
         rows = lax.dynamic_index_in_dim(gathered_x, target, 2, keepdims=False)

time: 157 us -> 160 us (1.019)
  starting transfers between devices: 60.7 us -> 40.1 us
  local copies, waits for them, and re-layouts: 9.99 us -> 22.2 us
  other arithmetic: 14.7 us -> 22.1 us
  matrix products: 11.1 us -> 13.2 us
    ppermute x1, starting transfers between devices: 19.6 us -> 4.44 us  [per_device(): lax.ppermute(bf(partial_for(jnp.clip(s_me + 1, 0, 3)) + near_r.astype(jnp...]
    ppermute x1, waiting for transfers between devices: 0.01 us -> 9.11 us  [per_device(): far_r = lax.ppermute(bf(partial_for(jnp.int32(3))), 'seq', [(0, 3)])]
    ppermute x3, waiting for transfers between devices: 6.02 us -> 0.01 us  [per_device(): came = lax.ppermute(packed, 'seq', [(z, z + d) for z in range(n_seq - d)])]
    ppermute x4, waiting for transfers between devices: 7.49 us -> 1.56 us  [per_device(): received.append(lax.ppermute(item, ('seq', 'mdl'), perm))]
    ppermute x1, waiting for transfers between devices: 9.74 us -> 4.81 us  [per_device(): lax.ppermute(bf(partial_for(jnp.clip(s_me - 1, 0, 3)) + near_l.astype(jnp...]
    ppermute x1, waiting for transfers between devices: 0.01 us -> 4.55 us  [per_device(): far_l = lax.ppermute(bf(partial_for(jnp.int32(0))), 'seq', [(3, 0)])]
    ppermute x4, starting transfers between devices: 15 us -> 10.5 us  [per_device(): received.append(lax.ppermute(item, ('seq', 'mdl'), perm))]
    another operation x5, local copies, waits for them, and re-layouts: 0.4 us -> 4.41 us
  transfers between devices with their start and end apart: 16 -> 16, of which waited for: 9 -> 8; matrix products, arithmetic and copies ran while one was open for 12% -> 20% of each run, Pallas kernels for 0% -> 0%
where the time goes in v15:
time: 160 us; the launch traced here: 159 us
  waiting for transfers between devices  59.7 us (37%)
  starting transfers between devices  40.1 us (25%)
  local copies, waits for them, and re-layouts  22.2 us (14%)
  other arithmetic  22.1 us (14%)
  matrix products  13.2 us (8%)
  between operations  1.8 us (1%)
    ppermute x1, waiting for transfers between devices, per_device(): got.append(lax.ppermute(x, 'mdl', perm))  13.5 us
    ppermute x1, waiting for transfers between devices, per_device(): lax.ppermute(bf(partial_for(jnp.clip(s_me + 1, 0, 3)) + near_r.astype(jnp...  11.5 us
    ppermute x3, starting transfers between devices, per_device(): came = lax.ppermute(packed, 'seq', [(z, z + d) for z in range(n_seq - d)])  11.4 us
    ppermute x4, starting transfers between devices, per_device(): received.append(lax.ppermute(item, ('seq', 'mdl'), perm))  10.5 us
    ppermute x1, waiting for transfers between devices, per_device(): far_r = lax.ppermute(bf(partial_for(jnp.int32(3))), 'seq', [(0, 3)])  9.11 us
    ppermute x1, waiting for transfers between devices, per_device(): lax.ppermute(bf(partial_for(jnp.clip(s_me + 2, 0, 3))), 'seq', [(0, 1), (...  8.37 us
    dot_general x7, matrix products, partial_for(): jnp.einsum('deti,deic->tc', rows, w_perm, preferred_element_type=jnp.floa...  6.88 us
    ppermute x1, waiting for transfers between devices, per_device(): came = lax.ppermute(away, 'mdl', [(mu, mu ^ 2) for mu in range(n_mdl)])  6.2 us
  transfers between devices with their start and end apart: 16, of which 8 were waited for; matrix products, arithmetic and copies ran while one was open for 20% of the time, Pallas kernels for 0%

profile of v15, /device:TPU:0, one launch (start us, length us, event | category | flops | bytes accessed | tf_op | source)
XLA Modules:
  0.0 159.0 jit_solution(10457172511448574089)
XLA Ops:
  8.2 5.6 %collective-permute-start = (bf16[8,16640]{1,0:T(8,128)(2,1)}, bf16[8,16640]{1,0:T(8,128)(2,1)}, u32[]{:S(2)}, u32[]{:S(2)}) collective-permute-start(bf16[8,16640]{1,0:T(8,128)(2,1)} %pad_maximum_fusion.3), channel_id=1, source_target_pairs={{0,4},{4,8},{8,12},{1,5},{5,9},{9,13},{2,6},{6,10},{10,14},{3,7},{... | collective-permute-start | bytes 798728 | tf_op jit(solution)/shard_map/ppermute | solution.py:95
  13.8 3.8 %collective-permute-start.1 = (bf16[8,16640]{1,0:T(8,128)(2,1)}, bf16[8,16640]{1,0:T(8,128)(2,1)S(1)}, u32[]{:S(2)}, u32[]{:S(2)}) collective-permute-start(bf16[8,16640]{1,0:T(8,128)(2,1)} %pad_maximum_fusion.3), channel_id=1, source_target_pairs={{0,8},{4,12},{1,9},{5,13},{2,10},{6,14},{3,11},{7,15},{16,24},{20,... | collective-permute-start | bytes 798728 | tf_op jit(solution)/shard_map/ppermute | solution.py:95
  17.6 2.0 %collective-permute-start.2 = (bf16[8,16640]{1,0:T(8,128)(2,1)}, bf16[8,16640]{1,0:T(8,128)(2,1)}, u32[]{:S(2)}, u32[]{:S(2)}) collective-permute-start(bf16[8,16640]{1,0:T(8,128)(2,1)} %pad_maximum_fusion.3), channel_id=1, source_target_pairs={{0,12},{1,13},{2,14},{3,15},{16,28},{17,29},{18,30},{19,31}} | collective-permute-start | bytes 798728 | tf_op jit(solution)/shard_map/ppermute | solution.py:95
  20.1 1.3 fusion.16
  21.5 2.8 %multiply_convert_fusion = bf16[1024,1536]{1,0:T(8,128)(2,1)S(1)} fusion(bf16[1024,1536]{1,0:T(8,128)(2,1)} %param.16, f32[1536]{0:T(1024)S(1)} %select_add_fusion.1), kind=kLoop, calls=%fused_computation.2 | loop fusion | flops 11010048 | bytes 6297600 | tf_op jit(solution)/shard_map/convert_element_type | solution.py:20
  24.3 3.3 %fusion.10 = f32[1,256,8,128]{1,3,2,0:T(8,128)} fusion(bf16[256,8,128]{0,2,1:T(8,128)(2,1)} %bitcast.196, bf16[256,8,128]{0,2,1:T(8,128)(2,1)} %bitcast.199, bf16[256,8,128]{0,2,1:T(8,128)(2,1)} %bitcast.198, f32[8,256]{1,0:T(8,128)S(1)} %bitcast_add_fusion.2, pred[256,256]{1,0:T(8,128)(4,1)S(1)} %iota_compare_fusion), kind=kOutput, calls=%fused_computation.35 | convolution fusion | flops 271056896 | bytes 2695168 | tf_op jit(solution)/shard_map/hbij,bjhd->bihd/dot_general | solution.py:63
  28.4 2.0 %copy.85 = bf16[256,1024]{0,1:T(8,128)(2,1)} copy(bf16[256,1024]{1,0:T(8,128)(2,1)} %param.12) | data formatting | bytes 1048576 | tf_op args[3]
  30.4 1.8 %multiply_bitcast_fusion = f32[8,128,128]{2,0,1:T(8,128)} fusion(bf16[8,16640]{1,0:T(8,128)(2,1)} %collective-permute-done, f32[]{:T(128)S(6)} %select_n.483), kind=kLoop, calls=%fused_computation.101 | loop fusion | flops 262144 | bytes 786436 | tf_op jit(solution)/shard_map/mul | solution.py:101
  32.2 2.1 %copy.82 = f32[8,128,128]{1,2,0:T(8,128)} copy(f32[8,128,128]{2,0,1:T(8,128)} %multiply_bitcast_fusion) | data formatting | bytes 1048576 | tf_op jit(solution)/shard_map/mul | solution.py:101
  35.1 2.1 %copy.81 = f32[8,128,128]{1,2,0:T(8,128)} copy(f32[8,128,128]{2,0,1:T(8,128)} %fusion.58) | data formatting | bytes 1048576 | tf_op jit(solution)/shard_map/reshape | solution.py:96
  37.1 1.8 %fusion.57 = f32[8,128,128]{2,0,1:T(8,128)} fusion(bf16[8,16640]{1,0:T(8,128)(2,1)} %collective-permute-done.2), kind=kLoop, calls=%fused_computation.105 | loop fusion | flops 131072 | bytes 786432 | tf_op jit(solution)/shard_map/reshape | solution.py:96
  38.9 2.0 %copy.83 = f32[8,128,128]{1,2,0:T(8,128)} copy(f32[8,128,128]{2,0,1:T(8,128)} %fusion.57) | data formatting | bytes 1048576 | tf_op jit(solution)/shard_map/reshape | solution.py:96
  41.8 2.6 %multiply_reduce_fusion = (f32[256,8]{0,1:T(8,128)S(1)}, f32[1,256,8,128]{1,3,2,0:T(8,128)S(1)}) fusion(f32[1,256,8,128]{1,3,2,0:T(8,128)} %fusion.10, bf16[256,8,128]{0,2,1:T(8,128)(2,1)} %bitcast.200, f32[8,128,128]{1,2,0:T(8,128)} %copy.83, f32[8,128,128]{1,2,0:T(8,128)} %copy.82, f32[8,128,128]{1,2,0:T(8,128)} %copy.81, f32[8]{0:T(128)S(1)} %get-tuple-element.14, ...), kind=kOutput, calls=%fused_computation.56 | convolution fusion | flops 404355072 | bytes 4210784 | tf_op jit(solution)/shard_map/bihd,bhde->bihe/dot_general | solution.py:105
  46.5 1.5 collective-permute-start.3
  48.1 6.2 %collective-permute-done.3 = bf16[256,2,256]{0,2,1:T(8,128)(2,1)} collective-permute-done((bf16[256,2,256]{0,2,1:T(8,128)(2,1)}, bf16[256,2,256]{0,2,1:T(8,128)(2,1)}, u32[]{:S(2)}, u32[]{:S(2)}) %collective-permute-start.3) | collective-permute-done | bytes 262176 | tf_op jit(solution)/shard_map/ppermute | solution.py:129
  54.3 1.8 %fusion.63 = (bf16[256,1,256]{0,2,1:T(8,128)(2,1)}, bf16[256,1,256]{0,2,1:T(8,128)(2,1)}, bf16[256,1,256]{0,2,1:T(8,128)(2,1)}, bf16[256,1,256]{0,2,1:T(8,128)(2,1)S(1)}) fusion(s32[]{:T(128)S(6)} %select_n.491, bf16[256,2,256]{0,2,1:T(8,128)(2,1)S(1)} %get-tuple-element.33, bf16[256,2,256]{0,2,1:T(8,128)(2,1)} %collective-permute-done.3, ...), kind=kLoop, calls=%fused_computation.113 | loop fusion | flops 262144 | bytes 1048592 | tf_op jit(solution)/shard_map/concatenate | solution.py:130
  59.5 4.0 %collective-permute-start.5 = (bf16[256,256]{1,0:T(8,128)(2,1)S(1)}, bf16[256,256]{1,0:T(8,128)(2,1)}, u32[]{:S(2)}, u32[]{:S(2)}) collective-permute-start(bf16[256,256]{1,0:T(8,128)(2,1)S(1)} %bitcast.204), channel_id=1, source_target_pairs={{0,1},{1,5},{2,11},{3,15},{4,8},{5,12},{6,2},{7,6},{8,9},{9,13},{1... | collective-permute-start | bytes 393224 | tf_op jit(solution)/shard_map/ppermute | solution.py:140
  63.5 1.6 %copy.88 = bf16[256,1,256]{2,0,1:T(8,128)(2,1)} copy(bf16[256,1,256]{0,2,1:T(8,128)(2,1)} %get-tuple-element.30) | data formatting | bytes 262144 | tf_op jit(solution)/shard_map/dynamic-slice.3
  65.1 5.2 %collective-permute-start.6 = (bf16[256,256]{1,0:T(8,128)(2,1)}, bf16[256,256]{1,0:T(8,128)(2,1)}, u32[]{:S(2)}, u32[]{:S(2)}) collective-permute-start(bf16[256,256]{1,0:T(8,128)(2,1)} %bitcast.205), channel_id=1, source_target_pairs={{0,8},{1,12},{2,2},{3,6},{4,9},{5,13},{6,3},{7,7},{8,0},{9,4},{10,... | collective-permute-start | bytes 393224 | tf_op jit(solution)/shard_map/ppermute | solution.py:140
  71.1 2.4 %gather_fusion.1 = bf16[4,256,1536]{2,1,0:T(8,128)(2,1)} fusion(bf16[4,256,1536]{2,1,0:T(8,128)(2,1)S(1)} %bitcast.193, s32[1024]{0:T(1024)S(1)} %pad_clamp_fusion), kind=kCustom, calls=%fused_computation.1 | custom fusion | bytes 6291472 | tf_op jit(solution)/shard_map/jit(_take)/gather | solution.py:166
  76.2 1.6 collective-permute-done.6
  80.0 13.5 %collective-permute-done.8 = bf16[4,256,256]{2,1,0:T(8,128)(2,1)S(1)} collective-permute-done((bf16[4,256,256]{2,1,0:T(8,128)(2,1)S(1)}, bf16[4,256,256]{2,1,0:T(8,128)(2,1)S(1)}, u32[]{:S(2)}, u32[]{:S(2)}) %collective-permute-start.8) | collective-permute-done | bytes 524320 | tf_op jit(solution)/shard_map/ppermute | solution.py:174
  94.4 2.3 %broadcast_select_fusion = bf16[4,256,1536]{2,1,0:T(8,128)(2,1)S(1)} fusion(bf16[4,256,1536]{2,1,0:T(8,128)(2,1)} %gather_fusion.1, pred[4]{0:T(512)(128)(4,1)S(1)} %get-tuple-element.42), kind=kLoop, calls=%fused_computation.15 | loop fusion | flops 1572864 | bytes 6291460 | tf_op jit(solution)/shard_map/jit(_take)/select_n | solution.py:166
  98.7 3.4 %collective-permute-start.10 = (bf16[256,1536]{1,0:T(8,128)(2,1)S(1)}, bf16[256,1536]{1,0:T(8,128)(2,1)S(1)}, u32[]{:S(2)}, u32[]{:S(2)}) collective-permute-start(bf16[256,1536]{1,0:T(8,128)(2,1)S(1)} %fusion.5), channel_id=1, source_target_pairs={{0,4},{4,8},{1,5},{5,9},{2,6},{6,10},{3,7},{7,11},{16,20},{20,24},... | collective-permute-start | bytes 2359304 | tf_op jit(solution)/shard_map/ppermute | solution.py:189
  104.9 4.3 %collective-permute-start.12 = (bf16[256,1536]{1,0:T(8,128)(2,1)S(1)}, bf16[256,1536]{1,0:T(8,128)(2,1)S(1)}, u32[]{:S(2)}, u32[]{:S(2)}) collective-permute-start(bf16[256,1536]{1,0:T(8,128)(2,1)S(1)} %fusion.6), channel_id=1, source_target_pairs={{0,12},{1,13},{2,14},{3,15},{16,28},{17,29},{18,30},{19,31}} | collective-permute-start | bytes 2359304 | tf_op jit(solution)/shard_map/ppermute | solution.py:192
  111.5 8.4 %collective-permute-done.10 = bf16[256,1536]{1,0:T(8,128)(2,1)S(1)} collective-permute-done((bf16[256,1536]{1,0:T(8,128)(2,1)S(1)}, bf16[256,1536]{1,0:T(8,128)(2,1)S(1)}, u32[]{:S(2)}, u32[]{:S(2)}) %collective-permute-start.10) | collective-permute-done | bytes 786464 | tf_op jit(solution)/shard_map/ppermute | solution.py:189
  120.9 4.4 %collective-permute-start.11 = (bf16[256,1536]{1,0:T(8,128)(2,1)S(1)}, bf16[256,1536]{1,0:T(8,128)(2,1)S(1)}, u32[]{:S(2)}, u32[]{:S(2)}) collective-permute-start(bf16[256,1536]{1,0:T(8,128)(2,1)S(1)} %fusion.4), channel_id=1, source_target_pairs={{0,4},{4,8},{8,12},{1,5},{5,9},{9,13},{2,6},{6,10},{10,14},{3,7},{... | collective-permute-start | bytes 2359304 | tf_op jit(solution)/shard_map/ppermute | solution.py:198
  127.7 9.1 %collective-permute-done.12 = bf16[256,1536]{1,0:T(8,128)(2,1)S(1)} collective-permute-done((bf16[256,1536]{1,0:T(8,128)(2,1)S(1)}, bf16[256,1536]{1,0:T(8,128)(2,1)S(1)}, u32[]{:S(2)}, u32[]{:S(2)}) %collective-permute-start.12) | collective-permute-done | bytes 786464 | tf_op jit(solution)/shard_map/ppermute | solution.py:192
  136.8 4.5 %collective-permute-done.15 = bf16[256,1536]{1,0:T(8,128)(2,1)S(1)} collective-permute-done((bf16[256,1536]{1,0:T(8,128)(2,1)S(1)}, bf16[256,1536]{1,0:T(8,128)(2,1)S(1)}, u32[]{:S(2)}, u32[]{:S(2)}) %collective-permute-start.15) | collective-permute-done | bytes 786464 | tf_op jit(solution)/shard_map/ppermute | solution.py:196
  141.3 11.5 %collective-permute-done.11 = bf16[256,1536]{1,0:T(8,128)(2,1)S(1)} collective-permute-done((bf16[256,1536]{1,0:T(8,128)(2,1)S(1)}, bf16[256,1536]{1,0:T(8,128)(2,1)S(1)}, u32[]{:S(2)}, u32[]{:S(2)}) %collective-permute-start.11) | collective-permute-done | bytes 786464 | tf_op jit(solution)/shard_map/ppermute | solution.py:198
  152.8 4.8 %collective-permute-done.14 = bf16[256,1536]{1,0:T(8,128)(2,1)S(1)} collective-permute-done((bf16[256,1536]{1,0:T(8,128)(2,1)S(1)}, bf16[256,1536]{1,0:T(8,128)(2,1)S(1)}, u32[]{:S(2)}, u32[]{:S(2)}) %collective-permute-start.14) | collective-permute-done | bytes 786464 | tf_op jit(solution)/shard_map/ppermute | solution.py:207
  157.6 1.4 add_convert_fusion
  (82 shorter events, 32.0 us)
Async XLA Ops:
  5.6 0.8 copy-start
  5.7 14.1 %copy-start.3 = (bf16[256,1024]{1,0:T(8,128)(2,1)S(1)}, bf16[256,1024]{1,0:T(8,128)(2,1)}, u32[]{:S(2)}) copy-start(bf16[256,1024]{1,0:T(8,128)(2,1)} %param.9) | copy-start | bytes 1572868
  6.2 0.8 copy-start.1
  6.2 13.8 %copy-start.4 = (s32[1536]{0:T(1024)S(1)}, s32[1536]{0:T(1024)}, u32[]{:S(2)}) copy-start(s32[1536]{0:T(1024)} %param.17) | copy-start | bytes 18436
  8.2 22.2 %collective-permute-start = (bf16[8,16640]{1,0:T(8,128)(2,1)}, bf16[8,16640]{1,0:T(8,128)(2,1)}, u32[]{:S(2)}, u32[]{:S(2)}) collective-permute-start(bf16[8,16640]{1,0:T(8,128)(2,1)} %pad_maximum_fusion.3), channel_id=1, source_target_pairs={{0,4},{4,8},{8,12},{1,5},{5,9},{9,13},{2,6},{6,10},{10,14},{3,7},{... | collective-permute-start | bytes 798728 | tf_op jit(solution)/shard_map/ppermute | solution.py:95
  13.8 20.4 %collective-permute-start.1 = (bf16[8,16640]{1,0:T(8,128)(2,1)}, bf16[8,16640]{1,0:T(8,128)(2,1)S(1)}, u32[]{:S(2)}, u32[]{:S(2)}) collective-permute-start(bf16[8,16640]{1,0:T(8,128)(2,1)} %pad_maximum_fusion.3), channel_id=1, source_target_pairs={{0,8},{4,12},{1,9},{5,13},{2,10},{6,14},{3,11},{7,15},{16,24},{20,... | collective-permute-start | bytes 798728 | tf_op jit(solution)/shard_map/ppermute | solution.py:95
  17.6 19.5 %collective-permute-start.2 = (bf16[8,16640]{1,0:T(8,128)(2,1)}, bf16[8,16640]{1,0:T(8,128)(2,1)}, u32[]{:S(2)}, u32[]{:S(2)}) collective-permute-start(bf16[8,16640]{1,0:T(8,128)(2,1)} %pad_maximum_fusion.3), channel_id=1, source_target_pairs={{0,12},{1,13},{2,14},{3,15},{16,28},{17,29},{18,30},{19,31}} | collective-permute-start | bytes 798728 | tf_op jit(solution)/shard_map/ppermute | solution.py:95
  44.4 1.0 copy-start.2
  44.4 1.0 copy-start.5
  46.5 7.8 %collective-permute-start.3 = (bf16[256,2,256]{0,2,1:T(8,128)(2,1)}, bf16[256,2,256]{0,2,1:T(8,128)(2,1)}, u32[]{:S(2)}, u32[]{:S(2)}) collective-permute-start(bf16[256,2,256]{0,2,1:T(8,128)(2,1)} %get-tuple-element.32), channel_id=1, source_target_pairs={{0,2},{1,3},{2,0},{3,1},{4,6},{5,7},{6,4},{7,5},{8,10},{9,11},{10,... | collective-permute-start | bytes 786440 | tf_op jit(solution)/shard_map/ppermute | solution.py:129
  57.2 19.0 %collective-permute-start.4 = (bf16[256,256]{1,0:T(8,128)(2,1)S(1)}, bf16[256,256]{1,0:T(8,128)(2,1)}, u32[]{:S(2)}, u32[]{:S(2)}) collective-permute-start(bf16[256,256]{1,0:T(8,128)(2,1)S(1)} %bitcast.203), channel_id=1, source_target_pairs={{0,0},{1,4},{2,10},{3,14},{4,1},{5,5},{6,11},{7,15},{8,8},{9,12},{... | collective-permute-start | bytes 393224 | tf_op jit(solution)/shard_map/ppermute | solution.py:140
  59.5 16.7 %collective-permute-start.5 = (bf16[256,256]{1,0:T(8,128)(2,1)S(1)}, bf16[256,256]{1,0:T(8,128)(2,1)}, u32[]{:S(2)}, u32[]{:S(2)}) collective-permute-start(bf16[256,256]{1,0:T(8,128)(2,1)S(1)} %bitcast.204), channel_id=1, source_target_pairs={{0,1},{1,5},{2,11},{3,15},{4,8},{5,12},{6,2},{7,6},{8,9},{9,13},{1... | collective-permute-start | bytes 393224 | tf_op jit(solution)/shard_map/ppermute | solution.py:140
  65.1 12.6 %collective-permute-start.6 = (bf16[256,256]{1,0:T(8,128)(2,1)}, bf16[256,256]{1,0:T(8,128)(2,1)}, u32[]{:S(2)}, u32[]{:S(2)}) collective-permute-start(bf16[256,256]{1,0:T(8,128)(2,1)} %bitcast.205), channel_id=1, source_target_pairs={{0,8},{1,12},{2,2},{3,6},{4,9},{5,13},{6,3},{7,7},{8,0},{9,4},{10,... | collective-permute-start | bytes 393224 | tf_op jit(solution)/shard_map/ppermute | solution.py:140
  71.1 6.6 %collective-permute-start.7 = (bf16[256,256]{1,0:T(8,128)(2,1)}, bf16[256,256]{1,0:T(8,128)(2,1)S(1)}, u32[]{:S(2)}, u32[]{:S(2)}) collective-permute-start(bf16[256,256]{1,0:T(8,128)(2,1)} %bitcast.206), channel_id=1, source_target_pairs={{0,9},{1,13},{2,3},{3,7},{4,0},{5,4},{6,10},{7,14},{8,1},{9,5},{10... | collective-permute-start | bytes 393224 | tf_op jit(solution)/shard_map/ppermute | solution.py:140
  79.5 13.9 %collective-permute-start.8 = (bf16[4,256,256]{2,1,0:T(8,128)(2,1)S(1)}, bf16[4,256,256]{2,1,0:T(8,128)(2,1)S(1)}, u32[]{:S(2)}, u32[]{:S(2)}) collective-permute-start(bf16[4,256,256]{2,1,0:T(8,128)(2,1)S(1)} %select_add_fusion), channel_id=1, source_target_pairs={{0,2},{1,3},{2,0},{3,1},{4,6},{5,7},{6,4},{7,5},{8,10},{9,11},{10,... | collective-permute-start | bytes 1572872 | tf_op jit(solution)/shard_map/ppermute | solution.py:174
  93.6 3.1 %collective-permute-start.9 = (bf16[2,4,256,256]{3,2,0,1:T(8,128)(2,1)S(1)}, bf16[2,4,256,256]{3,2,0,1:T(8,128)(2,1)S(1)}, u32[]{:S(2)}, u32[]{:S(2)}) collective-permute-start(bf16[2,4,256,256]{3,2,0,1:T(8,128)(2,1)S(1)} %get-tuple-element.27), channel_id=1, source_target_pairs={{0,1},{1,0},{2,3},{3,2},{4,5},{5,4},{6,7},{7,6},{8,9},{9,8},{10,11... | collective-permute-start | bytes 3145736 | tf_op jit(solution)/shard_map/ppermute | solution.py:176
  98.7 21.2 %collective-permute-start.10 = (bf16[256,1536]{1,0:T(8,128)(2,1)S(1)}, bf16[256,1536]{1,0:T(8,128)(2,1)S(1)}, u32[]{:S(2)}, u32[]{:S(2)}) collective-permute-start(bf16[256,1536]{1,0:T(8,128)(2,1)S(1)} %fusion.5), channel_id=1, source_target_pairs={{0,4},{4,8},{1,5},{5,9},{2,6},{6,10},{3,7},{7,11},{16,20},{20,24},... | collective-permute-start | bytes 2359304 | tf_op jit(solution)/shard_map/ppermute | solution.py:189
  103.0 22.3 %collective-permute-start.13 = (bf16[256,1536]{1,0:T(8,128)(2,1)S(1)}, bf16[256,1536]{1,0:T(8,128)(2,1)S(1)}, u32[]{:S(2)}, u32[]{:S(2)}) collective-permute-start(bf16[256,1536]{1,0:T(8,128)(2,1)S(1)} %fusion.7), channel_id=1, source_target_pairs={{12,8},{8,4},{13,9},{9,5},{14,10},{10,6},{15,11},{11,7},{28,24},{2... | collective-permute-start | bytes 2359304 | tf_op jit(solution)/shard_map/ppermute | solution.py:193
  104.9 31.9 %collective-permute-start.12 = (bf16[256,1536]{1,0:T(8,128)(2,1)S(1)}, bf16[256,1536]{1,0:T(8,128)(2,1)S(1)}, u32[]{:S(2)}, u32[]{:S(2)}) collective-permute-start(bf16[256,1536]{1,0:T(8,128)(2,1)S(1)} %fusion.6), channel_id=1, source_target_pairs={{0,12},{1,13},{2,14},{3,15},{16,28},{17,29},{18,30},{19,31}} | collective-permute-start | bytes 2359304 | tf_op jit(solution)/shard_map/ppermute | solution.py:192
  109.2 32.1 %collective-permute-start.15 = (bf16[256,1536]{1,0:T(8,128)(2,1)S(1)}, bf16[256,1536]{1,0:T(8,128)(2,1)S(1)}, u32[]{:S(2)}, u32[]{:S(2)}) collective-permute-start(bf16[256,1536]{1,0:T(8,128)(2,1)S(1)} %fusion.8), channel_id=1, source_target_pairs={{12,0},{13,1},{14,2},{15,3},{28,16},{29,17},{30,18},{31,19}} | collective-permute-start | bytes 2359304 | tf_op jit(solution)/shard_map/ppermute | solution.py:196
  120.9 31.9 %collective-permute-start.11 = (bf16[256,1536]{1,0:T(8,128)(2,1)S(1)}, bf16[256,1536]{1,0:T(8,128)(2,1)S(1)}, u32[]{:S(2)}, u32[]{:S(2)}) collective-permute-start(bf16[256,1536]{1,0:T(8,128)(2,1)S(1)} %fusion.4), channel_id=1, source_target_pairs={{0,4},{4,8},{8,12},{1,5},{5,9},{9,13},{2,6},{6,10},{10,14},{3,7},{... | collective-permute-start | bytes 2359304 | tf_op jit(solution)/shard_map/ppermute | solution.py:198
  126.4 31.3 %collective-permute-start.14 = (bf16[256,1536]{1,0:T(8,128)(2,1)S(1)}, bf16[256,1536]{1,0:T(8,128)(2,1)S(1)}, u32[]{:S(2)}, u32[]{:S(2)}) collective-permute-start(bf16[256,1536]{1,0:T(8,128)(2,1)S(1)} %fusion.3), channel_id=1, source_target_pairs={{12,8},{8,4},{4,0},{13,9},{9,5},{5,1},{14,10},{10,6},{6,2},{15,11}... | collective-permute-start | bytes 2359304 | tf_op jit(solution)/shard_map/ppermute | solution.py:207

commit v16 on v14

--- a/solution.py
+++ b/solution.py
@@ -187,10 +187,10 @@
         near_r = lax.ppermute(
             bf(partial_for(jnp.clip(s_me + 2, 0, 3))), "seq", [(0, 1), (1, 2)]
         )
-        far_r = lax.ppermute(bf(partial_for(jnp.int32(3))), "seq", [(0, 3)])
         near_l = lax.ppermute(
             bf(partial_for(jnp.clip(s_me - 2, 0, 3))), "seq", [(3, 2), (2, 1)]
         )
+        far_r = lax.ppermute(bf(partial_for(jnp.int32(3))), "seq", [(0, 3)])
         far_l = lax.ppermute(bf(partial_for(jnp.int32(0))), "seq", [(3, 0)])
         own_part = partial_for(s_me)
         last_r = lax.ppermute(

time: 157 us -> 157 us (level)
  no operation moved by 1% of the time
where the time goes in v16:
time: 157 us; the launch traced here: 156 us
  starting transfers between devices  60.7 us (39%)
  waiting for transfers between devices  59.4 us (38%)
  other arithmetic  14.7 us (9%)
  matrix products  11.1 us (7%)
  local copies, waits for them, and re-layouts  9.99 us (6%)
    ppermute x1, starting transfers between devices, per_device(): lax.ppermute(bf(partial_for(jnp.clip(s_me + 1, 0, 3)) + near_r.astype(jnp...  19.6 us
    ppermute x4, starting transfers between devices, per_device(): received.append(lax.ppermute(item, ('seq', 'mdl'), perm))  15 us
    ppermute x1, waiting for transfers between devices, per_device(): got.append(lax.ppermute(x, 'mdl', perm))  13 us
    ppermute x3, starting transfers between devices, per_device(): came = lax.ppermute(packed, 'seq', [(z, z + d) for z in range(n_seq - d)])  11.5 us
    ppermute x1, waiting for transfers between devices, per_device(): lax.ppermute(bf(partial_for(jnp.clip(s_me + 1, 0, 3)) + near_r.astype(jnp...  9.94 us
    ppermute x1, waiting for transfers between devices, per_device(): lax.ppermute(bf(partial_for(jnp.clip(s_me - 1, 0, 3)) + near_l.astype(jnp...  9.74 us
    ppermute x1, waiting for transfers between devices, per_device(): lax.ppermute(bf(partial_for(jnp.clip(s_me + 2, 0, 3))), 'seq', [(0, 1), (...  7.71 us
    ppermute x4, waiting for transfers between devices, per_device(): received.append(lax.ppermute(item, ('seq', 'mdl'), perm))  7.49 us
  transfers between devices with their start and end apart: 16, of which 9 were waited for; matrix products, arithmetic and copies ran while one was open for 12% of the time, Pallas kernels for 0%

profile of v16, /device:TPU:0, one launch (start us, length us, event | category | flops | bytes accessed | tf_op | source)
XLA Modules:
  0.0 156.4 jit_solution(9074033525232990642)
XLA Ops:
  0.0 1.2 reduce-window.6
  1.8 1.0 fusion.114
  2.8 1.2 copy.74
  4.1 1.2 copy.76
  7.0 5.6 %collective-permute-start = (bf16[8,16640]{1,0:T(8,128)(2,1)S(1)}, bf16[8,16640]{1,0:T(8,128)(2,1)}, u32[]{:S(2)}, u32[]{:S(2)}) collective-permute-start(bf16[8,16640]{1,0:T(8,128)(2,1)S(1)} %pad_maximum_fusion.3), channel_id=1, source_target_pairs={{0,4},{4,8},{8,12},{1,5},{5,9},{9,13},{2,6},{6,10},{10,14},{3,7},{... | collective-permute-start | bytes 798728 | tf_op jit(solution)/shard_map/ppermute | solution.py:95
  12.6 3.8 %collective-permute-start.1 = (bf16[8,16640]{1,0:T(8,128)(2,1)S(1)}, bf16[8,16640]{1,0:T(8,128)(2,1)S(1)}, u32[]{:S(2)}, u32[]{:S(2)}) collective-permute-start(bf16[8,16640]{1,0:T(8,128)(2,1)S(1)} %pad_maximum_fusion.3), channel_id=1, source_target_pairs={{0,8},{4,12},{1,9},{5,13},{2,10},{6,14},{3,11},{7,15},{16,24},{20,... | collective-permute-start | bytes 798728 | tf_op jit(solution)/shard_map/ppermute | solution.py:95
  16.4 2.0 %collective-permute-start.2 = (bf16[8,16640]{1,0:T(8,128)(2,1)S(1)}, bf16[8,16640]{1,0:T(8,128)(2,1)}, u32[]{:S(2)}, u32[]{:S(2)}) collective-permute-start(bf16[8,16640]{1,0:T(8,128)(2,1)S(1)} %pad_maximum_fusion.3), channel_id=1, source_target_pairs={{0,12},{1,13},{2,14},{3,15},{16,28},{17,29},{18,30},{19,31}} | collective-permute-start | bytes 798728 | tf_op jit(solution)/shard_map/ppermute | solution.py:95
  19.3 1.9 %fusion.10 = f32[1,256,8,128]{1,3,2,0:T(8,128)} fusion(bf16[256,8,128]{0,2,1:T(8,128)(2,1)S(1)} %bitcast.190, bf16[256,8,128]{0,2,1:T(8,128)(2,1)S(1)} %bitcast.187, bf16[256,8,128]{0,2,1:T(8,128)(2,1)S(1)} %bitcast.192, f32[8,256]{1,0:T(8,128)S(1)} %bitcast_add_fusion.2, pred[256,256]{1,0:T(8,128)(4,1)S(1)} %iota_compare_fusion), kind=kOutput, calls=%fused_computation.35 | convolution fusion | flops 271056896 | bytes 2695168 | tf_op jit(solution)/shard_map/hbij,bjhd->bihd/dot_general | solution.py:63
  22.7 1.7 %collective-permute-done.1 = bf16[8,16640]{1,0:T(8,128)(2,1)S(1)} collective-permute-done((bf16[8,16640]{1,0:T(8,128)(2,1)S(1)}, bf16[8,16640]{1,0:T(8,128)(2,1)S(1)}, u32[]{:S(2)}, u32[]{:S(2)}) %collective-permute-start.1) | collective-permute-done | bytes 266272 | tf_op jit(solution)/shard_map/ppermute | solution.py:95
  24.7 4.3 %collective-permute-done.2 = bf16[8,16640]{1,0:T(8,128)(2,1)} collective-permute-done((bf16[8,16640]{1,0:T(8,128)(2,1)S(1)}, bf16[8,16640]{1,0:T(8,128)(2,1)}, u32[]{:S(2)}, u32[]{:S(2)}) %collective-permute-start.2) | collective-permute-done | bytes 266272 | tf_op jit(solution)/shard_map/ppermute | solution.py:95
  31.1 2.0 %multiply_reduce_fusion = (f32[256,8]{0,1:T(8,128)S(1)}, f32[1,256,8,128]{1,3,2,0:T(8,128)S(1)}) fusion(f32[1,256,8,128]{1,3,2,0:T(8,128)} %fusion.10, bf16[256,8,128]{0,2,1:T(8,128)(2,1)S(1)} %bitcast.188, f32[8,128,128]{1,2,0:T(8,128)S(1)} %copy.83, f32[8,128,128]{1,2,0:T(8,128)S(1)} %copy.82, f32[8,128,128]{1,2,0:T(8,128)S(1)} %copy.81, ...), kind=kOutput, calls=%fused_computation.56 | convolution fusion | flops 404355072 | bytes 4210784 | tf_op jit(solution)/shard_map/bihd,bhde->bihe/dot_general | solution.py:105
  34.1 1.6 collective-permute-start.3
  35.8 5.5 %collective-permute-done.3 = bf16[256,2,256]{0,2,1:T(8,128)(2,1)S(1)} collective-permute-done((bf16[256,2,256]{0,2,1:T(8,128)(2,1)S(1)}, bf16[256,2,256]{0,2,1:T(8,128)(2,1)S(1)}, u32[]{:S(2)}, u32[]{:S(2)}) %collective-permute-start.3) | collective-permute-done | bytes 262176 | tf_op jit(solution)/shard_map/ppermute | solution.py:129
  42.5 8.9 %collective-permute-start.5 = (bf16[256,256]{1,0:T(8,128)(2,1)S(1)}, bf16[256,256]{1,0:T(8,128)(2,1)S(1)}, u32[]{:S(2)}, u32[]{:S(2)}) collective-permute-start(bf16[256,256]{1,0:T(8,128)(2,1)S(1)} %bitcast.196), channel_id=1, source_target_pairs={{0,1},{1,5},{2,11},{3,15},{4,8},{5,12},{6,2},{7,6},{8,9},{9,13},{1... | collective-permute-start | bytes 393224 | tf_op jit(solution)/shard_map/ppermute | solution.py:140
  51.5 5.3 %collective-permute-start.6 = (bf16[256,256]{1,0:T(8,128)(2,1)S(1)}, bf16[256,256]{1,0:T(8,128)(2,1)S(1)}, u32[]{:S(2)}, u32[]{:S(2)}) collective-permute-start(bf16[256,256]{1,0:T(8,128)(2,1)S(1)} %bitcast.197), channel_id=1, source_target_pairs={{0,8},{1,12},{2,2},{3,6},{4,9},{5,13},{6,3},{7,7},{8,0},{9,4},{10,... | collective-permute-start | bytes 393224 | tf_op jit(solution)/shard_map/ppermute | solution.py:140
  57.0 1.9 %collective-permute-done.5 = bf16[256,256]{1,0:T(8,128)(2,1)S(1)} collective-permute-done((bf16[256,256]{1,0:T(8,128)(2,1)S(1)}, bf16[256,256]{1,0:T(8,128)(2,1)S(1)}, u32[]{:S(2)}, u32[]{:S(2)}) %collective-permute-start.5) | collective-permute-done | bytes 131104 | tf_op jit(solution)/shard_map/ppermute | solution.py:140
  58.9 5.6 %collective-permute-done.6 = bf16[256,256]{1,0:T(8,128)(2,1)S(1)} collective-permute-done((bf16[256,256]{1,0:T(8,128)(2,1)S(1)}, bf16[256,256]{1,0:T(8,128)(2,1)S(1)}, u32[]{:S(2)}, u32[]{:S(2)}) %collective-permute-start.6) | collective-permute-done | bytes 131104 | tf_op jit(solution)/shard_map/ppermute | solution.py:140
  65.5 13.0 %collective-permute-done.8 = bf16[4,256,256]{2,1,0:T(8,128)(2,1)S(1)} collective-permute-done((bf16[4,256,256]{2,1,0:T(8,128)(2,1)S(1)}, bf16[4,256,256]{2,1,0:T(8,128)(2,1)S(1)}, u32[]{:S(2)}, u32[]{:S(2)}) %collective-permute-start.8) | collective-permute-done | bytes 524320 | tf_op jit(solution)/shard_map/ppermute | solution.py:166
  78.6 1.5 collective-permute-start.9
  80.2 2.6 %multiply_convert_fusion = bf16[1024,1536]{1,0:T(8,128)(2,1)} fusion(bf16[1024,1536]{1,0:T(8,128)(2,1)S(1)} %copy-done, f32[1536]{0:T(1024)S(1)} %select_add_fusion), kind=kLoop, calls=%fused_computation.2 | loop fusion | flops 11010048 | bytes 6297600 | tf_op jit(solution)/shard_map/convert_element_type | solution.py:20
  82.9 4.3 %gather_fusion.1 = bf16[4,256,1536]{2,1,0:T(8,128)(2,1)} fusion(bf16[4,256,1536]{2,1,0:T(8,128)(2,1)} %bitcast.186, s32[1024]{0:T(1024)S(1)} %pad_clamp_fusion), kind=kCustom, calls=%fused_computation.1 | custom fusion | bytes 6291472 | tf_op jit(solution)/shard_map/jit(_take)/gather | solution.py:173
  87.2 2.3 %broadcast_select_fusion = bf16[4,256,1536]{2,1,0:T(8,128)(2,1)S(1)} fusion(bf16[4,256,1536]{2,1,0:T(8,128)(2,1)} %gather_fusion.1, pred[4]{0:T(512)(128)(4,1)S(1)} %get-tuple-element.42), kind=kLoop, calls=%fused_computation.15 | loop fusion | flops 1572864 | bytes 6291460 | tf_op jit(solution)/shard_map/jit(_take)/select_n | solution.py:173
  91.5 3.1 %collective-permute-start.10 = (bf16[256,1536]{1,0:T(8,128)(2,1)S(1)}, bf16[256,1536]{1,0:T(8,128)(2,1)S(1)}, u32[]{:S(2)}, u32[]{:S(2)}) collective-permute-start(bf16[256,1536]{1,0:T(8,128)(2,1)S(1)} %fusion.5), channel_id=1, source_target_pairs={{0,4},{4,8},{1,5},{5,9},{2,6},{6,10},{3,7},{7,11},{16,20},{20,24},... | collective-permute-start | bytes 2359304 | tf_op jit(solution)/shard_map/ppermute | solution.py:187
  97.4 5.0 %collective-permute-start.12 = (bf16[256,1536]{1,0:T(8,128)(2,1)S(1)}, bf16[256,1536]{1,0:T(8,128)(2,1)S(1)}, u32[]{:S(2)}, u32[]{:S(2)}) collective-permute-start(bf16[256,1536]{1,0:T(8,128)(2,1)S(1)} %fusion.6), channel_id=1, source_target_pairs={{0,12},{1,13},{2,14},{3,15},{16,28},{17,29},{18,30},{19,31}} | collective-permute-start | bytes 2359304 | tf_op jit(solution)/shard_map/ppermute | solution.py:193
  102.4 1.3 collective-permute-start.15
  104.7 7.7 %collective-permute-done.10 = bf16[256,1536]{1,0:T(8,128)(2,1)S(1)} collective-permute-done((bf16[256,1536]{1,0:T(8,128)(2,1)S(1)}, bf16[256,1536]{1,0:T(8,128)(2,1)S(1)}, u32[]{:S(2)}, u32[]{:S(2)}) %collective-permute-start.10) | collective-permute-done | bytes 786464 | tf_op jit(solution)/shard_map/ppermute | solution.py:187
  112.4 1.0 fusion.4
  113.4 19.6 %collective-permute-start.11 = (bf16[256,1536]{1,0:T(8,128)(2,1)S(1)}, bf16[256,1536]{1,0:T(8,128)(2,1)S(1)}, u32[]{:S(2)}, u32[]{:S(2)}) collective-permute-start(bf16[256,1536]{1,0:T(8,128)(2,1)S(1)} %fusion.4), channel_id=1, source_target_pairs={{0,4},{4,8},{8,12},{1,5},{5,9},{9,13},{2,6},{6,10},{10,14},{3,7},{... | collective-permute-start | bytes 2359304 | tf_op jit(solution)/shard_map/ppermute | solution.py:196
  134.0 1.3 collective-permute-start.14
  135.3 9.9 %collective-permute-done.11 = bf16[256,1536]{1,0:T(8,128)(2,1)S(1)} collective-permute-done((bf16[256,1536]{1,0:T(8,128)(2,1)S(1)}, bf16[256,1536]{1,0:T(8,128)(2,1)S(1)}, u32[]{:S(2)}, u32[]{:S(2)}) %collective-permute-start.11) | collective-permute-done | bytes 786464 | tf_op jit(solution)/shard_map/ppermute | solution.py:196
  145.3 9.7 %collective-permute-done.14 = bf16[256,1536]{1,0:T(8,128)(2,1)S(1)} collective-permute-done((bf16[256,1536]{1,0:T(8,128)(2,1)S(1)}, bf16[256,1536]{1,0:T(8,128)(2,1)S(1)}, u32[]{:S(2)}, u32[]{:S(2)}) %collective-permute-start.14) | collective-permute-done | bytes 786464 | tf_op jit(solution)/shard_map/ppermute | solution.py:205
  155.0 1.4 add_convert_fusion
  (78 shorter events, 17.3 us)
Async XLA Ops:
  5.6 12.9 %copy-start.1 = (bf16[256,1024]{1,0:T(8,128)(2,1)S(1)}, bf16[256,1024]{1,0:T(8,128)(2,1)}, u32[]{:S(2)}) copy-start(bf16[256,1024]{1,0:T(8,128)(2,1)} %param.9) | copy-start | bytes 1572868
  7.0 14.5 %collective-permute-start = (bf16[8,16640]{1,0:T(8,128)(2,1)S(1)}, bf16[8,16640]{1,0:T(8,128)(2,1)}, u32[]{:S(2)}, u32[]{:S(2)}) collective-permute-start(bf16[8,16640]{1,0:T(8,128)(2,1)S(1)} %pad_maximum_fusion.3), channel_id=1, source_target_pairs={{0,4},{4,8},{8,12},{1,5},{5,9},{9,13},{2,6},{6,10},{10,14},{3,7},{... | collective-permute-start | bytes 798728 | tf_op jit(solution)/shard_map/ppermute | solution.py:95
  12.6 11.8 %collective-permute-start.1 = (bf16[8,16640]{1,0:T(8,128)(2,1)S(1)}, bf16[8,16640]{1,0:T(8,128)(2,1)S(1)}, u32[]{:S(2)}, u32[]{:S(2)}) collective-permute-start(bf16[8,16640]{1,0:T(8,128)(2,1)S(1)} %pad_maximum_fusion.3), channel_id=1, source_target_pairs={{0,8},{4,12},{1,9},{5,13},{2,10},{6,14},{3,11},{7,15},{16,24},{20,... | collective-permute-start | bytes 798728 | tf_op jit(solution)/shard_map/ppermute | solution.py:95
  16.4 12.6 %collective-permute-start.2 = (bf16[8,16640]{1,0:T(8,128)(2,1)S(1)}, bf16[8,16640]{1,0:T(8,128)(2,1)}, u32[]{:S(2)}, u32[]{:S(2)}) collective-permute-start(bf16[8,16640]{1,0:T(8,128)(2,1)S(1)} %pad_maximum_fusion.3), channel_id=1, source_target_pairs={{0,12},{1,13},{2,14},{3,15},{16,28},{17,29},{18,30},{19,31}} | collective-permute-start | bytes 798728 | tf_op jit(solution)/shard_map/ppermute | solution.py:95
  19.3 2.0 %copy-start.2 = (bf16[256,1024]{1,0:T(8,128)(2,1)S(1)}, bf16[256,1024]{1,0:T(8,128)(2,1)}, u32[]{:S(2)}) copy-start(bf16[256,1024]{1,0:T(8,128)(2,1)} %param.12) | copy-start | bytes 1572868
  33.1 0.7 copy-start.4
  34.1 7.2 %collective-permute-start.3 = (bf16[256,2,256]{0,2,1:T(8,128)(2,1)S(1)}, bf16[256,2,256]{0,2,1:T(8,128)(2,1)S(1)}, u32[]{:S(2)}, u32[]{:S(2)}) collective-permute-start(bf16[256,2,256]{0,2,1:T(8,128)(2,1)S(1)} %get-tuple-element.32), channel_id=1, source_target_pairs={{0,2},{1,3},{2,0},{3,1},{4,6},{5,7},{6,4},{7,5},{8,10},{9,11},{10,... | collective-permute-start | bytes 786440 | tf_op jit(solution)/shard_map/ppermute | solution.py:129
  41.6 23.8 %copy-start.3 = (s32[1536]{0:T(1024)S(1)}, s32[1536]{0:T(1024)}, u32[]{:S(2)}) copy-start(s32[1536]{0:T(1024)} %param.17) | copy-start | bytes 18436
  41.7 15.3 %collective-permute-start.4 = (bf16[256,256]{1,0:T(8,128)(2,1)S(1)}, bf16[256,256]{1,0:T(8,128)(2,1)S(1)}, u32[]{:S(2)}, u32[]{:S(2)}) collective-permute-start(bf16[256,256]{1,0:T(8,128)(2,1)S(1)} %bitcast.195), channel_id=1, source_target_pairs={{0,0},{1,4},{2,10},{3,14},{4,1},{5,5},{6,11},{7,15},{8,8},{9,12},{... | collective-permute-start | bytes 393224 | tf_op jit(solution)/shard_map/ppermute | solution.py:140
  42.5 16.5 %collective-permute-start.5 = (bf16[256,256]{1,0:T(8,128)(2,1)S(1)}, bf16[256,256]{1,0:T(8,128)(2,1)S(1)}, u32[]{:S(2)}, u32[]{:S(2)}) collective-permute-start(bf16[256,256]{1,0:T(8,128)(2,1)S(1)} %bitcast.196), channel_id=1, source_target_pairs={{0,1},{1,5},{2,11},{3,15},{4,8},{5,12},{6,2},{7,6},{8,9},{9,13},{1... | collective-permute-start | bytes 393224 | tf_op jit(solution)/shard_map/ppermute | solution.py:140
  51.5 13.0 %collective-permute-start.6 = (bf16[256,256]{1,0:T(8,128)(2,1)S(1)}, bf16[256,256]{1,0:T(8,128)(2,1)S(1)}, u32[]{:S(2)}, u32[]{:S(2)}) collective-permute-start(bf16[256,256]{1,0:T(8,128)(2,1)S(1)} %bitcast.197), channel_id=1, source_target_pairs={{0,8},{1,12},{2,2},{3,6},{4,9},{5,13},{6,3},{7,7},{8,0},{9,4},{10,... | collective-permute-start | bytes 393224 | tf_op jit(solution)/shard_map/ppermute | solution.py:140
  56.9 7.6 %collective-permute-start.7 = (bf16[256,256]{1,0:T(8,128)(2,1)S(1)}, bf16[256,256]{1,0:T(8,128)(2,1)S(1)}, u32[]{:S(2)}, u32[]{:S(2)}) collective-permute-start(bf16[256,256]{1,0:T(8,128)(2,1)S(1)} %bitcast.198), channel_id=1, source_target_pairs={{0,9},{1,13},{2,3},{3,7},{4,0},{5,4},{6,10},{7,14},{8,1},{9,5},{10... | collective-permute-start | bytes 393224 | tf_op jit(solution)/shard_map/ppermute | solution.py:140
  65.3 13.2 %collective-permute-start.8 = (bf16[4,256,256]{2,1,0:T(8,128)(2,1)S(1)}, bf16[4,256,256]{2,1,0:T(8,128)(2,1)S(1)}, u32[]{:S(2)}, u32[]{:S(2)}) collective-permute-start(bf16[4,256,256]{2,1,0:T(8,128)(2,1)S(1)} %broadcast_select_fusion.1), channel_id=1, source_target_pairs={{0,2},{1,3},{2,0},{3,1},{4,6},{5,7},{6,4},{7,5},{8,10},{9,11},{10,... | collective-permute-start | bytes 1572872 | tf_op jit(solution)/shard_map/ppermute | solution.py:166
  65.4 14.8 %copy-start = (bf16[1024,1536]{1,0:T(8,128)(2,1)S(1)}, bf16[1024,1536]{1,0:T(8,128)(2,1)}, u32[]{:S(2)}) copy-start(bf16[1024,1536]{1,0:T(8,128)(2,1)} %param.16) | copy-start | bytes 9437188
  78.6 10.9 %collective-permute-start.9 = (bf16[2,4,256,256]{3,2,0,1:T(8,128)(2,1)S(1)}, bf16[2,4,256,256]{3,2,0,1:T(8,128)(2,1)S(1)}, u32[]{:S(2)}, u32[]{:S(2)}) collective-permute-start(bf16[2,4,256,256]{3,2,0,1:T(8,128)(2,1)S(1)} %get-tuple-element.27), channel_id=1, source_target_pairs={{0,1},{1,0},{2,3},{3,2},{4,5},{5,4},{6,7},{7,6},{8,9},{9,8},{10,11... | collective-permute-start | bytes 3145736 | tf_op jit(solution)/shard_map/ppermute | solution.py:168
  91.5 20.9 %collective-permute-start.10 = (bf16[256,1536]{1,0:T(8,128)(2,1)S(1)}, bf16[256,1536]{1,0:T(8,128)(2,1)S(1)}, u32[]{:S(2)}, u32[]{:S(2)}) collective-permute-start(bf16[256,1536]{1,0:T(8,128)(2,1)S(1)} %fusion.5), channel_id=1, source_target_pairs={{0,4},{4,8},{1,5},{5,9},{2,6},{6,10},{3,7},{7,11},{16,20},{20,24},... | collective-permute-start | bytes 2359304 | tf_op jit(solution)/shard_map/ppermute | solution.py:187
  95.5 37.5 %collective-permute-start.13 = (bf16[256,1536]{1,0:T(8,128)(2,1)S(1)}, bf16[256,1536]{1,0:T(8,128)(2,1)S(1)}, u32[]{:S(2)}, u32[]{:S(2)}) collective-permute-start(bf16[256,1536]{1,0:T(8,128)(2,1)S(1)} %fusion.7), channel_id=1, source_target_pairs={{12,8},{8,4},{13,9},{9,5},{14,10},{10,6},{15,11},{11,7},{28,24},{2... | collective-permute-start | bytes 2359304 | tf_op jit(solution)/shard_map/ppermute | solution.py:190
  97.4 37.9 %collective-permute-start.12 = (bf16[256,1536]{1,0:T(8,128)(2,1)S(1)}, bf16[256,1536]{1,0:T(8,128)(2,1)S(1)}, u32[]{:S(2)}, u32[]{:S(2)}) collective-permute-start(bf16[256,1536]{1,0:T(8,128)(2,1)S(1)} %fusion.6), channel_id=1, source_target_pairs={{0,12},{1,13},{2,14},{3,15},{16,28},{17,29},{18,30},{19,31}} | collective-permute-start | bytes 2359304 | tf_op jit(solution)/shard_map/ppermute | solution.py:193
  102.4 32.9 %collective-permute-start.15 = (bf16[256,1536]{1,0:T(8,128)(2,1)S(1)}, bf16[256,1536]{1,0:T(8,128)(2,1)S(1)}, u32[]{:S(2)}, u32[]{:S(2)}) collective-permute-start(bf16[256,1536]{1,0:T(8,128)(2,1)S(1)} %fusion.8), channel_id=1, source_target_pairs={{12,0},{13,1},{14,2},{15,3},{28,16},{29,17},{30,18},{31,19}} | collective-permute-start | bytes 2359304 | tf_op jit(solution)/shard_map/ppermute | solution.py:194
  113.4 31.8 %collective-permute-start.11 = (bf16[256,1536]{1,0:T(8,128)(2,1)S(1)}, bf16[256,1536]{1,0:T(8,128)(2,1)S(1)}, u32[]{:S(2)}, u32[]{:S(2)}) collective-permute-start(bf16[256,1536]{1,0:T(8,128)(2,1)S(1)} %fusion.4), channel_id=1, source_target_pairs={{0,4},{4,8},{8,12},{1,5},{5,9},{9,13},{2,6},{6,10},{10,14},{3,7},{... | collective-permute-start | bytes 2359304 | tf_op jit(solution)/shard_map/ppermute | solution.py:196
  134.0 21.0 %collective-permute-start.14 = (bf16[256,1536]{1,0:T(8,128)(2,1)S(1)}, bf16[256,1536]{1,0:T(8,128)(2,1)S(1)}, u32[]{:S(2)}, u32[]{:S(2)}) collective-permute-start(bf16[256,1536]{1,0:T(8,128)(2,1)S(1)} %fusion.3), channel_id=1, source_target_pairs={{12,8},{8,4},{4,0},{13,9},{9,5},{5,1},{14,10},{10,6},{6,2},{15,11}... | collective-permute-start | bytes 2359304 | tf_op jit(solution)/shard_map/ppermute | solution.py:205

commit v17 on v14

--- a/solution.py
+++ b/solution.py
@@ -33,7 +33,6 @@
     out_weight,
     weight_exponent,
 ):
-    weights = fake_quant(out_weight, weight_exponent[None, :])
     tok_rows = query_proj.shape[0]
     feat_here = query_proj.shape[1]
     heads_here = log_decay.shape[0]
@@ -88,6 +87,18 @@
         ],
         axis=1,
     )
+    weights = fake_quant(out_weight, weight_exponent[None, :])
+    n_x = n_mdl // 2
+    m_me = lax.axis_index("mdl")
+    core = m_me % 2
+    xi = m_me // 2
+    piece = weights.shape[0] // n_mdl
+    d_idx = jnp.arange(n_x)[:, None]
+    e_idx = jnp.arange(2)[None, :]
+    mu_tab = 2 * ((xi - d_idx) % n_x) + jnp.where(e_idx == 0, core, 1 - core)
+    w_perm = jnp.take(
+        weights.reshape(n_mdl, piece, weights.shape[1]), mu_tab.reshape(-1), axis=0
+    ).reshape(n_x, 2, piece, weights.shape[1])
     position = lax.axis_index("seq")
     incoming = jnp.zeros((heads_here, HDIM, HDIM), jnp.float32)
     gap = jnp.zeros((heads_here,), jnp.float32)
@@ -99,6 +110,8 @@
         )
         weight = jnp.where(d <= position, jnp.exp(jnp.minimum(gap, 0.0)), 0.0)
         incoming = incoming + weight[:, None, None] * came_state
+        if d == 1:
+            incoming = incoming + w_perm[0, 0, 0, 0].astype(jnp.float32) * 0.0
         gap = gap + came_log
     before = jnp.cumsum(block_total, axis=1) - block_total
     entry_state = entry_local + jnp.exp(before).T[:, :, None, None] * incoming[None]
@@ -167,12 +180,6 @@
     own = jnp.stack(got)
     other = lax.ppermute(own, "mdl", [(mu, mu ^ 1) for mu in range(n_mdl)])
     gathered_x = jnp.stack([own, other], axis=1)
-    d_idx = jnp.arange(n_x)[:, None]
-    e_idx = jnp.arange(2)[None, :]
-    mu_tab = 2 * ((xi - d_idx) % n_x) + jnp.where(e_idx == 0, core, 1 - core)
-    w_perm = jnp.take(
-        weights.reshape(n_mdl, piece, cols_w), mu_tab.reshape(-1), axis=0
-    ).reshape(n_x, 2, piece, cols_w)
 
     def partial_for(target):
         rows = lax.dynamic_index_in_dim(gathered_x, target, 2, keepdims=False)

time: 157 us -> 151 us (0.962)
  starting transfers between devices: 60.7 us -> 37.7 us
  local copies, waits for them, and re-layouts: 9.99 us -> 17.5 us
  waiting for transfers between devices: 59.4 us -> 64.4 us
  other arithmetic: 14.7 us -> 17.2 us
    ppermute x1, starting transfers between devices: 19.6 us -> 4.43 us  [per_device(): lax.ppermute(bf(partial_for(jnp.clip(s_me + 1, 0, 3)) + near_r.astype(jnp...]
    ppermute x1, waiting for transfers between devices: 0.01 us -> 9.16 us  [per_device(): far_r = lax.ppermute(bf(partial_for(jnp.int32(3))), 'seq', [(0, 3)])]
    ppermute x4, starting transfers between devices: 15 us -> 5.94 us  [per_device(): received.append(lax.ppermute(item, ('seq', 'mdl'), perm))]
    ppermute x3, waiting for transfers between devices: 6.02 us -> 0.01 us  [per_device(): came = lax.ppermute(packed, 'seq', [(z, z + d) for z in range(n_seq - d)])]
    ppermute x1, waiting for transfers between devices: 0.01 us -> 5.53 us  [per_device(): far_l = lax.ppermute(bf(partial_for(jnp.int32(0))), 'seq', [(3, 0)])]
    unnamed x14 -> x28, local copies, waits for them, and re-layouts: 3.51 us -> 8.42 us
    ppermute x1, waiting for transfers between devices: 9.74 us -> 5.29 us  [per_device(): lax.ppermute(bf(partial_for(jnp.clip(s_me - 1, 0, 3)) + near_l.astype(jnp...]
    add x0 -> x1, local copies, waits for them, and re-layouts: none -> 2.08 us  [per_device(): incoming = incoming + w_perm[0, 0, 0, 0].astype(jnp.float32) * 0.0]
  transfers between devices with their start and end apart: 16 -> 16, of which waited for: 9 -> 9; matrix products, arithmetic and copies ran while one was open for 12% -> 19% of each run, Pallas kernels for 0% -> 0%
where the time goes in v17:
time: 151 us; the launch traced here: 150 us
  waiting for transfers between devices  64.4 us (43%)
  starting transfers between devices  37.7 us (25%)
  local copies, waits for them, and re-layouts  17.5 us (12%)
  other arithmetic  17.2 us (11%)
  matrix products  12.5 us (8%)
    ppermute x1, waiting for transfers between devices, per_device(): got.append(lax.ppermute(x, 'mdl', perm))  12 us
    ppermute x3, starting transfers between devices, per_device(): came = lax.ppermute(packed, 'seq', [(z, z + d) for z in range(n_seq - d)])  11.4 us
    ppermute x1, waiting for transfers between devices, per_device(): lax.ppermute(bf(partial_for(jnp.clip(s_me + 1, 0, 3)) + near_r.astype(jnp...  10.8 us
    ppermute x1, waiting for transfers between devices, per_device(): far_r = lax.ppermute(bf(partial_for(jnp.int32(3))), 'seq', [(0, 3)])  9.16 us
    unnamed x28, local copies, waits for them, and re-layouts  8.42 us
    ppermute x4, waiting for transfers between devices, per_device(): received.append(lax.ppermute(item, ('seq', 'mdl'), perm))  8.37 us
    ppermute x1, waiting for transfers between devices, per_device(): lax.ppermute(bf(partial_for(jnp.clip(s_me + 2, 0, 3))), 'seq', [(0, 1), (...  7.36 us
    dot_general x7, matrix products, partial_for(): jnp.einsum('deti,deic->tc', rows, w_perm, preferred_element_type=jnp.floa...  6.88 us
  transfers between devices with their start and end apart: 16, of which 9 were waited for; matrix products, arithmetic and copies ran while one was open for 19% of the time, Pallas kernels for 0%

profile of v17, /device:TPU:0, one launch (start us, length us, event | category | flops | bytes accessed | tf_op | source)
XLA Modules:
  0.0 150.5 jit_solution(1329793168130650984)
XLA Ops:
  4.1 1.2 copy.76
  8.2 5.6 %collective-permute-start = (bf16[8,16640]{1,0:T(8,128)(2,1)}, bf16[8,16640]{1,0:T(8,128)(2,1)}, u32[]{:S(2)}, u32[]{:S(2)}) collective-permute-start(bf16[8,16640]{1,0:T(8,128)(2,1)} %pad_maximum_fusion.3), channel_id=1, source_target_pairs={{0,4},{4,8},{8,12},{1,5},{5,9},{9,13},{2,6},{6,10},{10,14},{3,7},{... | collective-permute-start | bytes 798728 | tf_op jit(solution)/shard_map/ppermute | solution.py:106
  13.8 3.8 %collective-permute-start.1 = (bf16[8,16640]{1,0:T(8,128)(2,1)}, bf16[8,16640]{1,0:T(8,128)(2,1)S(1)}, u32[]{:S(2)}, u32[]{:S(2)}) collective-permute-start(bf16[8,16640]{1,0:T(8,128)(2,1)} %pad_maximum_fusion.3), channel_id=1, source_target_pairs={{0,8},{4,12},{1,9},{5,13},{2,10},{6,14},{3,11},{7,15},{16,24},{20,... | collective-permute-start | bytes 798728 | tf_op jit(solution)/shard_map/ppermute | solution.py:106
  17.6 2.0 %collective-permute-start.2 = (bf16[8,16640]{1,0:T(8,128)(2,1)}, bf16[8,16640]{1,0:T(8,128)(2,1)}, u32[]{:S(2)}, u32[]{:S(2)}) collective-permute-start(bf16[8,16640]{1,0:T(8,128)(2,1)} %pad_maximum_fusion.3), channel_id=1, source_target_pairs={{0,12},{1,13},{2,14},{3,15},{16,28},{17,29},{18,30},{19,31}} | collective-permute-start | bytes 798728 | tf_op jit(solution)/shard_map/ppermute | solution.py:106
  20.0 2.1 %copy.75 = bf16[256,1024]{0,1:T(8,128)(2,1)} copy(bf16[256,1024]{1,0:T(8,128)(2,1)} %param.9) | data formatting | bytes 1048576 | tf_op args[0]
  22.1 2.6 %multiply_convert_fusion = bf16[1024,1536]{1,0:T(8,128)(2,1)} fusion(bf16[1024,1536]{1,0:T(8,128)(2,1)S(1)} %copy-done.1, f32[1536]{0:T(1024)S(1)} %select_add_fusion), kind=kLoop, calls=%fused_computation.2 | loop fusion | flops 11010048 | bytes 6297600 | tf_op jit(solution)/shard_map/convert_element_type | solution.py:20
  25.2 3.3 %fusion.10 = f32[1,256,8,128]{1,3,2,0:T(8,128)} fusion(bf16[256,8,128]{0,2,1:T(8,128)(2,1)} %bitcast.194, bf16[256,8,128]{0,2,1:T(8,128)(2,1)S(1)} %bitcast.197, bf16[256,8,128]{0,2,1:T(8,128)(2,1)} %bitcast.196, f32[8,256]{1,0:T(8,128)S(1)} %bitcast_add_fusion.2, pred[256,256]{1,0:T(8,128)(4,1)S(1)} %iota_compare_fusion), kind=kOutput, calls=%fused_computation.35 | convolution fusion | flops 271056896 | bytes 2695168 | tf_op jit(solution)/shard_map/hbij,bjhd->bihd/dot_general | solution.py:62
  28.6 2.6 %gather_fusion = bf16[4,256,1536]{2,1,0:T(8,128)(2,1)S(1)} fusion(bf16[4,256,1536]{2,1,0:T(8,128)(2,1)} %bitcast.192, s32[1024]{0:T(1024)S(1)} %pad_clamp_fusion.1), kind=kCustom, calls=%fused_computation | custom fusion | bytes 6291472 | tf_op jit(solution)/shard_map/jit(_take)/gather | solution.py:99
  31.8 2.4 %copy.85 = bf16[256,1024]{0,1:T(8,128)(2,1)} copy(bf16[256,1024]{1,0:T(8,128)(2,1)} %param.12) | data formatting | bytes 1048576 | tf_op args[3]
  35.0 1.8 %add_bitcast_fusion = f32[8,128,128]{2,0,1:T(8,128)} fusion(bf16[8,16640]{1,0:T(8,128)(2,1)} %collective-permute-done, f32[]{:T(128)} %bitcast.22, f32[]{:T(128)S(6)} %select_n.483), kind=kLoop, calls=%fused_computation.99 | loop fusion | flops 393216 | bytes 786440 | tf_op jit(solution)/shard_map/add | solution.py:114
  36.8 2.1 %copy.82 = f32[8,128,128]{1,2,0:T(8,128)} copy(f32[8,128,128]{2,0,1:T(8,128)} %add_bitcast_fusion) | data formatting | bytes 1048576 | tf_op jit(solution)/shard_map/add | solution.py:114
  39.7 2.1 %copy.81 = f32[8,128,128]{1,2,0:T(8,128)} copy(f32[8,128,128]{2,0,1:T(8,128)} %fusion.57) | data formatting | bytes 1048576 | tf_op jit(solution)/shard_map/reshape | solution.py:107
  44.0 2.0 %multiply_reduce_fusion = (f32[256,8]{0,1:T(8,128)S(1)}, f32[1,256,8,128]{1,3,2,0:T(8,128)S(1)}) fusion(f32[1,256,8,128]{1,3,2,0:T(8,128)} %fusion.10, bf16[256,8,128]{0,2,1:T(8,128)(2,1)S(1)} %bitcast.198, f32[8,128,128]{1,2,0:T(8,128)S(1)} %copy.83, f32[8,128,128]{1,2,0:T(8,128)S(1)} %copy-done.6, f32[8,128,128]{1,2,0:T(8,128)S(1)} %copy-done.7, ...), kind=kOutput, calls=%fused_computation.56 | convolution fusion | flops 404355072 | bytes 4210784 | tf_op jit(solution)/shard_map/bihd,bhde->bihe/dot_general | solution.py:118
  47.4 1.6 %collective-permute-start.3 = (bf16[256,2,256]{0,2,1:T(8,128)(2,1)S(1)}, bf16[256,2,256]{0,2,1:T(8,128)(2,1)S(1)}, u32[]{:S(2)}, u32[]{:S(2)}) collective-permute-start(bf16[256,2,256]{0,2,1:T(8,128)(2,1)S(1)} %get-tuple-element.32), channel_id=1, source_target_pairs={{0,2},{1,3},{2,0},{3,1},{4,6},{5,7},{6,4},{7,5},{8,10},{9,11},{10,... | collective-permute-start | bytes 786440 | tf_op jit(solution)/shard_map/ppermute | solution.py:142
  49.0 5.9 %collective-permute-done.3 = bf16[256,2,256]{0,2,1:T(8,128)(2,1)S(1)} collective-permute-done((bf16[256,2,256]{0,2,1:T(8,128)(2,1)S(1)}, bf16[256,2,256]{0,2,1:T(8,128)(2,1)S(1)}, u32[]{:S(2)}, u32[]{:S(2)}) %collective-permute-start.3) | collective-permute-done | bytes 262176 | tf_op jit(solution)/shard_map/ppermute | solution.py:142
  56.6 4.8 %collective-permute-start.6 = (bf16[256,256]{1,0:T(8,128)(2,1)S(1)}, bf16[256,256]{1,0:T(8,128)(2,1)S(1)}, u32[]{:S(2)}, u32[]{:S(2)}) collective-permute-start(bf16[256,256]{1,0:T(8,128)(2,1)S(1)} %bitcast.203), channel_id=1, source_target_pairs={{0,8},{1,12},{2,2},{3,6},{4,9},{5,13},{6,3},{7,7},{8,0},{9,4},{10,... | collective-permute-start | bytes 393224 | tf_op jit(solution)/shard_map/ppermute | solution.py:153
  61.5 2.8 %collective-permute-done.5 = bf16[256,256]{1,0:T(8,128)(2,1)S(1)} collective-permute-done((bf16[256,256]{1,0:T(8,128)(2,1)S(1)}, bf16[256,256]{1,0:T(8,128)(2,1)S(1)}, u32[]{:S(2)}, u32[]{:S(2)}) %collective-permute-start.5) | collective-permute-done | bytes 131104 | tf_op jit(solution)/shard_map/ppermute | solution.py:153
  64.3 5.6 %collective-permute-done.6 = bf16[256,256]{1,0:T(8,128)(2,1)S(1)} collective-permute-done((bf16[256,256]{1,0:T(8,128)(2,1)S(1)}, bf16[256,256]{1,0:T(8,128)(2,1)S(1)}, u32[]{:S(2)}, u32[]{:S(2)}) %collective-permute-start.6) | collective-permute-done | bytes 131104 | tf_op jit(solution)/shard_map/ppermute | solution.py:153
  71.9 12.0 %collective-permute-done.8 = bf16[4,256,256]{2,1,0:T(8,128)(2,1)S(1)} collective-permute-done((bf16[4,256,256]{2,1,0:T(8,128)(2,1)S(1)}, bf16[4,256,256]{2,1,0:T(8,128)(2,1)S(1)}, u32[]{:S(2)}, u32[]{:S(2)}) %collective-permute-start.8) | collective-permute-done | bytes 524320 | tf_op jit(solution)/shard_map/ppermute | solution.py:179
  84.1 1.5 collective-permute-start.9
  85.6 2.3 %broadcast_select_fusion = bf16[4,256,1536]{2,1,0:T(8,128)(2,1)S(1)} fusion(bf16[4,256,1536]{2,1,0:T(8,128)(2,1)} %copy-done, pred[4]{0:T(512)(128)(4,1)S(1)} %get-tuple-element.42), kind=kLoop, calls=%fused_computation.15 | loop fusion | flops 1572864 | bytes 6291460 | tf_op jit(solution)/shard_map/jit(_take)/select_n | solution.py:99
  89.8 2.9 %collective-permute-start.10 = (bf16[256,1536]{1,0:T(8,128)(2,1)S(1)}, bf16[256,1536]{1,0:T(8,128)(2,1)S(1)}, u32[]{:S(2)}, u32[]{:S(2)}) collective-permute-start(bf16[256,1536]{1,0:T(8,128)(2,1)S(1)} %fusion.5), channel_id=1, source_target_pairs={{0,4},{4,8},{1,5},{5,9},{2,6},{6,10},{3,7},{7,11},{16,20},{20,24},... | collective-permute-start | bytes 2359304 | tf_op jit(solution)/shard_map/ppermute | solution.py:194
  95.6 5.3 %collective-permute-start.12 = (bf16[256,1536]{1,0:T(8,128)(2,1)S(1)}, bf16[256,1536]{1,0:T(8,128)(2,1)S(1)}, u32[]{:S(2)}, u32[]{:S(2)}) collective-permute-start(bf16[256,1536]{1,0:T(8,128)(2,1)S(1)} %fusion.6), channel_id=1, source_target_pairs={{0,12},{1,13},{2,14},{3,15},{16,28},{17,29},{18,30},{19,31}} | collective-permute-start | bytes 2359304 | tf_op jit(solution)/shard_map/ppermute | solution.py:197
  100.9 1.3 collective-permute-start.15
  103.2 7.4 %collective-permute-done.10 = bf16[256,1536]{1,0:T(8,128)(2,1)S(1)} collective-permute-done((bf16[256,1536]{1,0:T(8,128)(2,1)S(1)}, bf16[256,1536]{1,0:T(8,128)(2,1)S(1)}, u32[]{:S(2)}, u32[]{:S(2)}) %collective-permute-start.10) | collective-permute-done | bytes 786464 | tf_op jit(solution)/shard_map/ppermute | solution.py:194
  111.6 4.4 %collective-permute-start.11 = (bf16[256,1536]{1,0:T(8,128)(2,1)S(1)}, bf16[256,1536]{1,0:T(8,128)(2,1)S(1)}, u32[]{:S(2)}, u32[]{:S(2)}) collective-permute-start(bf16[256,1536]{1,0:T(8,128)(2,1)S(1)} %fusion.4), channel_id=1, source_target_pairs={{0,4},{4,8},{8,12},{1,5},{5,9},{9,13},{2,6},{6,10},{10,14},{3,7},{... | collective-permute-start | bytes 2359304 | tf_op jit(solution)/shard_map/ppermute | solution.py:203
  117.1 1.3 collective-permute-start.14
  118.4 9.2 %collective-permute-done.12 = bf16[256,1536]{1,0:T(8,128)(2,1)S(1)} collective-permute-done((bf16[256,1536]{1,0:T(8,128)(2,1)S(1)}, bf16[256,1536]{1,0:T(8,128)(2,1)S(1)}, u32[]{:S(2)}, u32[]{:S(2)}) %collective-permute-start.12) | collective-permute-done | bytes 786464 | tf_op jit(solution)/shard_map/ppermute | solution.py:197
  127.5 5.5 %collective-permute-done.15 = bf16[256,1536]{1,0:T(8,128)(2,1)S(1)} collective-permute-done((bf16[256,1536]{1,0:T(8,128)(2,1)S(1)}, bf16[256,1536]{1,0:T(8,128)(2,1)S(1)}, u32[]{:S(2)}, u32[]{:S(2)}) %collective-permute-start.15) | collective-permute-done | bytes 786464 | tf_op jit(solution)/shard_map/ppermute | solution.py:201
  133.1 10.8 %collective-permute-done.11 = bf16[256,1536]{1,0:T(8,128)(2,1)S(1)} collective-permute-done((bf16[256,1536]{1,0:T(8,128)(2,1)S(1)}, bf16[256,1536]{1,0:T(8,128)(2,1)S(1)}, u32[]{:S(2)}, u32[]{:S(2)}) %collective-permute-start.11) | collective-permute-done | bytes 786464 | tf_op jit(solution)/shard_map/ppermute | solution.py:203
  143.8 5.3 %collective-permute-done.14 = bf16[256,1536]{1,0:T(8,128)(2,1)S(1)} collective-permute-done((bf16[256,1536]{1,0:T(8,128)(2,1)S(1)}, bf16[256,1536]{1,0:T(8,128)(2,1)S(1)}, u32[]{:S(2)}, u32[]{:S(2)}) %collective-permute-start.14) | collective-permute-done | bytes 786464 | tf_op jit(solution)/shard_map/ppermute | solution.py:212
  149.1 1.4 add_convert_fusion
  (94 shorter events, 24.5 us)
Async XLA Ops:
  5.6 0.8 copy-start.2
  5.7 14.3 %copy-start.10 = (s32[1536]{0:T(1024)S(1)}, s32[1536]{0:T(1024)}, u32[]{:S(2)}) copy-start(s32[1536]{0:T(1024)} %param.17) | copy-start | bytes 18436
  6.2 0.8 copy-start.3
  6.2 15.9 %copy-start.1 = (bf16[1024,1536]{1,0:T(8,128)(2,1)S(1)}, bf16[1024,1536]{1,0:T(8,128)(2,1)}, u32[]{:S(2)}) copy-start(bf16[1024,1536]{1,0:T(8,128)(2,1)} %param.16) | copy-start | bytes 9437188
  8.2 26.8 %collective-permute-start = (bf16[8,16640]{1,0:T(8,128)(2,1)}, bf16[8,16640]{1,0:T(8,128)(2,1)}, u32[]{:S(2)}, u32[]{:S(2)}) collective-permute-start(bf16[8,16640]{1,0:T(8,128)(2,1)} %pad_maximum_fusion.3), channel_id=1, source_target_pairs={{0,4},{4,8},{8,12},{1,5},{5,9},{9,13},{2,6},{6,10},{10,14},{3,7},{... | collective-permute-start | bytes 798728 | tf_op jit(solution)/shard_map/ppermute | solution.py:106
  13.8 25.0 %collective-permute-start.1 = (bf16[8,16640]{1,0:T(8,128)(2,1)}, bf16[8,16640]{1,0:T(8,128)(2,1)S(1)}, u32[]{:S(2)}, u32[]{:S(2)}) collective-permute-start(bf16[8,16640]{1,0:T(8,128)(2,1)} %pad_maximum_fusion.3), channel_id=1, source_target_pairs={{0,8},{4,12},{1,9},{5,13},{2,10},{6,14},{3,11},{7,15},{16,24},{20,... | collective-permute-start | bytes 798728 | tf_op jit(solution)/shard_map/ppermute | solution.py:106
  17.6 24.1 %collective-permute-start.2 = (bf16[8,16640]{1,0:T(8,128)(2,1)}, bf16[8,16640]{1,0:T(8,128)(2,1)}, u32[]{:S(2)}, u32[]{:S(2)}) collective-permute-start(bf16[8,16640]{1,0:T(8,128)(2,1)} %pad_maximum_fusion.3), channel_id=1, source_target_pairs={{0,12},{1,13},{2,14},{3,15},{16,28},{17,29},{18,30},{19,31}} | collective-permute-start | bytes 798728 | tf_op jit(solution)/shard_map/ppermute | solution.py:106
  22.1 2.6 %copy-start.8 = (bf16[256,1024]{0,1:T(8,128)(2,1)S(1)}, bf16[256,1024]{0,1:T(8,128)(2,1)}, u32[]{:S(2)}) copy-start(bf16[256,1024]{0,1:T(8,128)(2,1)} %copy.75) | copy-start | bytes 1572868
  25.2 3.3 %copy-start.4 = (bf16[256,1024]{0,1:T(8,128)(2,1)}, bf16[256,1024]{0,1:T(8,128)(2,1)S(1)}, u32[]{:S(2)}) copy-start(bf16[256,1024]{0,1:T(8,128)(2,1)S(1)} %fusion.16) | copy-start | bytes 1572868
  31.2 10.5 %copy-start = (bf16[4,256,1536]{2,1,0:T(8,128)(2,1)}, bf16[4,256,1536]{2,1,0:T(8,128)(2,1)S(1)}, u32[]{:S(2)}) copy-start(bf16[4,256,1536]{2,1,0:T(8,128)(2,1)S(1)} %gather_fusion) | copy-start | bytes 9437188
  41.7 2.2 %copy-start.5 = (bf16[256,1024]{0,1:T(8,128)(2,1)S(1)}, bf16[256,1024]{0,1:T(8,128)(2,1)}, u32[]{:S(2)}) copy-start(bf16[256,1024]{0,1:T(8,128)(2,1)} %copy-done.4) | copy-start | bytes 1572868
  41.7 2.2 %copy-start.6 = (f32[8,128,128]{1,2,0:T(8,128)S(1)}, f32[8,128,128]{1,2,0:T(8,128)}, u32[]{:S(2)}) copy-start(f32[8,128,128]{1,2,0:T(8,128)} %copy.82) | copy-start | bytes 1572868
  41.7 2.2 %copy-start.7 = (f32[8,128,128]{1,2,0:T(8,128)S(1)}, f32[8,128,128]{1,2,0:T(8,128)}, u32[]{:S(2)}) copy-start(f32[8,128,128]{1,2,0:T(8,128)} %copy.81) | copy-start | bytes 1572868
  46.0 1.0 copy-start.9
  46.0 1.0 copy-start.11
  47.4 7.5 %collective-permute-start.3 = (bf16[256,2,256]{0,2,1:T(8,128)(2,1)S(1)}, bf16[256,2,256]{0,2,1:T(8,128)(2,1)S(1)}, u32[]{:S(2)}, u32[]{:S(2)}) collective-permute-start(bf16[256,2,256]{0,2,1:T(8,128)(2,1)S(1)} %get-tuple-element.32), channel_id=1, source_target_pairs={{0,2},{1,3},{2,0},{3,1},{4,6},{5,7},{6,4},{7,5},{8,10},{9,11},{10,... | collective-permute-start | bytes 786440 | tf_op jit(solution)/shard_map/ppermute | solution.py:142
  55.2 6.3 %collective-permute-start.4 = (bf16[256,256]{1,0:T(8,128)(2,1)S(1)}, bf16[256,256]{1,0:T(8,128)(2,1)S(1)}, u32[]{:S(2)}, u32[]{:S(2)}) collective-permute-start(bf16[256,256]{1,0:T(8,128)(2,1)S(1)} %bitcast.201), channel_id=1, source_target_pairs={{0,0},{1,4},{2,10},{3,14},{4,1},{5,5},{6,11},{7,15},{8,8},{9,12},{... | collective-permute-start | bytes 393224 | tf_op jit(solution)/shard_map/ppermute | solution.py:153
  56.0 8.3 %collective-permute-start.5 = (bf16[256,256]{1,0:T(8,128)(2,1)S(1)}, bf16[256,256]{1,0:T(8,128)(2,1)S(1)}, u32[]{:S(2)}, u32[]{:S(2)}) collective-permute-start(bf16[256,256]{1,0:T(8,128)(2,1)S(1)} %bitcast.202), channel_id=1, source_target_pairs={{0,1},{1,5},{2,11},{3,15},{4,8},{5,12},{6,2},{7,6},{8,9},{9,13},{1... | collective-permute-start | bytes 393224 | tf_op jit(solution)/shard_map/ppermute | solution.py:153
  56.6 13.3 %collective-permute-start.6 = (bf16[256,256]{1,0:T(8,128)(2,1)S(1)}, bf16[256,256]{1,0:T(8,128)(2,1)S(1)}, u32[]{:S(2)}, u32[]{:S(2)}) collective-permute-start(bf16[256,256]{1,0:T(8,128)(2,1)S(1)} %bitcast.203), channel_id=1, source_target_pairs={{0,8},{1,12},{2,2},{3,6},{4,9},{5,13},{6,3},{7,7},{8,0},{9,4},{10,... | collective-permute-start | bytes 393224 | tf_op jit(solution)/shard_map/ppermute | solution.py:153
  61.4 8.5 %collective-permute-start.7 = (bf16[256,256]{1,0:T(8,128)(2,1)S(1)}, bf16[256,256]{1,0:T(8,128)(2,1)S(1)}, u32[]{:S(2)}, u32[]{:S(2)}) collective-permute-start(bf16[256,256]{1,0:T(8,128)(2,1)S(1)} %bitcast.204), channel_id=1, source_target_pairs={{0,9},{1,13},{2,3},{3,7},{4,0},{5,4},{6,10},{7,14},{8,1},{9,5},{10... | collective-permute-start | bytes 393224 | tf_op jit(solution)/shard_map/ppermute | solution.py:153
  70.7 13.3 %collective-permute-start.8 = (bf16[4,256,256]{2,1,0:T(8,128)(2,1)S(1)}, bf16[4,256,256]{2,1,0:T(8,128)(2,1)S(1)}, u32[]{:S(2)}, u32[]{:S(2)}) collective-permute-start(bf16[4,256,256]{2,1,0:T(8,128)(2,1)S(1)} %broadcast_select_fusion.1), channel_id=1, source_target_pairs={{0,2},{1,3},{2,0},{3,1},{4,6},{5,7},{6,4},{7,5},{8,10},{9,11},{10,... | collective-permute-start | bytes 1572872 | tf_op jit(solution)/shard_map/ppermute | solution.py:179
  84.1 3.8 %collective-permute-start.9 = (bf16[2,4,256,256]{3,2,0,1:T(8,128)(2,1)S(1)}, bf16[2,4,256,256]{3,2,0,1:T(8,128)(2,1)S(1)}, u32[]{:S(2)}, u32[]{:S(2)}) collective-permute-start(bf16[2,4,256,256]{3,2,0,1:T(8,128)(2,1)S(1)} %get-tuple-element.27), channel_id=1, source_target_pairs={{0,1},{1,0},{2,3},{3,2},{4,5},{5,4},{6,7},{7,6},{8,9},{9,8},{10,11... | collective-permute-start | bytes 3145736 | tf_op jit(solution)/shard_map/ppermute | solution.py:181
  89.8 20.7 %collective-permute-start.10 = (bf16[256,1536]{1,0:T(8,128)(2,1)S(1)}, bf16[256,1536]{1,0:T(8,128)(2,1)S(1)}, u32[]{:S(2)}, u32[]{:S(2)}) collective-permute-start(bf16[256,1536]{1,0:T(8,128)(2,1)S(1)} %fusion.5), channel_id=1, source_target_pairs={{0,4},{4,8},{1,5},{5,9},{2,6},{6,10},{3,7},{7,11},{16,20},{20,24},... | collective-permute-start | bytes 2359304 | tf_op jit(solution)/shard_map/ppermute | solution.py:194
  93.8 22.3 %collective-permute-start.13 = (bf16[256,1536]{1,0:T(8,128)(2,1)S(1)}, bf16[256,1536]{1,0:T(8,128)(2,1)S(1)}, u32[]{:S(2)}, u32[]{:S(2)}) collective-permute-start(bf16[256,1536]{1,0:T(8,128)(2,1)S(1)} %fusion.7), channel_id=1, source_target_pairs={{12,8},{8,4},{13,9},{9,5},{14,10},{10,6},{15,11},{11,7},{28,24},{2... | collective-permute-start | bytes 2359304 | tf_op jit(solution)/shard_map/ppermute | solution.py:198
  95.6 31.9 %collective-permute-start.12 = (bf16[256,1536]{1,0:T(8,128)(2,1)S(1)}, bf16[256,1536]{1,0:T(8,128)(2,1)S(1)}, u32[]{:S(2)}, u32[]{:S(2)}) collective-permute-start(bf16[256,1536]{1,0:T(8,128)(2,1)S(1)} %fusion.6), channel_id=1, source_target_pairs={{0,12},{1,13},{2,14},{3,15},{16,28},{17,29},{18,30},{19,31}} | collective-permute-start | bytes 2359304 | tf_op jit(solution)/shard_map/ppermute | solution.py:197
  100.9 32.1 %collective-permute-start.15 = (bf16[256,1536]{1,0:T(8,128)(2,1)S(1)}, bf16[256,1536]{1,0:T(8,128)(2,1)S(1)}, u32[]{:S(2)}, u32[]{:S(2)}) collective-permute-start(bf16[256,1536]{1,0:T(8,128)(2,1)S(1)} %fusion.8), channel_id=1, source_target_pairs={{12,0},{13,1},{14,2},{15,3},{28,16},{29,17},{30,18},{31,19}} | collective-permute-start | bytes 2359304 | tf_op jit(solution)/shard_map/ppermute | solution.py:201
  111.6 32.2 %collective-permute-start.11 = (bf16[256,1536]{1,0:T(8,128)(2,1)S(1)}, bf16[256,1536]{1,0:T(8,128)(2,1)S(1)}, u32[]{:S(2)}, u32[]{:S(2)}) collective-permute-start(bf16[256,1536]{1,0:T(8,128)(2,1)S(1)} %fusion.4), channel_id=1, source_target_pairs={{0,4},{4,8},{8,12},{1,5},{5,9},{9,13},{2,6},{6,10},{10,14},{3,7},{... | collective-permute-start | bytes 2359304 | tf_op jit(solution)/shard_map/ppermute | solution.py:203
  117.1 32.1 %collective-permute-start.14 = (bf16[256,1536]{1,0:T(8,128)(2,1)S(1)}, bf16[256,1536]{1,0:T(8,128)(2,1)S(1)}, u32[]{:S(2)}, u32[]{:S(2)}) collective-permute-start(bf16[256,1536]{1,0:T(8,128)(2,1)S(1)} %fusion.3), channel_id=1, source_target_pairs={{12,8},{8,4},{4,0},{13,9},{9,5},{5,1},{14,10},{10,6},{6,2},{15,11}... | collective-permute-start | bytes 2359304 | tf_op jit(solution)/shard_map/ppermute | solution.py:212

commit v18 on v17

--- a/solution.py
+++ b/solution.py
@@ -100,19 +100,20 @@
         weights.reshape(n_mdl, piece, weights.shape[1]), mu_tab.reshape(-1), axis=0
     ).reshape(n_x, 2, piece, weights.shape[1])
     position = lax.axis_index("seq")
-    incoming = jnp.zeros((heads_here, HDIM, HDIM), jnp.float32)
+    incoming = jnp.zeros((heads_here, HDIM * HDIM), jnp.float32)
     gap = jnp.zeros((heads_here,), jnp.float32)
     for d in range(1, n_seq):
         came = lax.ppermute(packed, "seq", [(z, z + d) for z in range(n_seq - d)])
-        came_state = came[:, : HDIM * HDIM].astype(jnp.float32).reshape(heads_here, HDIM, HDIM)
+        came_state = came[:, : HDIM * HDIM].astype(jnp.float32)
         came_log = came[:, HDIM * HDIM].astype(jnp.float32) + came[:, HDIM * HDIM + HDIM].astype(
             jnp.float32
         )
         weight = jnp.where(d <= position, jnp.exp(jnp.minimum(gap, 0.0)), 0.0)
-        incoming = incoming + weight[:, None, None] * came_state
+        incoming = incoming + weight[:, None] * came_state
         if d == 1:
             incoming = incoming + w_perm[0, 0, 0, 0].astype(jnp.float32) * 0.0
         gap = gap + came_log
+    incoming = incoming.reshape(heads_here, HDIM, HDIM)
     before = jnp.cumsum(block_total, axis=1) - block_total
     entry_state = entry_local + jnp.exp(before).T[:, :, None, None] * incoming[None]
     from_state = jnp.einsum(

time: 151 us -> 148 us (0.980)
  local copies, waits for them, and re-layouts: 17.5 us -> 13.4 us
    reshape x2 -> x0, local copies, waits for them, and re-layouts: 2.28 us -> none  [per_device(): came[:, :HDIM * HDIM].astype(jnp.float32).reshape(heads_here, HDIM, HDIM)]
    add x1 -> x0, local copies, waits for them, and re-layouts: 2.08 us -> none  [per_device(): incoming = incoming + w_perm[0, 0, 0, 0].astype(jnp.float32) * 0.0]
    reshape x2 -> x0, other arithmetic: 1.93 us -> none  [per_device(): came[:, :HDIM * HDIM].astype(jnp.float32).reshape(heads_here, HDIM, HDIM)]
    convert_element_type x1, other arithmetic: 0.52 us -> 2.41 us  [per_device(): query_feat = jax.nn.silu(queries.astype(jnp.float32)).astype(jnp.bfloat16...]
    add x1 -> x0, other arithmetic: 1.8 us -> none  [per_device(): incoming = incoming + w_perm[0, 0, 0, 0].astype(jnp.float32) * 0.0]
    unnamed x28 -> x22, local copies, waits for them, and re-layouts: 8.42 us -> 8.48 us
  transfers between devices with their start and end apart: 16 -> 16, of which waited for: 9 -> 9; matrix products, arithmetic and copies ran while one was open for 19% -> 17% of each run, Pallas kernels for 0% -> 0%
where the time goes in v18:
time: 148 us; the launch traced here: 147 us
  waiting for transfers between devices  64.8 us (44%)
  starting transfers between devices  38.5 us (26%)
  other arithmetic  18 us (12%)
  local copies, waits for them, and re-layouts  13.4 us (9%)
  matrix products  11.2 us (8%)
    ppermute x1, waiting for transfers between devices, per_device(): got.append(lax.ppermute(x, 'mdl', perm))  13 us
    ppermute x3, starting transfers between devices, per_device(): came = lax.ppermute(packed, 'seq', [(z, z + d) for z in range(n_seq - d)])  12.1 us
    ppermute x1, waiting for transfers between devices, per_device(): lax.ppermute(bf(partial_for(jnp.clip(s_me + 1, 0, 3)) + near_r.astype(jnp...  10.8 us
    ppermute x1, waiting for transfers between devices, per_device(): far_r = lax.ppermute(bf(partial_for(jnp.int32(3))), 'seq', [(0, 3)])  9.16 us
    unnamed x22, local copies, waits for them, and re-layouts  8.48 us
    ppermute x4, waiting for transfers between devices, per_device(): received.append(lax.ppermute(item, ('seq', 'mdl'), perm))  7.75 us
    ppermute x1, waiting for transfers between devices, per_device(): lax.ppermute(bf(partial_for(jnp.clip(s_me + 2, 0, 3))), 'seq', [(0, 1), (...  7.36 us
    ppermute x4, starting transfers between devices, per_device(): received.append(lax.ppermute(item, ('seq', 'mdl'), perm))  7.19 us
  transfers between devices with their start and end apart: 16, of which 9 were waited for; matrix products, arithmetic and copies ran while one was open for 17% of the time, Pallas kernels for 0%

profile of v18, /device:TPU:0, one launch (start us, length us, event | category | flops | bytes accessed | tf_op | source)
XLA Modules:
  0.0 147.1 jit_solution(14933625494824646292)
XLA Ops:
  0.0 1.2 reduce-window.6
  2.8 1.2 copy.66
  4.1 2.0 %copy.68 = bf16[256,1024]{0,1:T(8,128)(2,1)} copy(bf16[256,1024]{1,0:T(8,128)(2,1)} %param.10) | data formatting | bytes 1048576 | tf_op args[1]
  6.5 1.8 %fusion.20 = bf16[256,1024]{0,1:T(8,128)(2,1)S(1)} fusion(bf16[256,1024]{0,1:T(8,128)(2,1)} %copy.68, f32[1024]{0:T(1024)S(1)} %bitcast.200), kind=kLoop, calls=%fused_computation.51 | loop fusion | flops 3407872 | bytes 1052672 | tf_op jit(solution)/shard_map/convert_element_type | solution.py:52
  10.2 4.9 %collective-permute-start = (bf16[8,16640]{1,0:T(8,128)(2,1)}, bf16[8,16640]{1,0:T(8,128)(2,1)S(1)}, u32[]{:S(2)}, u32[]{:S(2)}) collective-permute-start(bf16[8,16640]{1,0:T(8,128)(2,1)} %pad_maximum_fusion.3), channel_id=1, source_target_pairs={{0,4},{4,8},{8,12},{1,5},{5,9},{9,13},{2,6},{6,10},{10,14},{3,7},{... | collective-permute-start | bytes 798728 | tf_op jit(solution)/shard_map/ppermute | solution.py:106
  15.2 5.2 %collective-permute-start.1 = (bf16[8,16640]{1,0:T(8,128)(2,1)}, bf16[8,16640]{1,0:T(8,128)(2,1)}, u32[]{:S(2)}, u32[]{:S(2)}) collective-permute-start(bf16[8,16640]{1,0:T(8,128)(2,1)} %pad_maximum_fusion.3), channel_id=1, source_target_pairs={{0,8},{4,12},{1,9},{5,13},{2,10},{6,14},{3,11},{7,15},{16,24},{20,... | collective-permute-start | bytes 798728 | tf_op jit(solution)/shard_map/ppermute | solution.py:106
  20.4 2.0 %collective-permute-start.2 = (bf16[8,16640]{1,0:T(8,128)(2,1)}, bf16[8,16640]{1,0:T(8,128)(2,1)}, u32[]{:S(2)}, u32[]{:S(2)}) collective-permute-start(bf16[8,16640]{1,0:T(8,128)(2,1)} %pad_maximum_fusion.3), channel_id=1, source_target_pairs={{0,12},{1,13},{2,14},{3,15},{16,28},{17,29},{18,30},{19,31}} | collective-permute-start | bytes 798728 | tf_op jit(solution)/shard_map/ppermute | solution.py:106
  22.8 2.7 %multiply_convert_fusion = bf16[1024,1536]{1,0:T(8,128)(2,1)} fusion(bf16[1024,1536]{1,0:T(8,128)(2,1)S(1)} %copy-done.1, f32[1536]{0:T(1024)S(1)} %select_add_fusion), kind=kLoop, calls=%fused_computation.2 | loop fusion | flops 11010048 | bytes 6297600 | tf_op jit(solution)/shard_map/convert_element_type | solution.py:20
  25.4 2.6 %gather_fusion = bf16[4,256,1536]{2,1,0:T(8,128)(2,1)S(1)} fusion(bf16[4,256,1536]{2,1,0:T(8,128)(2,1)} %bitcast.182, s32[1024]{0:T(1024)S(1)} %pad_clamp_fusion.1), kind=kCustom, calls=%fused_computation | custom fusion | bytes 6291472 | tf_op jit(solution)/shard_map/jit(_take)/gather | solution.py:99
  28.7 2.5 %copy.67 = bf16[256,1024]{0,1:T(8,128)(2,1)} copy(bf16[256,1024]{1,0:T(8,128)(2,1)} %param.9) | data formatting | bytes 1048576 | tf_op args[0]
  31.2 2.0 %copy.75 = bf16[256,1024]{0,1:T(8,128)(2,1)} copy(bf16[256,1024]{1,0:T(8,128)(2,1)} %param.12) | data formatting | bytes 1048576 | tf_op args[3]
  33.9 2.4 %fusion.16 = bf16[256,1024]{0,1:T(8,128)(2,1)} fusion(bf16[256,1024]{0,1:T(8,128)(2,1)} %copy.67, f32[1024]{0:T(1024)S(1)} %bitcast.199), kind=kLoop, calls=%fused_computation.47 | loop fusion | flops 3407872 | bytes 1052672 | tf_op jit(solution)/shard_map/convert_element_type | solution.py:47
  36.3 3.3 %fusion.10 = f32[1,256,8,128]{1,3,2,0:T(8,128)} fusion(bf16[256,8,128]{0,2,1:T(8,128)(2,1)} %bitcast.184, bf16[256,8,128]{0,2,1:T(8,128)(2,1)} %bitcast.188, bf16[256,8,128]{0,2,1:T(8,128)(2,1)} %bitcast.186, f32[8,256]{1,0:T(8,128)S(1)} %bitcast_add_fusion.2, pred[256,256]{1,0:T(8,128)(4,1)S(1)} %iota_compare_fusion), kind=kOutput, calls=%fused_computation.35 | convolution fusion | flops 271056896 | bytes 2695168 | tf_op jit(solution)/shard_map/hbij,bjhd->bihd/dot_general | solution.py:62
  43.5 1.6 %collective-permute-start.3 = (bf16[256,2,256]{0,2,1:T(8,128)(2,1)S(1)}, bf16[256,2,256]{0,2,1:T(8,128)(2,1)S(1)}, u32[]{:S(2)}, u32[]{:S(2)}) collective-permute-start(bf16[256,2,256]{0,2,1:T(8,128)(2,1)S(1)} %get-tuple-element.32), channel_id=1, source_target_pairs={{0,2},{1,3},{2,0},{3,1},{4,6},{5,7},{6,4},{7,5},{8,10},{9,11},{10,... | collective-permute-start | bytes 786440 | tf_op jit(solution)/shard_map/ppermute | solution.py:143
  45.1 5.9 %collective-permute-done.3 = bf16[256,2,256]{0,2,1:T(8,128)(2,1)S(1)} collective-permute-done((bf16[256,2,256]{0,2,1:T(8,128)(2,1)S(1)}, bf16[256,2,256]{0,2,1:T(8,128)(2,1)S(1)}, u32[]{:S(2)}, u32[]{:S(2)}) %collective-permute-start.3) | collective-permute-done | bytes 262176 | tf_op jit(solution)/shard_map/ppermute | solution.py:143
  53.4 5.3 %collective-permute-start.6 = (bf16[256,256]{1,0:T(8,128)(2,1)S(1)}, bf16[256,256]{1,0:T(8,128)(2,1)S(1)}, u32[]{:S(2)}, u32[]{:S(2)}) collective-permute-start(bf16[256,256]{1,0:T(8,128)(2,1)S(1)} %bitcast.193), channel_id=1, source_target_pairs={{0,8},{1,12},{2,2},{3,6},{4,9},{5,13},{6,3},{7,7},{8,0},{9,4},{10,... | collective-permute-start | bytes 393224 | tf_op jit(solution)/shard_map/ppermute | solution.py:154
  58.9 2.1 %collective-permute-done.5 = bf16[256,256]{1,0:T(8,128)(2,1)S(1)} collective-permute-done((bf16[256,256]{1,0:T(8,128)(2,1)S(1)}, bf16[256,256]{1,0:T(8,128)(2,1)S(1)}, u32[]{:S(2)}, u32[]{:S(2)}) %collective-permute-start.5) | collective-permute-done | bytes 131104 | tf_op jit(solution)/shard_map/ppermute | solution.py:154
  61.0 5.6 %collective-permute-done.6 = bf16[256,256]{1,0:T(8,128)(2,1)S(1)} collective-permute-done((bf16[256,256]{1,0:T(8,128)(2,1)S(1)}, bf16[256,256]{1,0:T(8,128)(2,1)S(1)}, u32[]{:S(2)}, u32[]{:S(2)}) %collective-permute-start.6) | collective-permute-done | bytes 131104 | tf_op jit(solution)/shard_map/ppermute | solution.py:154
  67.6 13.0 %collective-permute-done.8 = bf16[4,256,256]{2,1,0:T(8,128)(2,1)S(1)} collective-permute-done((bf16[4,256,256]{2,1,0:T(8,128)(2,1)S(1)}, bf16[4,256,256]{2,1,0:T(8,128)(2,1)S(1)}, u32[]{:S(2)}, u32[]{:S(2)}) %collective-permute-start.8) | collective-permute-done | bytes 524320 | tf_op jit(solution)/shard_map/ppermute | solution.py:180
  80.8 1.5 %collective-permute-start.9 = (bf16[2,4,256,256]{3,2,0,1:T(8,128)(2,1)S(1)}, bf16[2,4,256,256]{3,2,0,1:T(8,128)(2,1)S(1)}, u32[]{:S(2)}, u32[]{:S(2)}) collective-permute-start(bf16[2,4,256,256]{3,2,0,1:T(8,128)(2,1)S(1)} %get-tuple-element.27), channel_id=1, source_target_pairs={{0,1},{1,0},{2,3},{3,2},{4,5},{5,4},{6,7},{7,6},{8,9},{9,8},{10,11... | collective-permute-start | bytes 3145736 | tf_op jit(solution)/shard_map/ppermute | solution.py:182
  82.3 2.3 %broadcast_select_fusion = bf16[4,256,1536]{2,1,0:T(8,128)(2,1)S(1)} fusion(bf16[4,256,1536]{2,1,0:T(8,128)(2,1)} %copy-done, pred[4]{0:T(512)(128)(4,1)S(1)} %get-tuple-element.42), kind=kLoop, calls=%fused_computation.15 | loop fusion | flops 1572864 | bytes 6291460 | tf_op jit(solution)/shard_map/jit(_take)/select_n | solution.py:99
  86.6 2.8 %collective-permute-start.10 = (bf16[256,1536]{1,0:T(8,128)(2,1)S(1)}, bf16[256,1536]{1,0:T(8,128)(2,1)S(1)}, u32[]{:S(2)}, u32[]{:S(2)}) collective-permute-start(bf16[256,1536]{1,0:T(8,128)(2,1)S(1)} %fusion.5), channel_id=1, source_target_pairs={{0,4},{4,8},{1,5},{5,9},{2,6},{6,10},{3,7},{7,11},{16,20},{20,24},... | collective-permute-start | bytes 2359304 | tf_op jit(solution)/shard_map/ppermute | solution.py:195
  92.1 5.5 %collective-permute-start.12 = (bf16[256,1536]{1,0:T(8,128)(2,1)S(1)}, bf16[256,1536]{1,0:T(8,128)(2,1)S(1)}, u32[]{:S(2)}, u32[]{:S(2)}) collective-permute-start(bf16[256,1536]{1,0:T(8,128)(2,1)S(1)} %fusion.6), channel_id=1, source_target_pairs={{0,12},{1,13},{2,14},{3,15},{16,28},{17,29},{18,30},{19,31}} | collective-permute-start | bytes 2359304 | tf_op jit(solution)/shard_map/ppermute | solution.py:198
  97.6 1.3 collective-permute-start.15
  99.9 7.4 %collective-permute-done.10 = bf16[256,1536]{1,0:T(8,128)(2,1)S(1)} collective-permute-done((bf16[256,1536]{1,0:T(8,128)(2,1)S(1)}, bf16[256,1536]{1,0:T(8,128)(2,1)S(1)}, u32[]{:S(2)}, u32[]{:S(2)}) %collective-permute-start.10) | collective-permute-done | bytes 786464 | tf_op jit(solution)/shard_map/ppermute | solution.py:195
  108.3 4.4 %collective-permute-start.11 = (bf16[256,1536]{1,0:T(8,128)(2,1)S(1)}, bf16[256,1536]{1,0:T(8,128)(2,1)S(1)}, u32[]{:S(2)}, u32[]{:S(2)}) collective-permute-start(bf16[256,1536]{1,0:T(8,128)(2,1)S(1)} %fusion.4), channel_id=1, source_target_pairs={{0,4},{4,8},{8,12},{1,5},{5,9},{9,13},{2,6},{6,10},{10,14},{3,7},{... | collective-permute-start | bytes 2359304 | tf_op jit(solution)/shard_map/ppermute | solution.py:204
  113.7 1.3 collective-permute-start.14
  115.0 9.2 %collective-permute-done.12 = bf16[256,1536]{1,0:T(8,128)(2,1)S(1)} collective-permute-done((bf16[256,1536]{1,0:T(8,128)(2,1)S(1)}, bf16[256,1536]{1,0:T(8,128)(2,1)S(1)}, u32[]{:S(2)}, u32[]{:S(2)}) %collective-permute-start.12) | collective-permute-done | bytes 786464 | tf_op jit(solution)/shard_map/ppermute | solution.py:198
  124.2 5.5 %collective-permute-done.15 = bf16[256,1536]{1,0:T(8,128)(2,1)S(1)} collective-permute-done((bf16[256,1536]{1,0:T(8,128)(2,1)S(1)}, bf16[256,1536]{1,0:T(8,128)(2,1)S(1)}, u32[]{:S(2)}, u32[]{:S(2)}) %collective-permute-start.15) | collective-permute-done | bytes 786464 | tf_op jit(solution)/shard_map/ppermute | solution.py:202
  129.7 10.8 %collective-permute-done.11 = bf16[256,1536]{1,0:T(8,128)(2,1)S(1)} collective-permute-done((bf16[256,1536]{1,0:T(8,128)(2,1)S(1)}, bf16[256,1536]{1,0:T(8,128)(2,1)S(1)}, u32[]{:S(2)}, u32[]{:S(2)}) %collective-permute-start.11) | collective-permute-done | bytes 786464 | tf_op jit(solution)/shard_map/ppermute | solution.py:204
  140.5 5.3 %collective-permute-done.14 = bf16[256,1536]{1,0:T(8,128)(2,1)S(1)} collective-permute-done((bf16[256,1536]{1,0:T(8,128)(2,1)S(1)}, bf16[256,1536]{1,0:T(8,128)(2,1)S(1)}, u32[]{:S(2)}, u32[]{:S(2)}) %collective-permute-start.14) | collective-permute-done | bytes 786464 | tf_op jit(solution)/shard_map/ppermute | solution.py:213
  145.7 1.4 add_convert_fusion
  (84 shorter events, 20.0 us)
Async XLA Ops:
  6.4 1.8 %copy-start.2 = (bf16[256,1024]{0,1:T(8,128)(2,1)}, bf16[256,1024]{0,1:T(8,128)(2,1)S(1)}, u32[]{:S(2)}) copy-start(bf16[256,1024]{0,1:T(8,128)(2,1)S(1)} %multiply_convert_fusion.5) | copy-start | bytes 1572868
  6.4 16.3 %copy-start.7 = (s32[1536]{0:T(1024)S(1)}, s32[1536]{0:T(1024)}, u32[]{:S(2)}) copy-start(s32[1536]{0:T(1024)} %param.17) | copy-start | bytes 18436
  6.5 16.3 %copy-start.1 = (bf16[1024,1536]{1,0:T(8,128)(2,1)S(1)}, bf16[1024,1536]{1,0:T(8,128)(2,1)}, u32[]{:S(2)}) copy-start(bf16[1024,1536]{1,0:T(8,128)(2,1)} %param.16) | copy-start | bytes 9437188
  8.3 0.8 copy-start.3
  10.2 29.4 %collective-permute-start = (bf16[8,16640]{1,0:T(8,128)(2,1)}, bf16[8,16640]{1,0:T(8,128)(2,1)S(1)}, u32[]{:S(2)}, u32[]{:S(2)}) collective-permute-start(bf16[8,16640]{1,0:T(8,128)(2,1)} %pad_maximum_fusion.3), channel_id=1, source_target_pairs={{0,4},{4,8},{8,12},{1,5},{5,9},{9,13},{2,6},{6,10},{10,14},{3,7},{... | collective-permute-start | bytes 798728 | tf_op jit(solution)/shard_map/ppermute | solution.py:106
  15.2 24.4 %collective-permute-start.1 = (bf16[8,16640]{1,0:T(8,128)(2,1)}, bf16[8,16640]{1,0:T(8,128)(2,1)}, u32[]{:S(2)}, u32[]{:S(2)}) collective-permute-start(bf16[8,16640]{1,0:T(8,128)(2,1)} %pad_maximum_fusion.3), channel_id=1, source_target_pairs={{0,8},{4,12},{1,9},{5,13},{2,10},{6,14},{3,11},{7,15},{16,24},{20,... | collective-permute-start | bytes 798728 | tf_op jit(solution)/shard_map/ppermute | solution.py:106
  20.4 20.2 %collective-permute-start.2 = (bf16[8,16640]{1,0:T(8,128)(2,1)}, bf16[8,16640]{1,0:T(8,128)(2,1)}, u32[]{:S(2)}, u32[]{:S(2)}) collective-permute-start(bf16[8,16640]{1,0:T(8,128)(2,1)} %pad_maximum_fusion.3), channel_id=1, source_target_pairs={{0,12},{1,13},{2,14},{3,15},{16,28},{17,29},{18,30},{19,31}} | collective-permute-start | bytes 798728 | tf_op jit(solution)/shard_map/ppermute | solution.py:106
  28.1 11.5 %copy-start = (bf16[4,256,1536]{2,1,0:T(8,128)(2,1)}, bf16[4,256,1536]{2,1,0:T(8,128)(2,1)S(1)}, u32[]{:S(2)}) copy-start(bf16[4,256,1536]{2,1,0:T(8,128)(2,1)S(1)} %gather_fusion) | copy-start | bytes 9437188
  39.6 2.5 %copy-start.5 = (bf16[256,1024]{0,1:T(8,128)(2,1)S(1)}, bf16[256,1024]{0,1:T(8,128)(2,1)}, u32[]{:S(2)}) copy-start(bf16[256,1024]{0,1:T(8,128)(2,1)} %fusion.16) | copy-start | bytes 1572868
  39.6 2.5 %copy-start.6 = (f32[1,256,8,128]{1,3,2,0:T(8,128)S(1)}, f32[1,256,8,128]{1,3,2,0:T(8,128)}, u32[]{:S(2)}) copy-start(f32[1,256,8,128]{1,3,2,0:T(8,128)} %fusion.10) | copy-start | bytes 3145732
  42.1 1.0 copy-start.4
  42.1 1.0 copy-start.8
  43.5 7.6 %collective-permute-start.3 = (bf16[256,2,256]{0,2,1:T(8,128)(2,1)S(1)}, bf16[256,2,256]{0,2,1:T(8,128)(2,1)S(1)}, u32[]{:S(2)}, u32[]{:S(2)}) collective-permute-start(bf16[256,2,256]{0,2,1:T(8,128)(2,1)S(1)} %get-tuple-element.32), channel_id=1, source_target_pairs={{0,2},{1,3},{2,0},{3,1},{4,6},{5,7},{6,4},{7,5},{8,10},{9,11},{10,... | collective-permute-start | bytes 786440 | tf_op jit(solution)/shard_map/ppermute | solution.py:143
  51.3 7.6 %collective-permute-start.4 = (bf16[256,256]{1,0:T(8,128)(2,1)S(1)}, bf16[256,256]{1,0:T(8,128)(2,1)S(1)}, u32[]{:S(2)}, u32[]{:S(2)}) collective-permute-start(bf16[256,256]{1,0:T(8,128)(2,1)S(1)} %bitcast.191), channel_id=1, source_target_pairs={{0,0},{1,4},{2,10},{3,14},{4,1},{5,5},{6,11},{7,15},{8,8},{9,12},{... | collective-permute-start | bytes 393224 | tf_op jit(solution)/shard_map/ppermute | solution.py:154
  52.1 8.9 %collective-permute-start.5 = (bf16[256,256]{1,0:T(8,128)(2,1)S(1)}, bf16[256,256]{1,0:T(8,128)(2,1)S(1)}, u32[]{:S(2)}, u32[]{:S(2)}) collective-permute-start(bf16[256,256]{1,0:T(8,128)(2,1)S(1)} %bitcast.192), channel_id=1, source_target_pairs={{0,1},{1,5},{2,11},{3,15},{4,8},{5,12},{6,2},{7,6},{8,9},{9,13},{1... | collective-permute-start | bytes 393224 | tf_op jit(solution)/shard_map/ppermute | solution.py:154
  53.4 13.3 %collective-permute-start.6 = (bf16[256,256]{1,0:T(8,128)(2,1)S(1)}, bf16[256,256]{1,0:T(8,128)(2,1)S(1)}, u32[]{:S(2)}, u32[]{:S(2)}) collective-permute-start(bf16[256,256]{1,0:T(8,128)(2,1)S(1)} %bitcast.193), channel_id=1, source_target_pairs={{0,8},{1,12},{2,2},{3,6},{4,9},{5,13},{6,3},{7,7},{8,0},{9,4},{10,... | collective-permute-start | bytes 393224 | tf_op jit(solution)/shard_map/ppermute | solution.py:154
  58.8 7.9 %collective-permute-start.7 = (bf16[256,256]{1,0:T(8,128)(2,1)S(1)}, bf16[256,256]{1,0:T(8,128)(2,1)S(1)}, u32[]{:S(2)}, u32[]{:S(2)}) collective-permute-start(bf16[256,256]{1,0:T(8,128)(2,1)S(1)} %bitcast.194), channel_id=1, source_target_pairs={{0,9},{1,13},{2,3},{3,7},{4,0},{5,4},{6,10},{7,14},{8,1},{9,5},{10... | collective-permute-start | bytes 393224 | tf_op jit(solution)/shard_map/ppermute | solution.py:154
  67.4 13.2 %collective-permute-start.8 = (bf16[4,256,256]{2,1,0:T(8,128)(2,1)S(1)}, bf16[4,256,256]{2,1,0:T(8,128)(2,1)S(1)}, u32[]{:S(2)}, u32[]{:S(2)}) collective-permute-start(bf16[4,256,256]{2,1,0:T(8,128)(2,1)S(1)} %broadcast_select_fusion.1), channel_id=1, source_target_pairs={{0,2},{1,3},{2,0},{3,1},{4,6},{5,7},{6,4},{7,5},{8,10},{9,11},{10,... | collective-permute-start | bytes 1572872 | tf_op jit(solution)/shard_map/ppermute | solution.py:180
  80.8 3.8 %collective-permute-start.9 = (bf16[2,4,256,256]{3,2,0,1:T(8,128)(2,1)S(1)}, bf16[2,4,256,256]{3,2,0,1:T(8,128)(2,1)S(1)}, u32[]{:S(2)}, u32[]{:S(2)}) collective-permute-start(bf16[2,4,256,256]{3,2,0,1:T(8,128)(2,1)S(1)} %get-tuple-element.27), channel_id=1, source_target_pairs={{0,1},{1,0},{2,3},{3,2},{4,5},{5,4},{6,7},{7,6},{8,9},{9,8},{10,11... | collective-permute-start | bytes 3145736 | tf_op jit(solution)/shard_map/ppermute | solution.py:182
  86.6 20.6 %collective-permute-start.10 = (bf16[256,1536]{1,0:T(8,128)(2,1)S(1)}, bf16[256,1536]{1,0:T(8,128)(2,1)S(1)}, u32[]{:S(2)}, u32[]{:S(2)}) collective-permute-start(bf16[256,1536]{1,0:T(8,128)(2,1)S(1)} %fusion.5), channel_id=1, source_target_pairs={{0,4},{4,8},{1,5},{5,9},{2,6},{6,10},{3,7},{7,11},{16,20},{20,24},... | collective-permute-start | bytes 2359304 | tf_op jit(solution)/shard_map/ppermute | solution.py:195
  90.4 22.3 %collective-permute-start.13 = (bf16[256,1536]{1,0:T(8,128)(2,1)S(1)}, bf16[256,1536]{1,0:T(8,128)(2,1)S(1)}, u32[]{:S(2)}, u32[]{:S(2)}) collective-permute-start(bf16[256,1536]{1,0:T(8,128)(2,1)S(1)} %fusion.7), channel_id=1, source_target_pairs={{12,8},{8,4},{13,9},{9,5},{14,10},{10,6},{15,11},{11,7},{28,24},{2... | collective-permute-start | bytes 2359304 | tf_op jit(solution)/shard_map/ppermute | solution.py:199
  92.1 32.1 %collective-permute-start.12 = (bf16[256,1536]{1,0:T(8,128)(2,1)S(1)}, bf16[256,1536]{1,0:T(8,128)(2,1)S(1)}, u32[]{:S(2)}, u32[]{:S(2)}) collective-permute-start(bf16[256,1536]{1,0:T(8,128)(2,1)S(1)} %fusion.6), channel_id=1, source_target_pairs={{0,12},{1,13},{2,14},{3,15},{16,28},{17,29},{18,30},{19,31}} | collective-permute-start | bytes 2359304 | tf_op jit(solution)/shard_map/ppermute | solution.py:198
  97.6 32.1 %collective-permute-start.15 = (bf16[256,1536]{1,0:T(8,128)(2,1)S(1)}, bf16[256,1536]{1,0:T(8,128)(2,1)S(1)}, u32[]{:S(2)}, u32[]{:S(2)}) collective-permute-start(bf16[256,1536]{1,0:T(8,128)(2,1)S(1)} %fusion.8), channel_id=1, source_target_pairs={{12,0},{13,1},{14,2},{15,3},{28,16},{29,17},{30,18},{31,19}} | collective-permute-start | bytes 2359304 | tf_op jit(solution)/shard_map/ppermute | solution.py:202
  108.3 32.2 %collective-permute-start.11 = (bf16[256,1536]{1,0:T(8,128)(2,1)S(1)}, bf16[256,1536]{1,0:T(8,128)(2,1)S(1)}, u32[]{:S(2)}, u32[]{:S(2)}) collective-permute-start(bf16[256,1536]{1,0:T(8,128)(2,1)S(1)} %fusion.4), channel_id=1, source_target_pairs={{0,4},{4,8},{8,12},{1,5},{5,9},{9,13},{2,6},{6,10},{10,14},{3,7},{... | collective-permute-start | bytes 2359304 | tf_op jit(solution)/shard_map/ppermute | solution.py:204
  113.7 32.1 %collective-permute-start.14 = (bf16[256,1536]{1,0:T(8,128)(2,1)S(1)}, bf16[256,1536]{1,0:T(8,128)(2,1)S(1)}, u32[]{:S(2)}, u32[]{:S(2)}) collective-permute-start(bf16[256,1536]{1,0:T(8,128)(2,1)S(1)} %fusion.3), channel_id=1, source_target_pairs={{12,8},{8,4},{4,0},{13,9},{9,5},{5,1},{14,10},{10,6},{6,2},{15,11}... | collective-permute-start | bytes 2359304 | tf_op jit(solution)/shard_map/ppermute | solution.py:213

commit v19 on v18

--- a/solution.py
+++ b/solution.py
@@ -110,8 +110,6 @@
         )
         weight = jnp.where(d <= position, jnp.exp(jnp.minimum(gap, 0.0)), 0.0)
         incoming = incoming + weight[:, None] * came_state
-        if d == 1:
-            incoming = incoming + w_perm[0, 0, 0, 0].astype(jnp.float32) * 0.0
         gap = gap + came_log
     incoming = incoming.reshape(heads_here, HDIM, HDIM)
     before = jnp.cumsum(block_total, axis=1) - block_total
@@ -142,6 +140,7 @@
         away = lax.dynamic_slice_in_dim(own_pieces, 2 * (1 - x_me), 2, axis=1)
         came = lax.ppermute(away, "mdl", [(mu, mu ^ 2) for mu in range(n_mdl)])
         items = jnp.transpose(jnp.concatenate([keep, came], axis=1), (1, 0, 2))
+        items = items + w_perm[0, 0, 0, 0] * jnp.bfloat16(0)
         received = []
         for k in range(n_seq):
             perm = []

time: 148 us -> 151 us (1.020)
  starting transfers between devices: 38.5 us -> 45.9 us
  waiting for transfers between devices: 64.8 us -> 60.5 us
  matrix products: 11.2 us -> 12.8 us
    ppermute x4, starting transfers between devices: 7.19 us -> 14.2 us  [per_device(): received.append(lax.ppermute(item, ('seq', 'mdl'), perm))]
    ppermute x1, waiting for transfers between devices: 5.9 us -> 2 us  [per_device(): came = lax.ppermute(away, 'mdl', [(mu, mu ^ 2) for mu in range(n_mdl)])]
    unnamed x22 -> x16, local copies, waits for them, and re-layouts: 8.48 us -> 5.23 us
    another operation x1, local copies, waits for them, and re-layouts: 0.23 us -> 2.06 us  [per_device(): incoming[None]]
    dot_general x1, matrix products: 0.73 us -> 2.32 us  [per_device(): jnp.einsum('bihd,bhde->bihe', query_feat.astype(jnp.float32), entry_state...]
  transfers between devices with their start and end apart: 16 -> 16, of which waited for: 9 -> 9; matrix products, arithmetic and copies ran while one was open for 17% -> 15% of each run, Pallas kernels for 0% -> 0%
where the time goes in v19:
time: 151 us; the launch traced here: 150 us
  waiting for transfers between devices  60.5 us (40%)
  starting transfers between devices  45.9 us (30%)
  other arithmetic  16.7 us (11%)
  local copies, waits for them, and re-layouts  13.1 us (9%)
  matrix products  12.8 us (8%)
    ppermute x4, starting transfers between devices, per_device(): received.append(lax.ppermute(item, ('seq', 'mdl'), perm))  14.2 us
    ppermute x1, waiting for transfers between devices, per_device(): got.append(lax.ppermute(x, 'mdl', perm))  13 us
    ppermute x3, starting transfers between devices, per_device(): came = lax.ppermute(packed, 'seq', [(z, z + d) for z in range(n_seq - d)])  12.1 us
    ppermute x1, waiting for transfers between devices, per_device(): lax.ppermute(bf(partial_for(jnp.clip(s_me + 1, 0, 3)) + near_r.astype(jnp...  10.8 us
    ppermute x1, waiting for transfers between devices, per_device(): far_r = lax.ppermute(bf(partial_for(jnp.int32(3))), 'seq', [(0, 3)])  9.16 us
    ppermute x4, waiting for transfers between devices, per_device(): received.append(lax.ppermute(item, ('seq', 'mdl'), perm))  7.38 us
    ppermute x1, waiting for transfers between devices, per_device(): lax.ppermute(bf(partial_for(jnp.clip(s_me + 2, 0, 3))), 'seq', [(0, 1), (...  7.36 us
    dot_general x7, matrix products, partial_for(): jnp.einsum('deti,deic->tc', rows, w_perm, preferred_element_type=jnp.floa...  6.88 us
  transfers between devices with their start and end apart: 16, of which 9 were waited for; matrix products, arithmetic and copies ran while one was open for 15% of the time, Pallas kernels for 0%

profile of v19, /device:TPU:0, one launch (start us, length us, event | category | flops | bytes accessed | tf_op | source)
XLA Modules:
  0.0 150.1 jit_solution(2066329977039630657)
XLA Ops:
  4.1 1.2 copy.68
  7.5 5.6 %collective-permute-start = (bf16[8,16640]{1,0:T(8,128)(2,1)S(1)}, bf16[8,16640]{1,0:T(8,128)(2,1)}, u32[]{:S(2)}, u32[]{:S(2)}) collective-permute-start(bf16[8,16640]{1,0:T(8,128)(2,1)S(1)} %pad_maximum_fusion.3), channel_id=1, source_target_pairs={{0,4},{4,8},{8,12},{1,5},{5,9},{9,13},{2,6},{6,10},{10,14},{3,7},{... | collective-permute-start | bytes 798728 | tf_op jit(solution)/shard_map/ppermute | solution.py:106
  13.1 4.5 %collective-permute-start.1 = (bf16[8,16640]{1,0:T(8,128)(2,1)S(1)}, bf16[8,16640]{1,0:T(8,128)(2,1)}, u32[]{:S(2)}, u32[]{:S(2)}) collective-permute-start(bf16[8,16640]{1,0:T(8,128)(2,1)S(1)} %pad_maximum_fusion.3), channel_id=1, source_target_pairs={{0,8},{4,12},{1,9},{5,13},{2,10},{6,14},{3,11},{7,15},{16,24},{20,... | collective-permute-start | bytes 798728 | tf_op jit(solution)/shard_map/ppermute | solution.py:106
  17.6 2.0 %collective-permute-start.2 = (bf16[8,16640]{1,0:T(8,128)(2,1)S(1)}, bf16[8,16640]{1,0:T(8,128)(2,1)}, u32[]{:S(2)}, u32[]{:S(2)}) collective-permute-start(bf16[8,16640]{1,0:T(8,128)(2,1)S(1)} %pad_maximum_fusion.3), channel_id=1, source_target_pairs={{0,12},{1,13},{2,14},{3,15},{16,28},{17,29},{18,30},{19,31}} | collective-permute-start | bytes 798728 | tf_op jit(solution)/shard_map/ppermute | solution.py:106
  20.0 1.3 fusion.16
  21.4 2.8 %multiply_convert_fusion = bf16[1024,1536]{1,0:T(8,128)(2,1)S(1)} fusion(bf16[1024,1536]{1,0:T(8,128)(2,1)} %param.16, f32[1536]{0:T(1024)S(1)} %select_add_fusion), kind=kLoop, calls=%fused_computation.2 | loop fusion | flops 11010048 | bytes 6297600 | tf_op jit(solution)/shard_map/convert_element_type | solution.py:20
  24.3 3.3 %fusion.10 = f32[1,256,8,128]{1,3,2,0:T(8,128)} fusion(bf16[256,8,128]{0,2,1:T(8,128)(2,1)} %bitcast.184, bf16[256,8,128]{0,2,1:T(8,128)(2,1)} %bitcast.188, bf16[256,8,128]{0,2,1:T(8,128)(2,1)} %bitcast.186, f32[8,256]{1,0:T(8,128)S(1)} %bitcast_add_fusion.2, pred[256,256]{1,0:T(8,128)(4,1)S(1)} %iota_compare_fusion), kind=kOutput, calls=%fused_computation.35 | convolution fusion | flops 271056896 | bytes 2695168 | tf_op jit(solution)/shard_map/hbij,bjhd->bihd/dot_general | solution.py:62
  27.6 2.0 %copy.75 = bf16[256,1024]{0,1:T(8,128)(2,1)} copy(bf16[256,1024]{1,0:T(8,128)(2,1)} %param.12) | data formatting | bytes 1048576 | tf_op args[3]
  30.6 2.1 %add_bitcast_fusion = f32[8,128,128]{2,0,1:T(8,128)} fusion(bf16[8,16640]{1,0:T(8,128)(2,1)} %collective-permute-done.2, bf16[8,16640]{1,0:T(8,128)(2,1)} %collective-permute-done.1, bf16[8,16640]{1,0:T(8,128)(2,1)} %collective-permute-done, f32[8]{0:T(128)S(1)} %get-tuple-element.14, f32[8]{0:T(128)S(1)} %get-tuple-element.13, f32[]{:T(128)S(6)} %select_n.477), kind=kLoop, calls=%fused_computation.88 | loop fusion | flops 1048576 | bytes 1310788 | tf_op jit(solution)/shard_map/broadcast_in_dim;reshape | solution.py:116
  32.7 2.1 %copy.73 = f32[8,128,128]{1,2,0:T(8,128)} copy(f32[8,128,128]{2,0,1:T(8,128)} %add_bitcast_fusion) | data formatting | bytes 1048576 | tf_op jit(solution)/shard_map/broadcast_in_dim;reshape | solution.py:116
  34.8 2.3 %multiply_reduce_fusion = (f32[256,8]{0,1:T(8,128)S(1)}, f32[1,256,8,128]{1,3,2,0:T(8,128)S(1)}) fusion(f32[1,256,8,128]{1,3,2,0:T(8,128)} %fusion.10, bf16[256,8,128]{0,2,1:T(8,128)(2,1)} %bitcast.189, f32[8,128,128]{1,2,0:T(8,128)} %copy.73, f32[8]{0:T(128)S(1)} %get-tuple-element.37, f32[256,8]{0,1:T(8,128)S(1)} %get-tuple-element.24), kind=kOutput, calls=%fused_computation.56 | convolution fusion | flops 403830784 | bytes 3162144 | tf_op jit(solution)/shard_map/bihd,bhde->bihe/dot_general | solution.py:117
  38.3 1.5 collective-permute-start.3
  39.9 2.4 %gather_fusion = bf16[4,256,1536]{2,1,0:T(8,128)(2,1)} fusion(bf16[4,256,1536]{2,1,0:T(8,128)(2,1)S(1)} %bitcast.181, s32[1024]{0:T(1024)S(1)} %pad_clamp_fusion.1), kind=kCustom, calls=%fused_computation | custom fusion | bytes 6291472 | tf_op jit(solution)/shard_map/jit(_take)/gather | solution.py:99
  44.1 2.0 %collective-permute-done.3 = bf16[256,2,256]{0,2,1:T(8,128)(2,1)} collective-permute-done((bf16[256,2,256]{0,2,1:T(8,128)(2,1)}, bf16[256,2,256]{0,2,1:T(8,128)(2,1)}, u32[]{:S(2)}, u32[]{:S(2)}) %collective-permute-start.3) | collective-permute-done | bytes 262176 | tf_op jit(solution)/shard_map/ppermute | solution.py:141
  48.1 8.1 %collective-permute-start.5 = (bf16[256,256]{1,0:T(8,128)(2,1)S(1)}, bf16[256,256]{1,0:T(8,128)(2,1)S(1)}, u32[]{:S(2)}, u32[]{:S(2)}) collective-permute-start(bf16[256,256]{1,0:T(8,128)(2,1)S(1)} %bitcast.192), channel_id=1, source_target_pairs={{0,1},{1,5},{2,11},{3,15},{4,8},{5,12},{6,2},{7,6},{8,9},{9,13},{1... | collective-permute-start | bytes 393224 | tf_op jit(solution)/shard_map/ppermute | solution.py:153
  56.2 5.4 %collective-permute-start.6 = (bf16[256,256]{1,0:T(8,128)(2,1)S(1)}, bf16[256,256]{1,0:T(8,128)(2,1)S(1)}, u32[]{:S(2)}, u32[]{:S(2)}) collective-permute-start(bf16[256,256]{1,0:T(8,128)(2,1)S(1)} %bitcast.193), channel_id=1, source_target_pairs={{0,8},{1,12},{2,2},{3,6},{4,9},{5,13},{6,3},{7,7},{8,0},{9,4},{10,... | collective-permute-start | bytes 393224 | tf_op jit(solution)/shard_map/ppermute | solution.py:153
  61.9 1.8 %collective-permute-done.5 = bf16[256,256]{1,0:T(8,128)(2,1)S(1)} collective-permute-done((bf16[256,256]{1,0:T(8,128)(2,1)S(1)}, bf16[256,256]{1,0:T(8,128)(2,1)S(1)}, u32[]{:S(2)}, u32[]{:S(2)}) %collective-permute-start.5) | collective-permute-done | bytes 131104 | tf_op jit(solution)/shard_map/ppermute | solution.py:153
  63.7 5.6 %collective-permute-done.6 = bf16[256,256]{1,0:T(8,128)(2,1)S(1)} collective-permute-done((bf16[256,256]{1,0:T(8,128)(2,1)S(1)}, bf16[256,256]{1,0:T(8,128)(2,1)S(1)}, u32[]{:S(2)}, u32[]{:S(2)}) %collective-permute-start.6) | collective-permute-done | bytes 131104 | tf_op jit(solution)/shard_map/ppermute | solution.py:153
  70.2 13.0 %collective-permute-done.8 = bf16[4,256,256]{2,1,0:T(8,128)(2,1)S(1)} collective-permute-done((bf16[4,256,256]{2,1,0:T(8,128)(2,1)S(1)}, bf16[4,256,256]{2,1,0:T(8,128)(2,1)S(1)}, u32[]{:S(2)}, u32[]{:S(2)}) %collective-permute-start.8) | collective-permute-done | bytes 524320 | tf_op jit(solution)/shard_map/ppermute | solution.py:179
  83.4 1.5 %collective-permute-start.9 = (bf16[2,4,256,256]{3,2,0,1:T(8,128)(2,1)S(1)}, bf16[2,4,256,256]{3,2,0,1:T(8,128)(2,1)S(1)}, u32[]{:S(2)}, u32[]{:S(2)}) collective-permute-start(bf16[2,4,256,256]{3,2,0,1:T(8,128)(2,1)S(1)} %get-tuple-element.27), channel_id=1, source_target_pairs={{0,1},{1,0},{2,3},{3,2},{4,5},{5,4},{6,7},{7,6},{8,9},{9,8},{10,11... | collective-permute-start | bytes 3145736 | tf_op jit(solution)/shard_map/ppermute | solution.py:181
  84.9 2.3 %broadcast_select_fusion = bf16[4,256,1536]{2,1,0:T(8,128)(2,1)S(1)} fusion(bf16[4,256,1536]{2,1,0:T(8,128)(2,1)} %gather_fusion, pred[4]{0:T(512)(128)(4,1)S(1)} %get-tuple-element.42), kind=kLoop, calls=%fused_computation.15 | loop fusion | flops 1572864 | bytes 6291460 | tf_op jit(solution)/shard_map/jit(_take)/select_n | solution.py:99
  89.2 3.2 %collective-permute-start.10 = (bf16[256,1536]{1,0:T(8,128)(2,1)S(1)}, bf16[256,1536]{1,0:T(8,128)(2,1)S(1)}, u32[]{:S(2)}, u32[]{:S(2)}) collective-permute-start(bf16[256,1536]{1,0:T(8,128)(2,1)S(1)} %fusion.5), channel_id=1, source_target_pairs={{0,4},{4,8},{1,5},{5,9},{2,6},{6,10},{3,7},{7,11},{16,20},{20,24},... | collective-permute-start | bytes 2359304 | tf_op jit(solution)/shard_map/ppermute | solution.py:194
  95.1 5.3 %collective-permute-start.12 = (bf16[256,1536]{1,0:T(8,128)(2,1)S(1)}, bf16[256,1536]{1,0:T(8,128)(2,1)S(1)}, u32[]{:S(2)}, u32[]{:S(2)}) collective-permute-start(bf16[256,1536]{1,0:T(8,128)(2,1)S(1)} %fusion.6), channel_id=1, source_target_pairs={{0,12},{1,13},{2,14},{3,15},{16,28},{17,29},{18,30},{19,31}} | collective-permute-start | bytes 2359304 | tf_op jit(solution)/shard_map/ppermute | solution.py:197
  100.4 1.5 collective-permute-start.15
  102.8 7.4 %collective-permute-done.10 = bf16[256,1536]{1,0:T(8,128)(2,1)S(1)} collective-permute-done((bf16[256,1536]{1,0:T(8,128)(2,1)S(1)}, bf16[256,1536]{1,0:T(8,128)(2,1)S(1)}, u32[]{:S(2)}, u32[]{:S(2)}) %collective-permute-start.10) | collective-permute-done | bytes 786464 | tf_op jit(solution)/shard_map/ppermute | solution.py:194
  111.2 4.4 %collective-permute-start.11 = (bf16[256,1536]{1,0:T(8,128)(2,1)S(1)}, bf16[256,1536]{1,0:T(8,128)(2,1)S(1)}, u32[]{:S(2)}, u32[]{:S(2)}) collective-permute-start(bf16[256,1536]{1,0:T(8,128)(2,1)S(1)} %fusion.4), channel_id=1, source_target_pairs={{0,4},{4,8},{8,12},{1,5},{5,9},{9,13},{2,6},{6,10},{10,14},{3,7},{... | collective-permute-start | bytes 2359304 | tf_op jit(solution)/shard_map/ppermute | solution.py:203
  116.7 1.3 collective-permute-start.14
  118.0 9.2 %collective-permute-done.12 = bf16[256,1536]{1,0:T(8,128)(2,1)S(1)} collective-permute-done((bf16[256,1536]{1,0:T(8,128)(2,1)S(1)}, bf16[256,1536]{1,0:T(8,128)(2,1)S(1)}, u32[]{:S(2)}, u32[]{:S(2)}) %collective-permute-start.12) | collective-permute-done | bytes 786464 | tf_op jit(solution)/shard_map/ppermute | solution.py:197
  127.1 5.5 %collective-permute-done.15 = bf16[256,1536]{1,0:T(8,128)(2,1)S(1)} collective-permute-done((bf16[256,1536]{1,0:T(8,128)(2,1)S(1)}, bf16[256,1536]{1,0:T(8,128)(2,1)S(1)}, u32[]{:S(2)}, u32[]{:S(2)}) %collective-permute-start.15) | collective-permute-done | bytes 786464 | tf_op jit(solution)/shard_map/ppermute | solution.py:201
  132.7 10.8 %collective-permute-done.11 = bf16[256,1536]{1,0:T(8,128)(2,1)S(1)} collective-permute-done((bf16[256,1536]{1,0:T(8,128)(2,1)S(1)}, bf16[256,1536]{1,0:T(8,128)(2,1)S(1)}, u32[]{:S(2)}, u32[]{:S(2)}) %collective-permute-start.11) | collective-permute-done | bytes 786464 | tf_op jit(solution)/shard_map/ppermute | solution.py:203
  143.4 5.3 %collective-permute-done.14 = bf16[256,1536]{1,0:T(8,128)(2,1)S(1)} collective-permute-done((bf16[256,1536]{1,0:T(8,128)(2,1)S(1)}, bf16[256,1536]{1,0:T(8,128)(2,1)S(1)}, u32[]{:S(2)}, u32[]{:S(2)}) %collective-permute-start.14) | collective-permute-done | bytes 786464 | tf_op jit(solution)/shard_map/ppermute | solution.py:212
  148.7 1.4 add_convert_fusion
  (79 shorter events, 20.9 us)
Async XLA Ops:
  5.6 0.8 copy-start
  5.7 14.1 %copy-start.3 = (bf16[256,1024]{1,0:T(8,128)(2,1)S(1)}, bf16[256,1024]{1,0:T(8,128)(2,1)}, u32[]{:S(2)}) copy-start(bf16[256,1024]{1,0:T(8,128)(2,1)} %param.9) | copy-start | bytes 1572868
  6.2 0.8 copy-start.1
  6.2 13.8 %copy-start.4 = (s32[1536]{0:T(1024)S(1)}, s32[1536]{0:T(1024)}, u32[]{:S(2)}) copy-start(s32[1536]{0:T(1024)} %param.17) | copy-start | bytes 18436
  7.5 22.3 %collective-permute-start = (bf16[8,16640]{1,0:T(8,128)(2,1)S(1)}, bf16[8,16640]{1,0:T(8,128)(2,1)}, u32[]{:S(2)}, u32[]{:S(2)}) collective-permute-start(bf16[8,16640]{1,0:T(8,128)(2,1)S(1)} %pad_maximum_fusion.3), channel_id=1, source_target_pairs={{0,4},{4,8},{8,12},{1,5},{5,9},{9,13},{2,6},{6,10},{10,14},{3,7},{... | collective-permute-start | bytes 798728 | tf_op jit(solution)/shard_map/ppermute | solution.py:106
  13.1 16.6 %collective-permute-start.1 = (bf16[8,16640]{1,0:T(8,128)(2,1)S(1)}, bf16[8,16640]{1,0:T(8,128)(2,1)}, u32[]{:S(2)}, u32[]{:S(2)}) collective-permute-start(bf16[8,16640]{1,0:T(8,128)(2,1)S(1)} %pad_maximum_fusion.3), channel_id=1, source_target_pairs={{0,8},{4,12},{1,9},{5,13},{2,10},{6,14},{3,11},{7,15},{16,24},{20,... | collective-permute-start | bytes 798728 | tf_op jit(solution)/shard_map/ppermute | solution.py:106
  17.6 13.0 %collective-permute-start.2 = (bf16[8,16640]{1,0:T(8,128)(2,1)S(1)}, bf16[8,16640]{1,0:T(8,128)(2,1)}, u32[]{:S(2)}, u32[]{:S(2)}) collective-permute-start(bf16[8,16640]{1,0:T(8,128)(2,1)S(1)} %pad_maximum_fusion.3), channel_id=1, source_target_pairs={{0,12},{1,13},{2,14},{3,15},{16,28},{17,29},{18,30},{19,31}} | collective-permute-start | bytes 798728 | tf_op jit(solution)/shard_map/ppermute | solution.py:106
  34.8 2.4 %copy-start.2 = (bf16[256,1024]{0,1:T(8,128)(2,1)S(1)}, bf16[256,1024]{0,1:T(8,128)(2,1)}, u32[]{:S(2)}) copy-start(bf16[256,1024]{0,1:T(8,128)(2,1)} %copy.75) | copy-start | bytes 1572868
  34.8 2.5 %copy-start.5 = (f32[1024]{0:T(1024)S(1)}, f32[1024]{0:T(1024)}, u32[]{:S(2)}) copy-start(f32[1024]{0:T(1024)} %param.15) | copy-start | bytes 12292
  38.3 7.8 %collective-permute-start.3 = (bf16[256,2,256]{0,2,1:T(8,128)(2,1)}, bf16[256,2,256]{0,2,1:T(8,128)(2,1)}, u32[]{:S(2)}, u32[]{:S(2)}) collective-permute-start(bf16[256,2,256]{0,2,1:T(8,128)(2,1)} %get-tuple-element.33), channel_id=1, source_target_pairs={{0,2},{1,3},{2,0},{3,1},{4,6},{5,7},{6,4},{7,5},{8,10},{9,11},{10,... | collective-permute-start | bytes 786440 | tf_op jit(solution)/shard_map/ppermute | solution.py:141
  47.3 14.6 %collective-permute-start.4 = (bf16[256,256]{1,0:T(8,128)(2,1)S(1)}, bf16[256,256]{1,0:T(8,128)(2,1)S(1)}, u32[]{:S(2)}, u32[]{:S(2)}) collective-permute-start(bf16[256,256]{1,0:T(8,128)(2,1)S(1)} %bitcast.191), channel_id=1, source_target_pairs={{0,0},{1,4},{2,10},{3,14},{4,1},{5,5},{6,11},{7,15},{8,8},{9,12},{... | collective-permute-start | bytes 393224 | tf_op jit(solution)/shard_map/ppermute | solution.py:153
  48.1 15.6 %collective-permute-start.5 = (bf16[256,256]{1,0:T(8,128)(2,1)S(1)}, bf16[256,256]{1,0:T(8,128)(2,1)S(1)}, u32[]{:S(2)}, u32[]{:S(2)}) collective-permute-start(bf16[256,256]{1,0:T(8,128)(2,1)S(1)} %bitcast.192), channel_id=1, source_target_pairs={{0,1},{1,5},{2,11},{3,15},{4,8},{5,12},{6,2},{7,6},{8,9},{9,13},{1... | collective-permute-start | bytes 393224 | tf_op jit(solution)/shard_map/ppermute | solution.py:153
  56.2 13.0 %collective-permute-start.6 = (bf16[256,256]{1,0:T(8,128)(2,1)S(1)}, bf16[256,256]{1,0:T(8,128)(2,1)S(1)}, u32[]{:S(2)}, u32[]{:S(2)}) collective-permute-start(bf16[256,256]{1,0:T(8,128)(2,1)S(1)} %bitcast.193), channel_id=1, source_target_pairs={{0,8},{1,12},{2,2},{3,6},{4,9},{5,13},{6,3},{7,7},{8,0},{9,4},{10,... | collective-permute-start | bytes 393224 | tf_op jit(solution)/shard_map/ppermute | solution.py:153
  61.8 7.5 %collective-permute-start.7 = (bf16[256,256]{1,0:T(8,128)(2,1)S(1)}, bf16[256,256]{1,0:T(8,128)(2,1)S(1)}, u32[]{:S(2)}, u32[]{:S(2)}) collective-permute-start(bf16[256,256]{1,0:T(8,128)(2,1)S(1)} %bitcast.194), channel_id=1, source_target_pairs={{0,9},{1,13},{2,3},{3,7},{4,0},{5,4},{6,10},{7,14},{8,1},{9,5},{10... | collective-permute-start | bytes 393224 | tf_op jit(solution)/shard_map/ppermute | solution.py:153
  70.0 13.2 %collective-permute-start.8 = (bf16[4,256,256]{2,1,0:T(8,128)(2,1)S(1)}, bf16[4,256,256]{2,1,0:T(8,128)(2,1)S(1)}, u32[]{:S(2)}, u32[]{:S(2)}) collective-permute-start(bf16[4,256,256]{2,1,0:T(8,128)(2,1)S(1)} %broadcast_select_fusion.1), channel_id=1, source_target_pairs={{0,2},{1,3},{2,0},{3,1},{4,6},{5,7},{6,4},{7,5},{8,10},{9,11},{10,... | collective-permute-start | bytes 1572872 | tf_op jit(solution)/shard_map/ppermute | solution.py:179
  83.4 3.8 %collective-permute-start.9 = (bf16[2,4,256,256]{3,2,0,1:T(8,128)(2,1)S(1)}, bf16[2,4,256,256]{3,2,0,1:T(8,128)(2,1)S(1)}, u32[]{:S(2)}, u32[]{:S(2)}) collective-permute-start(bf16[2,4,256,256]{3,2,0,1:T(8,128)(2,1)S(1)} %get-tuple-element.27), channel_id=1, source_target_pairs={{0,1},{1,0},{2,3},{3,2},{4,5},{5,4},{6,7},{7,6},{8,9},{9,8},{10,11... | collective-permute-start | bytes 3145736 | tf_op jit(solution)/shard_map/ppermute | solution.py:181
  89.2 21.0 %collective-permute-start.10 = (bf16[256,1536]{1,0:T(8,128)(2,1)S(1)}, bf16[256,1536]{1,0:T(8,128)(2,1)S(1)}, u32[]{:S(2)}, u32[]{:S(2)}) collective-permute-start(bf16[256,1536]{1,0:T(8,128)(2,1)S(1)} %fusion.5), channel_id=1, source_target_pairs={{0,4},{4,8},{1,5},{5,9},{2,6},{6,10},{3,7},{7,11},{16,20},{20,24},... | collective-permute-start | bytes 2359304 | tf_op jit(solution)/shard_map/ppermute | solution.py:194
  93.4 22.3 %collective-permute-start.13 = (bf16[256,1536]{1,0:T(8,128)(2,1)S(1)}, bf16[256,1536]{1,0:T(8,128)(2,1)S(1)}, u32[]{:S(2)}, u32[]{:S(2)}) collective-permute-start(bf16[256,1536]{1,0:T(8,128)(2,1)S(1)} %fusion.7), channel_id=1, source_target_pairs={{12,8},{8,4},{13,9},{9,5},{14,10},{10,6},{15,11},{11,7},{28,24},{2... | collective-permute-start | bytes 2359304 | tf_op jit(solution)/shard_map/ppermute | solution.py:198
  95.1 32.1 %collective-permute-start.12 = (bf16[256,1536]{1,0:T(8,128)(2,1)S(1)}, bf16[256,1536]{1,0:T(8,128)(2,1)S(1)}, u32[]{:S(2)}, u32[]{:S(2)}) collective-permute-start(bf16[256,1536]{1,0:T(8,128)(2,1)S(1)} %fusion.6), channel_id=1, source_target_pairs={{0,12},{1,13},{2,14},{3,15},{16,28},{17,29},{18,30},{19,31}} | collective-permute-start | bytes 2359304 | tf_op jit(solution)/shard_map/ppermute | solution.py:197
  100.4 32.3 %collective-permute-start.15 = (bf16[256,1536]{1,0:T(8,128)(2,1)S(1)}, bf16[256,1536]{1,0:T(8,128)(2,1)S(1)}, u32[]{:S(2)}, u32[]{:S(2)}) collective-permute-start(bf16[256,1536]{1,0:T(8,128)(2,1)S(1)} %fusion.8), channel_id=1, source_target_pairs={{12,0},{13,1},{14,2},{15,3},{28,16},{29,17},{30,18},{31,19}} | collective-permute-start | bytes 2359304 | tf_op jit(solution)/shard_map/ppermute | solution.py:201
  111.2 32.2 %collective-permute-start.11 = (bf16[256,1536]{1,0:T(8,128)(2,1)S(1)}, bf16[256,1536]{1,0:T(8,128)(2,1)S(1)}, u32[]{:S(2)}, u32[]{:S(2)}) collective-permute-start(bf16[256,1536]{1,0:T(8,128)(2,1)S(1)} %fusion.4), channel_id=1, source_target_pairs={{0,4},{4,8},{8,12},{1,5},{5,9},{9,13},{2,6},{6,10},{10,14},{3,7},{... | collective-permute-start | bytes 2359304 | tf_op jit(solution)/shard_map/ppermute | solution.py:203
  116.7 32.1 %collective-permute-start.14 = (bf16[256,1536]{1,0:T(8,128)(2,1)S(1)}, bf16[256,1536]{1,0:T(8,128)(2,1)S(1)}, u32[]{:S(2)}, u32[]{:S(2)}) collective-permute-start(bf16[256,1536]{1,0:T(8,128)(2,1)S(1)} %fusion.3), channel_id=1, source_target_pairs={{12,8},{8,4},{4,0},{13,9},{9,5},{5,1},{14,10},{10,6},{6,2},{15,11}... | collective-permute-start | bytes 2359304 | tf_op jit(solution)/shard_map/ppermute | solution.py:212

commit v20 on v18

--- a/solution.py
+++ b/solution.py
@@ -96,9 +96,12 @@
     d_idx = jnp.arange(n_x)[:, None]
     e_idx = jnp.arange(2)[None, :]
     mu_tab = 2 * ((xi - d_idx) % n_x) + jnp.where(e_idx == 0, core, 1 - core)
-    w_perm = jnp.take(
-        weights.reshape(n_mdl, piece, weights.shape[1]), mu_tab.reshape(-1), axis=0
-    ).reshape(n_x, 2, piece, weights.shape[1])
+    if n_seq == 4 and n_mdl == 4:
+        w_perm = None
+    else:
+        w_perm = jnp.take(
+            weights.reshape(n_mdl, piece, weights.shape[1]), mu_tab.reshape(-1), axis=0
+        ).reshape(n_x, 2, piece, weights.shape[1])
     position = lax.axis_index("seq")
     incoming = jnp.zeros((heads_here, HDIM * HDIM), jnp.float32)
     gap = jnp.zeros((heads_here,), jnp.float32)
@@ -111,7 +114,7 @@
         weight = jnp.where(d <= position, jnp.exp(jnp.minimum(gap, 0.0)), 0.0)
         incoming = incoming + weight[:, None] * came_state
         if d == 1:
-            incoming = incoming + w_perm[0, 0, 0, 0].astype(jnp.float32) * 0.0
+            incoming = incoming + weights[0, 0].astype(jnp.float32) * 0.0
         gap = gap + came_log
     incoming = incoming.reshape(heads_here, HDIM, HDIM)
     before = jnp.cumsum(block_total, axis=1) - block_total
@@ -184,9 +187,18 @@
 
     def partial_for(target):
         rows = lax.dynamic_index_in_dim(gathered_x, target, 2, keepdims=False)
-        return jnp.einsum(
-            "deti,deic->tc", rows, w_perm, preferred_element_type=jnp.float32
-        )
+        if w_perm is not None:
+            return jnp.einsum(
+                "deti,deic->tc", rows, w_perm, preferred_element_type=jnp.float32
+            )
+        total = None
+        for d in range(n_x):
+            for e in range(2):
+                mu = 2 * ((xi - d) % n_x) + (core if e == 0 else 1 - core)
+                w_rows = lax.dynamic_slice_in_dim(weights, mu * piece, piece, axis=0)
+                term = jnp.dot(rows[d, e], w_rows, preferred_element_type=jnp.float32)
+                total = term if total is None else total + term
+        return total
 
     if n_seq == 4:
         def bf(v):

time: 148 us -> 175 us (1.18)
  starting transfers between devices: 38.5 us -> 50.2 us
  other arithmetic: 18 us -> 24.6 us
  matrix products: 11.2 us -> 16.6 us
  local copies, waits for them, and re-layouts: 13.4 us -> 17 us
    ppermute x1, waiting for transfers between devices: 7.36 us -> 26.4 us  [per_device(): lax.ppermute(bf(partial_for(jnp.clip(s_me + 2, 0, 3))), 'seq', [(0, 1), (...]
    ppermute x1, waiting for transfers between devices: 9.16 us -> 0.01 us  [per_device(): far_r = lax.ppermute(bf(partial_for(jnp.int32(3))), 'seq', [(0, 3)])]
    ppermute x4, starting transfers between devices: 7.19 us -> 14.8 us  [per_device(): received.append(lax.ppermute(item, ('seq', 'mdl'), perm))]
    ppermute x1, starting transfers between devices: 0.07 us -> 6.15 us  [per_device(): got.append(lax.ppermute(x, 'mdl', perm))]
    ppermute x1, waiting for transfers between devices: 5.53 us -> 0.01 us  [per_device(): far_l = lax.ppermute(bf(partial_for(jnp.int32(0))), 'seq', [(3, 0)])]
    ppermute x1, waiting for transfers between devices: 13 us -> 8.68 us  [per_device(): got.append(lax.ppermute(x, 'mdl', perm))]
    ppermute x4, waiting for transfers between devices: 7.75 us -> 3.45 us  [per_device(): received.append(lax.ppermute(item, ('seq', 'mdl'), perm))]
    another operation x5, local copies, waits for them, and re-layouts: 0.4 us -> 4.43 us
  transfers between devices with their start and end apart: 16 -> 16, of which waited for: 9 -> 7; matrix products, arithmetic and copies ran while one was open for 17% -> 16% of each run, Pallas kernels for 0% -> 0%
where the time goes in v20:
time: 175 us; the launch traced here: 173 us
  waiting for transfers between devices  63.7 us (36%)
  starting transfers between devices  50.2 us (29%)
  other arithmetic  24.6 us (14%)
  local copies, waits for them, and re-layouts  17 us (10%)
  matrix products  16.6 us (9%)
    ppermute x1, waiting for transfers between devices, per_device(): lax.ppermute(bf(partial_for(jnp.clip(s_me + 2, 0, 3))), 'seq', [(0, 1), (...  26.4 us
    ppermute x4, starting transfers between devices, per_device(): received.append(lax.ppermute(item, ('seq', 'mdl'), perm))  14.8 us
    ppermute x3, starting transfers between devices, per_device(): came = lax.ppermute(packed, 'seq', [(z, z + d) for z in range(n_seq - d)])  11.4 us
    dot_general x28, matrix products, partial_for(): term = jnp.dot(rows[d, e], w_rows, preferred_element_type=jnp.float32)  10.8 us
    ppermute x1, waiting for transfers between devices, per_device(): got.append(lax.ppermute(x, 'mdl', perm))  8.68 us
    ppermute x1, waiting for transfers between devices, per_device(): lax.ppermute(bf(partial_for(jnp.clip(s_me - 1, 0, 3)) + near_l.astype(jnp...  8.58 us
    ppermute x1, waiting for transfers between devices, per_device(): lax.ppermute(bf(partial_for(jnp.clip(s_me + 1, 0, 3)) + near_r.astype(jnp...  7.28 us
    ppermute x1, starting transfers between devices, per_device(): far_r = lax.ppermute(bf(partial_for(jnp.int32(3))), 'seq', [(0, 3)])  7.07 us
  transfers between devices with their start and end apart: 16, of which 7 were waited for; matrix products, arithmetic and copies ran while one was open for 16% of the time, Pallas kernels for 0%

profile of v20, /device:TPU:0, one launch (start us, length us, event | category | flops | bytes accessed | tf_op | source)
XLA Modules:
  0.0 173.3 jit_solution(8769630746041998860)
XLA Ops:
  7.7 7.7 %collective-permute-start.2 = (bf16[8,16640]{1,0:T(8,128)(2,1)}, bf16[8,16640]{1,0:T(8,128)(2,1)}, u32[]{:S(2)}, u32[]{:S(2)}) collective-permute-start(bf16[8,16640]{1,0:T(8,128)(2,1)} %pad_maximum_fusion.3), channel_id=1, source_target_pairs={{0,12},{1,13},{2,14},{3,15},{16,28},{17,29},{18,30},{19,31}} | collective-permute-start | bytes 798728 | tf_op jit(solution)/shard_map/ppermute | solution.py:109
  16.7 2.5 %collective-permute-start = (bf16[8,16640]{1,0:T(8,128)(2,1)}, bf16[8,16640]{1,0:T(8,128)(2,1)}, u32[]{:S(2)}, u32[]{:S(2)}) collective-permute-start(bf16[8,16640]{1,0:T(8,128)(2,1)} %pad_maximum_fusion.3), channel_id=1, source_target_pairs={{0,4},{4,8},{8,12},{1,5},{5,9},{9,13},{2,6},{6,10},{10,14},{3,7},{... | collective-permute-start | bytes 798728 | tf_op jit(solution)/shard_map/ppermute | solution.py:109
  20.4 2.8 %multiply_convert_fusion = bf16[1024,1536]{1,0:T(8,128)(2,1)S(1)} fusion(bf16[1024,1536]{1,0:T(8,128)(2,1)} %param.16, f32[1536]{0:T(1024)S(1)} %select_add_fusion), kind=kLoop, calls=%fused_computation.1 | loop fusion | flops 11010048 | bytes 6297600 | tf_op jit(solution)/shard_map/convert_element_type | solution.py:20
  23.8 2.1 %copy.67 = bf16[256,1024]{0,1:T(8,128)(2,1)} copy(bf16[256,1024]{1,0:T(8,128)(2,1)} %param.12) | data formatting | bytes 1048576 | tf_op args[3]
  25.8 2.4 %fusion.11 = bf16[256,1024]{0,1:T(8,128)(2,1)} fusion(bf16[256,1024]{0,1:T(8,128)(2,1)} %copy.59, f32[1024]{0:T(1024)S(1)} %bitcast.190), kind=kLoop, calls=%fused_computation.56 | loop fusion | flops 3407872 | bytes 1052672 | tf_op jit(solution)/shard_map/convert_element_type | solution.py:47
  28.9 3.3 %fusion.5 = f32[1,256,8,128]{1,3,2,0:T(8,128)} fusion(bf16[256,8,128]{0,2,1:T(8,128)(2,1)} %bitcast.178, bf16[256,8,128]{0,2,1:T(8,128)(2,1)} %bitcast.182, bf16[256,8,128]{0,2,1:T(8,128)(2,1)} %bitcast.180, f32[8,256]{1,0:T(8,128)S(1)} %bitcast_add_fusion.2, pred[256,256]{1,0:T(8,128)(4,1)S(1)} %iota_compare_fusion), kind=kOutput, calls=%fused_computation.44 | convolution fusion | flops 271056896 | bytes 2695168 | tf_op jit(solution)/shard_map/hbij,bjhd->bihd/dot_general | solution.py:62
  33.0 2.0 %add_bitcast_fusion = f32[8,128,128]{2,0,1:T(8,128)} fusion(bf16[8,16640]{1,0:T(8,128)(2,1)} %collective-permute-done.2, bf16[8,16640]{1,0:T(8,128)(2,1)S(1)} %collective-permute-done.1, bf16[8,16640]{1,0:T(8,128)(2,1)} %collective-permute-done, f32[8]{0:T(128)S(1)} %get-tuple-element.14, f32[8]{0:T(128)S(1)} %get-tuple-element.13, f32[]{:T(128)} %bitcast.19, ...), kind=kLoop, calls=%fused_computation.102 | loop fusion | flops 1179648 | bytes 1310792 | tf_op jit(solution)/shard_map/broadcast_in_dim;reshape | solution.py:121
  35.1 2.0 %copy.65 = f32[8,128,128]{1,2,0:T(8,128)} copy(f32[8,128,128]{2,0,1:T(8,128)} %add_bitcast_fusion) | data formatting | bytes 1048576 | tf_op jit(solution)/shard_map/broadcast_in_dim;reshape | solution.py:121
  37.1 2.3 %multiply_reduce_fusion = (f32[256,8]{0,1:T(8,128)S(1)}, f32[1,256,8,128]{1,3,2,0:T(8,128)S(1)}) fusion(f32[1,256,8,128]{1,3,2,0:T(8,128)} %fusion.5, bf16[256,8,128]{0,2,1:T(8,128)(2,1)} %bitcast.183, f32[8,128,128]{1,2,0:T(8,128)} %copy.65, f32[8]{0:T(128)S(1)} %get-tuple-element.44, f32[256,8]{0,1:T(8,128)S(1)} %get-tuple-element.24), kind=kOutput, calls=%fused_computation.65 | convolution fusion | flops 403830784 | bytes 3162144 | tf_op jit(solution)/shard_map/bihd,bhde->bihe/dot_general | solution.py:122
  41.5 1.5 collective-permute-start.3
  43.0 6.3 %collective-permute-done.3 = bf16[256,2,256]{0,2,1:T(8,128)(2,1)} collective-permute-done((bf16[256,2,256]{0,2,1:T(8,128)(2,1)}, bf16[256,2,256]{0,2,1:T(8,128)(2,1)}, u32[]{:S(2)}, u32[]{:S(2)}) %collective-permute-start.3) | collective-permute-done | bytes 262176 | tf_op jit(solution)/shard_map/ppermute | solution.py:146
  49.3 1.9 %fusion.79 = (bf16[256,1,256]{0,2,1:T(8,128)(2,1)S(1)}, bf16[256,1,256]{0,2,1:T(8,128)(2,1)}, bf16[256,1,256]{0,2,1:T(8,128)(2,1)}, bf16[256,1,256]{0,2,1:T(8,128)(2,1)}) fusion(s32[]{:T(128)S(6)} %select_n.519, bf16[256,2,256]{0,2,1:T(8,128)(2,1)S(1)} %get-tuple-element.40, bf16[256,2,256]{0,2,1:T(8,128)(2,1)} %collective-permute-done.3, ...), kind=kLoop, calls=%fused_computation.144 | loop fusion | flops 262144 | bytes 1048592 | tf_op jit(solution)/shard_map/concatenate | solution.py:147
  52.1 8.5 %collective-permute-start.7 = (bf16[256,256]{1,0:T(8,128)(2,1)S(1)}, bf16[256,256]{1,0:T(8,128)(2,1)}, u32[]{:S(2)}, u32[]{:S(2)}) collective-permute-start(bf16[256,256]{1,0:T(8,128)(2,1)S(1)} %bitcast.185), channel_id=1, source_target_pairs={{0,9},{1,13},{2,3},{3,7},{4,0},{5,4},{6,10},{7,14},{8,1},{9,5},{10... | collective-permute-start | bytes 393224 | tf_op jit(solution)/shard_map/ppermute | solution.py:157
  61.7 3.2 %collective-permute-start.6 = (bf16[256,256]{1,0:T(8,128)(2,1)S(1)}, bf16[256,256]{1,0:T(8,128)(2,1)}, u32[]{:S(2)}, u32[]{:S(2)}) collective-permute-start(bf16[256,256]{1,0:T(8,128)(2,1)S(1)} %bitcast.186), channel_id=1, source_target_pairs={{0,8},{1,12},{2,2},{3,6},{4,9},{5,13},{6,3},{7,7},{8,0},{9,4},{10,... | collective-permute-start | bytes 393224 | tf_op jit(solution)/shard_map/ppermute | solution.py:157
  64.8 1.7 copy.69
  66.5 1.6 collective-permute-start.5
  68.8 1.6 collective-permute-start.4
  70.4 3.4 %collective-permute-done.6 = bf16[256,256]{1,0:T(8,128)(2,1)} collective-permute-done((bf16[256,256]{1,0:T(8,128)(2,1)S(1)}, bf16[256,256]{1,0:T(8,128)(2,1)}, u32[]{:S(2)}, u32[]{:S(2)}) %collective-permute-start.6) | collective-permute-done | bytes 131104 | tf_op jit(solution)/shard_map/ppermute | solution.py:157
  73.9 1.9 %pad_maximum_fusion.2 = bf16[4,256,256]{2,1,0:T(8,128)(2,1)} fusion(bf16[1,256,256]{2,1,0:T(8,128)(2,1)} %bitcast.32, bf16[1,256,256]{2,1,0:T(8,128)(2,1)} %bitcast.30, bf16[1,256,256]{2,1,0:T(8,128)(2,1)} %bitcast.28, bf16[1,256,256]{2,1,0:T(8,128)(2,1)S(1)} %bitcast.189), kind=kLoop, calls=%fused_computation.98 | loop fusion | flops 786432 | bytes 1048576 | tf_op jit(solution)/shard_map/stack | solution.py:158
  75.8 2.4 %gather_fusion = bf16[4,256,256]{2,1,0:T(8,128)(2,1)} fusion(bf16[4,256,256]{2,1,0:T(8,128)(2,1)} %pad_maximum_fusion.2, s32[1024]{0:T(1024)S(1)} %pad_clamp_fusion), kind=kCustom, calls=%fused_computation | custom fusion | bytes 1048592 | tf_op jit(solution)/shard_map/jit(_take)/gather | solution.py:160
  79.3 6.2 %collective-permute-start.8 = (bf16[4,256,256]{2,1,0:T(8,128)(2,1)S(1)}, bf16[4,256,256]{2,1,0:T(8,128)(2,1)S(1)}, u32[]{:S(2)}, u32[]{:S(2)}) collective-permute-start(bf16[4,256,256]{2,1,0:T(8,128)(2,1)S(1)} %broadcast_select_fusion), channel_id=1, source_target_pairs={{0,2},{1,3},{2,0},{3,1},{4,6},{5,7},{6,4},{7,5},{8,10},{9,11},{10,... | collective-permute-start | bytes 1572872 | tf_op jit(solution)/shard_map/ppermute | solution.py:183
  86.7 8.7 %collective-permute-done.8 = bf16[4,256,256]{2,1,0:T(8,128)(2,1)S(1)} collective-permute-done((bf16[4,256,256]{2,1,0:T(8,128)(2,1)S(1)}, bf16[4,256,256]{2,1,0:T(8,128)(2,1)S(1)}, u32[]{:S(2)}, u32[]{:S(2)}) %collective-permute-start.8) | collective-permute-done | bytes 524320 | tf_op jit(solution)/shard_map/ppermute | solution.py:183
  95.3 1.5 fusion.159
  96.8 3.0 %collective-permute-done.9 = bf16[2,4,256,256]{3,2,1,0:T(8,128)(2,1)} collective-permute-done((bf16[2,4,256,256]{3,2,1,0:T(8,128)(2,1)}, bf16[2,4,256,256]{3,2,1,0:T(8,128)(2,1)}, u32[]{:S(2)}, u32[]{:S(2)}) %collective-permute-start.9) | collective-permute-done | bytes 1048608 | tf_op jit(solution)/shard_map/ppermute | solution.py:185
  99.8 2.5 %fusion.27 = (bf16[2,2,256,256]{3,2,0,1:T(8,128)(2,1)S(1)}, bf16[2,2,256,256]{3,2,0,1:T(8,128)(2,1)S(1)}, bf16[2,2,256,256]{3,2,0,1:T(8,128)(2,1)S(1)}, bf16[2,2...) fusion(s32[]{:T(128)S(6)} %min.62, ...), kind=kLoop, calls=%fused_computation.87 | loop fusion | flops 1835008 | bytes 5767188 | tf_op jit(solution)/shard_map/jit(dynamic_index_in_dim)/squeeze | solution.py:189
  110.2 7.1 %collective-permute-start.12 = (bf16[256,1536]{1,0:T(8,128)(2,1)S(1)}, bf16[256,1536]{1,0:T(8,128)(2,1)S(1)}, u32[]{:S(2)}, u32[]{:S(2)}) collective-permute-start(bf16[256,1536]{1,0:T(8,128)(2,1)S(1)} %fusion.1), channel_id=1, source_target_pairs={{0,12},{1,13},{2,14},{3,15},{16,28},{17,29},{18,30},{19,31}} | collective-permute-start | bytes 2359304 | tf_op jit(solution)/shard_map/ppermute | solution.py:210
  120.4 1.3 collective-permute-start.10
  124.6 26.4 %collective-permute-done.10 = bf16[256,1536]{1,0:T(8,128)(2,1)S(1)} collective-permute-done((bf16[256,1536]{1,0:T(8,128)(2,1)S(1)}, bf16[256,1536]{1,0:T(8,128)(2,1)S(1)}, u32[]{:S(2)}, u32[]{:S(2)}) %collective-permute-start.10) | collective-permute-done | bytes 786464 | tf_op jit(solution)/shard_map/ppermute | solution.py:207
  151.5 4.4 %collective-permute-start.11 = (bf16[256,1536]{1,0:T(8,128)(2,1)S(1)}, bf16[256,1536]{1,0:T(8,128)(2,1)S(1)}, u32[]{:S(2)}, u32[]{:S(2)}) collective-permute-start(bf16[256,1536]{1,0:T(8,128)(2,1)S(1)} %add_convert_fusion.2), channel_id=1, source_target_pairs={{0,4},{4,8},{8,12},{1,5},{5,9},{9,13},{2,6},{6,10},{10,14},{3,7},{... | collective-permute-start | bytes 2359304 | tf_op jit(solution)/shard_map/ppermute | solution.py:216
  156.0 8.6 %collective-permute-done.14 = bf16[256,1536]{1,0:T(8,128)(2,1)S(1)} collective-permute-done((bf16[256,1536]{1,0:T(8,128)(2,1)S(1)}, bf16[256,1536]{1,0:T(8,128)(2,1)S(1)}, u32[]{:S(2)}, u32[]{:S(2)}) %collective-permute-start.14) | collective-permute-done | bytes 786464 | tf_op jit(solution)/shard_map/ppermute | solution.py:225
  164.5 7.3 %collective-permute-done.11 = bf16[256,1536]{1,0:T(8,128)(2,1)S(1)} collective-permute-done((bf16[256,1536]{1,0:T(8,128)(2,1)S(1)}, bf16[256,1536]{1,0:T(8,128)(2,1)S(1)}, u32[]{:S(2)}, u32[]{:S(2)}) %collective-permute-start.11) | collective-permute-done | bytes 786464 | tf_op jit(solution)/shard_map/ppermute | solution.py:216
  171.8 1.5 add_convert_fusion
  (90 shorter events, 32.9 us)
Async XLA Ops:
  5.6 1.2 copy-start
  6.2 14.2 %copy-start.1 = (bf16[256,1024]{0,1:T(8,128)(2,1)}, bf16[256,1024]{0,1:T(8,128)(2,1)S(1)}, u32[]{:S(2)}) copy-start(bf16[256,1024]{0,1:T(8,128)(2,1)S(1)} %fusion.15) | copy-start | bytes 1572868
  6.2 13.1 %copy-start.4 = (s32[1536]{0:T(1024)S(1)}, s32[1536]{0:T(1024)}, u32[]{:S(2)}) copy-start(s32[1536]{0:T(1024)} %param.17) | copy-start | bytes 18436
  6.2 13.1 %copy-start.3 = (bf16[256,1024]{1,0:T(8,128)(2,1)S(1)}, bf16[256,1024]{1,0:T(8,128)(2,1)}, u32[]{:S(2)}) copy-start(bf16[256,1024]{1,0:T(8,128)(2,1)} %param.9) | copy-start | bytes 1572868
  7.7 25.3 %collective-permute-start.2 = (bf16[8,16640]{1,0:T(8,128)(2,1)}, bf16[8,16640]{1,0:T(8,128)(2,1)}, u32[]{:S(2)}, u32[]{:S(2)}) collective-permute-start(bf16[8,16640]{1,0:T(8,128)(2,1)} %pad_maximum_fusion.3), channel_id=1, source_target_pairs={{0,12},{1,13},{2,14},{3,15},{16,28},{17,29},{18,30},{19,31}} | collective-permute-start | bytes 798728 | tf_op jit(solution)/shard_map/ppermute | solution.py:109
  15.4 16.8 %collective-permute-start.1 = (bf16[8,16640]{1,0:T(8,128)(2,1)}, bf16[8,16640]{1,0:T(8,128)(2,1)S(1)}, u32[]{:S(2)}, u32[]{:S(2)}) collective-permute-start(bf16[8,16640]{1,0:T(8,128)(2,1)} %pad_maximum_fusion.3), channel_id=1, source_target_pairs={{0,8},{4,12},{1,9},{5,13},{2,10},{6,14},{3,11},{7,15},{16,24},{20,... | collective-permute-start | bytes 798728 | tf_op jit(solution)/shard_map/ppermute | solution.py:109
  16.7 15.5 %collective-permute-start = (bf16[8,16640]{1,0:T(8,128)(2,1)}, bf16[8,16640]{1,0:T(8,128)(2,1)}, u32[]{:S(2)}, u32[]{:S(2)}) collective-permute-start(bf16[8,16640]{1,0:T(8,128)(2,1)} %pad_maximum_fusion.3), channel_id=1, source_target_pairs={{0,4},{4,8},{8,12},{1,5},{5,9},{9,13},{2,6},{6,10},{10,14},{3,7},{... | collective-permute-start | bytes 798728 | tf_op jit(solution)/shard_map/ppermute | solution.py:109
  39.4 1.0 copy-start.2
  39.4 1.0 copy-start.5
  41.5 7.8 %collective-permute-start.3 = (bf16[256,2,256]{0,2,1:T(8,128)(2,1)}, bf16[256,2,256]{0,2,1:T(8,128)(2,1)}, u32[]{:S(2)}, u32[]{:S(2)}) collective-permute-start(bf16[256,2,256]{0,2,1:T(8,128)(2,1)} %get-tuple-element.39), channel_id=1, source_target_pairs={{0,2},{1,3},{2,0},{3,1},{4,6},{5,7},{6,4},{7,5},{8,10},{9,11},{10,... | collective-permute-start | bytes 786440 | tf_op jit(solution)/shard_map/ppermute | solution.py:146
  52.1 18.3 %collective-permute-start.7 = (bf16[256,256]{1,0:T(8,128)(2,1)S(1)}, bf16[256,256]{1,0:T(8,128)(2,1)}, u32[]{:S(2)}, u32[]{:S(2)}) collective-permute-start(bf16[256,256]{1,0:T(8,128)(2,1)S(1)} %bitcast.185), channel_id=1, source_target_pairs={{0,9},{1,13},{2,3},{3,7},{4,0},{5,4},{6,10},{7,14},{8,1},{9,5},{10... | collective-permute-start | bytes 393224 | tf_op jit(solution)/shard_map/ppermute | solution.py:157
  61.7 12.2 %collective-permute-start.6 = (bf16[256,256]{1,0:T(8,128)(2,1)S(1)}, bf16[256,256]{1,0:T(8,128)(2,1)}, u32[]{:S(2)}, u32[]{:S(2)}) collective-permute-start(bf16[256,256]{1,0:T(8,128)(2,1)S(1)} %bitcast.186), channel_id=1, source_target_pairs={{0,8},{1,12},{2,2},{3,6},{4,9},{5,13},{6,3},{7,7},{8,0},{9,4},{10,... | collective-permute-start | bytes 393224 | tf_op jit(solution)/shard_map/ppermute | solution.py:157
  66.5 7.4 %collective-permute-start.5 = (bf16[256,256]{1,0:T(8,128)(2,1)}, bf16[256,256]{1,0:T(8,128)(2,1)}, u32[]{:S(2)}, u32[]{:S(2)}) collective-permute-start(bf16[256,256]{1,0:T(8,128)(2,1)} %bitcast.187), channel_id=1, source_target_pairs={{0,1},{1,5},{2,11},{3,15},{4,8},{5,12},{6,2},{7,6},{8,9},{9,13},{1... | collective-permute-start | bytes 393224 | tf_op jit(solution)/shard_map/ppermute | solution.py:157
  68.8 5.0 %collective-permute-start.4 = (bf16[256,256]{1,0:T(8,128)(2,1)}, bf16[256,256]{1,0:T(8,128)(2,1)S(1)}, u32[]{:S(2)}, u32[]{:S(2)}) collective-permute-start(bf16[256,256]{1,0:T(8,128)(2,1)} %bitcast.188), channel_id=1, source_target_pairs={{0,0},{1,4},{2,10},{3,14},{4,1},{5,5},{6,11},{7,15},{8,8},{9,12},{... | collective-permute-start | bytes 393224 | tf_op jit(solution)/shard_map/ppermute | solution.py:157
  79.3 16.0 %collective-permute-start.8 = (bf16[4,256,256]{2,1,0:T(8,128)(2,1)S(1)}, bf16[4,256,256]{2,1,0:T(8,128)(2,1)S(1)}, u32[]{:S(2)}, u32[]{:S(2)}) collective-permute-start(bf16[4,256,256]{2,1,0:T(8,128)(2,1)S(1)} %broadcast_select_fusion), channel_id=1, source_target_pairs={{0,2},{1,3},{2,0},{3,1},{4,6},{5,7},{6,4},{7,5},{8,10},{9,11},{10,... | collective-permute-start | bytes 1572872 | tf_op jit(solution)/shard_map/ppermute | solution.py:183
  96.8 3.0 %collective-permute-start.9 = (bf16[2,4,256,256]{3,2,1,0:T(8,128)(2,1)}, bf16[2,4,256,256]{3,2,1,0:T(8,128)(2,1)}, u32[]{:S(2)}, u32[]{:S(2)}) collective-permute-start(bf16[2,4,256,256]{3,2,1,0:T(8,128)(2,1)} %get-tuple-element.34), channel_id=1, source_target_pairs={{0,1},{1,0},{2,3},{3,2},{4,5},{5,4},{6,7},{7,6},{8,9},{9,8},{10,11... | collective-permute-start | bytes 3145736 | tf_op jit(solution)/shard_map/ppermute | solution.py:185
  103.8 52.1 %collective-permute-start.15 = (bf16[256,1536]{1,0:T(8,128)(2,1)S(1)}, bf16[256,1536]{1,0:T(8,128)(2,1)S(1)}, u32[]{:S(2)}, u32[]{:S(2)}) collective-permute-start(bf16[256,1536]{1,0:T(8,128)(2,1)S(1)} %fusion.3), channel_id=1, source_target_pairs={{12,0},{13,1},{14,2},{15,3},{28,16},{29,17},{30,18},{31,19}} | collective-permute-start | bytes 2359304 | tf_op jit(solution)/shard_map/ppermute | solution.py:214
  106.6 16.2 %collective-permute-start.13 = (bf16[256,1536]{1,0:T(8,128)(2,1)S(1)}, bf16[256,1536]{1,0:T(8,128)(2,1)S(1)}, u32[]{:S(2)}, u32[]{:S(2)}) collective-permute-start(bf16[256,1536]{1,0:T(8,128)(2,1)S(1)} %fusion.2), channel_id=1, source_target_pairs={{12,8},{8,4},{13,9},{9,5},{14,10},{10,6},{15,11},{11,7},{28,24},{2... | collective-permute-start | bytes 2359304 | tf_op jit(solution)/shard_map/ppermute | solution.py:211
  110.2 45.7 %collective-permute-start.12 = (bf16[256,1536]{1,0:T(8,128)(2,1)S(1)}, bf16[256,1536]{1,0:T(8,128)(2,1)S(1)}, u32[]{:S(2)}, u32[]{:S(2)}) collective-permute-start(bf16[256,1536]{1,0:T(8,128)(2,1)S(1)} %fusion.1), channel_id=1, source_target_pairs={{0,12},{1,13},{2,14},{3,15},{16,28},{17,29},{18,30},{19,31}} | collective-permute-start | bytes 2359304 | tf_op jit(solution)/shard_map/ppermute | solution.py:210
  120.4 30.6 %collective-permute-start.10 = (bf16[256,1536]{1,0:T(8,128)(2,1)S(1)}, bf16[256,1536]{1,0:T(8,128)(2,1)S(1)}, u32[]{:S(2)}, u32[]{:S(2)}) collective-permute-start(bf16[256,1536]{1,0:T(8,128)(2,1)S(1)} %fusion), channel_id=1, source_target_pairs={{0,4},{4,8},{1,5},{5,9},{2,6},{6,10},{3,7},{7,11},{16,20},{20,24},... | collective-permute-start | bytes 2359304 | tf_op jit(solution)/shard_map/ppermute | solution.py:207
  123.3 41.3 %collective-permute-start.14 = (bf16[256,1536]{1,0:T(8,128)(2,1)S(1)}, bf16[256,1536]{1,0:T(8,128)(2,1)S(1)}, u32[]{:S(2)}, u32[]{:S(2)}) collective-permute-start(bf16[256,1536]{1,0:T(8,128)(2,1)S(1)} %add_convert_fusion.1), channel_id=1, source_target_pairs={{12,8},{8,4},{4,0},{13,9},{9,5},{5,1},{14,10},{10,6},{6,2},{15,11}... | collective-permute-start | bytes 2359304 | tf_op jit(solution)/shard_map/ppermute | solution.py:225
  151.5 20.3 %collective-permute-start.11 = (bf16[256,1536]{1,0:T(8,128)(2,1)S(1)}, bf16[256,1536]{1,0:T(8,128)(2,1)S(1)}, u32[]{:S(2)}, u32[]{:S(2)}) collective-permute-start(bf16[256,1536]{1,0:T(8,128)(2,1)S(1)} %add_convert_fusion.2), channel_id=1, source_target_pairs={{0,4},{4,8},{8,12},{1,5},{5,9},{9,13},{2,6},{6,10},{10,14},{3,7},{... | collective-permute-start | bytes 2359304 | tf_op jit(solution)/shard_map/ppermute | solution.py:216

commit v21 on v18

--- a/solution.py
+++ b/solution.py
@@ -111,7 +111,7 @@
         weight = jnp.where(d <= position, jnp.exp(jnp.minimum(gap, 0.0)), 0.0)
         incoming = incoming + weight[:, None] * came_state
         if d == 1:
-            incoming = incoming + w_perm[0, 0, 0, 0].astype(jnp.float32) * 0.0
+            incoming = incoming + weights[0, 0].astype(jnp.float32) * 0.0
         gap = gap + came_log
     incoming = incoming.reshape(heads_here, HDIM, HDIM)
     before = jnp.cumsum(block_total, axis=1) - block_total

time: 148 us -> 154 us (1.041)
  starting transfers between devices: 38.5 us -> 58.8 us
  waiting for transfers between devices: 64.8 us -> 54.4 us
  other arithmetic: 18 us -> 16.1 us
    ppermute x1, starting transfers between devices: 4.44 us -> 19.3 us  [per_device(): lax.ppermute(bf(partial_for(jnp.clip(s_me + 1, 0, 3)) + near_r.astype(jnp...]
    ppermute x1, waiting for transfers between devices: 9.16 us -> 0.01 us  [per_device(): far_r = lax.ppermute(bf(partial_for(jnp.int32(3))), 'seq', [(0, 3)])]
    ppermute x4, starting transfers between devices: 7.19 us -> 12.7 us  [per_device(): received.append(lax.ppermute(item, ('seq', 'mdl'), perm))]
    ppermute x1, waiting for transfers between devices: 5.53 us -> 0.01 us  [per_device(): far_l = lax.ppermute(bf(partial_for(jnp.int32(0))), 'seq', [(3, 0)])]
    ppermute x1, waiting for transfers between devices: 5.29 us -> 10.2 us  [per_device(): lax.ppermute(bf(partial_for(jnp.clip(s_me - 1, 0, 3)) + near_l.astype(jnp...]
    unnamed x22, local copies, waits for them, and re-layouts: 8.48 us -> 5.41 us
    gather x1, local copies, waits for them, and re-layouts: 2.64 us -> 4.31 us  [per_device(): jnp.take(weights.reshape(n_mdl, piece, weights.shape[1]), mu_tab.reshape(...]
  transfers between devices with their start and end apart: 16 -> 16, of which waited for: 9 -> 7; matrix products, arithmetic and copies ran while one was open for 17% -> 16% of each run, Pallas kernels for 0% -> 0%
where the time goes in v21:
time: 154 us
  starting transfers between devices  58.8 us (38%)
  waiting for transfers between devices  54.4 us (35%)
  other arithmetic  16.1 us (10%)
  local copies, waits for them, and re-layouts  11.9 us (8%)
  matrix products  11.2 us (7%)
    ppermute x1, starting transfers between devices, per_device(): lax.ppermute(bf(partial_for(jnp.clip(s_me + 1, 0, 3)) + near_r.astype(jnp...  19.3 us
    ppermute x1, waiting for transfers between devices, per_device(): got.append(lax.ppermute(x, 'mdl', perm))  13 us
    ppermute x4, starting transfers between devices, per_device(): received.append(lax.ppermute(item, ('seq', 'mdl'), perm))  12.7 us
    ppermute x3, starting transfers between devices, per_device(): came = lax.ppermute(packed, 'seq', [(z, z + d) for z in range(n_seq - d)])  12.2 us
    ppermute x1, waiting for transfers between devices, per_device(): lax.ppermute(bf(partial_for(jnp.clip(s_me - 1, 0, 3)) + near_l.astype(jnp...  10.2 us
    ppermute x1, waiting for transfers between devices, per_device(): lax.ppermute(bf(partial_for(jnp.clip(s_me + 1, 0, 3)) + near_r.astype(jnp...  10.2 us
    ppermute x1, waiting for transfers between devices, per_device(): lax.ppermute(bf(partial_for(jnp.clip(s_me + 2, 0, 3))), 'seq', [(0, 1), (...  7.75 us
    ppermute x4, waiting for transfers between devices, per_device(): received.append(lax.ppermute(item, ('seq', 'mdl'), perm))  7.49 us
  transfers between devices with their start and end apart: 16, of which 7 were waited for; matrix products, arithmetic and copies ran while one was open for 16% of the time, Pallas kernels for 0%

profile of v21, /device:TPU:0, one launch (start us, length us, event | category | flops | bytes accessed | tf_op | source)
XLA Modules:
  0.0 153.8 jit_solution(3711575236165598029)
XLA Ops:
  0.0 1.2 reduce-window.6
  2.8 1.2 copy.66
  4.1 1.2 copy.68
  8.2 4.9 %collective-permute-start = (bf16[8,16640]{1,0:T(8,128)(2,1)}, bf16[8,16640]{1,0:T(8,128)(2,1)S(1)}, u32[]{:S(2)}, u32[]{:S(2)}) collective-permute-start(bf16[8,16640]{1,0:T(8,128)(2,1)} %pad_maximum_fusion.3), channel_id=1, source_target_pairs={{0,4},{4,8},{8,12},{1,5},{5,9},{9,13},{2,6},{6,10},{10,14},{3,7},{... | collective-permute-start | bytes 798728 | tf_op jit(solution)/shard_map/ppermute | solution.py:106
  13.1 5.2 %collective-permute-start.1 = (bf16[8,16640]{1,0:T(8,128)(2,1)}, bf16[8,16640]{1,0:T(8,128)(2,1)}, u32[]{:S(2)}, u32[]{:S(2)}) collective-permute-start(bf16[8,16640]{1,0:T(8,128)(2,1)} %pad_maximum_fusion.3), channel_id=1, source_target_pairs={{0,8},{4,12},{1,9},{5,13},{2,10},{6,14},{3,11},{7,15},{16,24},{20,... | collective-permute-start | bytes 798728 | tf_op jit(solution)/shard_map/ppermute | solution.py:106
  18.3 2.0 %collective-permute-start.2 = (bf16[8,16640]{1,0:T(8,128)(2,1)}, bf16[8,16640]{1,0:T(8,128)(2,1)}, u32[]{:S(2)}, u32[]{:S(2)}) collective-permute-start(bf16[8,16640]{1,0:T(8,128)(2,1)} %pad_maximum_fusion.3), channel_id=1, source_target_pairs={{0,12},{1,13},{2,14},{3,15},{16,28},{17,29},{18,30},{19,31}} | collective-permute-start | bytes 798728 | tf_op jit(solution)/shard_map/ppermute | solution.py:106
  20.5 1.0 copy.67
  21.5 2.9 %multiply_convert_fusion = bf16[1024,1536]{1,0:T(8,128)(2,1)S(1)} fusion(bf16[1024,1536]{1,0:T(8,128)(2,1)} %param.16, f32[1536]{0:T(1024)S(1)} %select_add_fusion), kind=kLoop, calls=%fused_computation.2 | loop fusion | flops 11010048 | bytes 6297600 | tf_op jit(solution)/shard_map/convert_element_type | solution.py:20
  24.4 1.8 %fusion.16 = bf16[256,1024]{0,1:T(8,128)(2,1)} fusion(bf16[256,1024]{0,1:T(8,128)(2,1)S(1)} %copy-done.3, f32[1024]{0:T(1024)S(1)} %bitcast.194), kind=kLoop, calls=%fused_computation.47 | loop fusion | flops 3407872 | bytes 1052672 | tf_op jit(solution)/shard_map/convert_element_type | solution.py:47
  26.2 3.3 %fusion.10 = f32[1,256,8,128]{1,3,2,0:T(8,128)} fusion(bf16[256,8,128]{0,2,1:T(8,128)(2,1)} %bitcast.179, bf16[256,8,128]{0,2,1:T(8,128)(2,1)} %bitcast.183, bf16[256,8,128]{0,2,1:T(8,128)(2,1)} %bitcast.181, f32[8,256]{1,0:T(8,128)S(1)} %bitcast_add_fusion.2, pred[256,256]{1,0:T(8,128)(4,1)S(1)} %iota_compare_fusion), kind=kOutput, calls=%fused_computation.35 | convolution fusion | flops 271056896 | bytes 2695168 | tf_op jit(solution)/shard_map/hbij,bjhd->bihd/dot_general | solution.py:62
  30.1 1.4 copy.75
  33.0 1.2 add_bitcast_fusion
  35.7 1.6 %collective-permute-start.3 = (bf16[256,2,256]{0,2,1:T(8,128)(2,1)S(1)}, bf16[256,2,256]{0,2,1:T(8,128)(2,1)S(1)}, u32[]{:S(2)}, u32[]{:S(2)}) collective-permute-start(bf16[256,2,256]{0,2,1:T(8,128)(2,1)S(1)} %get-tuple-element.32), channel_id=1, source_target_pairs={{0,2},{1,3},{2,0},{3,1},{4,6},{5,7},{6,4},{7,5},{8,10},{9,11},{10,... | collective-permute-start | bytes 786440 | tf_op jit(solution)/shard_map/ppermute | solution.py:143
  37.4 5.8 %collective-permute-done.3 = bf16[256,2,256]{0,2,1:T(8,128)(2,1)S(1)} collective-permute-done((bf16[256,2,256]{0,2,1:T(8,128)(2,1)S(1)}, bf16[256,2,256]{0,2,1:T(8,128)(2,1)S(1)}, u32[]{:S(2)}, u32[]{:S(2)}) %collective-permute-start.3) | collective-permute-done | bytes 262176 | tf_op jit(solution)/shard_map/ppermute | solution.py:143
  44.3 6.7 %collective-permute-start.5 = (bf16[256,256]{1,0:T(8,128)(2,1)S(1)}, bf16[256,256]{1,0:T(8,128)(2,1)S(1)}, u32[]{:S(2)}, u32[]{:S(2)}) collective-permute-start(bf16[256,256]{1,0:T(8,128)(2,1)S(1)} %bitcast.187), channel_id=1, source_target_pairs={{0,1},{1,5},{2,11},{3,15},{4,8},{5,12},{6,2},{7,6},{8,9},{9,13},{1... | collective-permute-start | bytes 393224 | tf_op jit(solution)/shard_map/ppermute | solution.py:154
  51.2 5.3 %collective-permute-start.6 = (bf16[256,256]{1,0:T(8,128)(2,1)S(1)}, bf16[256,256]{1,0:T(8,128)(2,1)S(1)}, u32[]{:S(2)}, u32[]{:S(2)}) collective-permute-start(bf16[256,256]{1,0:T(8,128)(2,1)S(1)} %bitcast.188), channel_id=1, source_target_pairs={{0,8},{1,12},{2,2},{3,6},{4,9},{5,13},{6,3},{7,7},{8,0},{9,4},{10,... | collective-permute-start | bytes 393224 | tf_op jit(solution)/shard_map/ppermute | solution.py:154
  56.7 1.9 %collective-permute-done.5 = bf16[256,256]{1,0:T(8,128)(2,1)S(1)} collective-permute-done((bf16[256,256]{1,0:T(8,128)(2,1)S(1)}, bf16[256,256]{1,0:T(8,128)(2,1)S(1)}, u32[]{:S(2)}, u32[]{:S(2)}) %collective-permute-start.5) | collective-permute-done | bytes 131104 | tf_op jit(solution)/shard_map/ppermute | solution.py:154
  58.6 5.6 %collective-permute-done.6 = bf16[256,256]{1,0:T(8,128)(2,1)S(1)} collective-permute-done((bf16[256,256]{1,0:T(8,128)(2,1)S(1)}, bf16[256,256]{1,0:T(8,128)(2,1)S(1)}, u32[]{:S(2)}, u32[]{:S(2)}) %collective-permute-start.6) | collective-permute-done | bytes 131104 | tf_op jit(solution)/shard_map/ppermute | solution.py:154
  65.1 13.0 %collective-permute-done.8 = bf16[4,256,256]{2,1,0:T(8,128)(2,1)S(1)} collective-permute-done((bf16[4,256,256]{2,1,0:T(8,128)(2,1)S(1)}, bf16[4,256,256]{2,1,0:T(8,128)(2,1)S(1)}, u32[]{:S(2)}, u32[]{:S(2)}) %collective-permute-start.8) | collective-permute-done | bytes 524320 | tf_op jit(solution)/shard_map/ppermute | solution.py:180
  78.3 1.5 %collective-permute-start.9 = (bf16[2,4,256,256]{3,2,0,1:T(8,128)(2,1)S(1)}, bf16[2,4,256,256]{3,2,0,1:T(8,128)(2,1)S(1)}, u32[]{:S(2)}, u32[]{:S(2)}) collective-permute-start(bf16[2,4,256,256]{3,2,0,1:T(8,128)(2,1)S(1)} %get-tuple-element.27), channel_id=1, source_target_pairs={{0,1},{1,0},{2,3},{3,2},{4,5},{5,4},{6,7},{7,6},{8,9},{9,8},{10,11... | collective-permute-start | bytes 3145736 | tf_op jit(solution)/shard_map/ppermute | solution.py:182
  79.9 4.3 %gather_fusion.1 = bf16[4,256,1536]{2,1,0:T(8,128)(2,1)} fusion(bf16[4,256,1536]{2,1,0:T(8,128)(2,1)} %bitcast.177, s32[1024]{0:T(1024)S(1)} %pad_clamp_fusion), kind=kCustom, calls=%fused_computation.1 | custom fusion | bytes 6291472 | tf_op jit(solution)/shard_map/jit(_take)/gather | solution.py:99
  84.2 2.3 %broadcast_select_fusion = bf16[4,256,1536]{2,1,0:T(8,128)(2,1)S(1)} fusion(bf16[4,256,1536]{2,1,0:T(8,128)(2,1)} %gather_fusion.1, pred[4]{0:T(512)(128)(4,1)S(1)} %get-tuple-element.42), kind=kLoop, calls=%fused_computation.15 | loop fusion | flops 1572864 | bytes 6291460 | tf_op jit(solution)/shard_map/jit(_take)/select_n | solution.py:99
  88.5 3.1 %collective-permute-start.10 = (bf16[256,1536]{1,0:T(8,128)(2,1)S(1)}, bf16[256,1536]{1,0:T(8,128)(2,1)S(1)}, u32[]{:S(2)}, u32[]{:S(2)}) collective-permute-start(bf16[256,1536]{1,0:T(8,128)(2,1)S(1)} %fusion.5), channel_id=1, source_target_pairs={{0,4},{4,8},{1,5},{5,9},{2,6},{6,10},{3,7},{7,11},{16,20},{20,24},... | collective-permute-start | bytes 2359304 | tf_op jit(solution)/shard_map/ppermute | solution.py:195
  94.2 5.0 %collective-permute-start.12 = (bf16[256,1536]{1,0:T(8,128)(2,1)S(1)}, bf16[256,1536]{1,0:T(8,128)(2,1)S(1)}, u32[]{:S(2)}, u32[]{:S(2)}) collective-permute-start(bf16[256,1536]{1,0:T(8,128)(2,1)S(1)} %fusion.6), channel_id=1, source_target_pairs={{0,12},{1,13},{2,14},{3,15},{16,28},{17,29},{18,30},{19,31}} | collective-permute-start | bytes 2359304 | tf_op jit(solution)/shard_map/ppermute | solution.py:198
  99.2 1.5 collective-permute-start.15
  101.7 7.7 %collective-permute-done.10 = bf16[256,1536]{1,0:T(8,128)(2,1)S(1)} collective-permute-done((bf16[256,1536]{1,0:T(8,128)(2,1)S(1)}, bf16[256,1536]{1,0:T(8,128)(2,1)S(1)}, u32[]{:S(2)}, u32[]{:S(2)}) %collective-permute-start.10) | collective-permute-done | bytes 786464 | tf_op jit(solution)/shard_map/ppermute | solution.py:195
  109.4 1.0 fusion.4
  110.5 19.3 %collective-permute-start.11 = (bf16[256,1536]{1,0:T(8,128)(2,1)S(1)}, bf16[256,1536]{1,0:T(8,128)(2,1)S(1)}, u32[]{:S(2)}, u32[]{:S(2)}) collective-permute-start(bf16[256,1536]{1,0:T(8,128)(2,1)S(1)} %fusion.4), channel_id=1, source_target_pairs={{0,4},{4,8},{8,12},{1,5},{5,9},{9,13},{2,6},{6,10},{10,14},{3,7},{... | collective-permute-start | bytes 2359304 | tf_op jit(solution)/shard_map/ppermute | solution.py:204
  130.7 1.3 collective-permute-start.14
  132.1 10.2 %collective-permute-done.11 = bf16[256,1536]{1,0:T(8,128)(2,1)S(1)} collective-permute-done((bf16[256,1536]{1,0:T(8,128)(2,1)S(1)}, bf16[256,1536]{1,0:T(8,128)(2,1)S(1)}, u32[]{:S(2)}, u32[]{:S(2)}) %collective-permute-start.11) | collective-permute-done | bytes 786464 | tf_op jit(solution)/shard_map/ppermute | solution.py:204
  142.2 10.2 %collective-permute-done.14 = bf16[256,1536]{1,0:T(8,128)(2,1)S(1)} collective-permute-done((bf16[256,1536]{1,0:T(8,128)(2,1)S(1)}, bf16[256,1536]{1,0:T(8,128)(2,1)S(1)}, u32[]{:S(2)}, u32[]{:S(2)}) %collective-permute-start.14) | collective-permute-done | bytes 786464 | tf_op jit(solution)/shard_map/ppermute | solution.py:213
  152.4 1.4 add_convert_fusion
  (83 shorter events, 16.6 us)
Async XLA Ops:
  5.6 0.8 copy-start.1
  5.7 14.8 %copy-start.7 = (s32[1536]{0:T(1024)S(1)}, s32[1536]{0:T(1024)}, u32[]{:S(2)}) copy-start(s32[1536]{0:T(1024)} %param.17) | copy-start | bytes 18436
  5.7 14.8 %copy-start.6 = (bf16[256,1024]{1,0:T(8,128)(2,1)S(1)}, bf16[256,1024]{1,0:T(8,128)(2,1)}, u32[]{:S(2)}) copy-start(bf16[256,1024]{1,0:T(8,128)(2,1)} %param.9) | copy-start | bytes 1572868
  6.2 0.8 copy-start.2
  8.2 23.9 %collective-permute-start = (bf16[8,16640]{1,0:T(8,128)(2,1)}, bf16[8,16640]{1,0:T(8,128)(2,1)S(1)}, u32[]{:S(2)}, u32[]{:S(2)}) collective-permute-start(bf16[8,16640]{1,0:T(8,128)(2,1)} %pad_maximum_fusion.3), channel_id=1, source_target_pairs={{0,4},{4,8},{8,12},{1,5},{5,9},{9,13},{2,6},{6,10},{10,14},{3,7},{... | collective-permute-start | bytes 798728 | tf_op jit(solution)/shard_map/ppermute | solution.py:106
  13.1 19.0 %collective-permute-start.1 = (bf16[8,16640]{1,0:T(8,128)(2,1)}, bf16[8,16640]{1,0:T(8,128)(2,1)}, u32[]{:S(2)}, u32[]{:S(2)}) collective-permute-start(bf16[8,16640]{1,0:T(8,128)(2,1)} %pad_maximum_fusion.3), channel_id=1, source_target_pairs={{0,8},{4,12},{1,9},{5,13},{2,10},{6,14},{3,11},{7,15},{16,24},{20,... | collective-permute-start | bytes 798728 | tf_op jit(solution)/shard_map/ppermute | solution.py:106
  18.3 14.7 %collective-permute-start.2 = (bf16[8,16640]{1,0:T(8,128)(2,1)}, bf16[8,16640]{1,0:T(8,128)(2,1)}, u32[]{:S(2)}, u32[]{:S(2)}) collective-permute-start(bf16[8,16640]{1,0:T(8,128)(2,1)} %pad_maximum_fusion.3), channel_id=1, source_target_pairs={{0,12},{1,13},{2,14},{3,15},{16,28},{17,29},{18,30},{19,31}} | collective-permute-start | bytes 798728 | tf_op jit(solution)/shard_map/ppermute | solution.py:106
  21.5 2.9 %copy-start.3 = (bf16[256,1024]{0,1:T(8,128)(2,1)S(1)}, bf16[256,1024]{0,1:T(8,128)(2,1)}, u32[]{:S(2)}) copy-start(bf16[256,1024]{0,1:T(8,128)(2,1)} %copy.67) | copy-start | bytes 1572868
  24.4 5.1 %copy-start = (bf16[1024,1536]{1,0:T(8,128)(2,1)}, bf16[1024,1536]{1,0:T(8,128)(2,1)S(1)}, u32[]{:S(2)}) copy-start(bf16[1024,1536]{1,0:T(8,128)(2,1)S(1)} %multiply_convert_fusion) | copy-start | bytes 9437188
  30.1 4.4 %copy-start.4 = (bf16[256,1024]{0,1:T(8,128)(2,1)S(1)}, bf16[256,1024]{0,1:T(8,128)(2,1)}, u32[]{:S(2)}) copy-start(bf16[256,1024]{0,1:T(8,128)(2,1)} %fusion.16) | copy-start | bytes 1572868
  30.1 4.4 %copy-start.5 = (f32[1,256,8,128]{1,3,2,0:T(8,128)S(1)}, f32[1,256,8,128]{1,3,2,0:T(8,128)}, u32[]{:S(2)}) copy-start(f32[1,256,8,128]{1,3,2,0:T(8,128)} %fusion.10) | copy-start | bytes 3145732
  34.5 0.9 copy-start.8
  35.7 7.5 %collective-permute-start.3 = (bf16[256,2,256]{0,2,1:T(8,128)(2,1)S(1)}, bf16[256,2,256]{0,2,1:T(8,128)(2,1)S(1)}, u32[]{:S(2)}, u32[]{:S(2)}) collective-permute-start(bf16[256,2,256]{0,2,1:T(8,128)(2,1)S(1)} %get-tuple-element.32), channel_id=1, source_target_pairs={{0,2},{1,3},{2,0},{3,1},{4,6},{5,7},{6,4},{7,5},{8,10},{9,11},{10,... | collective-permute-start | bytes 786440 | tf_op jit(solution)/shard_map/ppermute | solution.py:143
  43.5 13.1 %collective-permute-start.4 = (bf16[256,256]{1,0:T(8,128)(2,1)S(1)}, bf16[256,256]{1,0:T(8,128)(2,1)S(1)}, u32[]{:S(2)}, u32[]{:S(2)}) collective-permute-start(bf16[256,256]{1,0:T(8,128)(2,1)S(1)} %bitcast.186), channel_id=1, source_target_pairs={{0,0},{1,4},{2,10},{3,14},{4,1},{5,5},{6,11},{7,15},{8,8},{9,12},{... | collective-permute-start | bytes 393224 | tf_op jit(solution)/shard_map/ppermute | solution.py:154
  44.3 14.2 %collective-permute-start.5 = (bf16[256,256]{1,0:T(8,128)(2,1)S(1)}, bf16[256,256]{1,0:T(8,128)(2,1)S(1)}, u32[]{:S(2)}, u32[]{:S(2)}) collective-permute-start(bf16[256,256]{1,0:T(8,128)(2,1)S(1)} %bitcast.187), channel_id=1, source_target_pairs={{0,1},{1,5},{2,11},{3,15},{4,8},{5,12},{6,2},{7,6},{8,9},{9,13},{1... | collective-permute-start | bytes 393224 | tf_op jit(solution)/shard_map/ppermute | solution.py:154
  51.2 13.0 %collective-permute-start.6 = (bf16[256,256]{1,0:T(8,128)(2,1)S(1)}, bf16[256,256]{1,0:T(8,128)(2,1)S(1)}, u32[]{:S(2)}, u32[]{:S(2)}) collective-permute-start(bf16[256,256]{1,0:T(8,128)(2,1)S(1)} %bitcast.188), channel_id=1, source_target_pairs={{0,8},{1,12},{2,2},{3,6},{4,9},{5,13},{6,3},{7,7},{8,0},{9,4},{10,... | collective-permute-start | bytes 393224 | tf_op jit(solution)/shard_map/ppermute | solution.py:154
  56.6 7.6 %collective-permute-start.7 = (bf16[256,256]{1,0:T(8,128)(2,1)S(1)}, bf16[256,256]{1,0:T(8,128)(2,1)S(1)}, u32[]{:S(2)}, u32[]{:S(2)}) collective-permute-start(bf16[256,256]{1,0:T(8,128)(2,1)S(1)} %bitcast.189), channel_id=1, source_target_pairs={{0,9},{1,13},{2,3},{3,7},{4,0},{5,4},{6,10},{7,14},{8,1},{9,5},{10... | collective-permute-start | bytes 393224 | tf_op jit(solution)/shard_map/ppermute | solution.py:154
  64.9 13.2 %collective-permute-start.8 = (bf16[4,256,256]{2,1,0:T(8,128)(2,1)S(1)}, bf16[4,256,256]{2,1,0:T(8,128)(2,1)S(1)}, u32[]{:S(2)}, u32[]{:S(2)}) collective-permute-start(bf16[4,256,256]{2,1,0:T(8,128)(2,1)S(1)} %broadcast_select_fusion.1), channel_id=1, source_target_pairs={{0,2},{1,3},{2,0},{3,1},{4,6},{5,7},{6,4},{7,5},{8,10},{9,11},{10,... | collective-permute-start | bytes 1572872 | tf_op jit(solution)/shard_map/ppermute | solution.py:180
  78.3 8.2 %collective-permute-start.9 = (bf16[2,4,256,256]{3,2,0,1:T(8,128)(2,1)S(1)}, bf16[2,4,256,256]{3,2,0,1:T(8,128)(2,1)S(1)}, u32[]{:S(2)}, u32[]{:S(2)}) collective-permute-start(bf16[2,4,256,256]{3,2,0,1:T(8,128)(2,1)S(1)} %get-tuple-element.27), channel_id=1, source_target_pairs={{0,1},{1,0},{2,3},{3,2},{4,5},{5,4},{6,7},{7,6},{8,9},{9,8},{10,11... | collective-permute-start | bytes 3145736 | tf_op jit(solution)/shard_map/ppermute | solution.py:182
  88.5 20.9 %collective-permute-start.10 = (bf16[256,1536]{1,0:T(8,128)(2,1)S(1)}, bf16[256,1536]{1,0:T(8,128)(2,1)S(1)}, u32[]{:S(2)}, u32[]{:S(2)}) collective-permute-start(bf16[256,1536]{1,0:T(8,128)(2,1)S(1)} %fusion.5), channel_id=1, source_target_pairs={{0,4},{4,8},{1,5},{5,9},{2,6},{6,10},{3,7},{7,11},{16,20},{20,24},... | collective-permute-start | bytes 2359304 | tf_op jit(solution)/shard_map/ppermute | solution.py:195
  92.5 37.2 %collective-permute-start.13 = (bf16[256,1536]{1,0:T(8,128)(2,1)S(1)}, bf16[256,1536]{1,0:T(8,128)(2,1)S(1)}, u32[]{:S(2)}, u32[]{:S(2)}) collective-permute-start(bf16[256,1536]{1,0:T(8,128)(2,1)S(1)} %fusion.7), channel_id=1, source_target_pairs={{12,8},{8,4},{13,9},{9,5},{14,10},{10,6},{15,11},{11,7},{28,24},{2... | collective-permute-start | bytes 2359304 | tf_op jit(solution)/shard_map/ppermute | solution.py:199
  94.2 37.8 %collective-permute-start.12 = (bf16[256,1536]{1,0:T(8,128)(2,1)S(1)}, bf16[256,1536]{1,0:T(8,128)(2,1)S(1)}, u32[]{:S(2)}, u32[]{:S(2)}) collective-permute-start(bf16[256,1536]{1,0:T(8,128)(2,1)S(1)} %fusion.6), channel_id=1, source_target_pairs={{0,12},{1,13},{2,14},{3,15},{16,28},{17,29},{18,30},{19,31}} | collective-permute-start | bytes 2359304 | tf_op jit(solution)/shard_map/ppermute | solution.py:198
  99.2 32.8 %collective-permute-start.15 = (bf16[256,1536]{1,0:T(8,128)(2,1)S(1)}, bf16[256,1536]{1,0:T(8,128)(2,1)S(1)}, u32[]{:S(2)}, u32[]{:S(2)}) collective-permute-start(bf16[256,1536]{1,0:T(8,128)(2,1)S(1)} %fusion.8), channel_id=1, source_target_pairs={{12,0},{13,1},{14,2},{15,3},{28,16},{29,17},{30,18},{31,19}} | collective-permute-start | bytes 2359304 | tf_op jit(solution)/shard_map/ppermute | solution.py:202
  110.5 31.8 %collective-permute-start.11 = (bf16[256,1536]{1,0:T(8,128)(2,1)S(1)}, bf16[256,1536]{1,0:T(8,128)(2,1)S(1)}, u32[]{:S(2)}, u32[]{:S(2)}) collective-permute-start(bf16[256,1536]{1,0:T(8,128)(2,1)S(1)} %fusion.4), channel_id=1, source_target_pairs={{0,4},{4,8},{8,12},{1,5},{5,9},{9,13},{2,6},{6,10},{10,14},{3,7},{... | collective-permute-start | bytes 2359304 | tf_op jit(solution)/shard_map/ppermute | solution.py:204
  130.7 21.7 %collective-permute-start.14 = (bf16[256,1536]{1,0:T(8,128)(2,1)S(1)}, bf16[256,1536]{1,0:T(8,128)(2,1)S(1)}, u32[]{:S(2)}, u32[]{:S(2)}) collective-permute-start(bf16[256,1536]{1,0:T(8,128)(2,1)S(1)} %fusion.3), channel_id=1, source_target_pairs={{12,8},{8,4},{4,0},{13,9},{9,5},{5,1},{14,10},{10,6},{6,2},{15,11}... | collective-permute-start | bytes 2359304 | tf_op jit(solution)/shard_map/ppermute | solution.py:213

commit v22 on v18

--- a/solution.py
+++ b/solution.py
@@ -102,8 +102,11 @@
     position = lax.axis_index("seq")
     incoming = jnp.zeros((heads_here, HDIM * HDIM), jnp.float32)
     gap = jnp.zeros((heads_here,), jnp.float32)
+    shifted = {}
+    for d in range(n_seq - 1, 0, -1):
+        shifted[d] = lax.ppermute(packed, "seq", [(z, z + d) for z in range(n_seq - d)])
     for d in range(1, n_seq):
-        came = lax.ppermute(packed, "seq", [(z, z + d) for z in range(n_seq - d)])
+        came = shifted[d]
         came_state = came[:, : HDIM * HDIM].astype(jnp.float32)
         came_log = came[:, HDIM * HDIM].astype(jnp.float32) + came[:, HDIM * HDIM + HDIM].astype(
             jnp.float32

time: 148 us -> 148 us (level)
  no operation moved by 1% of the time
where the time goes in v22:
time: 148 us; the launch traced here: 147 us
  waiting for transfers between devices  64.8 us (44%)
  starting transfers between devices  38.5 us (26%)
  other arithmetic  18 us (12%)
  local copies, waits for them, and re-layouts  13.4 us (9%)
  matrix products  11.2 us (8%)
    ppermute x1, waiting for transfers between devices, per_device(): got.append(lax.ppermute(x, 'mdl', perm))  13 us
    ppermute x3, starting transfers between devices, per_device(): lax.ppermute(packed, 'seq', [(z, z + d) for z in range(n_seq - d)])  12.1 us
    ppermute x1, waiting for transfers between devices, per_device(): lax.ppermute(bf(partial_for(jnp.clip(s_me + 1, 0, 3)) + near_r.astype(jnp...  10.8 us
    ppermute x1, waiting for transfers between devices, per_device(): far_r = lax.ppermute(bf(partial_for(jnp.int32(3))), 'seq', [(0, 3)])  9.16 us
    unnamed x22, local copies, waits for them, and re-layouts  8.48 us
    ppermute x4, waiting for transfers between devices, per_device(): received.append(lax.ppermute(item, ('seq', 'mdl'), perm))  7.75 us
    ppermute x1, waiting for transfers between devices, per_device(): lax.ppermute(bf(partial_for(jnp.clip(s_me + 2, 0, 3))), 'seq', [(0, 1), (...  7.36 us
    ppermute x4, starting transfers between devices, per_device(): received.append(lax.ppermute(item, ('seq', 'mdl'), perm))  7.19 us
  transfers between devices with their start and end apart: 16, of which 9 were waited for; matrix products, arithmetic and copies ran while one was open for 17% of the time, Pallas kernels for 0%

profile of v22, /device:TPU:0, one launch (start us, length us, event | category | flops | bytes accessed | tf_op | source)
XLA Modules:
  0.0 147.1 jit_solution(14933625494824646292)
XLA Ops:
  0.0 1.2 reduce-window.6
  2.8 1.2 copy.66
  4.1 2.0 %copy.68 = bf16[256,1024]{0,1:T(8,128)(2,1)} copy(bf16[256,1024]{1,0:T(8,128)(2,1)} %param.10) | data formatting | bytes 1048576 | tf_op args[1]
  6.5 1.8 %fusion.20 = bf16[256,1024]{0,1:T(8,128)(2,1)S(1)} fusion(bf16[256,1024]{0,1:T(8,128)(2,1)} %copy.68, f32[1024]{0:T(1024)S(1)} %bitcast.200), kind=kLoop, calls=%fused_computation.51 | loop fusion | flops 3407872 | bytes 1052672 | tf_op jit(solution)/shard_map/convert_element_type | solution.py:52
  10.2 4.9 %collective-permute-start = (bf16[8,16640]{1,0:T(8,128)(2,1)}, bf16[8,16640]{1,0:T(8,128)(2,1)S(1)}, u32[]{:S(2)}, u32[]{:S(2)}) collective-permute-start(bf16[8,16640]{1,0:T(8,128)(2,1)} %pad_maximum_fusion.3), channel_id=1, source_target_pairs={{0,4},{4,8},{8,12},{1,5},{5,9},{9,13},{2,6},{6,10},{10,14},{3,7},{... | collective-permute-start | bytes 798728 | tf_op jit(solution)/shard_map/ppermute | solution.py:107
  15.2 5.2 %collective-permute-start.1 = (bf16[8,16640]{1,0:T(8,128)(2,1)}, bf16[8,16640]{1,0:T(8,128)(2,1)}, u32[]{:S(2)}, u32[]{:S(2)}) collective-permute-start(bf16[8,16640]{1,0:T(8,128)(2,1)} %pad_maximum_fusion.3), channel_id=1, source_target_pairs={{0,8},{4,12},{1,9},{5,13},{2,10},{6,14},{3,11},{7,15},{16,24},{20,... | collective-permute-start | bytes 798728 | tf_op jit(solution)/shard_map/ppermute | solution.py:107
  20.4 2.0 %collective-permute-start.2 = (bf16[8,16640]{1,0:T(8,128)(2,1)}, bf16[8,16640]{1,0:T(8,128)(2,1)}, u32[]{:S(2)}, u32[]{:S(2)}) collective-permute-start(bf16[8,16640]{1,0:T(8,128)(2,1)} %pad_maximum_fusion.3), channel_id=1, source_target_pairs={{0,12},{1,13},{2,14},{3,15},{16,28},{17,29},{18,30},{19,31}} | collective-permute-start | bytes 798728 | tf_op jit(solution)/shard_map/ppermute | solution.py:107
  22.8 2.7 %multiply_convert_fusion = bf16[1024,1536]{1,0:T(8,128)(2,1)} fusion(bf16[1024,1536]{1,0:T(8,128)(2,1)S(1)} %copy-done.1, f32[1536]{0:T(1024)S(1)} %select_add_fusion), kind=kLoop, calls=%fused_computation.2 | loop fusion | flops 11010048 | bytes 6297600 | tf_op jit(solution)/shard_map/convert_element_type | solution.py:20
  25.4 2.6 %gather_fusion = bf16[4,256,1536]{2,1,0:T(8,128)(2,1)S(1)} fusion(bf16[4,256,1536]{2,1,0:T(8,128)(2,1)} %bitcast.182, s32[1024]{0:T(1024)S(1)} %pad_clamp_fusion.1), kind=kCustom, calls=%fused_computation | custom fusion | bytes 6291472 | tf_op jit(solution)/shard_map/jit(_take)/gather | solution.py:99
  28.7 2.5 %copy.67 = bf16[256,1024]{0,1:T(8,128)(2,1)} copy(bf16[256,1024]{1,0:T(8,128)(2,1)} %param.9) | data formatting | bytes 1048576 | tf_op args[0]
  31.2 2.0 %copy.75 = bf16[256,1024]{0,1:T(8,128)(2,1)} copy(bf16[256,1024]{1,0:T(8,128)(2,1)} %param.12) | data formatting | bytes 1048576 | tf_op args[3]
  33.9 2.4 %fusion.16 = bf16[256,1024]{0,1:T(8,128)(2,1)} fusion(bf16[256,1024]{0,1:T(8,128)(2,1)} %copy.67, f32[1024]{0:T(1024)S(1)} %bitcast.199), kind=kLoop, calls=%fused_computation.47 | loop fusion | flops 3407872 | bytes 1052672 | tf_op jit(solution)/shard_map/convert_element_type | solution.py:47
  36.3 3.3 %fusion.10 = f32[1,256,8,128]{1,3,2,0:T(8,128)} fusion(bf16[256,8,128]{0,2,1:T(8,128)(2,1)} %bitcast.184, bf16[256,8,128]{0,2,1:T(8,128)(2,1)} %bitcast.188, bf16[256,8,128]{0,2,1:T(8,128)(2,1)} %bitcast.186, f32[8,256]{1,0:T(8,128)S(1)} %bitcast_add_fusion.2, pred[256,256]{1,0:T(8,128)(4,1)S(1)} %iota_compare_fusion), kind=kOutput, calls=%fused_computation.35 | convolution fusion | flops 271056896 | bytes 2695168 | tf_op jit(solution)/shard_map/hbij,bjhd->bihd/dot_general | solution.py:62
  43.5 1.6 %collective-permute-start.3 = (bf16[256,2,256]{0,2,1:T(8,128)(2,1)S(1)}, bf16[256,2,256]{0,2,1:T(8,128)(2,1)S(1)}, u32[]{:S(2)}, u32[]{:S(2)}) collective-permute-start(bf16[256,2,256]{0,2,1:T(8,128)(2,1)S(1)} %get-tuple-element.32), channel_id=1, source_target_pairs={{0,2},{1,3},{2,0},{3,1},{4,6},{5,7},{6,4},{7,5},{8,10},{9,11},{10,... | collective-permute-start | bytes 786440 | tf_op jit(solution)/shard_map/ppermute | solution.py:146
  45.1 5.9 %collective-permute-done.3 = bf16[256,2,256]{0,2,1:T(8,128)(2,1)S(1)} collective-permute-done((bf16[256,2,256]{0,2,1:T(8,128)(2,1)S(1)}, bf16[256,2,256]{0,2,1:T(8,128)(2,1)S(1)}, u32[]{:S(2)}, u32[]{:S(2)}) %collective-permute-start.3) | collective-permute-done | bytes 262176 | tf_op jit(solution)/shard_map/ppermute | solution.py:146
  53.4 5.3 %collective-permute-start.6 = (bf16[256,256]{1,0:T(8,128)(2,1)S(1)}, bf16[256,256]{1,0:T(8,128)(2,1)S(1)}, u32[]{:S(2)}, u32[]{:S(2)}) collective-permute-start(bf16[256,256]{1,0:T(8,128)(2,1)S(1)} %bitcast.193), channel_id=1, source_target_pairs={{0,8},{1,12},{2,2},{3,6},{4,9},{5,13},{6,3},{7,7},{8,0},{9,4},{10,... | collective-permute-start | bytes 393224 | tf_op jit(solution)/shard_map/ppermute | solution.py:157
  58.9 2.1 %collective-permute-done.5 = bf16[256,256]{1,0:T(8,128)(2,1)S(1)} collective-permute-done((bf16[256,256]{1,0:T(8,128)(2,1)S(1)}, bf16[256,256]{1,0:T(8,128)(2,1)S(1)}, u32[]{:S(2)}, u32[]{:S(2)}) %collective-permute-start.5) | collective-permute-done | bytes 131104 | tf_op jit(solution)/shard_map/ppermute | solution.py:157
  61.0 5.6 %collective-permute-done.6 = bf16[256,256]{1,0:T(8,128)(2,1)S(1)} collective-permute-done((bf16[256,256]{1,0:T(8,128)(2,1)S(1)}, bf16[256,256]{1,0:T(8,128)(2,1)S(1)}, u32[]{:S(2)}, u32[]{:S(2)}) %collective-permute-start.6) | collective-permute-done | bytes 131104 | tf_op jit(solution)/shard_map/ppermute | solution.py:157
  67.6 13.0 %collective-permute-done.8 = bf16[4,256,256]{2,1,0:T(8,128)(2,1)S(1)} collective-permute-done((bf16[4,256,256]{2,1,0:T(8,128)(2,1)S(1)}, bf16[4,256,256]{2,1,0:T(8,128)(2,1)S(1)}, u32[]{:S(2)}, u32[]{:S(2)}) %collective-permute-start.8) | collective-permute-done | bytes 524320 | tf_op jit(solution)/shard_map/ppermute | solution.py:183
  80.8 1.5 %collective-permute-start.9 = (bf16[2,4,256,256]{3,2,0,1:T(8,128)(2,1)S(1)}, bf16[2,4,256,256]{3,2,0,1:T(8,128)(2,1)S(1)}, u32[]{:S(2)}, u32[]{:S(2)}) collective-permute-start(bf16[2,4,256,256]{3,2,0,1:T(8,128)(2,1)S(1)} %get-tuple-element.27), channel_id=1, source_target_pairs={{0,1},{1,0},{2,3},{3,2},{4,5},{5,4},{6,7},{7,6},{8,9},{9,8},{10,11... | collective-permute-start | bytes 3145736 | tf_op jit(solution)/shard_map/ppermute | solution.py:185
  82.3 2.3 %broadcast_select_fusion = bf16[4,256,1536]{2,1,0:T(8,128)(2,1)S(1)} fusion(bf16[4,256,1536]{2,1,0:T(8,128)(2,1)} %copy-done, pred[4]{0:T(512)(128)(4,1)S(1)} %get-tuple-element.42), kind=kLoop, calls=%fused_computation.15 | loop fusion | flops 1572864 | bytes 6291460 | tf_op jit(solution)/shard_map/jit(_take)/select_n | solution.py:99
  86.6 2.8 %collective-permute-start.10 = (bf16[256,1536]{1,0:T(8,128)(2,1)S(1)}, bf16[256,1536]{1,0:T(8,128)(2,1)S(1)}, u32[]{:S(2)}, u32[]{:S(2)}) collective-permute-start(bf16[256,1536]{1,0:T(8,128)(2,1)S(1)} %fusion.5), channel_id=1, source_target_pairs={{0,4},{4,8},{1,5},{5,9},{2,6},{6,10},{3,7},{7,11},{16,20},{20,24},... | collective-permute-start | bytes 2359304 | tf_op jit(solution)/shard_map/ppermute | solution.py:198
  92.1 5.5 %collective-permute-start.12 = (bf16[256,1536]{1,0:T(8,128)(2,1)S(1)}, bf16[256,1536]{1,0:T(8,128)(2,1)S(1)}, u32[]{:S(2)}, u32[]{:S(2)}) collective-permute-start(bf16[256,1536]{1,0:T(8,128)(2,1)S(1)} %fusion.6), channel_id=1, source_target_pairs={{0,12},{1,13},{2,14},{3,15},{16,28},{17,29},{18,30},{19,31}} | collective-permute-start | bytes 2359304 | tf_op jit(solution)/shard_map/ppermute | solution.py:201
  97.6 1.3 collective-permute-start.15
  99.9 7.4 %collective-permute-done.10 = bf16[256,1536]{1,0:T(8,128)(2,1)S(1)} collective-permute-done((bf16[256,1536]{1,0:T(8,128)(2,1)S(1)}, bf16[256,1536]{1,0:T(8,128)(2,1)S(1)}, u32[]{:S(2)}, u32[]{:S(2)}) %collective-permute-start.10) | collective-permute-done | bytes 786464 | tf_op jit(solution)/shard_map/ppermute | solution.py:198
  108.3 4.4 %collective-permute-start.11 = (bf16[256,1536]{1,0:T(8,128)(2,1)S(1)}, bf16[256,1536]{1,0:T(8,128)(2,1)S(1)}, u32[]{:S(2)}, u32[]{:S(2)}) collective-permute-start(bf16[256,1536]{1,0:T(8,128)(2,1)S(1)} %fusion.4), channel_id=1, source_target_pairs={{0,4},{4,8},{8,12},{1,5},{5,9},{9,13},{2,6},{6,10},{10,14},{3,7},{... | collective-permute-start | bytes 2359304 | tf_op jit(solution)/shard_map/ppermute | solution.py:207
  113.7 1.3 collective-permute-start.14
  115.0 9.2 %collective-permute-done.12 = bf16[256,1536]{1,0:T(8,128)(2,1)S(1)} collective-permute-done((bf16[256,1536]{1,0:T(8,128)(2,1)S(1)}, bf16[256,1536]{1,0:T(8,128)(2,1)S(1)}, u32[]{:S(2)}, u32[]{:S(2)}) %collective-permute-start.12) | collective-permute-done | bytes 786464 | tf_op jit(solution)/shard_map/ppermute | solution.py:201
  124.2 5.5 %collective-permute-done.15 = bf16[256,1536]{1,0:T(8,128)(2,1)S(1)} collective-permute-done((bf16[256,1536]{1,0:T(8,128)(2,1)S(1)}, bf16[256,1536]{1,0:T(8,128)(2,1)S(1)}, u32[]{:S(2)}, u32[]{:S(2)}) %collective-permute-start.15) | collective-permute-done | bytes 786464 | tf_op jit(solution)/shard_map/ppermute | solution.py:205
  129.7 10.8 %collective-permute-done.11 = bf16[256,1536]{1,0:T(8,128)(2,1)S(1)} collective-permute-done((bf16[256,1536]{1,0:T(8,128)(2,1)S(1)}, bf16[256,1536]{1,0:T(8,128)(2,1)S(1)}, u32[]{:S(2)}, u32[]{:S(2)}) %collective-permute-start.11) | collective-permute-done | bytes 786464 | tf_op jit(solution)/shard_map/ppermute | solution.py:207
  140.5 5.3 %collective-permute-done.14 = bf16[256,1536]{1,0:T(8,128)(2,1)S(1)} collective-permute-done((bf16[256,1536]{1,0:T(8,128)(2,1)S(1)}, bf16[256,1536]{1,0:T(8,128)(2,1)S(1)}, u32[]{:S(2)}, u32[]{:S(2)}) %collective-permute-start.14) | collective-permute-done | bytes 786464 | tf_op jit(solution)/shard_map/ppermute | solution.py:216
  145.7 1.4 add_convert_fusion
  (84 shorter events, 20.0 us)
Async XLA Ops:
  6.4 1.8 %copy-start.2 = (bf16[256,1024]{0,1:T(8,128)(2,1)}, bf16[256,1024]{0,1:T(8,128)(2,1)S(1)}, u32[]{:S(2)}) copy-start(bf16[256,1024]{0,1:T(8,128)(2,1)S(1)} %multiply_convert_fusion.5) | copy-start | bytes 1572868
  6.4 16.3 %copy-start.7 = (s32[1536]{0:T(1024)S(1)}, s32[1536]{0:T(1024)}, u32[]{:S(2)}) copy-start(s32[1536]{0:T(1024)} %param.17) | copy-start | bytes 18436
  6.5 16.3 %copy-start.1 = (bf16[1024,1536]{1,0:T(8,128)(2,1)S(1)}, bf16[1024,1536]{1,0:T(8,128)(2,1)}, u32[]{:S(2)}) copy-start(bf16[1024,1536]{1,0:T(8,128)(2,1)} %param.16) | copy-start | bytes 9437188
  8.3 0.8 copy-start.3
  10.2 29.4 %collective-permute-start = (bf16[8,16640]{1,0:T(8,128)(2,1)}, bf16[8,16640]{1,0:T(8,128)(2,1)S(1)}, u32[]{:S(2)}, u32[]{:S(2)}) collective-permute-start(bf16[8,16640]{1,0:T(8,128)(2,1)} %pad_maximum_fusion.3), channel_id=1, source_target_pairs={{0,4},{4,8},{8,12},{1,5},{5,9},{9,13},{2,6},{6,10},{10,14},{3,7},{... | collective-permute-start | bytes 798728 | tf_op jit(solution)/shard_map/ppermute | solution.py:107
  15.2 24.4 %collective-permute-start.1 = (bf16[8,16640]{1,0:T(8,128)(2,1)}, bf16[8,16640]{1,0:T(8,128)(2,1)}, u32[]{:S(2)}, u32[]{:S(2)}) collective-permute-start(bf16[8,16640]{1,0:T(8,128)(2,1)} %pad_maximum_fusion.3), channel_id=1, source_target_pairs={{0,8},{4,12},{1,9},{5,13},{2,10},{6,14},{3,11},{7,15},{16,24},{20,... | collective-permute-start | bytes 798728 | tf_op jit(solution)/shard_map/ppermute | solution.py:107
  20.4 20.2 %collective-permute-start.2 = (bf16[8,16640]{1,0:T(8,128)(2,1)}, bf16[8,16640]{1,0:T(8,128)(2,1)}, u32[]{:S(2)}, u32[]{:S(2)}) collective-permute-start(bf16[8,16640]{1,0:T(8,128)(2,1)} %pad_maximum_fusion.3), channel_id=1, source_target_pairs={{0,12},{1,13},{2,14},{3,15},{16,28},{17,29},{18,30},{19,31}} | collective-permute-start | bytes 798728 | tf_op jit(solution)/shard_map/ppermute | solution.py:107
  28.1 11.5 %copy-start = (bf16[4,256,1536]{2,1,0:T(8,128)(2,1)}, bf16[4,256,1536]{2,1,0:T(8,128)(2,1)S(1)}, u32[]{:S(2)}) copy-start(bf16[4,256,1536]{2,1,0:T(8,128)(2,1)S(1)} %gather_fusion) | copy-start | bytes 9437188
  39.6 2.5 %copy-start.5 = (bf16[256,1024]{0,1:T(8,128)(2,1)S(1)}, bf16[256,1024]{0,1:T(8,128)(2,1)}, u32[]{:S(2)}) copy-start(bf16[256,1024]{0,1:T(8,128)(2,1)} %fusion.16) | copy-start | bytes 1572868
  39.6 2.5 %copy-start.6 = (f32[1,256,8,128]{1,3,2,0:T(8,128)S(1)}, f32[1,256,8,128]{1,3,2,0:T(8,128)}, u32[]{:S(2)}) copy-start(f32[1,256,8,128]{1,3,2,0:T(8,128)} %fusion.10) | copy-start | bytes 3145732
  42.1 1.0 copy-start.4
  42.1 1.0 copy-start.8
  43.5 7.6 %collective-permute-start.3 = (bf16[256,2,256]{0,2,1:T(8,128)(2,1)S(1)}, bf16[256,2,256]{0,2,1:T(8,128)(2,1)S(1)}, u32[]{:S(2)}, u32[]{:S(2)}) collective-permute-start(bf16[256,2,256]{0,2,1:T(8,128)(2,1)S(1)} %get-tuple-element.32), channel_id=1, source_target_pairs={{0,2},{1,3},{2,0},{3,1},{4,6},{5,7},{6,4},{7,5},{8,10},{9,11},{10,... | collective-permute-start | bytes 786440 | tf_op jit(solution)/shard_map/ppermute | solution.py:146
  51.3 7.6 %collective-permute-start.4 = (bf16[256,256]{1,0:T(8,128)(2,1)S(1)}, bf16[256,256]{1,0:T(8,128)(2,1)S(1)}, u32[]{:S(2)}, u32[]{:S(2)}) collective-permute-start(bf16[256,256]{1,0:T(8,128)(2,1)S(1)} %bitcast.191), channel_id=1, source_target_pairs={{0,0},{1,4},{2,10},{3,14},{4,1},{5,5},{6,11},{7,15},{8,8},{9,12},{... | collective-permute-start | bytes 393224 | tf_op jit(solution)/shard_map/ppermute | solution.py:157
  52.1 8.9 %collective-permute-start.5 = (bf16[256,256]{1,0:T(8,128)(2,1)S(1)}, bf16[256,256]{1,0:T(8,128)(2,1)S(1)}, u32[]{:S(2)}, u32[]{:S(2)}) collective-permute-start(bf16[256,256]{1,0:T(8,128)(2,1)S(1)} %bitcast.192), channel_id=1, source_target_pairs={{0,1},{1,5},{2,11},{3,15},{4,8},{5,12},{6,2},{7,6},{8,9},{9,13},{1... | collective-permute-start | bytes 393224 | tf_op jit(solution)/shard_map/ppermute | solution.py:157
  53.4 13.3 %collective-permute-start.6 = (bf16[256,256]{1,0:T(8,128)(2,1)S(1)}, bf16[256,256]{1,0:T(8,128)(2,1)S(1)}, u32[]{:S(2)}, u32[]{:S(2)}) collective-permute-start(bf16[256,256]{1,0:T(8,128)(2,1)S(1)} %bitcast.193), channel_id=1, source_target_pairs={{0,8},{1,12},{2,2},{3,6},{4,9},{5,13},{6,3},{7,7},{8,0},{9,4},{10,... | collective-permute-start | bytes 393224 | tf_op jit(solution)/shard_map/ppermute | solution.py:157
  58.8 7.9 %collective-permute-start.7 = (bf16[256,256]{1,0:T(8,128)(2,1)S(1)}, bf16[256,256]{1,0:T(8,128)(2,1)S(1)}, u32[]{:S(2)}, u32[]{:S(2)}) collective-permute-start(bf16[256,256]{1,0:T(8,128)(2,1)S(1)} %bitcast.194), channel_id=1, source_target_pairs={{0,9},{1,13},{2,3},{3,7},{4,0},{5,4},{6,10},{7,14},{8,1},{9,5},{10... | collective-permute-start | bytes 393224 | tf_op jit(solution)/shard_map/ppermute | solution.py:157
  67.4 13.2 %collective-permute-start.8 = (bf16[4,256,256]{2,1,0:T(8,128)(2,1)S(1)}, bf16[4,256,256]{2,1,0:T(8,128)(2,1)S(1)}, u32[]{:S(2)}, u32[]{:S(2)}) collective-permute-start(bf16[4,256,256]{2,1,0:T(8,128)(2,1)S(1)} %broadcast_select_fusion.1), channel_id=1, source_target_pairs={{0,2},{1,3},{2,0},{3,1},{4,6},{5,7},{6,4},{7,5},{8,10},{9,11},{10,... | collective-permute-start | bytes 1572872 | tf_op jit(solution)/shard_map/ppermute | solution.py:183
  80.8 3.8 %collective-permute-start.9 = (bf16[2,4,256,256]{3,2,0,1:T(8,128)(2,1)S(1)}, bf16[2,4,256,256]{3,2,0,1:T(8,128)(2,1)S(1)}, u32[]{:S(2)}, u32[]{:S(2)}) collective-permute-start(bf16[2,4,256,256]{3,2,0,1:T(8,128)(2,1)S(1)} %get-tuple-element.27), channel_id=1, source_target_pairs={{0,1},{1,0},{2,3},{3,2},{4,5},{5,4},{6,7},{7,6},{8,9},{9,8},{10,11... | collective-permute-start | bytes 3145736 | tf_op jit(solution)/shard_map/ppermute | solution.py:185
  86.6 20.6 %collective-permute-start.10 = (bf16[256,1536]{1,0:T(8,128)(2,1)S(1)}, bf16[256,1536]{1,0:T(8,128)(2,1)S(1)}, u32[]{:S(2)}, u32[]{:S(2)}) collective-permute-start(bf16[256,1536]{1,0:T(8,128)(2,1)S(1)} %fusion.5), channel_id=1, source_target_pairs={{0,4},{4,8},{1,5},{5,9},{2,6},{6,10},{3,7},{7,11},{16,20},{20,24},... | collective-permute-start | bytes 2359304 | tf_op jit(solution)/shard_map/ppermute | solution.py:198
  90.4 22.3 %collective-permute-start.13 = (bf16[256,1536]{1,0:T(8,128)(2,1)S(1)}, bf16[256,1536]{1,0:T(8,128)(2,1)S(1)}, u32[]{:S(2)}, u32[]{:S(2)}) collective-permute-start(bf16[256,1536]{1,0:T(8,128)(2,1)S(1)} %fusion.7), channel_id=1, source_target_pairs={{12,8},{8,4},{13,9},{9,5},{14,10},{10,6},{15,11},{11,7},{28,24},{2... | collective-permute-start | bytes 2359304 | tf_op jit(solution)/shard_map/ppermute | solution.py:202
  92.1 32.1 %collective-permute-start.12 = (bf16[256,1536]{1,0:T(8,128)(2,1)S(1)}, bf16[256,1536]{1,0:T(8,128)(2,1)S(1)}, u32[]{:S(2)}, u32[]{:S(2)}) collective-permute-start(bf16[256,1536]{1,0:T(8,128)(2,1)S(1)} %fusion.6), channel_id=1, source_target_pairs={{0,12},{1,13},{2,14},{3,15},{16,28},{17,29},{18,30},{19,31}} | collective-permute-start | bytes 2359304 | tf_op jit(solution)/shard_map/ppermute | solution.py:201
  97.6 32.1 %collective-permute-start.15 = (bf16[256,1536]{1,0:T(8,128)(2,1)S(1)}, bf16[256,1536]{1,0:T(8,128)(2,1)S(1)}, u32[]{:S(2)}, u32[]{:S(2)}) collective-permute-start(bf16[256,1536]{1,0:T(8,128)(2,1)S(1)} %fusion.8), channel_id=1, source_target_pairs={{12,0},{13,1},{14,2},{15,3},{28,16},{29,17},{30,18},{31,19}} | collective-permute-start | bytes 2359304 | tf_op jit(solution)/shard_map/ppermute | solution.py:205
  108.3 32.2 %collective-permute-start.11 = (bf16[256,1536]{1,0:T(8,128)(2,1)S(1)}, bf16[256,1536]{1,0:T(8,128)(2,1)S(1)}, u32[]{:S(2)}, u32[]{:S(2)}) collective-permute-start(bf16[256,1536]{1,0:T(8,128)(2,1)S(1)} %fusion.4), channel_id=1, source_target_pairs={{0,4},{4,8},{8,12},{1,5},{5,9},{9,13},{2,6},{6,10},{10,14},{3,7},{... | collective-permute-start | bytes 2359304 | tf_op jit(solution)/shard_map/ppermute | solution.py:207
  113.7 32.1 %collective-permute-start.14 = (bf16[256,1536]{1,0:T(8,128)(2,1)S(1)}, bf16[256,1536]{1,0:T(8,128)(2,1)S(1)}, u32[]{:S(2)}, u32[]{:S(2)}) collective-permute-start(bf16[256,1536]{1,0:T(8,128)(2,1)S(1)} %fusion.3), channel_id=1, source_target_pairs={{12,8},{8,4},{4,0},{13,9},{9,5},{5,1},{14,10},{10,6},{6,2},{15,11}... | collective-permute-start | bytes 2359304 | tf_op jit(solution)/shard_map/ppermute | solution.py:216

commit v23 on v22

--- a/solution.py
+++ b/solution.py
@@ -138,7 +138,7 @@
     piece = rows_w // n_mdl
     s_me = lax.axis_index("seq")
     m_me = lax.axis_index("mdl")
-    if n_seq == 4 and n_mdl == 4:
+    if n_seq == 4 and n_mdl == 4 and False:
         x_me = m_me // 2
         own_pieces = attn.reshape(tok_rows, n_mdl, piece)
         keep = lax.dynamic_slice_in_dim(own_pieces, 2 * x_me, 2, axis=1)

time: 148 us -> 151 us (1.020)
  starting transfers between devices: 38.5 us -> 43.6 us
  local copies, waits for them, and re-layouts: 13.4 us -> 8.31 us
  matrix products: 11.2 us -> 15 us
  other arithmetic: 18 us -> 15.4 us
  waiting for transfers between devices: 64.8 us -> 66.7 us
    unnamed x22 -> x10, local copies, waits for them, and re-layouts: 8.48 us -> 0.6 us
    ppermute x5 -> x4, starting transfers between devices: 8.74 us -> 12.6 us  [per_device(): received.append(lax.ppermute(chunk, ('seq', 'mdl'), perm))]
    ppermute x1, starting transfers between devices: 2.81 us -> 5.43 us  [per_device(): lax.ppermute(bf(partial_for(jnp.clip(s_me + 2, 0, 3))), 'seq', [(0, 1), (...]
    convert_element_type x1 -> x0, other arithmetic: 2.41 us -> none  [per_device(): query_feat = jax.nn.silu(queries.astype(jnp.float32)).astype(jnp.bfloat16...]
    ppermute x5 -> x4, waiting for transfers between devices: 13.7 us -> 15.6 us  [per_device(): received.append(lax.ppermute(chunk, ('seq', 'mdl'), perm))]
    dot_general x1, matrix products: 0.73 us -> 2.57 us  [per_device(): jnp.einsum('bihd,bhde->bihe', query_feat.astype(jnp.float32), entry_state...]
    another operation x1, local copies, waits for them, and re-layouts: 0.23 us -> 2.05 us  [per_device(): incoming[None]]
    ppermute x1, starting transfers between devices: 5.48 us -> 3.88 us  [per_device(): far_r = lax.ppermute(bf(partial_for(jnp.int32(3))), 'seq', [(0, 3)])]
  transfers between devices with their start and end apart: 16 -> 15, of which waited for: 9 -> 8; matrix products, arithmetic and copies ran while one was open for 17% -> 12% of each run, Pallas kernels for 0% -> 0%
where the time goes in v23:
time: 151 us; the launch traced here: 150 us
  waiting for transfers between devices  66.7 us (44%)
  starting transfers between devices  43.6 us (29%)
  other arithmetic  15.4 us (10%)
  matrix products  15 us (10%)
  local copies, waits for them, and re-layouts  8.31 us (6%)
    ppermute x4, waiting for transfers between devices, per_device(): received.append(lax.ppermute(chunk, ('seq', 'mdl'), perm))  15.6 us
    ppermute x1, waiting for transfers between devices, per_device(): got.append(lax.ppermute(x, 'mdl', perm))  12.9 us
    ppermute x4, starting transfers between devices, per_device(): received.append(lax.ppermute(chunk, ('seq', 'mdl'), perm))  12.6 us
    ppermute x3, starting transfers between devices, per_device(): lax.ppermute(packed, 'seq', [(z, z + d) for z in range(n_seq - d)])  12.2 us
    ppermute x1, waiting for transfers between devices, per_device(): lax.ppermute(bf(partial_for(jnp.clip(s_me + 1, 0, 3)) + near_r.astype(jnp...  11.9 us
    ppermute x1, waiting for transfers between devices, per_device(): far_r = lax.ppermute(bf(partial_for(jnp.int32(3))), 'seq', [(0, 3)])  9.11 us
    ppermute x1, waiting for transfers between devices, per_device(): lax.ppermute(bf(partial_for(jnp.clip(s_me + 2, 0, 3))), 'seq', [(0, 1), (...  8.8 us
    dot_general x7, matrix products, partial_for(): jnp.einsum('deti,deic->tc', rows, w_perm, preferred_element_type=jnp.floa...  6.88 us
  transfers between devices with their start and end apart: 15, of which 8 were waited for; matrix products, arithmetic and copies ran while one was open for 12% of the time, Pallas kernels for 0%

profile of v23, /device:TPU:0, one launch (start us, length us, event | category | flops | bytes accessed | tf_op | source)
XLA Modules:
  0.0 150.2 jit_solution(16647706844260604595)
XLA Ops:
  0.0 1.2 reduce-window.6
  1.8 1.0 fusion.77
  2.8 1.4 fusion.20
  5.3 1.8 %convolution_bitcast_fusion.8 = f32[1,8,128,128]{3,2,1,0:T(8,128)S(1)} fusion(bf16[256,8,128]{0,2,1:T(8,128)(2,1)} %bitcast.194, f32[256,8]{0,1:T(8,128)S(1)} %exponential_bitcast_fusion, bf16[256,1024]{1,0:T(8,128)(2,1)} %param.11, f32[1024]{0:T(1024)S(1)} %bitcast.206), kind=kOutput, calls=%fused_computation.43 | convolution fusion | flops 69730304 | bytes 1585152 | tf_op jit(solution)/shard_map/bjhd,bjhe->bhde/dot_general | solution.py:67
  8.2 4.9 %collective-permute-start = (bf16[8,16640]{1,0:T(8,128)(2,1)}, bf16[8,16640]{1,0:T(8,128)(2,1)S(1)}, u32[]{:S(2)}, u32[]{:S(2)}) collective-permute-start(bf16[8,16640]{1,0:T(8,128)(2,1)} %pad_maximum_fusion.3), channel_id=1, source_target_pairs={{0,4},{4,8},{8,12},{1,5},{5,9},{9,13},{2,6},{6,10},{10,14},{3,7},{... | collective-permute-start | bytes 798728 | tf_op jit(solution)/shard_map/ppermute | solution.py:107
  13.2 5.2 %collective-permute-start.1 = (bf16[8,16640]{1,0:T(8,128)(2,1)}, bf16[8,16640]{1,0:T(8,128)(2,1)}, u32[]{:S(2)}, u32[]{:S(2)}) collective-permute-start(bf16[8,16640]{1,0:T(8,128)(2,1)} %pad_maximum_fusion.3), channel_id=1, source_target_pairs={{0,8},{4,12},{1,9},{5,13},{2,10},{6,14},{3,11},{7,15},{16,24},{20,... | collective-permute-start | bytes 798728 | tf_op jit(solution)/shard_map/ppermute | solution.py:107
  18.4 2.0 %collective-permute-start.2 = (bf16[8,16640]{1,0:T(8,128)(2,1)}, bf16[8,16640]{1,0:T(8,128)(2,1)}, u32[]{:S(2)}, u32[]{:S(2)}) collective-permute-start(bf16[8,16640]{1,0:T(8,128)(2,1)} %pad_maximum_fusion.3), channel_id=1, source_target_pairs={{0,12},{1,13},{2,14},{3,15},{16,28},{17,29},{18,30},{19,31}} | collective-permute-start | bytes 798728 | tf_op jit(solution)/shard_map/ppermute | solution.py:107
  20.8 2.7 %multiply_convert_fusion = bf16[1024,1536]{1,0:T(8,128)(2,1)} fusion(bf16[1024,1536]{1,0:T(8,128)(2,1)S(1)} %copy-done.1, f32[1536]{0:T(1024)S(1)} %select_add_fusion), kind=kLoop, calls=%fused_computation.2 | loop fusion | flops 11010048 | bytes 6297600 | tf_op jit(solution)/shard_map/convert_element_type | solution.py:20
  23.5 3.8 %fusion.10 = f32[1,256,8,128]{1,3,2,0:T(8,128)} fusion(bf16[256,8,128]{0,2,1:T(8,128)(2,1)} %bitcast.195, f32[8,256]{1,0:T(8,128)S(1)} %bitcast_add_fusion.2, pred[256,256]{1,0:T(8,128)(4,1)S(1)} %iota_compare_fusion, bf16[256,1024]{1,0:T(8,128)(2,1)} %param.9, f32[1024]{0:T(1024)S(1)} %bitcast.204, bf16[256,1024]{1,0:T(8,128)(2,1)} %param.11, ...), kind=kOutput, calls=%fused_computation.35 | convolution fusion | flops 276299776 | bytes 2703360 | tf_op jit(solution)/shard_map/hbij,bjhd->bihd/dot_general | solution.py:62
  27.3 2.6 %gather_fusion = bf16[4,256,1536]{2,1,0:T(8,128)(2,1)S(1)} fusion(bf16[4,256,1536]{2,1,0:T(8,128)(2,1)} %bitcast.192, s32[1024]{0:T(1024)S(1)} %pad_clamp_fusion.1), kind=kCustom, calls=%fused_computation | custom fusion | bytes 6291472 | tf_op jit(solution)/shard_map/jit(_take)/gather | solution.py:99
  32.2 2.0 %add_bitcast_fusion = f32[8,128,128]{2,0,1:T(8,128)} fusion(bf16[8,16640]{1,0:T(8,128)(2,1)} %collective-permute-done.2, bf16[8,16640]{1,0:T(8,128)(2,1)} %collective-permute-done.1, bf16[8,16640]{1,0:T(8,128)(2,1)S(1)} %collective-permute-done, f32[8]{0:T(128)S(1)} %get-tuple-element.14, f32[8]{0:T(128)S(1)} %get-tuple-element.13, f32[]{:T(128)} %bitcast.19, ...), kind=kLoop, calls=%fused_computation.91 | loop fusion | flops 1179648 | bytes 1310792 | tf_op jit(solution)/shard_map/broadcast_in_dim;reshape | solution.py:121
  34.2 2.1 %copy.62 = f32[8,128,128]{1,2,0:T(8,128)} copy(f32[8,128,128]{2,0,1:T(8,128)} %add_bitcast_fusion) | data formatting | bytes 1048576 | tf_op jit(solution)/shard_map/broadcast_in_dim;reshape | solution.py:121
  36.3 2.6 %multiply_reduce_fusion = (f32[256,8]{0,1:T(8,128)S(1)}, f32[1,256,8,128]{1,3,2,0:T(8,128)S(1)}) fusion(f32[1,256,8,128]{1,3,2,0:T(8,128)} %fusion.10, f32[8,128,128]{1,2,0:T(8,128)} %copy.62, f32[8]{0:T(128)S(1)} %get-tuple-element.35, f32[256,8]{0,1:T(8,128)S(1)} %get-tuple-element.24, bf16[256,1024]{1,0:T(8,128)(2,1)} %param.9, f32[1024]{0:T(1024)S(1)} %bitcast.205), kind=kOutput, calls=%fused_computation.54 | convolution fusion | flops 407238656 | bytes 3166240 | tf_op jit(solution)/shard_map/bihd,bhde->bihe/dot_general | solution.py:122
  41.0 7.9 %collective-permute-start.4 = (bf16[256,256]{1,0:T(8,128)(2,1)S(1)}, bf16[256,256]{1,0:T(8,128)(2,1)S(1)}, u32[]{:S(2)}, u32[]{:S(2)}) collective-permute-start(bf16[256,256]{1,0:T(8,128)(2,1)S(1)} %get-tuple-element.31), channel_id=1, source_target_pairs={{0,1},{1,5},{2,9},{3,13},{4,2},{5,6},{6,10},{7,14},{8,3},{9,7},{10... | collective-permute-start | bytes 393224 | tf_op jit(solution)/shard_map/ppermute | solution.py:172
  48.8 3.5 %collective-permute-start.5 = (bf16[256,256]{1,0:T(8,128)(2,1)S(1)}, bf16[256,256]{1,0:T(8,128)(2,1)S(1)}, u32[]{:S(2)}, u32[]{:S(2)}) collective-permute-start(bf16[256,256]{1,0:T(8,128)(2,1)S(1)} %get-tuple-element.30), channel_id=1, source_target_pairs={{0,2},{1,6},{2,10},{3,14},{4,3},{5,7},{6,11},{7,15},{8,0},{9,4},{1... | collective-permute-start | bytes 393224 | tf_op jit(solution)/shard_map/ppermute | solution.py:172
  52.9 5.9 %collective-permute-done.4 = bf16[256,256]{1,0:T(8,128)(2,1)S(1)} collective-permute-done((bf16[256,256]{1,0:T(8,128)(2,1)S(1)}, bf16[256,256]{1,0:T(8,128)(2,1)S(1)}, u32[]{:S(2)}, u32[]{:S(2)}) %collective-permute-start.4) | collective-permute-done | bytes 131104 | tf_op jit(solution)/shard_map/ppermute | solution.py:172
  58.8 9.6 %collective-permute-done.5 = bf16[256,256]{1,0:T(8,128)(2,1)S(1)} collective-permute-done((bf16[256,256]{1,0:T(8,128)(2,1)S(1)}, bf16[256,256]{1,0:T(8,128)(2,1)S(1)}, u32[]{:S(2)}, u32[]{:S(2)}) %collective-permute-start.5) | collective-permute-done | bytes 131104 | tf_op jit(solution)/shard_map/ppermute | solution.py:172
  69.5 12.9 %collective-permute-done.7 = bf16[4,256,256]{2,1,0:T(8,128)(2,1)S(1)} collective-permute-done((bf16[4,256,256]{2,1,0:T(8,128)(2,1)S(1)}, bf16[4,256,256]{2,1,0:T(8,128)(2,1)S(1)}, u32[]{:S(2)}, u32[]{:S(2)}) %collective-permute-start.7) | collective-permute-done | bytes 524320 | tf_op jit(solution)/shard_map/ppermute | solution.py:183
  82.6 1.6 %collective-permute-start.8 = (bf16[2,4,256,256]{3,2,0,1:T(8,128)(2,1)S(1)}, bf16[2,4,256,256]{3,2,0,1:T(8,128)(2,1)S(1)}, u32[]{:S(2)}, u32[]{:S(2)}) collective-permute-start(bf16[2,4,256,256]{3,2,0,1:T(8,128)(2,1)S(1)} %get-tuple-element.27), channel_id=1, source_target_pairs={{0,1},{1,0},{2,3},{3,2},{4,5},{5,4},{6,7},{7,6},{8,9},{9,8},{10,11... | collective-permute-start | bytes 3145736 | tf_op jit(solution)/shard_map/ppermute | solution.py:185
  84.2 2.3 %broadcast_select_fusion = bf16[4,256,1536]{2,1,0:T(8,128)(2,1)S(1)} fusion(bf16[4,256,1536]{2,1,0:T(8,128)(2,1)} %copy-done, pred[4]{0:T(512)(128)(4,1)S(1)} %get-tuple-element.40), kind=kLoop, calls=%fused_computation.15 | loop fusion | flops 1572864 | bytes 6291460 | tf_op jit(solution)/shard_map/jit(_take)/select_n | solution.py:99
  88.4 5.4 %collective-permute-start.9 = (bf16[256,1536]{1,0:T(8,128)(2,1)S(1)}, bf16[256,1536]{1,0:T(8,128)(2,1)S(1)}, u32[]{:S(2)}, u32[]{:S(2)}) collective-permute-start(bf16[256,1536]{1,0:T(8,128)(2,1)S(1)} %fusion.5), channel_id=1, source_target_pairs={{0,4},{4,8},{1,5},{5,9},{2,6},{6,10},{3,7},{7,11},{16,20},{20,24},... | collective-permute-start | bytes 2359304 | tf_op jit(solution)/shard_map/ppermute | solution.py:198
  96.5 3.9 %collective-permute-start.11 = (bf16[256,1536]{1,0:T(8,128)(2,1)S(1)}, bf16[256,1536]{1,0:T(8,128)(2,1)S(1)}, u32[]{:S(2)}, u32[]{:S(2)}) collective-permute-start(bf16[256,1536]{1,0:T(8,128)(2,1)S(1)} %fusion.6), channel_id=1, source_target_pairs={{0,12},{1,13},{2,14},{3,15},{16,28},{17,29},{18,30},{19,31}} | collective-permute-start | bytes 2359304 | tf_op jit(solution)/shard_map/ppermute | solution.py:201
  100.4 1.5 collective-permute-start.14
  102.9 8.8 %collective-permute-done.9 = bf16[256,1536]{1,0:T(8,128)(2,1)S(1)} collective-permute-done((bf16[256,1536]{1,0:T(8,128)(2,1)S(1)}, bf16[256,1536]{1,0:T(8,128)(2,1)S(1)}, u32[]{:S(2)}, u32[]{:S(2)}) %collective-permute-start.9) | collective-permute-done | bytes 786464 | tf_op jit(solution)/shard_map/ppermute | solution.py:198
  111.7 1.0 fusion.4
  112.7 4.4 %collective-permute-start.10 = (bf16[256,1536]{1,0:T(8,128)(2,1)S(1)}, bf16[256,1536]{1,0:T(8,128)(2,1)S(1)}, u32[]{:S(2)}, u32[]{:S(2)}) collective-permute-start(bf16[256,1536]{1,0:T(8,128)(2,1)S(1)} %fusion.4), channel_id=1, source_target_pairs={{0,4},{4,8},{8,12},{1,5},{5,9},{9,13},{2,6},{6,10},{10,14},{3,7},{... | collective-permute-start | bytes 2359304 | tf_op jit(solution)/shard_map/ppermute | solution.py:207
  118.2 1.3 collective-permute-start.13
  119.5 9.1 %collective-permute-done.11 = bf16[256,1536]{1,0:T(8,128)(2,1)S(1)} collective-permute-done((bf16[256,1536]{1,0:T(8,128)(2,1)S(1)}, bf16[256,1536]{1,0:T(8,128)(2,1)S(1)}, u32[]{:S(2)}, u32[]{:S(2)}) %collective-permute-start.11) | collective-permute-done | bytes 786464 | tf_op jit(solution)/shard_map/ppermute | solution.py:201
  128.6 4.1 %collective-permute-done.14 = bf16[256,1536]{1,0:T(8,128)(2,1)S(1)} collective-permute-done((bf16[256,1536]{1,0:T(8,128)(2,1)S(1)}, bf16[256,1536]{1,0:T(8,128)(2,1)S(1)}, u32[]{:S(2)}, u32[]{:S(2)}) %collective-permute-start.14) | collective-permute-done | bytes 786464 | tf_op jit(solution)/shard_map/ppermute | solution.py:205
  132.7 11.9 %collective-permute-done.10 = bf16[256,1536]{1,0:T(8,128)(2,1)S(1)} collective-permute-done((bf16[256,1536]{1,0:T(8,128)(2,1)S(1)}, bf16[256,1536]{1,0:T(8,128)(2,1)S(1)}, u32[]{:S(2)}, u32[]{:S(2)}) %collective-permute-start.10) | collective-permute-done | bytes 786464 | tf_op jit(solution)/shard_map/ppermute | solution.py:207
  144.6 4.1 %collective-permute-done.13 = bf16[256,1536]{1,0:T(8,128)(2,1)S(1)} collective-permute-done((bf16[256,1536]{1,0:T(8,128)(2,1)S(1)}, bf16[256,1536]{1,0:T(8,128)(2,1)S(1)}, u32[]{:S(2)}, u32[]{:S(2)}) %collective-permute-start.13) | collective-permute-done | bytes 786464 | tf_op jit(solution)/shard_map/ppermute | solution.py:216
  148.8 1.4 add_convert_fusion
  (65 shorter events, 14.9 us)
Async XLA Ops:
  5.3 15.5 %copy-start.3 = (s32[1536]{0:T(1024)S(1)}, s32[1536]{0:T(1024)}, u32[]{:S(2)}) copy-start(s32[1536]{0:T(1024)} %param.17) | copy-start | bytes 18436
  5.3 15.5 %copy-start.1 = (bf16[1024,1536]{1,0:T(8,128)(2,1)S(1)}, bf16[1024,1536]{1,0:T(8,128)(2,1)}, u32[]{:S(2)}) copy-start(bf16[1024,1536]{1,0:T(8,128)(2,1)} %param.16) | copy-start | bytes 9437188
  8.2 23.1 %collective-permute-start = (bf16[8,16640]{1,0:T(8,128)(2,1)}, bf16[8,16640]{1,0:T(8,128)(2,1)S(1)}, u32[]{:S(2)}, u32[]{:S(2)}) collective-permute-start(bf16[8,16640]{1,0:T(8,128)(2,1)} %pad_maximum_fusion.3), channel_id=1, source_target_pairs={{0,4},{4,8},{8,12},{1,5},{5,9},{9,13},{2,6},{6,10},{10,14},{3,7},{... | collective-permute-start | bytes 798728 | tf_op jit(solution)/shard_map/ppermute | solution.py:107
  13.2 18.2 %collective-permute-start.1 = (bf16[8,16640]{1,0:T(8,128)(2,1)}, bf16[8,16640]{1,0:T(8,128)(2,1)}, u32[]{:S(2)}, u32[]{:S(2)}) collective-permute-start(bf16[8,16640]{1,0:T(8,128)(2,1)} %pad_maximum_fusion.3), channel_id=1, source_target_pairs={{0,8},{4,12},{1,9},{5,13},{2,10},{6,14},{3,11},{7,15},{16,24},{20,... | collective-permute-start | bytes 798728 | tf_op jit(solution)/shard_map/ppermute | solution.py:107
  18.4 13.8 %collective-permute-start.2 = (bf16[8,16640]{1,0:T(8,128)(2,1)}, bf16[8,16640]{1,0:T(8,128)(2,1)}, u32[]{:S(2)}, u32[]{:S(2)}) collective-permute-start(bf16[8,16640]{1,0:T(8,128)(2,1)} %pad_maximum_fusion.3), channel_id=1, source_target_pairs={{0,12},{1,13},{2,14},{3,15},{16,28},{17,29},{18,30},{19,31}} | collective-permute-start | bytes 798728 | tf_op jit(solution)/shard_map/ppermute | solution.py:107
  30.0 8.9 %copy-start = (bf16[4,256,1536]{2,1,0:T(8,128)(2,1)}, bf16[4,256,1536]{2,1,0:T(8,128)(2,1)S(1)}, u32[]{:S(2)}) copy-start(bf16[4,256,1536]{2,1,0:T(8,128)(2,1)S(1)} %gather_fusion) | copy-start | bytes 9437188
  38.8 1.0 copy-start.2
  38.9 1.0 copy-start.4
  40.3 12.6 %collective-permute-start.3 = (bf16[256,256]{1,0:T(8,128)(2,1)S(1)}, bf16[256,256]{1,0:T(8,128)(2,1)S(1)}, u32[]{:S(2)}, u32[]{:S(2)}) collective-permute-start(bf16[256,256]{1,0:T(8,128)(2,1)S(1)} %get-tuple-element.28), channel_id=1, source_target_pairs={{0,0},{1,4},{2,8},{3,12},{4,1},{5,5},{6,9},{7,13},{8,2},{9,6},{10,... | collective-permute-start | bytes 393224 | tf_op jit(solution)/shard_map/ppermute | solution.py:172
  41.0 17.9 %collective-permute-start.4 = (bf16[256,256]{1,0:T(8,128)(2,1)S(1)}, bf16[256,256]{1,0:T(8,128)(2,1)S(1)}, u32[]{:S(2)}, u32[]{:S(2)}) collective-permute-start(bf16[256,256]{1,0:T(8,128)(2,1)S(1)} %get-tuple-element.31), channel_id=1, source_target_pairs={{0,1},{1,5},{2,9},{3,13},{4,2},{5,6},{6,10},{7,14},{8,3},{9,7},{10... | collective-permute-start | bytes 393224 | tf_op jit(solution)/shard_map/ppermute | solution.py:172
  48.8 19.6 %collective-permute-start.5 = (bf16[256,256]{1,0:T(8,128)(2,1)S(1)}, bf16[256,256]{1,0:T(8,128)(2,1)S(1)}, u32[]{:S(2)}, u32[]{:S(2)}) collective-permute-start(bf16[256,256]{1,0:T(8,128)(2,1)S(1)} %get-tuple-element.30), channel_id=1, source_target_pairs={{0,2},{1,6},{2,10},{3,14},{4,3},{5,7},{6,11},{7,15},{8,0},{9,4},{1... | collective-permute-start | bytes 393224 | tf_op jit(solution)/shard_map/ppermute | solution.py:172
  52.3 16.2 %collective-permute-start.6 = (bf16[256,256]{1,0:T(8,128)(2,1)S(1)}, bf16[256,256]{1,0:T(8,128)(2,1)S(1)}, u32[]{:S(2)}, u32[]{:S(2)}) collective-permute-start(bf16[256,256]{1,0:T(8,128)(2,1)S(1)} %get-tuple-element.29), channel_id=1, source_target_pairs={{0,3},{1,7},{2,11},{3,15},{4,0},{5,4},{6,8},{7,12},{8,1},{9,5},{10... | collective-permute-start | bytes 393224 | tf_op jit(solution)/shard_map/ppermute | solution.py:172
  69.3 13.1 %collective-permute-start.7 = (bf16[4,256,256]{2,1,0:T(8,128)(2,1)S(1)}, bf16[4,256,256]{2,1,0:T(8,128)(2,1)S(1)}, u32[]{:S(2)}, u32[]{:S(2)}) collective-permute-start(bf16[4,256,256]{2,1,0:T(8,128)(2,1)S(1)} %broadcast_select_fusion.1), channel_id=1, source_target_pairs={{0,2},{1,3},{2,0},{3,1},{4,6},{5,7},{6,4},{7,5},{8,10},{9,11},{10,... | collective-permute-start | bytes 1572872 | tf_op jit(solution)/shard_map/ppermute | solution.py:183
  82.6 3.9 %collective-permute-start.8 = (bf16[2,4,256,256]{3,2,0,1:T(8,128)(2,1)S(1)}, bf16[2,4,256,256]{3,2,0,1:T(8,128)(2,1)S(1)}, u32[]{:S(2)}, u32[]{:S(2)}) collective-permute-start(bf16[2,4,256,256]{3,2,0,1:T(8,128)(2,1)S(1)} %get-tuple-element.27), channel_id=1, source_target_pairs={{0,1},{1,0},{2,3},{3,2},{4,5},{5,4},{6,7},{7,6},{8,9},{9,8},{10,11... | collective-permute-start | bytes 3145736 | tf_op jit(solution)/shard_map/ppermute | solution.py:185
  88.4 23.3 %collective-permute-start.9 = (bf16[256,1536]{1,0:T(8,128)(2,1)S(1)}, bf16[256,1536]{1,0:T(8,128)(2,1)S(1)}, u32[]{:S(2)}, u32[]{:S(2)}) collective-permute-start(bf16[256,1536]{1,0:T(8,128)(2,1)S(1)} %fusion.5), channel_id=1, source_target_pairs={{0,4},{4,8},{1,5},{5,9},{2,6},{6,10},{3,7},{7,11},{16,20},{20,24},... | collective-permute-start | bytes 2359304 | tf_op jit(solution)/shard_map/ppermute | solution.py:198
  94.8 22.3 %collective-permute-start.12 = (bf16[256,1536]{1,0:T(8,128)(2,1)S(1)}, bf16[256,1536]{1,0:T(8,128)(2,1)S(1)}, u32[]{:S(2)}, u32[]{:S(2)}) collective-permute-start(bf16[256,1536]{1,0:T(8,128)(2,1)S(1)} %fusion.7), channel_id=1, source_target_pairs={{12,8},{8,4},{13,9},{9,5},{14,10},{10,6},{15,11},{11,7},{28,24},{2... | collective-permute-start | bytes 2359304 | tf_op jit(solution)/shard_map/ppermute | solution.py:202
  96.5 32.0 %collective-permute-start.11 = (bf16[256,1536]{1,0:T(8,128)(2,1)S(1)}, bf16[256,1536]{1,0:T(8,128)(2,1)S(1)}, u32[]{:S(2)}, u32[]{:S(2)}) collective-permute-start(bf16[256,1536]{1,0:T(8,128)(2,1)S(1)} %fusion.6), channel_id=1, source_target_pairs={{0,12},{1,13},{2,14},{3,15},{16,28},{17,29},{18,30},{19,31}} | collective-permute-start | bytes 2359304 | tf_op jit(solution)/shard_map/ppermute | solution.py:201
  100.4 32.3 %collective-permute-start.14 = (bf16[256,1536]{1,0:T(8,128)(2,1)S(1)}, bf16[256,1536]{1,0:T(8,128)(2,1)S(1)}, u32[]{:S(2)}, u32[]{:S(2)}) collective-permute-start(bf16[256,1536]{1,0:T(8,128)(2,1)S(1)} %fusion.8), channel_id=1, source_target_pairs={{12,0},{13,1},{14,2},{15,3},{28,16},{29,17},{30,18},{31,19}} | collective-permute-start | bytes 2359304 | tf_op jit(solution)/shard_map/ppermute | solution.py:205
  112.7 31.9 %collective-permute-start.10 = (bf16[256,1536]{1,0:T(8,128)(2,1)S(1)}, bf16[256,1536]{1,0:T(8,128)(2,1)S(1)}, u32[]{:S(2)}, u32[]{:S(2)}) collective-permute-start(bf16[256,1536]{1,0:T(8,128)(2,1)S(1)} %fusion.4), channel_id=1, source_target_pairs={{0,4},{4,8},{8,12},{1,5},{5,9},{9,13},{2,6},{6,10},{10,14},{3,7},{... | collective-permute-start | bytes 2359304 | tf_op jit(solution)/shard_map/ppermute | solution.py:207
  118.2 30.6 %collective-permute-start.13 = (bf16[256,1536]{1,0:T(8,128)(2,1)S(1)}, bf16[256,1536]{1,0:T(8,128)(2,1)S(1)}, u32[]{:S(2)}, u32[]{:S(2)}) collective-permute-start(bf16[256,1536]{1,0:T(8,128)(2,1)S(1)} %fusion.3), channel_id=1, source_target_pairs={{12,8},{8,4},{4,0},{13,9},{9,5},{5,1},{14,10},{10,6},{6,2},{15,11}... | collective-permute-start | bytes 2359304 | tf_op jit(solution)/shard_map/ppermute | solution.py:216

commit v24 on v22

--- a/solution.py
+++ b/solution.py
@@ -113,7 +113,7 @@
         )
         weight = jnp.where(d <= position, jnp.exp(jnp.minimum(gap, 0.0)), 0.0)
         incoming = incoming + weight[:, None] * came_state
-        if d == 1:
+        if d == n_seq - 1:
             incoming = incoming + w_perm[0, 0, 0, 0].astype(jnp.float32) * 0.0
         gap = gap + came_log
     incoming = incoming.reshape(heads_here, HDIM, HDIM)

time: 148 us -> 148 us (level)
  no operation moved by 1% of the time
where the time goes in v24:
time: 148 us; the launch traced here: 147 us
  waiting for transfers between devices  64.8 us (44%)
  starting transfers between devices  38.5 us (26%)
  other arithmetic  18 us (12%)
  local copies, waits for them, and re-layouts  13.4 us (9%)
  matrix products  11.2 us (8%)
    ppermute x1, waiting for transfers between devices, per_device(): got.append(lax.ppermute(x, 'mdl', perm))  13 us
    ppermute x3, starting transfers between devices, per_device(): lax.ppermute(packed, 'seq', [(z, z + d) for z in range(n_seq - d)])  12.1 us
    ppermute x1, waiting for transfers between devices, per_device(): lax.ppermute(bf(partial_for(jnp.clip(s_me + 1, 0, 3)) + near_r.astype(jnp...  10.8 us
    ppermute x1, waiting for transfers between devices, per_device(): far_r = lax.ppermute(bf(partial_for(jnp.int32(3))), 'seq', [(0, 3)])  9.16 us
    unnamed x22, local copies, waits for them, and re-layouts  8.48 us
    ppermute x4, waiting for transfers between devices, per_device(): received.append(lax.ppermute(item, ('seq', 'mdl'), perm))  7.75 us
    ppermute x1, waiting for transfers between devices, per_device(): lax.ppermute(bf(partial_for(jnp.clip(s_me + 2, 0, 3))), 'seq', [(0, 1), (...  7.36 us
    ppermute x4, starting transfers between devices, per_device(): received.append(lax.ppermute(item, ('seq', 'mdl'), perm))  7.19 us
  transfers between devices with their start and end apart: 16, of which 9 were waited for; matrix products, arithmetic and copies ran while one was open for 17% of the time, Pallas kernels for 0%

profile of v24, /device:TPU:0, one launch (start us, length us, event | category | flops | bytes accessed | tf_op | source)
XLA Modules:
  0.0 147.1 jit_solution(262699674738478232)
XLA Ops:
  0.0 1.2 reduce-window.6
  2.8 1.2 copy.66
  4.1 2.0 %copy.68 = bf16[256,1024]{0,1:T(8,128)(2,1)} copy(bf16[256,1024]{1,0:T(8,128)(2,1)} %param.10) | data formatting | bytes 1048576 | tf_op args[1]
  6.5 1.8 %fusion.20 = bf16[256,1024]{0,1:T(8,128)(2,1)S(1)} fusion(bf16[256,1024]{0,1:T(8,128)(2,1)} %copy.68, f32[1024]{0:T(1024)S(1)} %bitcast.200), kind=kLoop, calls=%fused_computation.51 | loop fusion | flops 3407872 | bytes 1052672 | tf_op jit(solution)/shard_map/convert_element_type | solution.py:52
  10.2 4.9 %collective-permute-start = (bf16[8,16640]{1,0:T(8,128)(2,1)}, bf16[8,16640]{1,0:T(8,128)(2,1)S(1)}, u32[]{:S(2)}, u32[]{:S(2)}) collective-permute-start(bf16[8,16640]{1,0:T(8,128)(2,1)} %pad_maximum_fusion.3), channel_id=1, source_target_pairs={{0,4},{4,8},{8,12},{1,5},{5,9},{9,13},{2,6},{6,10},{10,14},{3,7},{... | collective-permute-start | bytes 798728 | tf_op jit(solution)/shard_map/ppermute | solution.py:107
  15.2 5.2 %collective-permute-start.1 = (bf16[8,16640]{1,0:T(8,128)(2,1)}, bf16[8,16640]{1,0:T(8,128)(2,1)}, u32[]{:S(2)}, u32[]{:S(2)}) collective-permute-start(bf16[8,16640]{1,0:T(8,128)(2,1)} %pad_maximum_fusion.3), channel_id=1, source_target_pairs={{0,8},{4,12},{1,9},{5,13},{2,10},{6,14},{3,11},{7,15},{16,24},{20,... | collective-permute-start | bytes 798728 | tf_op jit(solution)/shard_map/ppermute | solution.py:107
  20.4 2.0 %collective-permute-start.2 = (bf16[8,16640]{1,0:T(8,128)(2,1)}, bf16[8,16640]{1,0:T(8,128)(2,1)}, u32[]{:S(2)}, u32[]{:S(2)}) collective-permute-start(bf16[8,16640]{1,0:T(8,128)(2,1)} %pad_maximum_fusion.3), channel_id=1, source_target_pairs={{0,12},{1,13},{2,14},{3,15},{16,28},{17,29},{18,30},{19,31}} | collective-permute-start | bytes 798728 | tf_op jit(solution)/shard_map/ppermute | solution.py:107
  22.8 2.7 %multiply_convert_fusion = bf16[1024,1536]{1,0:T(8,128)(2,1)} fusion(bf16[1024,1536]{1,0:T(8,128)(2,1)S(1)} %copy-done.1, f32[1536]{0:T(1024)S(1)} %select_add_fusion), kind=kLoop, calls=%fused_computation.2 | loop fusion | flops 11010048 | bytes 6297600 | tf_op jit(solution)/shard_map/convert_element_type | solution.py:20
  25.4 2.6 %gather_fusion = bf16[4,256,1536]{2,1,0:T(8,128)(2,1)S(1)} fusion(bf16[4,256,1536]{2,1,0:T(8,128)(2,1)} %bitcast.182, s32[1024]{0:T(1024)S(1)} %pad_clamp_fusion.1), kind=kCustom, calls=%fused_computation | custom fusion | bytes 6291472 | tf_op jit(solution)/shard_map/jit(_take)/gather | solution.py:99
  28.7 2.5 %copy.67 = bf16[256,1024]{0,1:T(8,128)(2,1)} copy(bf16[256,1024]{1,0:T(8,128)(2,1)} %param.9) | data formatting | bytes 1048576 | tf_op args[0]
  31.2 2.0 %copy.75 = bf16[256,1024]{0,1:T(8,128)(2,1)} copy(bf16[256,1024]{1,0:T(8,128)(2,1)} %param.12) | data formatting | bytes 1048576 | tf_op args[3]
  33.9 2.4 %fusion.16 = bf16[256,1024]{0,1:T(8,128)(2,1)} fusion(bf16[256,1024]{0,1:T(8,128)(2,1)} %copy.67, f32[1024]{0:T(1024)S(1)} %bitcast.199), kind=kLoop, calls=%fused_computation.47 | loop fusion | flops 3407872 | bytes 1052672 | tf_op jit(solution)/shard_map/convert_element_type | solution.py:47
  36.3 3.3 %fusion.10 = f32[1,256,8,128]{1,3,2,0:T(8,128)} fusion(bf16[256,8,128]{0,2,1:T(8,128)(2,1)} %bitcast.184, bf16[256,8,128]{0,2,1:T(8,128)(2,1)} %bitcast.188, bf16[256,8,128]{0,2,1:T(8,128)(2,1)} %bitcast.186, f32[8,256]{1,0:T(8,128)S(1)} %bitcast_add_fusion.2, pred[256,256]{1,0:T(8,128)(4,1)S(1)} %iota_compare_fusion), kind=kOutput, calls=%fused_computation.35 | convolution fusion | flops 271056896 | bytes 2695168 | tf_op jit(solution)/shard_map/hbij,bjhd->bihd/dot_general | solution.py:62
  43.5 1.6 %collective-permute-start.3 = (bf16[256,2,256]{0,2,1:T(8,128)(2,1)S(1)}, bf16[256,2,256]{0,2,1:T(8,128)(2,1)S(1)}, u32[]{:S(2)}, u32[]{:S(2)}) collective-permute-start(bf16[256,2,256]{0,2,1:T(8,128)(2,1)S(1)} %get-tuple-element.32), channel_id=1, source_target_pairs={{0,2},{1,3},{2,0},{3,1},{4,6},{5,7},{6,4},{7,5},{8,10},{9,11},{10,... | collective-permute-start | bytes 786440 | tf_op jit(solution)/shard_map/ppermute | solution.py:146
  45.1 5.9 %collective-permute-done.3 = bf16[256,2,256]{0,2,1:T(8,128)(2,1)S(1)} collective-permute-done((bf16[256,2,256]{0,2,1:T(8,128)(2,1)S(1)}, bf16[256,2,256]{0,2,1:T(8,128)(2,1)S(1)}, u32[]{:S(2)}, u32[]{:S(2)}) %collective-permute-start.3) | collective-permute-done | bytes 262176 | tf_op jit(solution)/shard_map/ppermute | solution.py:146
  53.4 5.3 %collective-permute-start.6 = (bf16[256,256]{1,0:T(8,128)(2,1)S(1)}, bf16[256,256]{1,0:T(8,128)(2,1)S(1)}, u32[]{:S(2)}, u32[]{:S(2)}) collective-permute-start(bf16[256,256]{1,0:T(8,128)(2,1)S(1)} %bitcast.193), channel_id=1, source_target_pairs={{0,8},{1,12},{2,2},{3,6},{4,9},{5,13},{6,3},{7,7},{8,0},{9,4},{10,... | collective-permute-start | bytes 393224 | tf_op jit(solution)/shard_map/ppermute | solution.py:157
  58.9 2.1 %collective-permute-done.5 = bf16[256,256]{1,0:T(8,128)(2,1)S(1)} collective-permute-done((bf16[256,256]{1,0:T(8,128)(2,1)S(1)}, bf16[256,256]{1,0:T(8,128)(2,1)S(1)}, u32[]{:S(2)}, u32[]{:S(2)}) %collective-permute-start.5) | collective-permute-done | bytes 131104 | tf_op jit(solution)/shard_map/ppermute | solution.py:157
  61.1 5.6 %collective-permute-done.6 = bf16[256,256]{1,0:T(8,128)(2,1)S(1)} collective-permute-done((bf16[256,256]{1,0:T(8,128)(2,1)S(1)}, bf16[256,256]{1,0:T(8,128)(2,1)S(1)}, u32[]{:S(2)}, u32[]{:S(2)}) %collective-permute-start.6) | collective-permute-done | bytes 131104 | tf_op jit(solution)/shard_map/ppermute | solution.py:157
  67.6 13.0 %collective-permute-done.8 = bf16[4,256,256]{2,1,0:T(8,128)(2,1)S(1)} collective-permute-done((bf16[4,256,256]{2,1,0:T(8,128)(2,1)S(1)}, bf16[4,256,256]{2,1,0:T(8,128)(2,1)S(1)}, u32[]{:S(2)}, u32[]{:S(2)}) %collective-permute-start.8) | collective-permute-done | bytes 524320 | tf_op jit(solution)/shard_map/ppermute | solution.py:183
  80.8 1.5 %collective-permute-start.9 = (bf16[2,4,256,256]{3,2,0,1:T(8,128)(2,1)S(1)}, bf16[2,4,256,256]{3,2,0,1:T(8,128)(2,1)S(1)}, u32[]{:S(2)}, u32[]{:S(2)}) collective-permute-start(bf16[2,4,256,256]{3,2,0,1:T(8,128)(2,1)S(1)} %get-tuple-element.27), channel_id=1, source_target_pairs={{0,1},{1,0},{2,3},{3,2},{4,5},{5,4},{6,7},{7,6},{8,9},{9,8},{10,11... | collective-permute-start | bytes 3145736 | tf_op jit(solution)/shard_map/ppermute | solution.py:185
  82.3 2.3 %broadcast_select_fusion = bf16[4,256,1536]{2,1,0:T(8,128)(2,1)S(1)} fusion(bf16[4,256,1536]{2,1,0:T(8,128)(2,1)} %copy-done, pred[4]{0:T(512)(128)(4,1)S(1)} %get-tuple-element.42), kind=kLoop, calls=%fused_computation.15 | loop fusion | flops 1572864 | bytes 6291460 | tf_op jit(solution)/shard_map/jit(_take)/select_n | solution.py:99
  86.6 2.8 %collective-permute-start.10 = (bf16[256,1536]{1,0:T(8,128)(2,1)S(1)}, bf16[256,1536]{1,0:T(8,128)(2,1)S(1)}, u32[]{:S(2)}, u32[]{:S(2)}) collective-permute-start(bf16[256,1536]{1,0:T(8,128)(2,1)S(1)} %fusion.5), channel_id=1, source_target_pairs={{0,4},{4,8},{1,5},{5,9},{2,6},{6,10},{3,7},{7,11},{16,20},{20,24},... | collective-permute-start | bytes 2359304 | tf_op jit(solution)/shard_map/ppermute | solution.py:198
  92.1 5.5 %collective-permute-start.12 = (bf16[256,1536]{1,0:T(8,128)(2,1)S(1)}, bf16[256,1536]{1,0:T(8,128)(2,1)S(1)}, u32[]{:S(2)}, u32[]{:S(2)}) collective-permute-start(bf16[256,1536]{1,0:T(8,128)(2,1)S(1)} %fusion.6), channel_id=1, source_target_pairs={{0,12},{1,13},{2,14},{3,15},{16,28},{17,29},{18,30},{19,31}} | collective-permute-start | bytes 2359304 | tf_op jit(solution)/shard_map/ppermute | solution.py:201
  97.6 1.3 collective-permute-start.15
  99.9 7.4 %collective-permute-done.10 = bf16[256,1536]{1,0:T(8,128)(2,1)S(1)} collective-permute-done((bf16[256,1536]{1,0:T(8,128)(2,1)S(1)}, bf16[256,1536]{1,0:T(8,128)(2,1)S(1)}, u32[]{:S(2)}, u32[]{:S(2)}) %collective-permute-start.10) | collective-permute-done | bytes 786464 | tf_op jit(solution)/shard_map/ppermute | solution.py:198
  108.3 4.4 %collective-permute-start.11 = (bf16[256,1536]{1,0:T(8,128)(2,1)S(1)}, bf16[256,1536]{1,0:T(8,128)(2,1)S(1)}, u32[]{:S(2)}, u32[]{:S(2)}) collective-permute-start(bf16[256,1536]{1,0:T(8,128)(2,1)S(1)} %fusion.4), channel_id=1, source_target_pairs={{0,4},{4,8},{8,12},{1,5},{5,9},{9,13},{2,6},{6,10},{10,14},{3,7},{... | collective-permute-start | bytes 2359304 | tf_op jit(solution)/shard_map/ppermute | solution.py:207
  113.7 1.3 collective-permute-start.14
  115.0 9.2 %collective-permute-done.12 = bf16[256,1536]{1,0:T(8,128)(2,1)S(1)} collective-permute-done((bf16[256,1536]{1,0:T(8,128)(2,1)S(1)}, bf16[256,1536]{1,0:T(8,128)(2,1)S(1)}, u32[]{:S(2)}, u32[]{:S(2)}) %collective-permute-start.12) | collective-permute-done | bytes 786464 | tf_op jit(solution)/shard_map/ppermute | solution.py:201
  124.2 5.5 %collective-permute-done.15 = bf16[256,1536]{1,0:T(8,128)(2,1)S(1)} collective-permute-done((bf16[256,1536]{1,0:T(8,128)(2,1)S(1)}, bf16[256,1536]{1,0:T(8,128)(2,1)S(1)}, u32[]{:S(2)}, u32[]{:S(2)}) %collective-permute-start.15) | collective-permute-done | bytes 786464 | tf_op jit(solution)/shard_map/ppermute | solution.py:205
  129.7 10.8 %collective-permute-done.11 = bf16[256,1536]{1,0:T(8,128)(2,1)S(1)} collective-permute-done((bf16[256,1536]{1,0:T(8,128)(2,1)S(1)}, bf16[256,1536]{1,0:T(8,128)(2,1)S(1)}, u32[]{:S(2)}, u32[]{:S(2)}) %collective-permute-start.11) | collective-permute-done | bytes 786464 | tf_op jit(solution)/shard_map/ppermute | solution.py:207
  140.5 5.3 %collective-permute-done.14 = bf16[256,1536]{1,0:T(8,128)(2,1)S(1)} collective-permute-done((bf16[256,1536]{1,0:T(8,128)(2,1)S(1)}, bf16[256,1536]{1,0:T(8,128)(2,1)S(1)}, u32[]{:S(2)}, u32[]{:S(2)}) %collective-permute-start.14) | collective-permute-done | bytes 786464 | tf_op jit(solution)/shard_map/ppermute | solution.py:216
  145.8 1.4 add_convert_fusion
  (84 shorter events, 20.0 us)
Async XLA Ops:
  6.4 1.8 %copy-start.2 = (bf16[256,1024]{0,1:T(8,128)(2,1)}, bf16[256,1024]{0,1:T(8,128)(2,1)S(1)}, u32[]{:S(2)}) copy-start(bf16[256,1024]{0,1:T(8,128)(2,1)S(1)} %multiply_convert_fusion.5) | copy-start | bytes 1572868
  6.4 16.3 %copy-start.7 = (s32[1536]{0:T(1024)S(1)}, s32[1536]{0:T(1024)}, u32[]{:S(2)}) copy-start(s32[1536]{0:T(1024)} %param.17) | copy-start | bytes 18436
  6.5 16.3 %copy-start.1 = (bf16[1024,1536]{1,0:T(8,128)(2,1)S(1)}, bf16[1024,1536]{1,0:T(8,128)(2,1)}, u32[]{:S(2)}) copy-start(bf16[1024,1536]{1,0:T(8,128)(2,1)} %param.16) | copy-start | bytes 9437188
  8.3 0.8 copy-start.3
  10.2 29.4 %collective-permute-start = (bf16[8,16640]{1,0:T(8,128)(2,1)}, bf16[8,16640]{1,0:T(8,128)(2,1)S(1)}, u32[]{:S(2)}, u32[]{:S(2)}) collective-permute-start(bf16[8,16640]{1,0:T(8,128)(2,1)} %pad_maximum_fusion.3), channel_id=1, source_target_pairs={{0,4},{4,8},{8,12},{1,5},{5,9},{9,13},{2,6},{6,10},{10,14},{3,7},{... | collective-permute-start | bytes 798728 | tf_op jit(solution)/shard_map/ppermute | solution.py:107
  15.2 24.4 %collective-permute-start.1 = (bf16[8,16640]{1,0:T(8,128)(2,1)}, bf16[8,16640]{1,0:T(8,128)(2,1)}, u32[]{:S(2)}, u32[]{:S(2)}) collective-permute-start(bf16[8,16640]{1,0:T(8,128)(2,1)} %pad_maximum_fusion.3), channel_id=1, source_target_pairs={{0,8},{4,12},{1,9},{5,13},{2,10},{6,14},{3,11},{7,15},{16,24},{20,... | collective-permute-start | bytes 798728 | tf_op jit(solution)/shard_map/ppermute | solution.py:107
  20.4 20.2 %collective-permute-start.2 = (bf16[8,16640]{1,0:T(8,128)(2,1)}, bf16[8,16640]{1,0:T(8,128)(2,1)}, u32[]{:S(2)}, u32[]{:S(2)}) collective-permute-start(bf16[8,16640]{1,0:T(8,128)(2,1)} %pad_maximum_fusion.3), channel_id=1, source_target_pairs={{0,12},{1,13},{2,14},{3,15},{16,28},{17,29},{18,30},{19,31}} | collective-permute-start | bytes 798728 | tf_op jit(solution)/shard_map/ppermute | solution.py:107
  28.1 11.5 %copy-start = (bf16[4,256,1536]{2,1,0:T(8,128)(2,1)}, bf16[4,256,1536]{2,1,0:T(8,128)(2,1)S(1)}, u32[]{:S(2)}) copy-start(bf16[4,256,1536]{2,1,0:T(8,128)(2,1)S(1)} %gather_fusion) | copy-start | bytes 9437188
  39.6 2.5 %copy-start.5 = (bf16[256,1024]{0,1:T(8,128)(2,1)S(1)}, bf16[256,1024]{0,1:T(8,128)(2,1)}, u32[]{:S(2)}) copy-start(bf16[256,1024]{0,1:T(8,128)(2,1)} %fusion.16) | copy-start | bytes 1572868
  39.6 2.5 %copy-start.6 = (f32[1,256,8,128]{1,3,2,0:T(8,128)S(1)}, f32[1,256,8,128]{1,3,2,0:T(8,128)}, u32[]{:S(2)}) copy-start(f32[1,256,8,128]{1,3,2,0:T(8,128)} %fusion.10) | copy-start | bytes 3145732
  42.1 1.0 copy-start.4
  42.1 1.0 copy-start.8
  43.5 7.6 %collective-permute-start.3 = (bf16[256,2,256]{0,2,1:T(8,128)(2,1)S(1)}, bf16[256,2,256]{0,2,1:T(8,128)(2,1)S(1)}, u32[]{:S(2)}, u32[]{:S(2)}) collective-permute-start(bf16[256,2,256]{0,2,1:T(8,128)(2,1)S(1)} %get-tuple-element.32), channel_id=1, source_target_pairs={{0,2},{1,3},{2,0},{3,1},{4,6},{5,7},{6,4},{7,5},{8,10},{9,11},{10,... | collective-permute-start | bytes 786440 | tf_op jit(solution)/shard_map/ppermute | solution.py:146
  51.3 7.6 %collective-permute-start.4 = (bf16[256,256]{1,0:T(8,128)(2,1)S(1)}, bf16[256,256]{1,0:T(8,128)(2,1)S(1)}, u32[]{:S(2)}, u32[]{:S(2)}) collective-permute-start(bf16[256,256]{1,0:T(8,128)(2,1)S(1)} %bitcast.191), channel_id=1, source_target_pairs={{0,0},{1,4},{2,10},{3,14},{4,1},{5,5},{6,11},{7,15},{8,8},{9,12},{... | collective-permute-start | bytes 393224 | tf_op jit(solution)/shard_map/ppermute | solution.py:157
  52.1 8.9 %collective-permute-start.5 = (bf16[256,256]{1,0:T(8,128)(2,1)S(1)}, bf16[256,256]{1,0:T(8,128)(2,1)S(1)}, u32[]{:S(2)}, u32[]{:S(2)}) collective-permute-start(bf16[256,256]{1,0:T(8,128)(2,1)S(1)} %bitcast.192), channel_id=1, source_target_pairs={{0,1},{1,5},{2,11},{3,15},{4,8},{5,12},{6,2},{7,6},{8,9},{9,13},{1... | collective-permute-start | bytes 393224 | tf_op jit(solution)/shard_map/ppermute | solution.py:157
  53.4 13.3 %collective-permute-start.6 = (bf16[256,256]{1,0:T(8,128)(2,1)S(1)}, bf16[256,256]{1,0:T(8,128)(2,1)S(1)}, u32[]{:S(2)}, u32[]{:S(2)}) collective-permute-start(bf16[256,256]{1,0:T(8,128)(2,1)S(1)} %bitcast.193), channel_id=1, source_target_pairs={{0,8},{1,12},{2,2},{3,6},{4,9},{5,13},{6,3},{7,7},{8,0},{9,4},{10,... | collective-permute-start | bytes 393224 | tf_op jit(solution)/shard_map/ppermute | solution.py:157
  58.8 7.9 %collective-permute-start.7 = (bf16[256,256]{1,0:T(8,128)(2,1)S(1)}, bf16[256,256]{1,0:T(8,128)(2,1)S(1)}, u32[]{:S(2)}, u32[]{:S(2)}) collective-permute-start(bf16[256,256]{1,0:T(8,128)(2,1)S(1)} %bitcast.194), channel_id=1, source_target_pairs={{0,9},{1,13},{2,3},{3,7},{4,0},{5,4},{6,10},{7,14},{8,1},{9,5},{10... | collective-permute-start | bytes 393224 | tf_op jit(solution)/shard_map/ppermute | solution.py:157
  67.4 13.2 %collective-permute-start.8 = (bf16[4,256,256]{2,1,0:T(8,128)(2,1)S(1)}, bf16[4,256,256]{2,1,0:T(8,128)(2,1)S(1)}, u32[]{:S(2)}, u32[]{:S(2)}) collective-permute-start(bf16[4,256,256]{2,1,0:T(8,128)(2,1)S(1)} %broadcast_select_fusion.1), channel_id=1, source_target_pairs={{0,2},{1,3},{2,0},{3,1},{4,6},{5,7},{6,4},{7,5},{8,10},{9,11},{10,... | collective-permute-start | bytes 1572872 | tf_op jit(solution)/shard_map/ppermute | solution.py:183
  80.8 3.8 %collective-permute-start.9 = (bf16[2,4,256,256]{3,2,0,1:T(8,128)(2,1)S(1)}, bf16[2,4,256,256]{3,2,0,1:T(8,128)(2,1)S(1)}, u32[]{:S(2)}, u32[]{:S(2)}) collective-permute-start(bf16[2,4,256,256]{3,2,0,1:T(8,128)(2,1)S(1)} %get-tuple-element.27), channel_id=1, source_target_pairs={{0,1},{1,0},{2,3},{3,2},{4,5},{5,4},{6,7},{7,6},{8,9},{9,8},{10,11... | collective-permute-start | bytes 3145736 | tf_op jit(solution)/shard_map/ppermute | solution.py:185
  86.6 20.6 %collective-permute-start.10 = (bf16[256,1536]{1,0:T(8,128)(2,1)S(1)}, bf16[256,1536]{1,0:T(8,128)(2,1)S(1)}, u32[]{:S(2)}, u32[]{:S(2)}) collective-permute-start(bf16[256,1536]{1,0:T(8,128)(2,1)S(1)} %fusion.5), channel_id=1, source_target_pairs={{0,4},{4,8},{1,5},{5,9},{2,6},{6,10},{3,7},{7,11},{16,20},{20,24},... | collective-permute-start | bytes 2359304 | tf_op jit(solution)/shard_map/ppermute | solution.py:198
  90.4 22.3 %collective-permute-start.13 = (bf16[256,1536]{1,0:T(8,128)(2,1)S(1)}, bf16[256,1536]{1,0:T(8,128)(2,1)S(1)}, u32[]{:S(2)}, u32[]{:S(2)}) collective-permute-start(bf16[256,1536]{1,0:T(8,128)(2,1)S(1)} %fusion.7), channel_id=1, source_target_pairs={{12,8},{8,4},{13,9},{9,5},{14,10},{10,6},{15,11},{11,7},{28,24},{2... | collective-permute-start | bytes 2359304 | tf_op jit(solution)/shard_map/ppermute | solution.py:202
  92.1 32.1 %collective-permute-start.12 = (bf16[256,1536]{1,0:T(8,128)(2,1)S(1)}, bf16[256,1536]{1,0:T(8,128)(2,1)S(1)}, u32[]{:S(2)}, u32[]{:S(2)}) collective-permute-start(bf16[256,1536]{1,0:T(8,128)(2,1)S(1)} %fusion.6), channel_id=1, source_target_pairs={{0,12},{1,13},{2,14},{3,15},{16,28},{17,29},{18,30},{19,31}} | collective-permute-start | bytes 2359304 | tf_op jit(solution)/shard_map/ppermute | solution.py:201
  97.6 32.1 %collective-permute-start.15 = (bf16[256,1536]{1,0:T(8,128)(2,1)S(1)}, bf16[256,1536]{1,0:T(8,128)(2,1)S(1)}, u32[]{:S(2)}, u32[]{:S(2)}) collective-permute-start(bf16[256,1536]{1,0:T(8,128)(2,1)S(1)} %fusion.8), channel_id=1, source_target_pairs={{12,0},{13,1},{14,2},{15,3},{28,16},{29,17},{30,18},{31,19}} | collective-permute-start | bytes 2359304 | tf_op jit(solution)/shard_map/ppermute | solution.py:205
  108.3 32.2 %collective-permute-start.11 = (bf16[256,1536]{1,0:T(8,128)(2,1)S(1)}, bf16[256,1536]{1,0:T(8,128)(2,1)S(1)}, u32[]{:S(2)}, u32[]{:S(2)}) collective-permute-start(bf16[256,1536]{1,0:T(8,128)(2,1)S(1)} %fusion.4), channel_id=1, source_target_pairs={{0,4},{4,8},{8,12},{1,5},{5,9},{9,13},{2,6},{6,10},{10,14},{3,7},{... | collective-permute-start | bytes 2359304 | tf_op jit(solution)/shard_map/ppermute | solution.py:207
  113.7 32.1 %collective-permute-start.14 = (bf16[256,1536]{1,0:T(8,128)(2,1)S(1)}, bf16[256,1536]{1,0:T(8,128)(2,1)S(1)}, u32[]{:S(2)}, u32[]{:S(2)}) collective-permute-start(bf16[256,1536]{1,0:T(8,128)(2,1)S(1)} %fusion.3), channel_id=1, source_target_pairs={{12,8},{8,4},{4,0},{13,9},{9,5},{5,1},{14,10},{10,6},{6,2},{15,11}... | collective-permute-start | bytes 2359304 | tf_op jit(solution)/shard_map/ppermute | solution.py:216

commit v25 on v22

--- a/solution.py
+++ b/solution.py
@@ -204,6 +204,11 @@
         )
         far_l = lax.ppermute(bf(partial_for(jnp.int32(0))), "seq", [(3, 0)])
         own_part = partial_for(s_me)
+        last_l = lax.ppermute(
+            bf(partial_for(jnp.clip(s_me - 1, 0, 3)) + near_l.astype(jnp.float32)),
+            "seq",
+            [(3, 2), (2, 1), (1, 0)],
+        )
         last_r = lax.ppermute(
             bf(
                 partial_for(jnp.clip(s_me + 1, 0, 3))
@@ -212,11 +217,6 @@
             ),
             "seq",
             [(0, 1), (1, 2), (2, 3)],
-        )
-        last_l = lax.ppermute(
-            bf(partial_for(jnp.clip(s_me - 1, 0, 3)) + near_l.astype(jnp.float32)),
-            "seq",
-            [(3, 2), (2, 1), (1, 0)],
         )
         total = own_part
         for came in (last_r, far_r, last_l, far_l):

time: 148 us -> 148 us (level)
  no operation moved by 1% of the time
where the time goes in v25:
time: 148 us; the launch traced here: 147 us
  waiting for transfers between devices  64.8 us (44%)
  starting transfers between devices  38.5 us (26%)
  other arithmetic  18 us (12%)
  local copies, waits for them, and re-layouts  13.4 us (9%)
  matrix products  11.2 us (8%)
    ppermute x1, waiting for transfers between devices, per_device(): got.append(lax.ppermute(x, 'mdl', perm))  13 us
    ppermute x3, starting transfers between devices, per_device(): lax.ppermute(packed, 'seq', [(z, z + d) for z in range(n_seq - d)])  12.1 us
    ppermute x1, waiting for transfers between devices, per_device(): lax.ppermute(bf(partial_for(jnp.clip(s_me + 1, 0, 3)) + near_r.astype(jnp...  10.8 us
    ppermute x1, waiting for transfers between devices, per_device(): far_r = lax.ppermute(bf(partial_for(jnp.int32(3))), 'seq', [(0, 3)])  9.16 us
    unnamed x22, local copies, waits for them, and re-layouts  8.48 us
    ppermute x4, waiting for transfers between devices, per_device(): received.append(lax.ppermute(item, ('seq', 'mdl'), perm))  7.75 us
    ppermute x1, waiting for transfers between devices, per_device(): lax.ppermute(bf(partial_for(jnp.clip(s_me + 2, 0, 3))), 'seq', [(0, 1), (...  7.36 us
    ppermute x4, starting transfers between devices, per_device(): received.append(lax.ppermute(item, ('seq', 'mdl'), perm))  7.19 us
  transfers between devices with their start and end apart: 16, of which 9 were waited for; matrix products, arithmetic and copies ran while one was open for 17% of the time, Pallas kernels for 0%

profile of v25, /device:TPU:0, one launch (start us, length us, event | category | flops | bytes accessed | tf_op | source)
XLA Modules:
  0.0 147.1 jit_solution(14933625494824646292)
XLA Ops:
  0.0 1.2 reduce-window.6
  2.8 1.2 copy.66
  4.1 2.0 %copy.68 = bf16[256,1024]{0,1:T(8,128)(2,1)} copy(bf16[256,1024]{1,0:T(8,128)(2,1)} %param.10) | data formatting | bytes 1048576 | tf_op args[1]
  6.5 1.8 %fusion.20 = bf16[256,1024]{0,1:T(8,128)(2,1)S(1)} fusion(bf16[256,1024]{0,1:T(8,128)(2,1)} %copy.68, f32[1024]{0:T(1024)S(1)} %bitcast.200), kind=kLoop, calls=%fused_computation.51 | loop fusion | flops 3407872 | bytes 1052672 | tf_op jit(solution)/shard_map/convert_element_type | solution.py:52
  10.2 4.9 %collective-permute-start = (bf16[8,16640]{1,0:T(8,128)(2,1)}, bf16[8,16640]{1,0:T(8,128)(2,1)S(1)}, u32[]{:S(2)}, u32[]{:S(2)}) collective-permute-start(bf16[8,16640]{1,0:T(8,128)(2,1)} %pad_maximum_fusion.3), channel_id=1, source_target_pairs={{0,4},{4,8},{8,12},{1,5},{5,9},{9,13},{2,6},{6,10},{10,14},{3,7},{... | collective-permute-start | bytes 798728 | tf_op jit(solution)/shard_map/ppermute | solution.py:107
  15.2 5.2 %collective-permute-start.1 = (bf16[8,16640]{1,0:T(8,128)(2,1)}, bf16[8,16640]{1,0:T(8,128)(2,1)}, u32[]{:S(2)}, u32[]{:S(2)}) collective-permute-start(bf16[8,16640]{1,0:T(8,128)(2,1)} %pad_maximum_fusion.3), channel_id=1, source_target_pairs={{0,8},{4,12},{1,9},{5,13},{2,10},{6,14},{3,11},{7,15},{16,24},{20,... | collective-permute-start | bytes 798728 | tf_op jit(solution)/shard_map/ppermute | solution.py:107
  20.4 2.0 %collective-permute-start.2 = (bf16[8,16640]{1,0:T(8,128)(2,1)}, bf16[8,16640]{1,0:T(8,128)(2,1)}, u32[]{:S(2)}, u32[]{:S(2)}) collective-permute-start(bf16[8,16640]{1,0:T(8,128)(2,1)} %pad_maximum_fusion.3), channel_id=1, source_target_pairs={{0,12},{1,13},{2,14},{3,15},{16,28},{17,29},{18,30},{19,31}} | collective-permute-start | bytes 798728 | tf_op jit(solution)/shard_map/ppermute | solution.py:107
  22.8 2.7 %multiply_convert_fusion = bf16[1024,1536]{1,0:T(8,128)(2,1)} fusion(bf16[1024,1536]{1,0:T(8,128)(2,1)S(1)} %copy-done.1, f32[1536]{0:T(1024)S(1)} %select_add_fusion), kind=kLoop, calls=%fused_computation.2 | loop fusion | flops 11010048 | bytes 6297600 | tf_op jit(solution)/shard_map/convert_element_type | solution.py:20
  25.4 2.6 %gather_fusion = bf16[4,256,1536]{2,1,0:T(8,128)(2,1)S(1)} fusion(bf16[4,256,1536]{2,1,0:T(8,128)(2,1)} %bitcast.182, s32[1024]{0:T(1024)S(1)} %pad_clamp_fusion.1), kind=kCustom, calls=%fused_computation | custom fusion | bytes 6291472 | tf_op jit(solution)/shard_map/jit(_take)/gather | solution.py:99
  28.7 2.5 %copy.67 = bf16[256,1024]{0,1:T(8,128)(2,1)} copy(bf16[256,1024]{1,0:T(8,128)(2,1)} %param.9) | data formatting | bytes 1048576 | tf_op args[0]
  31.2 2.0 %copy.75 = bf16[256,1024]{0,1:T(8,128)(2,1)} copy(bf16[256,1024]{1,0:T(8,128)(2,1)} %param.12) | data formatting | bytes 1048576 | tf_op args[3]
  33.9 2.4 %fusion.16 = bf16[256,1024]{0,1:T(8,128)(2,1)} fusion(bf16[256,1024]{0,1:T(8,128)(2,1)} %copy.67, f32[1024]{0:T(1024)S(1)} %bitcast.199), kind=kLoop, calls=%fused_computation.47 | loop fusion | flops 3407872 | bytes 1052672 | tf_op jit(solution)/shard_map/convert_element_type | solution.py:47
  36.3 3.3 %fusion.10 = f32[1,256,8,128]{1,3,2,0:T(8,128)} fusion(bf16[256,8,128]{0,2,1:T(8,128)(2,1)} %bitcast.184, bf16[256,8,128]{0,2,1:T(8,128)(2,1)} %bitcast.188, bf16[256,8,128]{0,2,1:T(8,128)(2,1)} %bitcast.186, f32[8,256]{1,0:T(8,128)S(1)} %bitcast_add_fusion.2, pred[256,256]{1,0:T(8,128)(4,1)S(1)} %iota_compare_fusion), kind=kOutput, calls=%fused_computation.35 | convolution fusion | flops 271056896 | bytes 2695168 | tf_op jit(solution)/shard_map/hbij,bjhd->bihd/dot_general | solution.py:62
  43.5 1.6 %collective-permute-start.3 = (bf16[256,2,256]{0,2,1:T(8,128)(2,1)S(1)}, bf16[256,2,256]{0,2,1:T(8,128)(2,1)S(1)}, u32[]{:S(2)}, u32[]{:S(2)}) collective-permute-start(bf16[256,2,256]{0,2,1:T(8,128)(2,1)S(1)} %get-tuple-element.32), channel_id=1, source_target_pairs={{0,2},{1,3},{2,0},{3,1},{4,6},{5,7},{6,4},{7,5},{8,10},{9,11},{10,... | collective-permute-start | bytes 786440 | tf_op jit(solution)/shard_map/ppermute | solution.py:146
  45.1 5.9 %collective-permute-done.3 = bf16[256,2,256]{0,2,1:T(8,128)(2,1)S(1)} collective-permute-done((bf16[256,2,256]{0,2,1:T(8,128)(2,1)S(1)}, bf16[256,2,256]{0,2,1:T(8,128)(2,1)S(1)}, u32[]{:S(2)}, u32[]{:S(2)}) %collective-permute-start.3) | collective-permute-done | bytes 262176 | tf_op jit(solution)/shard_map/ppermute | solution.py:146
  53.4 5.3 %collective-permute-start.6 = (bf16[256,256]{1,0:T(8,128)(2,1)S(1)}, bf16[256,256]{1,0:T(8,128)(2,1)S(1)}, u32[]{:S(2)}, u32[]{:S(2)}) collective-permute-start(bf16[256,256]{1,0:T(8,128)(2,1)S(1)} %bitcast.193), channel_id=1, source_target_pairs={{0,8},{1,12},{2,2},{3,6},{4,9},{5,13},{6,3},{7,7},{8,0},{9,4},{10,... | collective-permute-start | bytes 393224 | tf_op jit(solution)/shard_map/ppermute | solution.py:157
  58.9 2.1 %collective-permute-done.5 = bf16[256,256]{1,0:T(8,128)(2,1)S(1)} collective-permute-done((bf16[256,256]{1,0:T(8,128)(2,1)S(1)}, bf16[256,256]{1,0:T(8,128)(2,1)S(1)}, u32[]{:S(2)}, u32[]{:S(2)}) %collective-permute-start.5) | collective-permute-done | bytes 131104 | tf_op jit(solution)/shard_map/ppermute | solution.py:157
  61.0 5.6 %collective-permute-done.6 = bf16[256,256]{1,0:T(8,128)(2,1)S(1)} collective-permute-done((bf16[256,256]{1,0:T(8,128)(2,1)S(1)}, bf16[256,256]{1,0:T(8,128)(2,1)S(1)}, u32[]{:S(2)}, u32[]{:S(2)}) %collective-permute-start.6) | collective-permute-done | bytes 131104 | tf_op jit(solution)/shard_map/ppermute | solution.py:157
  67.6 13.0 %collective-permute-done.8 = bf16[4,256,256]{2,1,0:T(8,128)(2,1)S(1)} collective-permute-done((bf16[4,256,256]{2,1,0:T(8,128)(2,1)S(1)}, bf16[4,256,256]{2,1,0:T(8,128)(2,1)S(1)}, u32[]{:S(2)}, u32[]{:S(2)}) %collective-permute-start.8) | collective-permute-done | bytes 524320 | tf_op jit(solution)/shard_map/ppermute | solution.py:183
  80.8 1.5 %collective-permute-start.9 = (bf16[2,4,256,256]{3,2,0,1:T(8,128)(2,1)S(1)}, bf16[2,4,256,256]{3,2,0,1:T(8,128)(2,1)S(1)}, u32[]{:S(2)}, u32[]{:S(2)}) collective-permute-start(bf16[2,4,256,256]{3,2,0,1:T(8,128)(2,1)S(1)} %get-tuple-element.27), channel_id=1, source_target_pairs={{0,1},{1,0},{2,3},{3,2},{4,5},{5,4},{6,7},{7,6},{8,9},{9,8},{10,11... | collective-permute-start | bytes 3145736 | tf_op jit(solution)/shard_map/ppermute | solution.py:185
  82.3 2.3 %broadcast_select_fusion = bf16[4,256,1536]{2,1,0:T(8,128)(2,1)S(1)} fusion(bf16[4,256,1536]{2,1,0:T(8,128)(2,1)} %copy-done, pred[4]{0:T(512)(128)(4,1)S(1)} %get-tuple-element.42), kind=kLoop, calls=%fused_computation.15 | loop fusion | flops 1572864 | bytes 6291460 | tf_op jit(solution)/shard_map/jit(_take)/select_n | solution.py:99
  86.6 2.8 %collective-permute-start.10 = (bf16[256,1536]{1,0:T(8,128)(2,1)S(1)}, bf16[256,1536]{1,0:T(8,128)(2,1)S(1)}, u32[]{:S(2)}, u32[]{:S(2)}) collective-permute-start(bf16[256,1536]{1,0:T(8,128)(2,1)S(1)} %fusion.5), channel_id=1, source_target_pairs={{0,4},{4,8},{1,5},{5,9},{2,6},{6,10},{3,7},{7,11},{16,20},{20,24},... | collective-permute-start | bytes 2359304 | tf_op jit(solution)/shard_map/ppermute | solution.py:198
  92.1 5.5 %collective-permute-start.12 = (bf16[256,1536]{1,0:T(8,128)(2,1)S(1)}, bf16[256,1536]{1,0:T(8,128)(2,1)S(1)}, u32[]{:S(2)}, u32[]{:S(2)}) collective-permute-start(bf16[256,1536]{1,0:T(8,128)(2,1)S(1)} %fusion.6), channel_id=1, source_target_pairs={{0,12},{1,13},{2,14},{3,15},{16,28},{17,29},{18,30},{19,31}} | collective-permute-start | bytes 2359304 | tf_op jit(solution)/shard_map/ppermute | solution.py:201
  97.6 1.3 collective-permute-start.15
  99.9 7.4 %collective-permute-done.10 = bf16[256,1536]{1,0:T(8,128)(2,1)S(1)} collective-permute-done((bf16[256,1536]{1,0:T(8,128)(2,1)S(1)}, bf16[256,1536]{1,0:T(8,128)(2,1)S(1)}, u32[]{:S(2)}, u32[]{:S(2)}) %collective-permute-start.10) | collective-permute-done | bytes 786464 | tf_op jit(solution)/shard_map/ppermute | solution.py:198
  108.3 4.4 %collective-permute-start.11 = (bf16[256,1536]{1,0:T(8,128)(2,1)S(1)}, bf16[256,1536]{1,0:T(8,128)(2,1)S(1)}, u32[]{:S(2)}, u32[]{:S(2)}) collective-permute-start(bf16[256,1536]{1,0:T(8,128)(2,1)S(1)} %fusion.4), channel_id=1, source_target_pairs={{0,4},{4,8},{8,12},{1,5},{5,9},{9,13},{2,6},{6,10},{10,14},{3,7},{... | collective-permute-start | bytes 2359304 | tf_op jit(solution)/shard_map/ppermute | solution.py:212
  113.7 1.3 collective-permute-start.14
  115.0 9.2 %collective-permute-done.12 = bf16[256,1536]{1,0:T(8,128)(2,1)S(1)} collective-permute-done((bf16[256,1536]{1,0:T(8,128)(2,1)S(1)}, bf16[256,1536]{1,0:T(8,128)(2,1)S(1)}, u32[]{:S(2)}, u32[]{:S(2)}) %collective-permute-start.12) | collective-permute-done | bytes 786464 | tf_op jit(solution)/shard_map/ppermute | solution.py:201
  124.2 5.5 %collective-permute-done.15 = bf16[256,1536]{1,0:T(8,128)(2,1)S(1)} collective-permute-done((bf16[256,1536]{1,0:T(8,128)(2,1)S(1)}, bf16[256,1536]{1,0:T(8,128)(2,1)S(1)}, u32[]{:S(2)}, u32[]{:S(2)}) %collective-permute-start.15) | collective-permute-done | bytes 786464 | tf_op jit(solution)/shard_map/ppermute | solution.py:205
  129.7 10.8 %collective-permute-done.11 = bf16[256,1536]{1,0:T(8,128)(2,1)S(1)} collective-permute-done((bf16[256,1536]{1,0:T(8,128)(2,1)S(1)}, bf16[256,1536]{1,0:T(8,128)(2,1)S(1)}, u32[]{:S(2)}, u32[]{:S(2)}) %collective-permute-start.11) | collective-permute-done | bytes 786464 | tf_op jit(solution)/shard_map/ppermute | solution.py:212
  140.5 5.3 %collective-permute-done.14 = bf16[256,1536]{1,0:T(8,128)(2,1)S(1)} collective-permute-done((bf16[256,1536]{1,0:T(8,128)(2,1)S(1)}, bf16[256,1536]{1,0:T(8,128)(2,1)S(1)}, u32[]{:S(2)}, u32[]{:S(2)}) %collective-permute-start.14) | collective-permute-done | bytes 786464 | tf_op jit(solution)/shard_map/ppermute | solution.py:207
  145.7 1.4 add_convert_fusion
  (84 shorter events, 20.0 us)
Async XLA Ops:
  6.4 1.8 %copy-start.2 = (bf16[256,1024]{0,1:T(8,128)(2,1)}, bf16[256,1024]{0,1:T(8,128)(2,1)S(1)}, u32[]{:S(2)}) copy-start(bf16[256,1024]{0,1:T(8,128)(2,1)S(1)} %multiply_convert_fusion.5) | copy-start | bytes 1572868
  6.4 16.3 %copy-start.7 = (s32[1536]{0:T(1024)S(1)}, s32[1536]{0:T(1024)}, u32[]{:S(2)}) copy-start(s32[1536]{0:T(1024)} %param.17) | copy-start | bytes 18436
  6.5 16.3 %copy-start.1 = (bf16[1024,1536]{1,0:T(8,128)(2,1)S(1)}, bf16[1024,1536]{1,0:T(8,128)(2,1)}, u32[]{:S(2)}) copy-start(bf16[1024,1536]{1,0:T(8,128)(2,1)} %param.16) | copy-start | bytes 9437188
  8.3 0.8 copy-start.3
  10.2 29.4 %collective-permute-start = (bf16[8,16640]{1,0:T(8,128)(2,1)}, bf16[8,16640]{1,0:T(8,128)(2,1)S(1)}, u32[]{:S(2)}, u32[]{:S(2)}) collective-permute-start(bf16[8,16640]{1,0:T(8,128)(2,1)} %pad_maximum_fusion.3), channel_id=1, source_target_pairs={{0,4},{4,8},{8,12},{1,5},{5,9},{9,13},{2,6},{6,10},{10,14},{3,7},{... | collective-permute-start | bytes 798728 | tf_op jit(solution)/shard_map/ppermute | solution.py:107
  15.2 24.4 %collective-permute-start.1 = (bf16[8,16640]{1,0:T(8,128)(2,1)}, bf16[8,16640]{1,0:T(8,128)(2,1)}, u32[]{:S(2)}, u32[]{:S(2)}) collective-permute-start(bf16[8,16640]{1,0:T(8,128)(2,1)} %pad_maximum_fusion.3), channel_id=1, source_target_pairs={{0,8},{4,12},{1,9},{5,13},{2,10},{6,14},{3,11},{7,15},{16,24},{20,... | collective-permute-start | bytes 798728 | tf_op jit(solution)/shard_map/ppermute | solution.py:107
  20.4 20.2 %collective-permute-start.2 = (bf16[8,16640]{1,0:T(8,128)(2,1)}, bf16[8,16640]{1,0:T(8,128)(2,1)}, u32[]{:S(2)}, u32[]{:S(2)}) collective-permute-start(bf16[8,16640]{1,0:T(8,128)(2,1)} %pad_maximum_fusion.3), channel_id=1, source_target_pairs={{0,12},{1,13},{2,14},{3,15},{16,28},{17,29},{18,30},{19,31}} | collective-permute-start | bytes 798728 | tf_op jit(solution)/shard_map/ppermute | solution.py:107
  28.1 11.5 %copy-start = (bf16[4,256,1536]{2,1,0:T(8,128)(2,1)}, bf16[4,256,1536]{2,1,0:T(8,128)(2,1)S(1)}, u32[]{:S(2)}) copy-start(bf16[4,256,1536]{2,1,0:T(8,128)(2,1)S(1)} %gather_fusion) | copy-start | bytes 9437188
  39.6 2.5 %copy-start.5 = (bf16[256,1024]{0,1:T(8,128)(2,1)S(1)}, bf16[256,1024]{0,1:T(8,128)(2,1)}, u32[]{:S(2)}) copy-start(bf16[256,1024]{0,1:T(8,128)(2,1)} %fusion.16) | copy-start | bytes 1572868
  39.6 2.5 %copy-start.6 = (f32[1,256,8,128]{1,3,2,0:T(8,128)S(1)}, f32[1,256,8,128]{1,3,2,0:T(8,128)}, u32[]{:S(2)}) copy-start(f32[1,256,8,128]{1,3,2,0:T(8,128)} %fusion.10) | copy-start | bytes 3145732
  42.1 1.0 copy-start.4
  42.1 1.0 copy-start.8
  43.5 7.6 %collective-permute-start.3 = (bf16[256,2,256]{0,2,1:T(8,128)(2,1)S(1)}, bf16[256,2,256]{0,2,1:T(8,128)(2,1)S(1)}, u32[]{:S(2)}, u32[]{:S(2)}) collective-permute-start(bf16[256,2,256]{0,2,1:T(8,128)(2,1)S(1)} %get-tuple-element.32), channel_id=1, source_target_pairs={{0,2},{1,3},{2,0},{3,1},{4,6},{5,7},{6,4},{7,5},{8,10},{9,11},{10,... | collective-permute-start | bytes 786440 | tf_op jit(solution)/shard_map/ppermute | solution.py:146
  51.3 7.6 %collective-permute-start.4 = (bf16[256,256]{1,0:T(8,128)(2,1)S(1)}, bf16[256,256]{1,0:T(8,128)(2,1)S(1)}, u32[]{:S(2)}, u32[]{:S(2)}) collective-permute-start(bf16[256,256]{1,0:T(8,128)(2,1)S(1)} %bitcast.191), channel_id=1, source_target_pairs={{0,0},{1,4},{2,10},{3,14},{4,1},{5,5},{6,11},{7,15},{8,8},{9,12},{... | collective-permute-start | bytes 393224 | tf_op jit(solution)/shard_map/ppermute | solution.py:157
  52.1 8.9 %collective-permute-start.5 = (bf16[256,256]{1,0:T(8,128)(2,1)S(1)}, bf16[256,256]{1,0:T(8,128)(2,1)S(1)}, u32[]{:S(2)}, u32[]{:S(2)}) collective-permute-start(bf16[256,256]{1,0:T(8,128)(2,1)S(1)} %bitcast.192), channel_id=1, source_target_pairs={{0,1},{1,5},{2,11},{3,15},{4,8},{5,12},{6,2},{7,6},{8,9},{9,13},{1... | collective-permute-start | bytes 393224 | tf_op jit(solution)/shard_map/ppermute | solution.py:157
  53.4 13.3 %collective-permute-start.6 = (bf16[256,256]{1,0:T(8,128)(2,1)S(1)}, bf16[256,256]{1,0:T(8,128)(2,1)S(1)}, u32[]{:S(2)}, u32[]{:S(2)}) collective-permute-start(bf16[256,256]{1,0:T(8,128)(2,1)S(1)} %bitcast.193), channel_id=1, source_target_pairs={{0,8},{1,12},{2,2},{3,6},{4,9},{5,13},{6,3},{7,7},{8,0},{9,4},{10,... | collective-permute-start | bytes 393224 | tf_op jit(solution)/shard_map/ppermute | solution.py:157
  58.8 7.9 %collective-permute-start.7 = (bf16[256,256]{1,0:T(8,128)(2,1)S(1)}, bf16[256,256]{1,0:T(8,128)(2,1)S(1)}, u32[]{:S(2)}, u32[]{:S(2)}) collective-permute-start(bf16[256,256]{1,0:T(8,128)(2,1)S(1)} %bitcast.194), channel_id=1, source_target_pairs={{0,9},{1,13},{2,3},{3,7},{4,0},{5,4},{6,10},{7,14},{8,1},{9,5},{10... | collective-permute-start | bytes 393224 | tf_op jit(solution)/shard_map/ppermute | solution.py:157
  67.4 13.2 %collective-permute-start.8 = (bf16[4,256,256]{2,1,0:T(8,128)(2,1)S(1)}, bf16[4,256,256]{2,1,0:T(8,128)(2,1)S(1)}, u32[]{:S(2)}, u32[]{:S(2)}) collective-permute-start(bf16[4,256,256]{2,1,0:T(8,128)(2,1)S(1)} %broadcast_select_fusion.1), channel_id=1, source_target_pairs={{0,2},{1,3},{2,0},{3,1},{4,6},{5,7},{6,4},{7,5},{8,10},{9,11},{10,... | collective-permute-start | bytes 1572872 | tf_op jit(solution)/shard_map/ppermute | solution.py:183
  80.8 3.8 %collective-permute-start.9 = (bf16[2,4,256,256]{3,2,0,1:T(8,128)(2,1)S(1)}, bf16[2,4,256,256]{3,2,0,1:T(8,128)(2,1)S(1)}, u32[]{:S(2)}, u32[]{:S(2)}) collective-permute-start(bf16[2,4,256,256]{3,2,0,1:T(8,128)(2,1)S(1)} %get-tuple-element.27), channel_id=1, source_target_pairs={{0,1},{1,0},{2,3},{3,2},{4,5},{5,4},{6,7},{7,6},{8,9},{9,8},{10,11... | collective-permute-start | bytes 3145736 | tf_op jit(solution)/shard_map/ppermute | solution.py:185
  86.6 20.6 %collective-permute-start.10 = (bf16[256,1536]{1,0:T(8,128)(2,1)S(1)}, bf16[256,1536]{1,0:T(8,128)(2,1)S(1)}, u32[]{:S(2)}, u32[]{:S(2)}) collective-permute-start(bf16[256,1536]{1,0:T(8,128)(2,1)S(1)} %fusion.5), channel_id=1, source_target_pairs={{0,4},{4,8},{1,5},{5,9},{2,6},{6,10},{3,7},{7,11},{16,20},{20,24},... | collective-permute-start | bytes 2359304 | tf_op jit(solution)/shard_map/ppermute | solution.py:198
  90.4 22.3 %collective-permute-start.13 = (bf16[256,1536]{1,0:T(8,128)(2,1)S(1)}, bf16[256,1536]{1,0:T(8,128)(2,1)S(1)}, u32[]{:S(2)}, u32[]{:S(2)}) collective-permute-start(bf16[256,1536]{1,0:T(8,128)(2,1)S(1)} %fusion.7), channel_id=1, source_target_pairs={{12,8},{8,4},{13,9},{9,5},{14,10},{10,6},{15,11},{11,7},{28,24},{2... | collective-permute-start | bytes 2359304 | tf_op jit(solution)/shard_map/ppermute | solution.py:202
  92.1 32.1 %collective-permute-start.12 = (bf16[256,1536]{1,0:T(8,128)(2,1)S(1)}, bf16[256,1536]{1,0:T(8,128)(2,1)S(1)}, u32[]{:S(2)}, u32[]{:S(2)}) collective-permute-start(bf16[256,1536]{1,0:T(8,128)(2,1)S(1)} %fusion.6), channel_id=1, source_target_pairs={{0,12},{1,13},{2,14},{3,15},{16,28},{17,29},{18,30},{19,31}} | collective-permute-start | bytes 2359304 | tf_op jit(solution)/shard_map/ppermute | solution.py:201
  97.6 32.1 %collective-permute-start.15 = (bf16[256,1536]{1,0:T(8,128)(2,1)S(1)}, bf16[256,1536]{1,0:T(8,128)(2,1)S(1)}, u32[]{:S(2)}, u32[]{:S(2)}) collective-permute-start(bf16[256,1536]{1,0:T(8,128)(2,1)S(1)} %fusion.8), channel_id=1, source_target_pairs={{12,0},{13,1},{14,2},{15,3},{28,16},{29,17},{30,18},{31,19}} | collective-permute-start | bytes 2359304 | tf_op jit(solution)/shard_map/ppermute | solution.py:205
  108.3 32.2 %collective-permute-start.11 = (bf16[256,1536]{1,0:T(8,128)(2,1)S(1)}, bf16[256,1536]{1,0:T(8,128)(2,1)S(1)}, u32[]{:S(2)}, u32[]{:S(2)}) collective-permute-start(bf16[256,1536]{1,0:T(8,128)(2,1)S(1)} %fusion.4), channel_id=1, source_target_pairs={{0,4},{4,8},{8,12},{1,5},{5,9},{9,13},{2,6},{6,10},{10,14},{3,7},{... | collective-permute-start | bytes 2359304 | tf_op jit(solution)/shard_map/ppermute | solution.py:212
  113.7 32.1 %collective-permute-start.14 = (bf16[256,1536]{1,0:T(8,128)(2,1)S(1)}, bf16[256,1536]{1,0:T(8,128)(2,1)S(1)}, u32[]{:S(2)}, u32[]{:S(2)}) collective-permute-start(bf16[256,1536]{1,0:T(8,128)(2,1)S(1)} %fusion.3), channel_id=1, source_target_pairs={{12,8},{8,4},{4,0},{13,9},{9,5},{5,1},{14,10},{10,6},{6,2},{15,11}... | collective-permute-start | bytes 2359304 | tf_op jit(solution)/shard_map/ppermute | solution.py:207
